TPU v7x, 512 devices: a whole 4x8x8 slice. The times are simulated.
512 devices in a mesh: seq: 64 (over z, y), dp: 8 (over x, core).
Axes of the slice: x: 4, y: 8, z: 8, core: 2. Of those that a mesh axis runs over, the one named last changes fastest.
Arguments:
- queries: bfloat16 [8192, 2048], P('seq', 'dp'), may hold values from -11 to 11
- keys: bfloat16 [8192, 2048], P('seq', 'dp'), may hold values from -6 to 6
- values: bfloat16 [8192, 2048], P('seq', 'dp'), may hold values from -12 to 12
- cotangent: bfloat16 [8192, 2048], P('seq', 'dp'), may hold values from -16 to 16
- out_weight: bfloat16 [2048, 2048], P('seq', 'dp'), may hold values from -0.125 to 0.125
Outputs:
- attended: bfloat16 [8192, 2048], P('seq', 'dp')
- grad_queries: bfloat16 [8192, 2048], P('seq', 'dp')
- grad_keys: bfloat16 [8192, 2048], P('seq', 'dp')
- grad_values: bfloat16 [8192, 2048], P('seq', 'dp')
- grad_out_weight: float32 [2048, 2048], P('seq', 'dp')
All inputs are finite; a program needn't handle non-finite values.
Results may differ from a plain program's by a relative error of at most 0.008.
Values may be sent and summed in bfloat16 or wider, within the bound.
No kernel may reach another device: no remote copies, remote signals or barrier semaphores. Data moves between devices by JAX's collectives and lax.ppermute only.
A program may use at most 64 MiB of HBM per device.

v0:
```python
import math

import jax
import jax.numpy as jnp
from jax import lax
from jax.sharding import Mesh
from jax.sharding import PartitionSpec as P

HEAD = 128
SEQ = ("seq_0", "seq_1")


def from_partner(block, axis, apart):
    count = lax.axis_size(axis)
    route = []
    for low in range(count):
        high = low | 1 << apart
        if high != low and high < count:
            route += [(low, high), (high, low)]
    return lax.ppermute(block, axis, route)


def joined_along(blocks, dim):
    blocks = jnp.moveaxis(blocks, 0, dim)
    dims = blocks.shape
    return blocks.reshape(*dims[:dim], dims[dim] * dims[dim + 1], *dims[dim + 2 :])


def from_everyone(x, axis):
    copies = jnp.broadcast_to(x, (lax.axis_size(axis), *x.shape))
    return lax.all_to_all(copies, axis, split_axis=0, concat_axis=0, tiled=True)


def gathered_copies(x, axis, dim):
    return joined_along(from_everyone(x, axis), dim)


def own_rows(running, axes):
    for axis in axes:
        running = lax.psum_scatter(running, axis, scatter_dimension=0, tiled=True)
    return running


def pair_mean(table):
    paired = table.reshape(table.shape[0], table.shape[1] // 2, 2, table.shape[2])
    return (paired[:, :, 0] + paired[:, :, 1]) * 0.5


def spread_rows(table):
    doubled = jnp.broadcast_to(
        table[:, :, None], (table.shape[0], table.shape[1], 2, table.shape[2])
    )
    return doubled.reshape(table.shape[0], table.shape[1] * 2, table.shape[2])


def on_device(queries, keys, values, cotangent, out_weight):
    tokens = queries.shape[0]
    width = queries.shape[1]
    heads = width // HEAD
    coarse = tokens // 2
    scale = 1.0 / math.sqrt(HEAD)
    depth = lax.axis_size(SEQ).bit_length() - 1
    position = lax.axis_index(SEQ)
    own_table = pair_mean(jnp.stack([keys, values]).astype(jnp.float32))
    far_keys = []
    far_values = []
    for layer_bit in range(depth):
        far_table = from_partner(own_table, SEQ, layer_bit)
        far_keys.append(far_table[0].astype(jnp.bfloat16))
        far_values.append(far_table[1].astype(jnp.bfloat16))
        if layer_bit + 1 < depth:
            lower_half = position >> layer_bit & 1 == 0
            joined = jnp.concatenate(
                [
                    jnp.where(lower_half, own_table, far_table),
                    jnp.where(lower_half, far_table, own_table),
                ],
                axis=1,
            )
            own_table = pair_mean(joined)
    key_set = jnp.concatenate([keys] + far_keys, axis=0)
    value_set = jnp.concatenate([values] + far_values, axis=0)
    full_cot = gathered_copies(cotangent, "dp", 1)
    full_weight = gathered_copies(out_weight, SEQ, 0)
    grad_attended = jnp.dot(full_cot, full_weight, preferred_element_type=jnp.float32).astype(
        jnp.bfloat16
    )
    attended_parts = []
    grad_query_parts = []
    grad_key_parts = []
    grad_value_parts = []
    for head in range(heads):
        low = head * HEAD
        high = low + HEAD
        query_head = queries[:, low:high]
        key_head = key_set[:, low:high]
        value_head = value_set[:, low:high]
        grad_head = grad_attended[:, low:high]
        scores = (
            jnp.einsum("ta,ka->tk", query_head, key_head, preferred_element_type=jnp.float32)
            * scale
        )
        peak = jnp.max(scores, axis=-1, keepdims=True)
        expo = jnp.exp(scores - peak)
        prob = expo / jnp.sum(expo, axis=-1, keepdims=True)
        weights = prob.astype(jnp.bfloat16)
        attended_parts.append(
            jnp.dot(weights, value_head, preferred_element_type=jnp.float32).astype(jnp.bfloat16)
        )
        grad_weights = jnp.einsum(
            "ta,ka->tk", grad_head, value_head, preferred_element_type=jnp.float32
        )
        delta = jnp.sum(prob * grad_weights, axis=-1, keepdims=True)
        grad_scores = (prob * (grad_weights - delta) * scale).astype(jnp.bfloat16)
        grad_query_parts.append(
            jnp.dot(grad_scores, key_head, preferred_element_type=jnp.float32).astype(jnp.bfloat16)
        )
        grad_key_parts.append(
            jnp.einsum("tk,ta->ka", grad_scores, query_head, preferred_element_type=jnp.float32)
        )
        grad_value_parts.append(
            jnp.einsum("tk,ta->ka", weights, grad_head, preferred_element_type=jnp.float32)
        )
    attended = jnp.concatenate(attended_parts, axis=1)
    grad_queries = jnp.concatenate(grad_query_parts, axis=1)
    grad_sets = jnp.stack(
        [jnp.concatenate(grad_key_parts, axis=1), jnp.concatenate(grad_value_parts, axis=1)]
    )
    carried = jnp.zeros((2, coarse, width), jnp.float32)
    for layer_bit in reversed(range(depth)):
        first = tokens + layer_bit * coarse
        outgoing = grad_sets[:, first : first + coarse]
        kept = jnp.zeros((2, coarse, width), jnp.float32)
        if layer_bit + 1 < depth:
            lower_half = position >> layer_bit & 1 == 0
            spread = spread_rows(carried * 0.5)
            low_part = spread[:, :coarse]
            high_part = spread[:, coarse:]
            kept = jnp.where(lower_half, low_part, high_part)
            outgoing = outgoing + jnp.where(lower_half, high_part, low_part)
        incoming = from_partner(outgoing.astype(jnp.bfloat16), SEQ, layer_bit).astype(
            outgoing.dtype
        )
        carried = kept + incoming
    own_grads = grad_sets[:, :tokens] + spread_rows(carried * 0.5)
    grad_keys = own_grads[0].astype(jnp.bfloat16)
    grad_values = own_grads[1].astype(jnp.bfloat16)
    grad_out_weight = own_rows(
        lax.dot_general(
            full_cot, attended, (((0,), (0,)), ((), ())), preferred_element_type=jnp.float32
        ),
        SEQ,
    )
    return (attended, grad_queries, grad_keys, grad_values, grad_out_weight)


def solution(mesh):
    torus = Mesh(mesh.devices.reshape(8, 8, mesh.shape["dp"]), ("seq_0", "seq_1", "dp"))
    placed = (P(SEQ, "dp"), P(SEQ, "dp"), P(SEQ, "dp"), P(SEQ, "dp"), P(SEQ, "dp"))
    return jax.shard_map(
        on_device,
        mesh=torus,
        in_specs=placed,
        out_specs=(P(SEQ, "dp"), P(SEQ, "dp"), P(SEQ, "dp"), P(SEQ, "dp"), P(SEQ, "dp")),
        check_vma=False,
    )
```

profile of v0, /device:TPU:6, one launch (start us, length us, event | category | flops | bytes accessed | tf_op | source)
XLA Modules:
  0.0 207.9 jit_solution(13050485067645373853)
XLA Ops:
  7.2 0.9 stack.18
  8.1 0.9 stack.19
  9.1 3.5 %collective-permute-start = (f32[2,64,256]{2,1,0:T(8,128)S(1)}, f32[2,64,256]{2,1,0:T(8,128)S(1)}, u32[]{:S(2)}, u32[]{:S(2)}) collective-permute-start(f32[2,64,256]{2,1,0:T(8,128)S(1)} %fusion.30), channel_id=1, source_target_pairs={{0,8},{8,0},{16,24},{24,16},{32,40},{40,32},{48,56},{56,48},{64,72... | collective-permute-start | bytes 393224 | tf_op jit(solution)/shard_map/ppermute | solution.py:20
  12.6 1.0 copy.164
  13.5 0.9 broadcast_in_dim.16
  14.4 7.7 %all-to-all-start = ((bf16[8,128,256]{1,2,0:T(8,128)(2,1)}), bf16[8,128,256]{1,2,0:T(8,128)(2,1)S(1)}, u32[]{:S(2)}, u32[]{:S(2)}) async-start(bf16[8,128,256]{1,2,0:T(8,128)(2,1)} %broadcast_in_dim.16), calls=%async_computation | async-start | bytes 1048576 | tf_op jit(solution)/shard_map/all_to_all | solution.py:31
  22.2 0.2 copy.149
  22.5 1.9 collective-permute-start.1
  24.5 9.2 %collective-permute-done.1 = f32[2,64,256]{2,1,0:T(8,128)S(1)} collective-permute-done((f32[2,64,256]{2,1,0:T(8,128)S(1)}, f32[2,64,256]{2,1,0:T(8,128)S(1)}, u32[]{:S(2)}, u32[]{:S(2)}) %collective-permute-start.1) | collective-permute-done | bytes 131104 | tf_op jit(solution)/shard_map/ppermute | solution.py:20
  33.7 0.2 copy.152
  34.0 3.9 %collective-permute-start.2 = (f32[2,64,256]{2,1,0:T(8,128)S(1)}, f32[2,64,256]{2,1,0:T(8,128)S(1)}, u32[]{:S(2)}, u32[]{:S(2)}) collective-permute-start(f32[2,64,256]{2,1,0:T(8,128)S(1)} %fusion.38), channel_id=1, source_target_pairs={{0,32},{32,0},{8,40},{40,8},{16,48},{48,16},{24,56},{56,24},{64,96... | collective-permute-start | bytes 393224 | tf_op jit(solution)/shard_map/ppermute | solution.py:20
  38.0 8.0 %collective-permute-done.2 = f32[2,64,256]{2,1,0:T(8,128)S(1)} collective-permute-done((f32[2,64,256]{2,1,0:T(8,128)S(1)}, f32[2,64,256]{2,1,0:T(8,128)S(1)}, u32[]{:S(2)}, u32[]{:S(2)}) %collective-permute-start.2) | collective-permute-done | bytes 131104 | tf_op jit(solution)/shard_map/ppermute | solution.py:20
  46.0 0.2 copy.155
  46.3 3.3 %collective-permute-start.3 = (f32[2,64,256]{2,1,0:T(8,128)S(1)}, f32[2,64,256]{2,1,0:T(8,128)S(1)}, u32[]{:S(2)}, u32[]{:S(2)}) collective-permute-start(f32[2,64,256]{2,1,0:T(8,128)S(1)} %fusion.36), channel_id=1, source_target_pairs={{0,64},{64,0},{8,72},{72,8},{16,80},{80,16},{24,88},{88,24},{32,96... | collective-permute-start | bytes 393224 | tf_op jit(solution)/shard_map/ppermute | solution.py:20
  49.7 3.6 %collective-permute-done.3 = f32[2,64,256]{2,1,0:T(8,128)S(1)} collective-permute-done((f32[2,64,256]{2,1,0:T(8,128)S(1)}, f32[2,64,256]{2,1,0:T(8,128)S(1)}, u32[]{:S(2)}, u32[]{:S(2)}) %collective-permute-start.3) | collective-permute-done | bytes 131104 | tf_op jit(solution)/shard_map/ppermute | solution.py:20
  53.4 0.2 copy.158
  53.7 5.4 %collective-permute-start.4 = (f32[2,64,256]{2,1,0:T(8,128)S(1)}, f32[2,64,256]{2,1,0:T(8,128)S(1)}, u32[]{:S(2)}, u32[]{:S(2)}) collective-permute-start(f32[2,64,256]{2,1,0:T(8,128)S(1)} %fusion.34), channel_id=1, source_target_pairs={{0,128},{128,0},{8,136},{136,8},{16,144},{144,16},{24,152},{152,24... | collective-permute-start | bytes 393224 | tf_op jit(solution)/shard_map/ppermute | solution.py:20
  59.1 4.8 %collective-permute-done.4 = f32[2,64,256]{2,1,0:T(8,128)S(1)} collective-permute-done((f32[2,64,256]{2,1,0:T(8,128)S(1)}, f32[2,64,256]{2,1,0:T(8,128)S(1)}, u32[]{:S(2)}, u32[]{:S(2)}) %collective-permute-start.4) | collective-permute-done | bytes 131104 | tf_op jit(solution)/shard_map/ppermute | solution.py:20
  63.9 0.2 copy.161
  64.1 1.1 broadcast_in_dim.17
  65.3 11.4 %all-to-all-start.1 = ((bf16[64,32,256]{2,1,0:T(8,128)(2,1)}), bf16[64,32,256]{2,1,0:T(8,128)(2,1)S(1)}, u32[]{:S(2)}, u32[]{:S(2)}) async-start(bf16[64,32,256]{2,1,0:T(8,128)(2,1)} %broadcast_in_dim.17), calls=%async_computation.1 | async-start | bytes 2097152 | tf_op jit(solution)/shard_map/all_to_all | solution.py:31
  76.8 7.5 %collective-permute-start.5 = (bf16[2,64,256]{2,1,0:T(8,128)(2,1)S(1)}, bf16[2,64,256]{2,1,0:T(8,128)(2,1)S(1)}, u32[]{:S(2)}, u32[]{:S(2)}) collective-permute-start(bf16[2,64,256]{2,1,0:T(8,128)(2,1)S(1)} %fusion.32), channel_id=1, source_target_pairs={{0,256},{256,0},{8,264},{264,8},{16,272},{272,16},{24,280},{280,24... | collective-permute-start | bytes 196616 | tf_op jit(solution)/shard_map/ppermute | solution.py:20
  84.3 23.0 %collective-permute-done.5 = bf16[2,64,256]{2,1,0:T(8,128)(2,1)S(1)} collective-permute-done((bf16[2,64,256]{2,1,0:T(8,128)(2,1)S(1)}, bf16[2,64,256]{2,1,0:T(8,128)(2,1)S(1)}, u32[]{:S(2)}, u32[]{:S(2)}) %collective-permute-start.5) | collective-permute-done | bytes 65568 | tf_op jit(solution)/shard_map/ppermute | solution.py:20
  107.3 0.2 fusion.89
  107.5 0.1 fusion.12
  107.6 0.2 fusion.90
  107.9 0.1 fusion.10
  108.0 0.2 convolution_convert_fusion.3
  108.2 0.2 convolution_convert_fusion.4
  108.4 0.4 convolution_convert_fusion
  108.8 0.2 fusion.51
  109.0 0.2 fusion.52
  109.2 0.2 fusion.3
  109.4 0.2 fusion.6
  109.7 0.1 fusion.8
  109.8 0.2 fusion.72
  109.9 0.1 fusion.5
  110.0 0.2 fusion.69
  110.3 3.1 %collective-permute-start.6 = (bf16[2,64,256]{2,1,0:T(8,128)(2,1)S(1)}, bf16[2,64,256]{2,1,0:T(8,128)(2,1)S(1)}, u32[]{:S(2)}, u32[]{:S(2)}) collective-permute-start(bf16[2,64,256]{2,1,0:T(8,128)(2,1)S(1)} %fusion.17), channel_id=1, source_target_pairs={{0,256},{256,0},{8,264},{264,8},{16,272},{272,16},{24,280},{280,24... | collective-permute-start | bytes 196616 | tf_op jit(solution)/shard_map/ppermute | solution.py:20
  113.5 1.8 convolution_bitcast_fusion
  115.3 5.1 %collective-permute-done.6 = bf16[2,64,256]{2,1,0:T(8,128)(2,1)S(1)} collective-permute-done((bf16[2,64,256]{2,1,0:T(8,128)(2,1)S(1)}, bf16[2,64,256]{2,1,0:T(8,128)(2,1)S(1)}, u32[]{:S(2)}, u32[]{:S(2)}) %collective-permute-start.6) | collective-permute-done | bytes 65568 | tf_op jit(solution)/shard_map/ppermute | solution.py:20
  120.4 0.1 copy.173
  120.6 2.4 %collective-permute-start.7 = (bf16[2,64,256]{2,1,0:T(8,128)(2,1)S(1)}, bf16[2,64,256]{2,1,0:T(8,128)(2,1)S(1)}, u32[]{:S(2)}, u32[]{:S(2)}) collective-permute-start(bf16[2,64,256]{2,1,0:T(8,128)(2,1)S(1)} %fusion.20), channel_id=1, source_target_pairs={{0,128},{128,0},{8,136},{136,8},{16,144},{144,16},{24,152},{152,24... | collective-permute-start | bytes 196616 | tf_op jit(solution)/shard_map/ppermute | solution.py:20
  123.1 5.3 %collective-permute-done.7 = bf16[2,64,256]{2,1,0:T(8,128)(2,1)S(1)} collective-permute-done((bf16[2,64,256]{2,1,0:T(8,128)(2,1)S(1)}, bf16[2,64,256]{2,1,0:T(8,128)(2,1)S(1)}, u32[]{:S(2)}, u32[]{:S(2)}) %collective-permute-start.7) | collective-permute-done | bytes 65568 | tf_op jit(solution)/shard_map/ppermute | solution.py:20
  128.4 0.1 copy.176
  128.6 1.9 collective-permute-start.8
  130.6 0.7 copy.190
  131.3 4.4 %collective-permute-done.8 = bf16[2,64,256]{2,1,0:T(8,128)(2,1)S(1)} collective-permute-done((bf16[2,64,256]{2,1,0:T(8,128)(2,1)S(1)}, bf16[2,64,256]{2,1,0:T(8,128)(2,1)S(1)}, u32[]{:S(2)}, u32[]{:S(2)}) %collective-permute-start.8) | collective-permute-done | bytes 65568 | tf_op jit(solution)/shard_map/ppermute | solution.py:20
  135.7 0.1 copy.179
  136.0 6.7 %collective-permute-start.9 = (bf16[2,64,256]{2,1,0:T(8,128)(2,1)S(1)}, bf16[2,64,256]{2,1,0:T(8,128)(2,1)S(1)}, u32[]{:S(2)}, u32[]{:S(2)}) collective-permute-start(bf16[2,64,256]{2,1,0:T(8,128)(2,1)S(1)} %fusion.26), channel_id=1, source_target_pairs={{0,32},{32,0},{8,40},{40,8},{16,48},{48,16},{24,56},{56,24},{64,96... | collective-permute-start | bytes 196616 | tf_op jit(solution)/shard_map/ppermute | solution.py:20
  142.6 0.2 convolution_convert_fusion.1
  142.9 3.3 %collective-permute-done.9 = bf16[2,64,256]{2,1,0:T(8,128)(2,1)S(1)} collective-permute-done((bf16[2,64,256]{2,1,0:T(8,128)(2,1)S(1)}, bf16[2,64,256]{2,1,0:T(8,128)(2,1)S(1)}, u32[]{:S(2)}, u32[]{:S(2)}) %collective-permute-start.9) | collective-permute-done | bytes 65568 | tf_op jit(solution)/shard_map/ppermute | solution.py:20
  146.2 0.1 copy.182
  146.4 3.7 %collective-permute-start.10 = (bf16[2,64,256]{2,1,0:T(8,128)(2,1)S(1)}, bf16[2,64,256]{2,1,0:T(8,128)(2,1)S(1)}, u32[]{:S(2)}, u32[]{:S(2)}) collective-permute-start(bf16[2,64,256]{2,1,0:T(8,128)(2,1)S(1)} %fusion.15), channel_id=1, source_target_pairs={{0,16},{16,0},{8,24},{24,8},{32,48},{48,32},{40,56},{56,40},{64,80... | collective-permute-start | bytes 196616 | tf_op jit(solution)/shard_map/ppermute | solution.py:20
  150.1 0.2 convolution_convert_fusion.2
  150.4 3.8 %collective-permute-done.10 = bf16[2,64,256]{2,1,0:T(8,128)(2,1)S(1)} collective-permute-done((bf16[2,64,256]{2,1,0:T(8,128)(2,1)S(1)}, bf16[2,64,256]{2,1,0:T(8,128)(2,1)S(1)}, u32[]{:S(2)}, u32[]{:S(2)}) %collective-permute-start.10) | collective-permute-done | bytes 65568 | tf_op jit(solution)/shard_map/ppermute | solution.py:20
  154.2 0.1 copy.185
  154.4 2.1 collective-permute-start.11
  156.5 0.7 copy.191
  157.3 3.2 %reduce-scatter.5.cloned.1.call-done = f32[256,256]{0,1:T(8,128)} async-done(((f32[2048,256]{0,1:T(8,128)}), f32[256,256]{0,1:T(8,128)}) %reduce-scatter.5.cloned.1.call-update) | async-done | bytes 262160 | tf_op jit(solution)/shard_map/reduce_scatter | solution.py:40
  160.5 1.8 copy.199
  162.4 0.1 copy.188
  162.6 0.7 slice_bitcast_fusion
  163.3 37.8 %reduce-scatter.7.cloned.1.call-done = f32[32,256]{1,0:T(8,128)} async-done(((f32[256,256]{1,0:T(8,128)}), f32[32,256]{1,0:T(8,128)}) %reduce-scatter.7.cloned.1.call-update) | async-done | bytes 32784
  (75 shorter events, 1.8 us)
Async XLA Ops:
  7.2 15.0 %copy-start = (bf16[128,256]{1,0:T(8,128)(2,1)S(1)}, bf16[128,256]{1,0:T(8,128)(2,1)}, u32[]{:S(2)}) copy-start(bf16[128,256]{1,0:T(8,128)(2,1)} %param.6) | copy-start | bytes 196612
  7.2 15.0 %copy-start.1 = (bf16[128,256]{1,0:T(8,128)(2,1)S(1)}, bf16[128,256]{1,0:T(8,128)(2,1)}, u32[]{:S(2)}) copy-start(bf16[128,256]{1,0:T(8,128)(2,1)} %param.7) | copy-start | bytes 196612
  9.1 13.1 %collective-permute-start = (f32[2,64,256]{2,1,0:T(8,128)S(1)}, f32[2,64,256]{2,1,0:T(8,128)S(1)}, u32[]{:S(2)}, u32[]{:S(2)}) collective-permute-start(f32[2,64,256]{2,1,0:T(8,128)S(1)} %fusion.30), channel_id=1, source_target_pairs={{0,8},{8,0},{16,24},{24,16},{32,40},{40,32},{48,56},{56,48},{64,72... | collective-permute-start | bytes 393224 | tf_op jit(solution)/shard_map/ppermute | solution.py:20
  14.4 49.7 %all-to-all-start = ((bf16[8,128,256]{1,2,0:T(8,128)(2,1)}), bf16[8,128,256]{1,2,0:T(8,128)(2,1)S(1)}, u32[]{:S(2)}, u32[]{:S(2)}) async-start(bf16[8,128,256]{1,2,0:T(8,128)(2,1)} %broadcast_in_dim.16), calls=%async_computation | async-start | bytes 1048576 | tf_op jit(solution)/shard_map/all_to_all | solution.py:31
  22.5 11.2 %collective-permute-start.1 = (f32[2,64,256]{2,1,0:T(8,128)S(1)}, f32[2,64,256]{2,1,0:T(8,128)S(1)}, u32[]{:S(2)}, u32[]{:S(2)}) collective-permute-start(f32[2,64,256]{2,1,0:T(8,128)S(1)} %fusion.40), channel_id=1, source_target_pairs={{0,16},{16,0},{8,24},{24,8},{32,48},{48,32},{40,56},{56,40},{64,80... | collective-permute-start | bytes 393224 | tf_op jit(solution)/shard_map/ppermute | solution.py:20
  34.0 12.0 %collective-permute-start.2 = (f32[2,64,256]{2,1,0:T(8,128)S(1)}, f32[2,64,256]{2,1,0:T(8,128)S(1)}, u32[]{:S(2)}, u32[]{:S(2)}) collective-permute-start(f32[2,64,256]{2,1,0:T(8,128)S(1)} %fusion.38), channel_id=1, source_target_pairs={{0,32},{32,0},{8,40},{40,8},{16,48},{48,16},{24,56},{56,24},{64,96... | collective-permute-start | bytes 393224 | tf_op jit(solution)/shard_map/ppermute | solution.py:20
  46.3 7.0 %collective-permute-start.3 = (f32[2,64,256]{2,1,0:T(8,128)S(1)}, f32[2,64,256]{2,1,0:T(8,128)S(1)}, u32[]{:S(2)}, u32[]{:S(2)}) collective-permute-start(f32[2,64,256]{2,1,0:T(8,128)S(1)} %fusion.36), channel_id=1, source_target_pairs={{0,64},{64,0},{8,72},{72,8},{16,80},{80,16},{24,88},{88,24},{32,96... | collective-permute-start | bytes 393224 | tf_op jit(solution)/shard_map/ppermute | solution.py:20
  49.7 14.4 %copy-start.3 = (bf16[32,256]{1,0:T(8,128)(2,1)S(1)}, bf16[32,256]{1,0:T(8,128)(2,1)}, u32[]{:S(2)}) copy-start(bf16[32,256]{1,0:T(8,128)(2,1)} %param.9) | copy-start | bytes 49156
  53.7 10.1 %collective-permute-start.4 = (f32[2,64,256]{2,1,0:T(8,128)S(1)}, f32[2,64,256]{2,1,0:T(8,128)S(1)}, u32[]{:S(2)}, u32[]{:S(2)}) collective-permute-start(f32[2,64,256]{2,1,0:T(8,128)S(1)} %fusion.34), channel_id=1, source_target_pairs={{0,128},{128,0},{8,136},{136,8},{16,144},{144,16},{24,152},{152,24... | collective-permute-start | bytes 393224 | tf_op jit(solution)/shard_map/ppermute | solution.py:20
  64.1 43.2 %copy-start.2 = (bf16[128,256]{1,0:T(8,128)(2,1)S(1)}, bf16[128,256]{1,0:T(8,128)(2,1)}, u32[]{:S(2)}) copy-start(bf16[128,256]{1,0:T(8,128)(2,1)} %param.5) | copy-start | bytes 196612
  65.3 43.2 %all-to-all-start.1 = ((bf16[64,32,256]{2,1,0:T(8,128)(2,1)}), bf16[64,32,256]{2,1,0:T(8,128)(2,1)S(1)}, u32[]{:S(2)}, u32[]{:S(2)}) async-start(bf16[64,32,256]{2,1,0:T(8,128)(2,1)} %broadcast_in_dim.17), calls=%async_computation.1 | async-start | bytes 2097152 | tf_op jit(solution)/shard_map/all_to_all | solution.py:31
  76.6 83.9 %reduce-scatter.5.cloned.1.call-start = ((), (), s32[]{:S(2)}) async-start(), calls=%async_computation.4 | async-start | bytes 2359296 | tf_op jit(solution)/shard_map/reduce_scatter | solution.py:40
  76.8 30.5 %collective-permute-start.5 = (bf16[2,64,256]{2,1,0:T(8,128)(2,1)S(1)}, bf16[2,64,256]{2,1,0:T(8,128)(2,1)S(1)}, u32[]{:S(2)}, u32[]{:S(2)}) collective-permute-start(bf16[2,64,256]{2,1,0:T(8,128)(2,1)S(1)} %fusion.32), channel_id=1, source_target_pairs={{0,256},{256,0},{8,264},{264,8},{16,272},{272,16},{24,280},{280,24... | collective-permute-start | bytes 196616 | tf_op jit(solution)/shard_map/ppermute | solution.py:20
  110.3 10.1 %collective-permute-start.6 = (bf16[2,64,256]{2,1,0:T(8,128)(2,1)S(1)}, bf16[2,64,256]{2,1,0:T(8,128)(2,1)S(1)}, u32[]{:S(2)}, u32[]{:S(2)}) collective-permute-start(bf16[2,64,256]{2,1,0:T(8,128)(2,1)S(1)} %fusion.17), channel_id=1, source_target_pairs={{0,256},{256,0},{8,264},{264,8},{16,272},{272,16},{24,280},{280,24... | collective-permute-start | bytes 196616 | tf_op jit(solution)/shard_map/ppermute | solution.py:20
  115.3 85.8 %reduce-scatter.7.cloned.1.call-start = ((), (), s32[]{:S(2)}) async-start(), calls=%async_computation.5 | async-start | bytes 294912
  120.6 7.7 %collective-permute-start.7 = (bf16[2,64,256]{2,1,0:T(8,128)(2,1)S(1)}, bf16[2,64,256]{2,1,0:T(8,128)(2,1)S(1)}, u32[]{:S(2)}, u32[]{:S(2)}) collective-permute-start(bf16[2,64,256]{2,1,0:T(8,128)(2,1)S(1)} %fusion.20), channel_id=1, source_target_pairs={{0,128},{128,0},{8,136},{136,8},{16,144},{144,16},{24,152},{152,24... | collective-permute-start | bytes 196616 | tf_op jit(solution)/shard_map/ppermute | solution.py:20
  128.6 7.1 %collective-permute-start.8 = (bf16[2,64,256]{2,1,0:T(8,128)(2,1)S(1)}, bf16[2,64,256]{2,1,0:T(8,128)(2,1)S(1)}, u32[]{:S(2)}, u32[]{:S(2)}) collective-permute-start(bf16[2,64,256]{2,1,0:T(8,128)(2,1)S(1)} %fusion.23), channel_id=1, source_target_pairs={{0,64},{64,0},{8,72},{72,8},{16,80},{80,16},{24,88},{88,24},{32,96... | collective-permute-start | bytes 196616 | tf_op jit(solution)/shard_map/ppermute | solution.py:20
  136.0 10.2 %collective-permute-start.9 = (bf16[2,64,256]{2,1,0:T(8,128)(2,1)S(1)}, bf16[2,64,256]{2,1,0:T(8,128)(2,1)S(1)}, u32[]{:S(2)}, u32[]{:S(2)}) collective-permute-start(bf16[2,64,256]{2,1,0:T(8,128)(2,1)S(1)} %fusion.26), channel_id=1, source_target_pairs={{0,32},{32,0},{8,40},{40,8},{16,48},{48,16},{24,56},{56,24},{64,96... | collective-permute-start | bytes 196616 | tf_op jit(solution)/shard_map/ppermute | solution.py:20
  146.4 7.8 %collective-permute-start.10 = (bf16[2,64,256]{2,1,0:T(8,128)(2,1)S(1)}, bf16[2,64,256]{2,1,0:T(8,128)(2,1)S(1)}, u32[]{:S(2)}, u32[]{:S(2)}) collective-permute-start(bf16[2,64,256]{2,1,0:T(8,128)(2,1)S(1)} %fusion.15), channel_id=1, source_target_pairs={{0,16},{16,0},{8,24},{24,8},{32,48},{48,32},{40,56},{56,40},{64,80... | collective-permute-start | bytes 196616 | tf_op jit(solution)/shard_map/ppermute | solution.py:20
  154.4 7.9 %collective-permute-start.11 = (bf16[2,64,256]{2,1,0:T(8,128)(2,1)S(1)}, bf16[2,64,256]{2,1,0:T(8,128)(2,1)S(1)}, u32[]{:S(2)}, u32[]{:S(2)}) collective-permute-start(bf16[2,64,256]{2,1,0:T(8,128)(2,1)S(1)} %fusion.28), channel_id=1, source_target_pairs={{0,8},{8,0},{16,24},{24,16},{32,40},{40,32},{48,56},{56,48},{64,72... | collective-permute-start | bytes 196616 | tf_op jit(solution)/shard_map/ppermute | solution.py:20
Sparse Core Ops, SparseCore 0:
  115.4 45.1 reduce-scatter.4
  163.9 37.1 reduce-scatter.6
where the time goes:
time: 209 us; the launch traced here: 208 us
  waiting for transfers between devices  111 us (53%)
  starting transfers between devices  64.6 us (31%)
  between operations  14.8 us (7%)
  local copies, waits for them, and re-layouts  11.2 us (5%)
  matrix products  4.7 us (2%)
    ppermute x12, waiting for transfers between devices, from_partner(): return lax.ppermute(block, axis, route)  70.4 us
    ppermute x12, starting transfers between devices, from_partner(): return lax.ppermute(block, axis, route)  45.5 us
    unnamed x3, waiting for transfers between devices  37.8 us
    all_to_all x2, starting transfers between devices, from_everyone(): return lax.all_to_all(copies, axis, split_axis=0, concat_axis=0, tiled=True)  19.1 us
    unnamed x18, local copies, waits for them, and re-layouts  4.29 us
  transfers between devices with their start and end apart: 16, of which 12 were waited for; matrix products, arithmetic and copies ran while one was open for 6% of the time, Pallas kernels for 0%

commit v1 on v0

v1 whole, which is shorter than its diff:
```python
import math

import jax
import jax.numpy as jnp
from jax import lax
from jax.sharding import Mesh
from jax.sharding import PartitionSpec as P

HEAD = 128
SEQ = ("seq_0", "seq_1")
MINOR = "seq_1"


def top_bit(d):
    total = jnp.zeros_like(d) - 1
    for k in range(0, 7):
        total = total + (d >= (1 << k)).astype(d.dtype)
    return total


def pooled(table, factor):
    return table.reshape(table.shape[0], table.shape[1] // factor, factor, table.shape[2]).mean(axis=2)


def pad_rows(x, rows):
    return jnp.pad(x, ((0, 0), (0, rows - x.shape[1]), (0, 0)))


def pick_level(level_of, tables, lo):
    out = tables[-1]
    for i in range(len(tables) - 2, -1, -1):
        mask = (level_of == lo + i).reshape((-1,) + (1,) * (tables[i].ndim - 1))
        out = jnp.where(mask, tables[i], out)
    return out


def sibling_rows(recv, start, level, rows):
    count = 1 << level
    part = lax.dynamic_slice_in_dim(recv, start, count, axis=0)[:, :, :rows]
    part = jnp.moveaxis(part, 0, 1)
    return part.reshape(part.shape[0], count * rows, part.shape[3])


def on_device(queries, keys, values, cotangent, out_weight):
    tokens = queries.shape[0]
    width = queries.shape[1]
    heads = width // HEAD
    coarse = tokens // 2
    scale = 1.0 / math.sqrt(HEAD)
    n_minor = lax.axis_size(MINOR)
    n_seq = lax.axis_size(SEQ)
    depth = n_seq.bit_length() - 1
    minor_depth = n_minor.bit_length() - 1
    position = lax.axis_index(SEQ)
    minor_pos = lax.axis_index(MINOR)
    table = jnp.stack([keys, values]).astype(jnp.float32)
    means = [pooled(table, 2 << m).astype(jnp.bfloat16) for m in range(depth)]

    peers = jnp.arange(n_minor, dtype=jnp.int32)
    near_level = top_bit(minor_pos ^ peers)
    near_send = pick_level(
        near_level,
        [jnp.broadcast_to(pad_rows(means[m], coarse)[None], (n_minor, 2, coarse, width)) for m in range(minor_depth)],
        0,
    )
    near_recv = lax.all_to_all(near_send, MINOR, 0, 0, tiled=True)

    far_rows = coarse >> minor_depth
    w_rows = out_weight.shape[0]
    everyone = jnp.arange(n_seq, dtype=jnp.int32)
    far_level = top_bit(position ^ everyone)
    far_kv = pick_level(
        far_level,
        [jnp.broadcast_to(pad_rows(means[m], far_rows)[None], (n_seq, 2, far_rows, width)) for m in range(minor_depth, depth)],
        minor_depth,
    )
    far_send = jnp.concatenate(
        [jnp.broadcast_to(out_weight[None], (n_seq, w_rows, width)), far_kv.reshape(n_seq, 2 * far_rows, width)], axis=1
    )
    far_recv = lax.all_to_all(far_send, SEQ, 0, 0, tiled=True)
    full_weight = far_recv[:, :w_rows].reshape(n_seq * w_rows, width)
    far_kv_recv = far_recv[:, w_rows:].reshape(n_seq, 2, far_rows, width)

    levels_kv = []
    for m in range(depth):
        start = ((position >> m) ^ 1) << m
        if m < minor_depth:
            levels_kv.append(sibling_rows(near_recv, start & (n_minor - 1), m, coarse >> m))
        else:
            levels_kv.append(sibling_rows(far_kv_recv, start, m, coarse >> m))
    key_set = jnp.concatenate([keys] + [lv[0] for lv in levels_kv], axis=0)
    value_set = jnp.concatenate([values] + [lv[1] for lv in levels_kv], axis=0)

    full_cot = lax.all_to_all(
        jnp.broadcast_to(cotangent[None], (lax.axis_size("dp"),) + cotangent.shape), "dp", 0, 0, tiled=True
    )
    full_cot = jnp.moveaxis(full_cot, 0, 1).reshape(tokens, -1)
    grad_attended = jnp.dot(full_cot, full_weight, preferred_element_type=jnp.float32).astype(jnp.bfloat16)

    attended_parts = []
    grad_query_parts = []
    grad_key_parts = []
    grad_value_parts = []
    for head in range(heads):
        low = head * HEAD
        high = low + HEAD
        query_head = queries[:, low:high]
        key_head = key_set[:, low:high]
        value_head = value_set[:, low:high]
        grad_head = grad_attended[:, low:high]
        scores = (
            jnp.einsum("ta,ka->tk", query_head, key_head, preferred_element_type=jnp.float32)
            * scale
        )
        peak = jnp.max(scores, axis=-1, keepdims=True)
        expo = jnp.exp(scores - peak)
        prob = expo / jnp.sum(expo, axis=-1, keepdims=True)
        weights = prob.astype(jnp.bfloat16)
        attended_parts.append(
            jnp.dot(weights, value_head, preferred_element_type=jnp.float32).astype(jnp.bfloat16)
        )
        grad_weights = jnp.einsum(
            "ta,ka->tk", grad_head, value_head, preferred_element_type=jnp.float32
        )
        delta = jnp.sum(prob * grad_weights, axis=-1, keepdims=True)
        grad_scores = (prob * (grad_weights - delta) * scale).astype(jnp.bfloat16)
        grad_query_parts.append(
            jnp.dot(grad_scores, key_head, preferred_element_type=jnp.float32).astype(jnp.bfloat16)
        )
        grad_key_parts.append(
            jnp.einsum("tk,ta->ka", grad_scores, query_head, preferred_element_type=jnp.float32)
        )
        grad_value_parts.append(
            jnp.einsum("tk,ta->ka", weights, grad_head, preferred_element_type=jnp.float32)
        )
    attended = jnp.concatenate(attended_parts, axis=1)
    grad_queries = jnp.concatenate(grad_query_parts, axis=1)

    grad_out_weight = lax.dot_general(
        full_cot, attended, (((0,), (0,)), ((), ())), preferred_element_type=jnp.float32
    )
    for axis in SEQ:
        grad_out_weight = lax.psum_scatter(grad_out_weight, axis, scatter_dimension=0, tiled=True)

    grad_sets = jnp.stack(
        [jnp.concatenate(grad_key_parts, axis=1), jnp.concatenate(grad_value_parts, axis=1)]
    )
    level_grads = []
    for m in range(depth):
        first = tokens + m * coarse
        part = grad_sets[:, first : first + coarse].astype(jnp.bfloat16)
        level_grads.append(part.reshape(2, 1 << m, coarse >> m, width))

    near_back = pick_level(
        near_level,
        [
            jnp.stack([pad_rows(level_grads[m][:, k & ((1 << m) - 1)], coarse) for k in range(n_minor)])
            for m in range(minor_depth)
        ],
        0,
    )
    near_got = lax.all_to_all(near_back, MINOR, 0, 0, tiled=True).astype(jnp.float32)
    far_back = pick_level(
        far_level,
        [
            jnp.stack([pad_rows(level_grads[m][:, c & ((1 << m) - 1)], far_rows) for c in range(n_seq)])
            for m in range(minor_depth, depth)
        ],
        minor_depth,
    )
    far_got = lax.all_to_all(far_back, SEQ, 0, 0, tiled=True).astype(jnp.float32)

    own_grads = grad_sets[:, :tokens]
    for m in range(depth):
        rows = coarse >> m
        if m < minor_depth:
            got, level_of = near_got, near_level
        else:
            got, level_of = far_got, far_level
        mask = (level_of == m).reshape(-1, 1, 1, 1)
        summed = jnp.sum(jnp.where(mask, got[:, :, :rows], 0.0), axis=0)
        factor = 2 << m
        spread = jnp.broadcast_to((summed / factor)[:, :, None], (2, rows, factor, width))
        own_grads = own_grads + spread.reshape(2, tokens, width)
    grad_keys = own_grads[0].astype(jnp.bfloat16)
    grad_values = own_grads[1].astype(jnp.bfloat16)
    return (attended, grad_queries, grad_keys, grad_values, grad_out_weight)


def solution(mesh):
    n_seq = mesh.shape["seq"]
    minor = 1 << ((n_seq.bit_length() - 1 + 1) // 2)
    torus = Mesh(mesh.devices.reshape(n_seq // minor, minor, mesh.shape["dp"]), ("seq_0", "seq_1", "dp"))
    placed = (P(SEQ, "dp"),) * 5
    return jax.shard_map(
        on_device,
        mesh=torus,
        in_specs=placed,
        out_specs=(P(SEQ, "dp"),) * 5,
        check_vma=False,
    )
```

time: 209 us -> 228 us (1.091)
  waiting for transfers between devices: 111 us -> 150 us
  starting transfers between devices: 64.6 us -> 32.7 us
  other arithmetic: 1.14 us -> 7.88 us
  local copies, waits for them, and re-layouts: 11.2 us -> 14.7 us
    all_to_all x2 -> x5, waiting for transfers between devices: 0.01 us -> 96.3 us  [the longest x1 41.2 us: on_device(): far_recv = lax.all_to_all(far_send, SEQ, 0, 0, tiled=True)]
    ppermute x12 -> x0, waiting for transfers between devices: 70.4 us -> none  [from_partner(): return lax.ppermute(block, axis, route)]
    ppermute x12 -> x0, starting transfers between devices: 45.5 us -> none  [from_partner(): return lax.ppermute(block, axis, route)]
    all_to_all x2 -> x5, starting transfers between devices: 19.1 us -> 32.6 us  [the longest x1 11.3 us: on_device(): far_recv = lax.all_to_all(far_send, SEQ, 0, 0, tiled=True)]
    reduce_scatter x1, waiting for transfers between devices: 3.24 us -> 14.3 us  [on_device(): lax.psum_scatter(grad_out_weight, axis, scatter_dimension=0, tiled=True)]
    select_n x5 -> x4, other arithmetic: 0.13 us -> 3.12 us  [pick_level(): out = jnp.where(mask, tables[i], out)]
    unnamed x18 -> x287, local copies, waits for them, and re-layouts: 4.29 us -> 6.92 us
    reduce_sum x0 -> x12, other arithmetic: none -> 2.52 us  [the longest x6 1.6 us: pooled(): table.reshape(table.shape[0], table.shape[1] // factor, factor, table.sha...]
  transfers between devices with their start and end apart: 16 -> 7, of which waited for: 12 -> 7; matrix products, arithmetic and copies ran while one was open for 6% -> 4% of each run, Pallas kernels for 0% -> 0%
where the time goes in v1:
time: 228 us; the launch traced here: 227 us
  waiting for transfers between devices  150 us (66%)
  starting transfers between devices  32.7 us (14%)
  between operations  16.8 us (7%)
  local copies, waits for them, and re-layouts  14.7 us (6%)
  other arithmetic  7.88 us (3%)
  matrix products  4.96 us (2%)
    all_to_all x1, waiting for transfers between devices, on_device(): far_recv = lax.all_to_all(far_send, SEQ, 0, 0, tiled=True)  41.2 us
    unnamed x3, waiting for transfers between devices  39.2 us
    all_to_all x1, waiting for transfers between devices, on_device(): lax.all_to_all(far_back, SEQ, 0, 0, tiled=True).astype(jnp.float32)  17.3 us
    all_to_all x1, waiting for transfers between devices, on_device(): near_recv = lax.all_to_all(near_send, MINOR, 0, 0, tiled=True)  15.7 us
    all_to_all x1, waiting for transfers between devices, on_device(): lax.all_to_all(near_back, MINOR, 0, 0, tiled=True).astype(jnp.float32)  15.4 us
    reduce_scatter x1, waiting for transfers between devices, on_device(): lax.psum_scatter(grad_out_weight, axis, scatter_dimension=0, tiled=True)  14.3 us
    all_to_all x1, starting transfers between devices, on_device(): far_recv = lax.all_to_all(far_send, SEQ, 0, 0, tiled=True)  11.3 us
    all_to_all x1, starting transfers between devices, on_device(): near_recv = lax.all_to_all(near_send, MINOR, 0, 0, tiled=True)  7.1 us
  transfers between devices with their start and end apart: 7, of which 7 were waited for; matrix products, arithmetic and copies ran while one was open for 4% of the time, Pallas kernels for 0%

profile of v1, /device:TPU:6, one launch (start us, length us, event | category | flops | bytes accessed | tf_op | source)
XLA Modules:
  0.0 226.8 jit_solution(5256160872249068626)
XLA Ops:
  7.2 0.9 stack.182
  8.0 0.9 stack.179
  8.9 0.9 stack.181
  9.8 0.9 stack.178
  10.7 1.0 convert_reduce_fusion.3
  11.7 0.2 convert_reduce_fusion.4
  11.9 0.4 convert_reduce_fusion.5
  12.3 0.9 select_select_fusion.3
  13.3 7.1 %all-to-all-start = ((bf16[8,2,64,256]{3,2,1,0:T(8,128)(2,1)}), bf16[8,2,64,256]{3,2,1,0:T(8,128)(2,1)S(1)}, u32[]{:S(2)}, u32[]{:S(2)}) async-start(bf16[8,2,64,256]{3,2,1,0:T(8,128)(2,1)} %select_select_fusion.3), calls=%async_computation | async-start | bytes 1048576 | tf_op jit(solution)/shard_map/all_to_all | solution.py:66
  20.6 0.2 select_select_fusion.2
  20.8 0.1 broadcast_in_dim.209
  20.9 1.3 pad_maximum_fusion
  22.2 15.7 %all-to-all-done = bf16[8,2,64,256]{3,2,1,0:T(8,128)(2,1)S(1)} async-done(((bf16[8,2,64,256]{3,2,1,0:T(8,128)(2,1)}), bf16[8,2,64,256]{3,2,1,0:T(8,128)(2,1)S(1)}, u32[]{:S(2)}, u32[]{:S(2)}) %all-to-all-start) | async-done | bytes 524320 | tf_op jit(solution)/shard_map/all_to_all | solution.py:66
  37.9 11.3 %all-to-all-start.1 = ((bf16[64,48,256]{2,1,0:T(8,128)(2,1)}), bf16[64,48,256]{2,1,0:T(8,128)(2,1)S(1)}, u32[]{:S(2)}, u32[]{:S(2)}) async-start(bf16[64,48,256]{2,1,0:T(8,128)(2,1)} %pad_maximum_fusion), calls=%async_computation.1 | async-start | bytes 3145728 | tf_op jit(solution)/shard_map/all_to_all | solution.py:80
  49.2 0.1 copy.168
  49.6 41.2 %all-to-all-done.1 = bf16[64,48,256]{2,1,0:T(8,128)(2,1)S(1)} async-done(((bf16[64,48,256]{2,1,0:T(8,128)(2,1)}), bf16[64,48,256]{2,1,0:T(8,128)(2,1)S(1)}, u32[]{:S(2)}, u32[]{:S(2)}) %all-to-all-start.1) | async-done | bytes 1572896 | tf_op jit(solution)/shard_map/all_to_all | solution.py:80
  90.8 0.9 broadcast_in_dim.217
  91.7 4.9 %all-to-all-start.2 = ((bf16[8,128,256]{1,2,0:T(8,128)(2,1)}), bf16[8,128,256]{1,2,0:T(8,128)(2,1)S(1)}, u32[]{:S(2)}, u32[]{:S(2)}) async-start(bf16[8,128,256]{1,2,0:T(8,128)(2,1)} %broadcast_in_dim.217), calls=%async_computation.2 | async-start | bytes 1048576 | tf_op jit(solution)/shard_map/all_to_all | solution.py:94
  97.0 0.2 fusion.73
  97.2 0.2 fusion.74
  97.7 0.2 convolution_convert_fusion.3
  97.9 0.2 convolution_convert_fusion.4
  98.2 6.7 %all-to-all-done.2 = bf16[8,128,256]{1,2,0:T(8,128)(2,1)S(1)} async-done(((bf16[8,128,256]{1,2,0:T(8,128)(2,1)}), bf16[8,128,256]{1,2,0:T(8,128)(2,1)S(1)}, u32[]{:S(2)}, u32[]{:S(2)}) %all-to-all-start.2) | async-done | bytes 524320 | tf_op jit(solution)/shard_map/all_to_all | solution.py:94
  104.9 0.5 fusion
  105.4 0.2 fusion.14
  105.6 0.2 fusion.17
  105.8 0.2 fusion.35
  106.1 0.2 fusion.34
  106.4 0.2 convolution_convert_fusion.1
  106.6 0.2 fusion.40
  106.9 0.2 convolution_convert_fusion.2
  107.2 0.2 fusion.43
  107.5 0.2 fusion.65
  107.8 0.1 copy.211
  108.0 1.8 convolution_bitcast_fusion
  109.7 0.7 copy.247
  110.5 0.7 copy.248
  112.0 0.1 copy.194
  112.2 0.6 copy-done.6
  115.7 0.9 select_select_fusion.1
  116.6 4.4 %all-to-all-start.3 = ((bf16[8,2,64,256]{3,2,1,0:T(8,128)(2,1)}), bf16[8,2,64,256]{3,2,1,0:T(8,128)(2,1)S(1)}, u32[]{:S(2)}, u32[]{:S(2)}) async-start(bf16[8,2,64,256]{3,2,1,0:T(8,128)(2,1)} %select_select_fusion.1), calls=%async_computation.3 | async-start | bytes 1048576 | tf_op jit(solution)/shard_map/all_to_all | solution.py:162
  121.1 0.7 reduce-scatter.5.cloned.1.call-update
  121.9 1.0 select_select_fusion
  122.9 15.4 %all-to-all-done.3 = bf16[8,2,64,256]{3,2,1,0:T(8,128)(2,1)S(1)} async-done(((bf16[8,2,64,256]{3,2,1,0:T(8,128)(2,1)}), bf16[8,2,64,256]{3,2,1,0:T(8,128)(2,1)S(1)}, u32[]{:S(2)}, u32[]{:S(2)}) %all-to-all-start.3) | async-done | bytes 524320 | tf_op jit(solution)/shard_map/all_to_all | solution.py:162
  138.4 4.9 %all-to-all-start.4 = ((bf16[64,2,8,256]{3,2,1,0:T(8,128)(2,1)}), bf16[64,2,8,256]{3,2,1,0:T(8,128)(2,1)S(1)}, u32[]{:S(2)}, u32[]{:S(2)}) async-start(bf16[64,2,8,256]{3,2,1,0:T(8,128)(2,1)} %select_select_fusion), calls=%async_computation.4 | async-start | bytes 1048576 | tf_op jit(solution)/shard_map/all_to_all | solution.py:171
  143.3 0.1 convert_element_type.469
  143.5 0.9 copy.185
  144.6 0.1 copy.184
  144.8 0.2 select_reduce_fusion.1
  145.0 0.1 copy.181
  145.2 0.1 copy.182
  145.3 17.3 %all-to-all-done.4 = bf16[64,2,8,256]{3,2,1,0:T(8,128)(2,1)S(1)} async-done(((bf16[64,2,8,256]{3,2,1,0:T(8,128)(2,1)}), bf16[64,2,8,256]{3,2,1,0:T(8,128)(2,1)S(1)}, u32[]{:S(2)}, u32[]{:S(2)}) %all-to-all-start.4) | async-done | bytes 524320 | tf_op jit(solution)/shard_map/all_to_all | solution.py:171
  162.6 0.1 convert_element_type.470
  162.7 0.2 select_reduce_fusion
  162.9 0.2 fusion.2
  163.1 0.2 fusion.12
  163.3 14.3 %reduce-scatter.5.cloned.1.call-done = f32[256,256]{0,1:T(8,128)} async-done(((f32[2048,256]{0,1:T(8,128)}), f32[256,256]{0,1:T(8,128)}) %reduce-scatter.5.cloned.1.call-update) | async-done | bytes 262160 | tf_op jit(solution)/shard_map/reduce_scatter | solution.py:143
  177.6 1.8 copy.254
  179.4 0.1 copy.246
  179.6 0.1 copy.245
  179.7 0.1 copy.244
  180.0 0.7 copy.249
  180.7 0.7 copy.250
  181.5 38.5 %reduce-scatter.7.cloned.1.call-done = f32[32,256]{1,0:T(8,128)} async-done(((f32[256,256]{1,0:T(8,128)}), f32[32,256]{1,0:T(8,128)}) %reduce-scatter.7.cloned.1.call-update) | async-done | bytes 32784
  (358 shorter events, 3.8 us)
Async XLA Ops:
  9.8 10.6 %copy-start.1 = (bf16[128,256]{1,0:T(8,128)(2,1)S(1)}, bf16[128,256]{1,0:T(8,128)(2,1)}, u32[]{:S(2)}) copy-start(bf16[128,256]{1,0:T(8,128)(2,1)} %param.6) | copy-start | bytes 196612
  9.8 10.6 %copy-start.2 = (bf16[128,256]{1,0:T(8,128)(2,1)S(1)}, bf16[128,256]{1,0:T(8,128)(2,1)}, u32[]{:S(2)}) copy-start(bf16[128,256]{1,0:T(8,128)(2,1)} %param.7) | copy-start | bytes 196612
  12.3 8.5 %copy-start.10 = (bf16[32,256]{1,0:T(8,128)(2,1)S(1)}, bf16[32,256]{1,0:T(8,128)(2,1)}, u32[]{:S(2)}) copy-start(bf16[32,256]{1,0:T(8,128)(2,1)} %param.9) | copy-start | bytes 49156
  13.3 24.6 %all-to-all-start = ((bf16[8,2,64,256]{3,2,1,0:T(8,128)(2,1)}), bf16[8,2,64,256]{3,2,1,0:T(8,128)(2,1)S(1)}, u32[]{:S(2)}, u32[]{:S(2)}) async-start(bf16[8,2,64,256]{3,2,1,0:T(8,128)(2,1)} %select_select_fusion.3), calls=%async_computation | async-start | bytes 1048576 | tf_op jit(solution)/shard_map/all_to_all | solution.py:66
  22.2 27.0 %copy-start.9 = (bf16[128,256]{1,0:T(8,128)(2,1)S(1)}, bf16[128,256]{1,0:T(8,128)(2,1)}, u32[]{:S(2)}) copy-start(bf16[128,256]{1,0:T(8,128)(2,1)} %param.8) | copy-start | bytes 196612
  37.9 52.9 %all-to-all-start.1 = ((bf16[64,48,256]{2,1,0:T(8,128)(2,1)}), bf16[64,48,256]{2,1,0:T(8,128)(2,1)S(1)}, u32[]{:S(2)}, u32[]{:S(2)}) async-start(bf16[64,48,256]{2,1,0:T(8,128)(2,1)} %pad_maximum_fusion), calls=%async_computation.1 | async-start | bytes 3145728 | tf_op jit(solution)/shard_map/all_to_all | solution.py:80
  90.8 6.9 %copy-start = (bf16[64,48,256]{2,1,0:T(8,128)(2,1)}, bf16[64,48,256]{2,1,0:T(8,128)(2,1)S(1)}, u32[]{:S(2)}) copy-start(bf16[64,48,256]{2,1,0:T(8,128)(2,1)S(1)} %all-to-all-done.1) | copy-start | bytes 4718596
  91.7 5.2 %copy-start.8 = (bf16[128,256]{1,0:T(8,128)(2,1)S(1)}, bf16[128,256]{1,0:T(8,128)(2,1)}, u32[]{:S(2)}) copy-start(bf16[128,256]{1,0:T(8,128)(2,1)} %param.5) | copy-start | bytes 196612
  91.7 13.2 %all-to-all-start.2 = ((bf16[8,128,256]{1,2,0:T(8,128)(2,1)}), bf16[8,128,256]{1,2,0:T(8,128)(2,1)S(1)}, u32[]{:S(2)}, u32[]{:S(2)}) async-start(bf16[8,128,256]{1,2,0:T(8,128)(2,1)} %broadcast_in_dim.217), calls=%async_computation.2 | async-start | bytes 1048576 | tf_op jit(solution)/shard_map/all_to_all | solution.py:94
  97.7 7.2 %slice-start = ((bf16[64,48,256]{2,1,0:T(8,128)(2,1)}), bf16[64,32,256]{2,1,0:T(8,128)(2,1)S(1)}, s32[]{:S(2)}) async-start(bf16[64,48,256]{2,1,0:T(8,128)(2,1)} %copy-done), calls=%async_computation.9 | async-start | bytes 2097152 | tf_op jit(solution)/shard_map/slice | solution.py:81
  112.0 0.8 copy-start.6
  113.9 1.3 copy-start.4
  116.6 5.2 %copy-start.7 = (bf16[64,2,8,256]{3,2,1,0:T(8,128)(2,1)S(1)}, bf16[64,2,8,256]{3,2,1,0:T(8,128)(2,1)}, u32[]{:S(2)}) copy-start(bf16[64,2,8,256]{3,2,1,0:T(8,128)(2,1)} %copy-done.6) | copy-start | bytes 1572868
  116.6 5.3 %copy-start.5 = (bf16[64,2,8,256]{3,2,1,0:T(8,128)(2,1)S(1)}, bf16[64,2,8,256]{3,2,1,0:T(8,128)(2,1)}, u32[]{:S(2)}) copy-start(bf16[64,2,8,256]{3,2,1,0:T(8,128)(2,1)} %copy-done.4) | copy-start | bytes 1572868
  116.6 21.7 %all-to-all-start.3 = ((bf16[8,2,64,256]{3,2,1,0:T(8,128)(2,1)}), bf16[8,2,64,256]{3,2,1,0:T(8,128)(2,1)S(1)}, u32[]{:S(2)}, u32[]{:S(2)}) async-start(bf16[8,2,64,256]{3,2,1,0:T(8,128)(2,1)} %select_select_fusion.1), calls=%async_computation.3 | async-start | bytes 1048576 | tf_op jit(solution)/shard_map/all_to_all | solution.py:162
  121.1 56.5 %reduce-scatter.5.cloned.1.call-start = ((), (), s32[]{:S(2)}) async-start(), calls=%async_computation.7 | async-start | bytes 2359296 | tf_op jit(solution)/shard_map/reduce_scatter | solution.py:143
  138.4 24.2 %all-to-all-start.4 = ((bf16[64,2,8,256]{3,2,1,0:T(8,128)(2,1)}), bf16[64,2,8,256]{3,2,1,0:T(8,128)(2,1)S(1)}, u32[]{:S(2)}, u32[]{:S(2)}) async-start(bf16[64,2,8,256]{3,2,1,0:T(8,128)(2,1)} %select_select_fusion), calls=%async_computation.4 | async-start | bytes 1048576 | tf_op jit(solution)/shard_map/all_to_all | solution.py:171
  143.2 76.7 %reduce-scatter.7.cloned.1.call-start = ((), (), s32[]{:S(2)}) async-start(), calls=%async_computation.8 | async-start | bytes 294912
  163.3 16.6 %copy-start.3 = (f32[2,128,256]{1,2,0:T(8,128)S(1)}, f32[2,128,256]{1,2,0:T(8,128)}, u32[]{:S(2)}) copy-start(f32[2,128,256]{1,2,0:T(8,128)} %copy.185) | copy-start | bytes 786436
Sparse Core Ops, SparseCore 0:
  124.7 52.7 reduce-scatter.4
  180.9 38.9 reduce-scatter.6

commit v2 on v0

--- a/solution.py
+++ b/solution.py
@@ -36,9 +36,11 @@
 
 
 def own_rows(running, axes):
-    for axis in axes:
-        running = lax.psum_scatter(running, axis, scatter_dimension=0, tiled=True)
-    return running
+    first, last = axes
+    running = lax.psum_scatter(running, first, scatter_dimension=0, tiled=True)
+    count = lax.axis_size(last)
+    parts = running.reshape(count, running.shape[0] // count, running.shape[1])
+    return jnp.sum(lax.all_to_all(parts, last, 0, 0, tiled=True), axis=0)
 
 
 def pair_mean(table):

time: 209 us -> 188 us (0.90)
  waiting for transfers between devices: 111 us -> 83.5 us
  starting transfers between devices: 64.6 us -> 71.5 us
    unnamed x3 -> x1, waiting for transfers between devices: 37.8 us -> 0.02 us
    all_to_all x0 -> x1, waiting for transfers between devices: none -> 9.71 us  [own_rows(): return jnp.sum(lax.all_to_all(parts, last, 0, 0, tiled=True), axis=0)]
    all_to_all x0 -> x1, starting transfers between devices: none -> 6.88 us  [own_rows(): return jnp.sum(lax.all_to_all(parts, last, 0, 0, tiled=True), axis=0)]
    ppermute x12, waiting for transfers between devices: 70.4 us -> 73.7 us  [from_partner(): return lax.ppermute(block, axis, route)]
    reduce_scatter x1, waiting for transfers between devices: 3.24 us -> 0.02 us  [own_rows(): running = lax.psum_scatter(running, first, scatter_dimension=0, tiled=True)]
    unnamed x18 -> x17, local copies, waits for them, and re-layouts: 4.29 us -> 2.51 us
where the time goes in v2:
time: 188 us; the launch traced here: 187 us
  waiting for transfers between devices  83.5 us (44%)
  starting transfers between devices  71.5 us (38%)
  between operations  14.8 us (8%)
  local copies, waits for them, and re-layouts  11.2 us (6%)
  matrix products  4.7 us (2%)
    ppermute x12, waiting for transfers between devices, from_partner(): return lax.ppermute(block, axis, route)  73.7 us
    ppermute x12, starting transfers between devices, from_partner(): return lax.ppermute(block, axis, route)  45.5 us
    all_to_all x2, starting transfers between devices, from_everyone(): return lax.all_to_all(copies, axis, split_axis=0, concat_axis=0, tiled=True)  19.1 us
    all_to_all x1, waiting for transfers between devices, own_rows(): return jnp.sum(lax.all_to_all(parts, last, 0, 0, tiled=True), axis=0)  9.71 us
    all_to_all x1, starting transfers between devices, own_rows(): return jnp.sum(lax.all_to_all(parts, last, 0, 0, tiled=True), axis=0)  6.88 us
  transfers between devices with their start and end apart: 16, of which 12 were waited for; matrix products, arithmetic and copies ran while one was open for 6% of the time, Pallas kernels for 0%

profile of v2, /device:TPU:6, one launch (start us, length us, event | category | flops | bytes accessed | tf_op | source)
XLA Modules:
  0.0 187.4 jit_solution(14013105199571120602)
XLA Ops:
  7.2 0.9 stack.18
  8.1 0.9 stack.19
  9.1 3.5 %collective-permute-start = (f32[2,64,256]{2,1,0:T(8,128)S(1)}, f32[2,64,256]{2,1,0:T(8,128)S(1)}, u32[]{:S(2)}, u32[]{:S(2)}) collective-permute-start(f32[2,64,256]{2,1,0:T(8,128)S(1)} %fusion.30), channel_id=1, source_target_pairs={{0,8},{8,0},{16,24},{24,16},{32,40},{40,32},{48,56},{56,48},{64,72... | collective-permute-start | bytes 393224 | tf_op jit(solution)/shard_map/ppermute | solution.py:20
  12.6 1.0 copy.107
  13.5 0.9 broadcast_in_dim.16
  14.4 7.7 %all-to-all-start = ((bf16[8,128,256]{1,2,0:T(8,128)(2,1)}), bf16[8,128,256]{1,2,0:T(8,128)(2,1)S(1)}, u32[]{:S(2)}, u32[]{:S(2)}) async-start(bf16[8,128,256]{1,2,0:T(8,128)(2,1)} %broadcast_in_dim.16), calls=%async_computation | async-start | bytes 1048576 | tf_op jit(solution)/shard_map/all_to_all | solution.py:31
  22.2 0.2 copy.92
  22.5 1.9 %collective-permute-start.1 = (f32[2,64,256]{2,1,0:T(8,128)S(1)}, f32[2,64,256]{2,1,0:T(8,128)S(1)}, u32[]{:S(2)}, u32[]{:S(2)}) collective-permute-start(f32[2,64,256]{2,1,0:T(8,128)S(1)} %fusion.40), channel_id=1, source_target_pairs={{0,16},{16,0},{8,24},{24,8},{32,48},{48,32},{40,56},{56,40},{64,80... | collective-permute-start | bytes 393224 | tf_op jit(solution)/shard_map/ppermute | solution.py:20
  24.5 9.2 %collective-permute-done.1 = f32[2,64,256]{2,1,0:T(8,128)S(1)} collective-permute-done((f32[2,64,256]{2,1,0:T(8,128)S(1)}, f32[2,64,256]{2,1,0:T(8,128)S(1)}, u32[]{:S(2)}, u32[]{:S(2)}) %collective-permute-start.1) | collective-permute-done | bytes 131104 | tf_op jit(solution)/shard_map/ppermute | solution.py:20
  33.7 0.2 copy.95
  34.0 3.9 %collective-permute-start.2 = (f32[2,64,256]{2,1,0:T(8,128)S(1)}, f32[2,64,256]{2,1,0:T(8,128)S(1)}, u32[]{:S(2)}, u32[]{:S(2)}) collective-permute-start(f32[2,64,256]{2,1,0:T(8,128)S(1)} %fusion.38), channel_id=1, source_target_pairs={{0,32},{32,0},{8,40},{40,8},{16,48},{48,16},{24,56},{56,24},{64,96... | collective-permute-start | bytes 393224 | tf_op jit(solution)/shard_map/ppermute | solution.py:20
  38.0 8.0 %collective-permute-done.2 = f32[2,64,256]{2,1,0:T(8,128)S(1)} collective-permute-done((f32[2,64,256]{2,1,0:T(8,128)S(1)}, f32[2,64,256]{2,1,0:T(8,128)S(1)}, u32[]{:S(2)}, u32[]{:S(2)}) %collective-permute-start.2) | collective-permute-done | bytes 131104 | tf_op jit(solution)/shard_map/ppermute | solution.py:20
  46.0 0.2 copy.98
  46.3 3.3 %collective-permute-start.3 = (f32[2,64,256]{2,1,0:T(8,128)S(1)}, f32[2,64,256]{2,1,0:T(8,128)S(1)}, u32[]{:S(2)}, u32[]{:S(2)}) collective-permute-start(f32[2,64,256]{2,1,0:T(8,128)S(1)} %fusion.36), channel_id=1, source_target_pairs={{0,64},{64,0},{8,72},{72,8},{16,80},{80,16},{24,88},{88,24},{32,96... | collective-permute-start | bytes 393224 | tf_op jit(solution)/shard_map/ppermute | solution.py:20
  49.7 3.6 %collective-permute-done.3 = f32[2,64,256]{2,1,0:T(8,128)S(1)} collective-permute-done((f32[2,64,256]{2,1,0:T(8,128)S(1)}, f32[2,64,256]{2,1,0:T(8,128)S(1)}, u32[]{:S(2)}, u32[]{:S(2)}) %collective-permute-start.3) | collective-permute-done | bytes 131104 | tf_op jit(solution)/shard_map/ppermute | solution.py:20
  53.4 0.2 copy.101
  53.7 5.4 %collective-permute-start.4 = (f32[2,64,256]{2,1,0:T(8,128)S(1)}, f32[2,64,256]{2,1,0:T(8,128)S(1)}, u32[]{:S(2)}, u32[]{:S(2)}) collective-permute-start(f32[2,64,256]{2,1,0:T(8,128)S(1)} %fusion.34), channel_id=1, source_target_pairs={{0,128},{128,0},{8,136},{136,8},{16,144},{144,16},{24,152},{152,24... | collective-permute-start | bytes 393224 | tf_op jit(solution)/shard_map/ppermute | solution.py:20
  59.1 4.8 %collective-permute-done.4 = f32[2,64,256]{2,1,0:T(8,128)S(1)} collective-permute-done((f32[2,64,256]{2,1,0:T(8,128)S(1)}, f32[2,64,256]{2,1,0:T(8,128)S(1)}, u32[]{:S(2)}, u32[]{:S(2)}) %collective-permute-start.4) | collective-permute-done | bytes 131104 | tf_op jit(solution)/shard_map/ppermute | solution.py:20
  63.9 0.2 copy.104
  64.1 1.1 broadcast_in_dim.17
  65.3 11.4 %all-to-all-start.1 = ((bf16[64,32,256]{2,1,0:T(8,128)(2,1)}), bf16[64,32,256]{2,1,0:T(8,128)(2,1)S(1)}, u32[]{:S(2)}, u32[]{:S(2)}) async-start(bf16[64,32,256]{2,1,0:T(8,128)(2,1)} %broadcast_in_dim.17), calls=%async_computation.1 | async-start | bytes 2097152 | tf_op jit(solution)/shard_map/all_to_all | solution.py:31
  76.8 7.5 %collective-permute-start.5 = (bf16[2,64,256]{2,1,0:T(8,128)(2,1)S(1)}, bf16[2,64,256]{2,1,0:T(8,128)(2,1)S(1)}, u32[]{:S(2)}, u32[]{:S(2)}) collective-permute-start(bf16[2,64,256]{2,1,0:T(8,128)(2,1)S(1)} %fusion.32), channel_id=1, source_target_pairs={{0,256},{256,0},{8,264},{264,8},{16,272},{272,16},{24,280},{280,24... | collective-permute-start | bytes 196616 | tf_op jit(solution)/shard_map/ppermute | solution.py:20
  84.3 23.0 %collective-permute-done.5 = bf16[2,64,256]{2,1,0:T(8,128)(2,1)S(1)} collective-permute-done((bf16[2,64,256]{2,1,0:T(8,128)(2,1)S(1)}, bf16[2,64,256]{2,1,0:T(8,128)(2,1)S(1)}, u32[]{:S(2)}, u32[]{:S(2)}) %collective-permute-start.5) | collective-permute-done | bytes 65568 | tf_op jit(solution)/shard_map/ppermute | solution.py:20
  107.3 0.2 fusion.89
  107.6 0.1 fusion.12
  107.7 0.2 fusion.90
  107.9 0.1 fusion.10
  108.0 0.2 convolution_convert_fusion.3
  108.2 0.2 convolution_convert_fusion.4
  108.5 0.4 convolution_convert_fusion
  108.9 0.2 fusion.51
  109.0 0.2 fusion.52
  109.2 0.2 fusion.3
  109.4 0.2 fusion.6
  109.8 0.2 fusion.72
  110.0 0.2 fusion.69
  110.3 3.1 %collective-permute-start.6 = (bf16[2,64,256]{2,1,0:T(8,128)(2,1)S(1)}, bf16[2,64,256]{2,1,0:T(8,128)(2,1)S(1)}, u32[]{:S(2)}, u32[]{:S(2)}) collective-permute-start(bf16[2,64,256]{2,1,0:T(8,128)(2,1)S(1)} %fusion.17), channel_id=1, source_target_pairs={{0,256},{256,0},{8,264},{264,8},{16,272},{272,16},{24,280},{280,24... | collective-permute-start | bytes 196616 | tf_op jit(solution)/shard_map/ppermute | solution.py:20
  113.5 1.8 convolution_bitcast_fusion
  115.3 5.1 %collective-permute-done.6 = bf16[2,64,256]{2,1,0:T(8,128)(2,1)S(1)} collective-permute-done((bf16[2,64,256]{2,1,0:T(8,128)(2,1)S(1)}, bf16[2,64,256]{2,1,0:T(8,128)(2,1)S(1)}, u32[]{:S(2)}, u32[]{:S(2)}) %collective-permute-start.6) | collective-permute-done | bytes 65568 | tf_op jit(solution)/shard_map/ppermute | solution.py:20
  120.4 0.1 copy.116
  120.7 2.4 %collective-permute-start.7 = (bf16[2,64,256]{2,1,0:T(8,128)(2,1)S(1)}, bf16[2,64,256]{2,1,0:T(8,128)(2,1)S(1)}, u32[]{:S(2)}, u32[]{:S(2)}) collective-permute-start(bf16[2,64,256]{2,1,0:T(8,128)(2,1)S(1)} %fusion.20), channel_id=1, source_target_pairs={{0,128},{128,0},{8,136},{136,8},{16,144},{144,16},{24,152},{152,24... | collective-permute-start | bytes 196616 | tf_op jit(solution)/shard_map/ppermute | solution.py:20
  123.1 5.3 %collective-permute-done.7 = bf16[2,64,256]{2,1,0:T(8,128)(2,1)S(1)} collective-permute-done((bf16[2,64,256]{2,1,0:T(8,128)(2,1)S(1)}, bf16[2,64,256]{2,1,0:T(8,128)(2,1)S(1)}, u32[]{:S(2)}, u32[]{:S(2)}) %collective-permute-start.7) | collective-permute-done | bytes 65568 | tf_op jit(solution)/shard_map/ppermute | solution.py:20
  128.4 0.1 copy.119
  128.6 1.9 %collective-permute-start.8 = (bf16[2,64,256]{2,1,0:T(8,128)(2,1)S(1)}, bf16[2,64,256]{2,1,0:T(8,128)(2,1)S(1)}, u32[]{:S(2)}, u32[]{:S(2)}) collective-permute-start(bf16[2,64,256]{2,1,0:T(8,128)(2,1)S(1)} %fusion.23), channel_id=1, source_target_pairs={{0,64},{64,0},{8,72},{72,8},{16,80},{80,16},{24,88},{88,24},{32,96... | collective-permute-start | bytes 196616 | tf_op jit(solution)/shard_map/ppermute | solution.py:20
  130.6 0.7 copy.134
  131.3 4.4 %collective-permute-done.8 = bf16[2,64,256]{2,1,0:T(8,128)(2,1)S(1)} collective-permute-done((bf16[2,64,256]{2,1,0:T(8,128)(2,1)S(1)}, bf16[2,64,256]{2,1,0:T(8,128)(2,1)S(1)}, u32[]{:S(2)}, u32[]{:S(2)}) %collective-permute-start.8) | collective-permute-done | bytes 65568 | tf_op jit(solution)/shard_map/ppermute | solution.py:20
  135.7 0.1 copy.122
  136.0 6.7 %collective-permute-start.9 = (bf16[2,64,256]{2,1,0:T(8,128)(2,1)S(1)}, bf16[2,64,256]{2,1,0:T(8,128)(2,1)S(1)}, u32[]{:S(2)}, u32[]{:S(2)}) collective-permute-start(bf16[2,64,256]{2,1,0:T(8,128)(2,1)S(1)} %fusion.26), channel_id=1, source_target_pairs={{0,32},{32,0},{8,40},{40,8},{16,48},{48,16},{24,56},{56,24},{64,96... | collective-permute-start | bytes 196616 | tf_op jit(solution)/shard_map/ppermute | solution.py:20
  142.7 0.2 convolution_convert_fusion.1
  142.9 3.2 %collective-permute-done.9 = bf16[2,64,256]{2,1,0:T(8,128)(2,1)S(1)} collective-permute-done((bf16[2,64,256]{2,1,0:T(8,128)(2,1)S(1)}, bf16[2,64,256]{2,1,0:T(8,128)(2,1)S(1)}, u32[]{:S(2)}, u32[]{:S(2)}) %collective-permute-start.9) | collective-permute-done | bytes 65568 | tf_op jit(solution)/shard_map/ppermute | solution.py:20
  146.2 0.1 copy.125
  146.4 3.7 %collective-permute-start.10 = (bf16[2,64,256]{2,1,0:T(8,128)(2,1)S(1)}, bf16[2,64,256]{2,1,0:T(8,128)(2,1)S(1)}, u32[]{:S(2)}, u32[]{:S(2)}) collective-permute-start(bf16[2,64,256]{2,1,0:T(8,128)(2,1)S(1)} %fusion.15), channel_id=1, source_target_pairs={{0,16},{16,0},{8,24},{24,8},{32,48},{48,32},{40,56},{56,40},{64,80... | collective-permute-start | bytes 196616 | tf_op jit(solution)/shard_map/ppermute | solution.py:20
  150.1 0.2 convolution_convert_fusion.2
  150.4 3.8 %collective-permute-done.10 = bf16[2,64,256]{2,1,0:T(8,128)(2,1)S(1)} collective-permute-done((bf16[2,64,256]{2,1,0:T(8,128)(2,1)S(1)}, bf16[2,64,256]{2,1,0:T(8,128)(2,1)S(1)}, u32[]{:S(2)}, u32[]{:S(2)}) %collective-permute-start.10) | collective-permute-done | bytes 65568 | tf_op jit(solution)/shard_map/ppermute | solution.py:20
  154.2 0.1 copy.128
  154.5 2.1 %collective-permute-start.11 = (bf16[2,64,256]{2,1,0:T(8,128)(2,1)S(1)}, bf16[2,64,256]{2,1,0:T(8,128)(2,1)S(1)}, u32[]{:S(2)}, u32[]{:S(2)}) collective-permute-start(bf16[2,64,256]{2,1,0:T(8,128)(2,1)S(1)} %fusion.28), channel_id=1, source_target_pairs={{0,8},{8,0},{16,24},{24,16},{32,40},{40,32},{48,56},{56,48},{64,72... | collective-permute-start | bytes 196616 | tf_op jit(solution)/shard_map/ppermute | solution.py:20
  156.6 0.7 copy.135
  157.3 3.3 %collective-permute-done.11 = bf16[2,64,256]{2,1,0:T(8,128)(2,1)S(1)} collective-permute-done((bf16[2,64,256]{2,1,0:T(8,128)(2,1)S(1)}, bf16[2,64,256]{2,1,0:T(8,128)(2,1)S(1)}, u32[]{:S(2)}, u32[]{:S(2)}) %collective-permute-start.11) | collective-permute-done | bytes 65568 | tf_op jit(solution)/shard_map/ppermute | solution.py:20
  160.7 0.1 copy.131
  160.8 1.8 copy.133
  162.6 6.9 %all-to-all-start.2 = ((f32[8,32,256]{2,1,0:T(8,128)}), f32[8,32,256]{2,1,0:T(8,128)S(1)}, u32[]{:S(2)}, u32[]{:S(2)}) async-start(f32[8,32,256]{2,1,0:T(8,128)} %bitcast.40), calls=%async_computation.3 | async-start | bytes 524288 | tf_op jit(solution)/shard_map/all_to_all | solution.py:43
  169.6 0.7 slice_bitcast_fusion
  170.2 9.7 %all-to-all-done.2 = f32[8,32,256]{2,1,0:T(8,128)S(1)} async-done(((f32[8,32,256]{2,1,0:T(8,128)}), f32[8,32,256]{2,1,0:T(8,128)S(1)}, u32[]{:S(2)}, u32[]{:S(2)}) %all-to-all-start.2) | async-done | bytes 262176 | tf_op jit(solution)/shard_map/all_to_all | solution.py:43
  180.0 0.6 reduce_sum.49
  (75 shorter events, 1.9 us)
Async XLA Ops:
  7.2 15.0 %copy-start = (bf16[128,256]{1,0:T(8,128)(2,1)S(1)}, bf16[128,256]{1,0:T(8,128)(2,1)}, u32[]{:S(2)}) copy-start(bf16[128,256]{1,0:T(8,128)(2,1)} %param.6) | copy-start | bytes 196612
  7.2 15.0 %copy-start.1 = (bf16[128,256]{1,0:T(8,128)(2,1)S(1)}, bf16[128,256]{1,0:T(8,128)(2,1)}, u32[]{:S(2)}) copy-start(bf16[128,256]{1,0:T(8,128)(2,1)} %param.7) | copy-start | bytes 196612
  9.1 13.1 %collective-permute-start = (f32[2,64,256]{2,1,0:T(8,128)S(1)}, f32[2,64,256]{2,1,0:T(8,128)S(1)}, u32[]{:S(2)}, u32[]{:S(2)}) collective-permute-start(f32[2,64,256]{2,1,0:T(8,128)S(1)} %fusion.30), channel_id=1, source_target_pairs={{0,8},{8,0},{16,24},{24,16},{32,40},{40,32},{48,56},{56,48},{64,72... | collective-permute-start | bytes 393224 | tf_op jit(solution)/shard_map/ppermute | solution.py:20
  14.4 49.7 %all-to-all-start = ((bf16[8,128,256]{1,2,0:T(8,128)(2,1)}), bf16[8,128,256]{1,2,0:T(8,128)(2,1)S(1)}, u32[]{:S(2)}, u32[]{:S(2)}) async-start(bf16[8,128,256]{1,2,0:T(8,128)(2,1)} %broadcast_in_dim.16), calls=%async_computation | async-start | bytes 1048576 | tf_op jit(solution)/shard_map/all_to_all | solution.py:31
  22.5 11.2 %collective-permute-start.1 = (f32[2,64,256]{2,1,0:T(8,128)S(1)}, f32[2,64,256]{2,1,0:T(8,128)S(1)}, u32[]{:S(2)}, u32[]{:S(2)}) collective-permute-start(f32[2,64,256]{2,1,0:T(8,128)S(1)} %fusion.40), channel_id=1, source_target_pairs={{0,16},{16,0},{8,24},{24,8},{32,48},{48,32},{40,56},{56,40},{64,80... | collective-permute-start | bytes 393224 | tf_op jit(solution)/shard_map/ppermute | solution.py:20
  34.0 12.0 %collective-permute-start.2 = (f32[2,64,256]{2,1,0:T(8,128)S(1)}, f32[2,64,256]{2,1,0:T(8,128)S(1)}, u32[]{:S(2)}, u32[]{:S(2)}) collective-permute-start(f32[2,64,256]{2,1,0:T(8,128)S(1)} %fusion.38), channel_id=1, source_target_pairs={{0,32},{32,0},{8,40},{40,8},{16,48},{48,16},{24,56},{56,24},{64,96... | collective-permute-start | bytes 393224 | tf_op jit(solution)/shard_map/ppermute | solution.py:20
  46.3 7.0 %collective-permute-start.3 = (f32[2,64,256]{2,1,0:T(8,128)S(1)}, f32[2,64,256]{2,1,0:T(8,128)S(1)}, u32[]{:S(2)}, u32[]{:S(2)}) collective-permute-start(f32[2,64,256]{2,1,0:T(8,128)S(1)} %fusion.36), channel_id=1, source_target_pairs={{0,64},{64,0},{8,72},{72,8},{16,80},{80,16},{24,88},{88,24},{32,96... | collective-permute-start | bytes 393224 | tf_op jit(solution)/shard_map/ppermute | solution.py:20
  49.7 14.4 %copy-start.3 = (bf16[32,256]{1,0:T(8,128)(2,1)S(1)}, bf16[32,256]{1,0:T(8,128)(2,1)}, u32[]{:S(2)}) copy-start(bf16[32,256]{1,0:T(8,128)(2,1)} %param.9) | copy-start | bytes 49156
  53.7 10.1 %collective-permute-start.4 = (f32[2,64,256]{2,1,0:T(8,128)S(1)}, f32[2,64,256]{2,1,0:T(8,128)S(1)}, u32[]{:S(2)}, u32[]{:S(2)}) collective-permute-start(f32[2,64,256]{2,1,0:T(8,128)S(1)} %fusion.34), channel_id=1, source_target_pairs={{0,128},{128,0},{8,136},{136,8},{16,144},{144,16},{24,152},{152,24... | collective-permute-start | bytes 393224 | tf_op jit(solution)/shard_map/ppermute | solution.py:20
  64.1 43.2 %copy-start.2 = (bf16[128,256]{1,0:T(8,128)(2,1)S(1)}, bf16[128,256]{1,0:T(8,128)(2,1)}, u32[]{:S(2)}) copy-start(bf16[128,256]{1,0:T(8,128)(2,1)} %param.5) | copy-start | bytes 196612
  65.3 43.2 %all-to-all-start.1 = ((bf16[64,32,256]{2,1,0:T(8,128)(2,1)}), bf16[64,32,256]{2,1,0:T(8,128)(2,1)S(1)}, u32[]{:S(2)}, u32[]{:S(2)}) async-start(bf16[64,32,256]{2,1,0:T(8,128)(2,1)} %broadcast_in_dim.17), calls=%async_computation.1 | async-start | bytes 2097152 | tf_op jit(solution)/shard_map/all_to_all | solution.py:31
  76.6 84.1 %reduce-scatter.2.cloned.1.call-start = ((), (), s32[]{:S(2)}) async-start(), calls=%async_computation.4 | async-start | bytes 2359296 | tf_op jit(solution)/shard_map/reduce_scatter | solution.py:40
  76.8 30.5 %collective-permute-start.5 = (bf16[2,64,256]{2,1,0:T(8,128)(2,1)S(1)}, bf16[2,64,256]{2,1,0:T(8,128)(2,1)S(1)}, u32[]{:S(2)}, u32[]{:S(2)}) collective-permute-start(bf16[2,64,256]{2,1,0:T(8,128)(2,1)S(1)} %fusion.32), channel_id=1, source_target_pairs={{0,256},{256,0},{8,264},{264,8},{16,272},{272,16},{24,280},{280,24... | collective-permute-start | bytes 196616 | tf_op jit(solution)/shard_map/ppermute | solution.py:20
  110.3 10.1 %collective-permute-start.6 = (bf16[2,64,256]{2,1,0:T(8,128)(2,1)S(1)}, bf16[2,64,256]{2,1,0:T(8,128)(2,1)S(1)}, u32[]{:S(2)}, u32[]{:S(2)}) collective-permute-start(bf16[2,64,256]{2,1,0:T(8,128)(2,1)S(1)} %fusion.17), channel_id=1, source_target_pairs={{0,256},{256,0},{8,264},{264,8},{16,272},{272,16},{24,280},{280,24... | collective-permute-start | bytes 196616 | tf_op jit(solution)/shard_map/ppermute | solution.py:20
  120.7 7.7 %collective-permute-start.7 = (bf16[2,64,256]{2,1,0:T(8,128)(2,1)S(1)}, bf16[2,64,256]{2,1,0:T(8,128)(2,1)S(1)}, u32[]{:S(2)}, u32[]{:S(2)}) collective-permute-start(bf16[2,64,256]{2,1,0:T(8,128)(2,1)S(1)} %fusion.20), channel_id=1, source_target_pairs={{0,128},{128,0},{8,136},{136,8},{16,144},{144,16},{24,152},{152,24... | collective-permute-start | bytes 196616 | tf_op jit(solution)/shard_map/ppermute | solution.py:20
  128.6 7.1 %collective-permute-start.8 = (bf16[2,64,256]{2,1,0:T(8,128)(2,1)S(1)}, bf16[2,64,256]{2,1,0:T(8,128)(2,1)S(1)}, u32[]{:S(2)}, u32[]{:S(2)}) collective-permute-start(bf16[2,64,256]{2,1,0:T(8,128)(2,1)S(1)} %fusion.23), channel_id=1, source_target_pairs={{0,64},{64,0},{8,72},{72,8},{16,80},{80,16},{24,88},{88,24},{32,96... | collective-permute-start | bytes 196616 | tf_op jit(solution)/shard_map/ppermute | solution.py:20
  136.0 10.2 %collective-permute-start.9 = (bf16[2,64,256]{2,1,0:T(8,128)(2,1)S(1)}, bf16[2,64,256]{2,1,0:T(8,128)(2,1)S(1)}, u32[]{:S(2)}, u32[]{:S(2)}) collective-permute-start(bf16[2,64,256]{2,1,0:T(8,128)(2,1)S(1)} %fusion.26), channel_id=1, source_target_pairs={{0,32},{32,0},{8,40},{40,8},{16,48},{48,16},{24,56},{56,24},{64,96... | collective-permute-start | bytes 196616 | tf_op jit(solution)/shard_map/ppermute | solution.py:20
  146.4 7.8 %collective-permute-start.10 = (bf16[2,64,256]{2,1,0:T(8,128)(2,1)S(1)}, bf16[2,64,256]{2,1,0:T(8,128)(2,1)S(1)}, u32[]{:S(2)}, u32[]{:S(2)}) collective-permute-start(bf16[2,64,256]{2,1,0:T(8,128)(2,1)S(1)} %fusion.15), channel_id=1, source_target_pairs={{0,16},{16,0},{8,24},{24,8},{32,48},{48,32},{40,56},{56,40},{64,80... | collective-permute-start | bytes 196616 | tf_op jit(solution)/shard_map/ppermute | solution.py:20
  154.5 6.2 %collective-permute-start.11 = (bf16[2,64,256]{2,1,0:T(8,128)(2,1)S(1)}, bf16[2,64,256]{2,1,0:T(8,128)(2,1)S(1)}, u32[]{:S(2)}, u32[]{:S(2)}) collective-permute-start(bf16[2,64,256]{2,1,0:T(8,128)(2,1)S(1)} %fusion.28), channel_id=1, source_target_pairs={{0,8},{8,0},{16,24},{24,16},{32,40},{40,32},{48,56},{56,48},{64,72... | collective-permute-start | bytes 196616 | tf_op jit(solution)/shard_map/ppermute | solution.py:20
  162.6 17.4 %all-to-all-start.2 = ((f32[8,32,256]{2,1,0:T(8,128)}), f32[8,32,256]{2,1,0:T(8,128)S(1)}, u32[]{:S(2)}, u32[]{:S(2)}) async-start(f32[8,32,256]{2,1,0:T(8,128)} %bitcast.40), calls=%async_computation.3 | async-start | bytes 524288 | tf_op jit(solution)/shard_map/all_to_all | solution.py:43
Sparse Core Ops, SparseCore 0:
  115.4 45.1 reduce-scatter.1

commit v3 on v2

--- a/solution.py
+++ b/solution.py
@@ -55,6 +55,41 @@
     return doubled.reshape(table.shape[0], table.shape[1] * 2, table.shape[2])
 
 
+def top_bit(d):
+    total = jnp.zeros_like(d) - 1
+    for k in range(0, 7):
+        total = total + (d >= (1 << k)).astype(d.dtype)
+    return total
+
+
+def pooled(table, factor):
+    return table.reshape(table.shape[0], table.shape[1] // factor, factor, table.shape[2]).mean(axis=2)
+
+
+def pad_rows(x, rows):
+    return jnp.pad(x, ((0, 0), (0, rows - x.shape[1]), (0, 0)))
+
+
+def pick_level(level_of, tables, lo):
+    out = tables[-1]
+    for i in range(len(tables) - 2, -1, -1):
+        mask = (level_of == lo + i).reshape((-1,) + (1,) * (tables[i].ndim - 1))
+        out = jnp.where(mask, tables[i], out)
+    return out
+
+
+def sibling_rows(recv, start, level, rows):
+    count = 1 << level
+    part = lax.dynamic_slice_in_dim(recv, start, count, axis=0)[:, :, :rows]
+    part = jnp.moveaxis(part, 0, 1)
+    return part.reshape(part.shape[0], count * rows, part.shape[3])
+
+
+def swap_major(block, axis, bit):
+    count = lax.axis_size(axis)
+    return lax.ppermute(block, axis, [(i, i ^ (1 << bit)) for i in range(count)])
+
+
 def on_device(queries, keys, values, cotangent, out_weight):
     tokens = queries.shape[0]
     width = queries.shape[1]
@@ -63,25 +98,51 @@
     scale = 1.0 / math.sqrt(HEAD)
     depth = lax.axis_size(SEQ).bit_length() - 1
     position = lax.axis_index(SEQ)
-    own_table = pair_mean(jnp.stack([keys, values]).astype(jnp.float32))
-    far_keys = []
-    far_values = []
-    for layer_bit in range(depth):
-        far_table = from_partner(own_table, SEQ, layer_bit)
-        far_keys.append(far_table[0].astype(jnp.bfloat16))
-        far_values.append(far_table[1].astype(jnp.bfloat16))
-        if layer_bit + 1 < depth:
-            lower_half = position >> layer_bit & 1 == 0
-            joined = jnp.concatenate(
-                [
-                    jnp.where(lower_half, own_table, far_table),
-                    jnp.where(lower_half, far_table, own_table),
-                ],
-                axis=1,
+    major, minor = SEQ
+    n_minor = lax.axis_size(minor)
+    minor_depth = n_minor.bit_length() - 1
+    minor_pos = lax.axis_index(minor)
+    major_pos = lax.axis_index(major)
+    table = jnp.stack([keys, values]).astype(jnp.float32)
+    means = [pooled(table, 2 << m).astype(jnp.bfloat16) for m in range(depth)]
+    peers = jnp.arange(n_minor, dtype=jnp.int32)
+    near_level = top_bit(minor_pos ^ peers)
+    near_kv = pick_level(
+        near_level,
+        [jnp.broadcast_to(pad_rows(means[m], coarse)[None], (n_minor, 2, coarse, width)) for m in range(minor_depth)],
+        0,
+    )
+    upper = jnp.concatenate(means[minor_depth:], axis=1)
+    near_send = jnp.concatenate(
+        [near_kv, jnp.broadcast_to(upper[None], (n_minor,) + upper.shape)], axis=2
+    )
+    near_recv = lax.all_to_all(near_send, minor, 0, 0, tiled=True)
+    levels_kv = []
+    for m in range(minor_depth):
+        start = ((minor_pos >> m) ^ 1) << m
+        levels_kv.append(sibling_rows(near_recv[:, :, :coarse], start, m, coarse >> m))
+    slices = []
+    offset = coarse
+    for m in range(minor_depth, depth):
+        rows = coarse >> m
+        part = jnp.moveaxis(near_recv[:, :, offset : offset + rows], 0, 1)
+        slices.append(part.reshape(2, n_minor * rows, width))
+        offset += rows
+    for r in range(depth - minor_depth):
+        got = swap_major(jnp.concatenate(slices, axis=1), major, r)
+        levels_kv.append(got[:, :coarse])
+        lower_half = (major_pos >> r) & 1 == 0
+        joined = []
+        used = coarse
+        for own in slices[1:]:
+            far = got[:, used : used + own.shape[1]]
+            used += own.shape[1]
+            joined.append(
+                jnp.where(lower_half, jnp.concatenate([own, far], 1), jnp.concatenate([far, own], 1))
             )
-            own_table = pair_mean(joined)
-    key_set = jnp.concatenate([keys] + far_keys, axis=0)
-    value_set = jnp.concatenate([values] + far_values, axis=0)
+        slices = joined
+    key_set = jnp.concatenate([keys] + [lv[0] for lv in levels_kv], axis=0)
+    value_set = jnp.concatenate([values] + [lv[1] for lv in levels_kv], axis=0)
     full_cot = gathered_copies(cotangent, "dp", 1)
     full_weight = gathered_copies(out_weight, SEQ, 0)
     grad_attended = jnp.dot(full_cot, full_weight, preferred_element_type=jnp.float32).astype(

time: 188 us -> 192 us (1.021)
  other arithmetic: 1.77 us -> 8.03 us
  starting transfers between devices: 71.5 us -> 67.3 us
    ppermute x12 -> x6, waiting for transfers between devices: 73.7 us -> 20.8 us  [from_partner(): return lax.ppermute(block, axis, route)]
    ppermute x0 -> x3, waiting for transfers between devices: none -> 33.4 us  [swap_major(): return lax.ppermute(block, axis, [(i, i ^ 1 << bit) for i in range(count)])]
    ppermute x12 -> x6, starting transfers between devices: 45.5 us -> 23.9 us  [from_partner(): return lax.ppermute(block, axis, route)]
    all_to_all x0 -> x1, waiting for transfers between devices: none -> 19.8 us  [on_device(): near_recv = lax.all_to_all(near_send, minor, 0, 0, tiled=True)]
    ppermute x0 -> x3, starting transfers between devices: none -> 14.1 us  [swap_major(): return lax.ppermute(block, axis, [(i, i ^ 1 << bit) for i in range(count)])]
    all_to_all x0 -> x1, starting transfers between devices: none -> 7.1 us  [on_device(): near_recv = lax.all_to_all(near_send, minor, 0, 0, tiled=True)]
    reduce_sum x0 -> x6, other arithmetic: none -> 4.22 us  [pooled(): table.reshape(table.shape[0], table.shape[1] // factor, factor, table.sha...]
    all_to_all x2, starting transfers between devices: 19.1 us -> 16 us  [from_everyone(): return lax.all_to_all(copies, axis, split_axis=0, concat_axis=0, tiled=True)]
  transfers between devices with their start and end apart: 16 -> 14, of which waited for: 12 -> 11; matrix products, arithmetic and copies ran while one was open for 6% -> 4% of each run, Pallas kernels for 0% -> 0%
where the time goes in v3:
time: 192 us; the launch traced here: 190 us
  waiting for transfers between devices  83.6 us (44%)
  starting transfers between devices  67.3 us (35%)
  between operations  14.9 us (8%)
  local copies, waits for them, and re-layouts  11.7 us (6%)
  other arithmetic  8.03 us (4%)
  matrix products  4.71 us (2%)
    ppermute x3, waiting for transfers between devices, swap_major(): return lax.ppermute(block, axis, [(i, i ^ 1 << bit) for i in range(count)])  33.4 us
    ppermute x6, starting transfers between devices, from_partner(): return lax.ppermute(block, axis, route)  23.9 us
    ppermute x6, waiting for transfers between devices, from_partner(): return lax.ppermute(block, axis, route)  20.8 us
    all_to_all x1, waiting for transfers between devices, on_device(): near_recv = lax.all_to_all(near_send, minor, 0, 0, tiled=True)  19.8 us
    all_to_all x2, starting transfers between devices, from_everyone(): return lax.all_to_all(copies, axis, split_axis=0, concat_axis=0, tiled=True)  16 us
    ppermute x3, starting transfers between devices, swap_major(): return lax.ppermute(block, axis, [(i, i ^ 1 << bit) for i in range(count)])  14.1 us
    all_to_all x1, waiting for transfers between devices, own_rows(): return jnp.sum(lax.all_to_all(parts, last, 0, 0, tiled=True), axis=0)  9.71 us
    all_to_all x1, starting transfers between devices, on_device(): near_recv = lax.all_to_all(near_send, minor, 0, 0, tiled=True)  7.1 us
  transfers between devices with their start and end apart: 14, of which 11 were waited for; matrix products, arithmetic and copies ran while one was open for 4% of the time, Pallas kernels for 0%

profile of v3, /device:TPU:6, one launch (start us, length us, event | category | flops | bytes accessed | tf_op | source)
XLA Modules:
  0.0 190.3 jit_solution(17403855463173331930)
XLA Ops:
  7.2 0.9 stack.52
  8.0 0.9 stack.49
  8.9 0.9 stack.51
  9.8 0.9 stack.48
  10.6 0.9 convert_reduce_fusion
  11.6 0.9 convert_reduce_fusion.1
  12.5 0.9 convert_reduce_fusion.2
  13.5 1.0 convert_reduce_fusion.3
  14.5 0.2 convert_reduce_fusion.4
  14.8 0.4 convert_reduce_fusion.5
  15.3 0.7 broadcast_select_fusion
  16.0 1.7 pad_maximum_fusion
  17.7 7.1 %all-to-all-start = ((bf16[8,2,78,256]{3,1,2,0:T(2,128)(2,1)}), bf16[8,2,78,256]{3,1,2,0:T(2,128)(2,1)S(1)}, u32[]{:S(2)}, u32[]{:S(2)}) async-start(bf16[8,2,78,256]{3,1,2,0:T(2,128)(2,1)} %pad_maximum_fusion), calls=%async_computation | async-start | bytes 1277952 | tf_op jit(solution)/shard_map/all_to_all | solution.py:119
  24.8 0.1 copy.178
  25.0 19.8 %all-to-all-done = bf16[8,2,78,256]{3,1,2,0:T(2,128)(2,1)S(1)} async-done(((bf16[8,2,78,256]{3,1,2,0:T(2,128)(2,1)}), bf16[8,2,78,256]{3,1,2,0:T(2,128)(2,1)S(1)}, u32[]{:S(2)}, u32[]{:S(2)}) %all-to-all-start) | async-done | bytes 639008 | tf_op jit(solution)/shard_map/all_to_all | solution.py:119
  44.8 0.9 broadcast_in_dim.43
  45.6 4.9 %all-to-all-start.1 = ((bf16[8,128,256]{1,2,0:T(8,128)(2,1)}), bf16[8,128,256]{1,2,0:T(8,128)(2,1)S(1)}, u32[]{:S(2)}, u32[]{:S(2)}) async-start(bf16[8,128,256]{1,2,0:T(8,128)(2,1)} %broadcast_in_dim.43), calls=%async_computation.1 | async-start | bytes 1048576 | tf_op jit(solution)/shard_map/all_to_all | solution.py:31
  50.5 0.4 slice.209
  51.2 4.3 %collective-permute-start = (bf16[2,112,256]{2,1,0:T(8,128)(2,1)S(1)}, bf16[2,112,256]{2,1,0:T(8,128)(2,1)S(1)}, u32[]{:S(2)}, u32[]{:S(2)}) collective-permute-start(bf16[2,112,256]{2,1,0:T(8,128)(2,1)S(1)} %pad_maximum_fusion.2), channel_id=1, source_target_pairs={{0,64},{64,0},{128,192},{192,128},{256,320},{320,256},{384,448},{4... | collective-permute-start | bytes 344072 | tf_op jit(solution)/shard_map/ppermute | solution.py:90
  55.5 0.1 constant_dynamic-slice_fusion
  55.7 3.2 %collective-permute-done = bf16[2,112,256]{2,1,0:T(8,128)(2,1)S(1)} collective-permute-done((bf16[2,112,256]{2,1,0:T(8,128)(2,1)S(1)}, bf16[2,112,256]{2,1,0:T(8,128)(2,1)S(1)}, u32[]{:S(2)}, u32[]{:S(2)}) %collective-permute-start) | collective-permute-done | bytes 114720 | tf_op jit(solution)/shard_map/ppermute | solution.py:90
  59.1 1.1 broadcast_in_dim.44
  60.2 11.1 %all-to-all-start.2 = ((bf16[64,32,256]{2,1,0:T(8,128)(2,1)}), bf16[64,32,256]{2,1,0:T(8,128)(2,1)S(1)}, u32[]{:S(2)}, u32[]{:S(2)}) async-start(bf16[64,32,256]{2,1,0:T(8,128)(2,1)} %broadcast_in_dim.44), calls=%async_computation.2 | async-start | bytes 2097152 | tf_op jit(solution)/shard_map/all_to_all | solution.py:31
  71.3 4.4 %collective-permute-start.1 = (bf16[2,96,256]{2,1,0:T(8,128)(2,1)S(1)}, bf16[2,96,256]{2,1,0:T(8,128)(2,1)S(1)}, u32[]{:S(2)}, u32[]{:S(2)}) collective-permute-start(bf16[2,96,256]{2,1,0:T(8,128)(2,1)S(1)} %pad_maximum_fusion.3), channel_id=1, source_target_pairs={{0,128},{64,192},{128,0},{192,64},{256,384},{320,448},{384,256},{4... | collective-permute-start | bytes 294920 | tf_op jit(solution)/shard_map/ppermute | solution.py:90
  75.7 24.9 %collective-permute-done.1 = bf16[2,96,256]{2,1,0:T(8,128)(2,1)S(1)} collective-permute-done((bf16[2,96,256]{2,1,0:T(8,128)(2,1)S(1)}, bf16[2,96,256]{2,1,0:T(8,128)(2,1)S(1)}, u32[]{:S(2)}, u32[]{:S(2)}) %collective-permute-start.1) | collective-permute-done | bytes 98336 | tf_op jit(solution)/shard_map/ppermute | solution.py:90
  100.6 5.5 %collective-permute-start.2 = (bf16[2,64,256]{2,1,0:T(8,128)(2,1)S(1)}, bf16[2,64,256]{2,1,0:T(8,128)(2,1)S(1)}, u32[]{:S(2)}, u32[]{:S(2)}) collective-permute-start(bf16[2,64,256]{2,1,0:T(8,128)(2,1)S(1)} %maximum_select_fusion.1), channel_id=1, source_target_pairs={{0,256},{64,320},{128,384},{192,448},{256,0},{320,64},{384,128},{4... | collective-permute-start | bytes 196616 | tf_op jit(solution)/shard_map/ppermute | solution.py:90
  106.1 5.3 %collective-permute-done.2 = bf16[2,64,256]{2,1,0:T(8,128)(2,1)S(1)} collective-permute-done((bf16[2,64,256]{2,1,0:T(8,128)(2,1)S(1)}, bf16[2,64,256]{2,1,0:T(8,128)(2,1)S(1)}, u32[]{:S(2)}, u32[]{:S(2)}) %collective-permute-start.2) | collective-permute-done | bytes 65568 | tf_op jit(solution)/shard_map/ppermute | solution.py:90
  111.4 0.2 fusion.77
  111.7 0.2 fusion.78
  112.1 0.2 convolution_convert_fusion.3
  112.3 0.2 convolution_convert_fusion.4
  112.5 0.4 convolution_convert_fusion
  112.9 0.2 fusion.3
  113.2 0.2 fusion.6
  113.4 0.2 fusion.40
  113.6 0.2 fusion.39
  113.8 0.2 fusion.53
  114.1 0.2 fusion.56
  114.4 4.8 %collective-permute-start.3 = (bf16[2,64,256]{2,1,0:T(8,128)(2,1)S(1)}, bf16[2,64,256]{2,1,0:T(8,128)(2,1)S(1)}, u32[]{:S(2)}, u32[]{:S(2)}) collective-permute-start(bf16[2,64,256]{2,1,0:T(8,128)(2,1)S(1)} %fusion.17), channel_id=1, source_target_pairs={{0,256},{256,0},{8,264},{264,8},{16,272},{272,16},{24,280},{280,24... | collective-permute-start | bytes 196616 | tf_op jit(solution)/shard_map/ppermute | solution.py:20
  119.2 1.8 convolution_bitcast_fusion
  121.0 3.8 %collective-permute-done.3 = bf16[2,64,256]{2,1,0:T(8,128)(2,1)S(1)} collective-permute-done((bf16[2,64,256]{2,1,0:T(8,128)(2,1)S(1)}, bf16[2,64,256]{2,1,0:T(8,128)(2,1)S(1)}, u32[]{:S(2)}, u32[]{:S(2)}) %collective-permute-start.3) | collective-permute-done | bytes 65568 | tf_op jit(solution)/shard_map/ppermute | solution.py:20
  124.8 0.1 copy.187
  125.0 1.9 %collective-permute-start.4 = (bf16[2,64,256]{2,1,0:T(8,128)(2,1)S(1)}, bf16[2,64,256]{2,1,0:T(8,128)(2,1)S(1)}, u32[]{:S(2)}, u32[]{:S(2)}) collective-permute-start(bf16[2,64,256]{2,1,0:T(8,128)(2,1)S(1)} %fusion.20), channel_id=1, source_target_pairs={{0,128},{128,0},{8,136},{136,8},{16,144},{144,16},{24,152},{152,24... | collective-permute-start | bytes 196616 | tf_op jit(solution)/shard_map/ppermute | solution.py:20
  127.0 5.1 %collective-permute-done.4 = bf16[2,64,256]{2,1,0:T(8,128)(2,1)S(1)} collective-permute-done((bf16[2,64,256]{2,1,0:T(8,128)(2,1)S(1)}, bf16[2,64,256]{2,1,0:T(8,128)(2,1)S(1)}, u32[]{:S(2)}, u32[]{:S(2)}) %collective-permute-start.4) | collective-permute-done | bytes 65568 | tf_op jit(solution)/shard_map/ppermute | solution.py:20
  132.1 0.1 copy.190
  132.4 1.9 %collective-permute-start.5 = (bf16[2,64,256]{2,1,0:T(8,128)(2,1)S(1)}, bf16[2,64,256]{2,1,0:T(8,128)(2,1)S(1)}, u32[]{:S(2)}, u32[]{:S(2)}) collective-permute-start(bf16[2,64,256]{2,1,0:T(8,128)(2,1)S(1)} %fusion.23), channel_id=1, source_target_pairs={{0,64},{64,0},{8,72},{72,8},{16,80},{80,16},{24,88},{88,24},{32,96... | collective-permute-start | bytes 196616 | tf_op jit(solution)/shard_map/ppermute | solution.py:20
  134.3 0.7 copy.205
  135.1 4.0 %collective-permute-done.5 = bf16[2,64,256]{2,1,0:T(8,128)(2,1)S(1)} collective-permute-done((bf16[2,64,256]{2,1,0:T(8,128)(2,1)S(1)}, bf16[2,64,256]{2,1,0:T(8,128)(2,1)S(1)}, u32[]{:S(2)}, u32[]{:S(2)}) %collective-permute-start.5) | collective-permute-done | bytes 65568 | tf_op jit(solution)/shard_map/ppermute | solution.py:20
  139.0 0.1 copy.193
  139.3 6.6 %collective-permute-start.6 = (bf16[2,64,256]{2,1,0:T(8,128)(2,1)S(1)}, bf16[2,64,256]{2,1,0:T(8,128)(2,1)S(1)}, u32[]{:S(2)}, u32[]{:S(2)}) collective-permute-start(bf16[2,64,256]{2,1,0:T(8,128)(2,1)S(1)} %fusion.26), channel_id=1, source_target_pairs={{0,32},{32,0},{8,40},{40,8},{16,48},{48,16},{24,56},{56,24},{64,96... | collective-permute-start | bytes 196616 | tf_op jit(solution)/shard_map/ppermute | solution.py:20
  145.9 0.2 convolution_convert_fusion.1
  146.1 3.2 %collective-permute-done.6 = bf16[2,64,256]{2,1,0:T(8,128)(2,1)S(1)} collective-permute-done((bf16[2,64,256]{2,1,0:T(8,128)(2,1)S(1)}, bf16[2,64,256]{2,1,0:T(8,128)(2,1)S(1)}, u32[]{:S(2)}, u32[]{:S(2)}) %collective-permute-start.6) | collective-permute-done | bytes 65568 | tf_op jit(solution)/shard_map/ppermute | solution.py:20
  149.4 0.1 copy.196
  149.6 5.6 %collective-permute-start.7 = (bf16[2,64,256]{2,1,0:T(8,128)(2,1)S(1)}, bf16[2,64,256]{2,1,0:T(8,128)(2,1)S(1)}, u32[]{:S(2)}, u32[]{:S(2)}) collective-permute-start(bf16[2,64,256]{2,1,0:T(8,128)(2,1)S(1)} %fusion.15), channel_id=1, source_target_pairs={{0,16},{16,0},{8,24},{24,8},{32,48},{48,32},{40,56},{56,40},{64,80... | collective-permute-start | bytes 196616 | tf_op jit(solution)/shard_map/ppermute | solution.py:20
  155.2 0.2 convolution_convert_fusion.2
  155.5 2.3 %collective-permute-done.7 = bf16[2,64,256]{2,1,0:T(8,128)(2,1)S(1)} collective-permute-done((bf16[2,64,256]{2,1,0:T(8,128)(2,1)S(1)}, bf16[2,64,256]{2,1,0:T(8,128)(2,1)S(1)}, u32[]{:S(2)}, u32[]{:S(2)}) %collective-permute-start.7) | collective-permute-done | bytes 65568 | tf_op jit(solution)/shard_map/ppermute | solution.py:20
  158.1 3.0 %collective-permute-start.8 = (bf16[2,64,256]{2,1,0:T(8,128)(2,1)S(1)}, bf16[2,64,256]{2,1,0:T(8,128)(2,1)S(1)}, u32[]{:S(2)}, u32[]{:S(2)}) collective-permute-start(bf16[2,64,256]{2,1,0:T(8,128)(2,1)S(1)} %fusion.28), channel_id=1, source_target_pairs={{0,8},{8,0},{16,24},{24,16},{32,40},{40,32},{48,56},{56,48},{64,72... | collective-permute-start | bytes 196616 | tf_op jit(solution)/shard_map/ppermute | solution.py:20
  161.1 0.7 copy.206
  161.9 2.3 %collective-permute-done.8 = bf16[2,64,256]{2,1,0:T(8,128)(2,1)S(1)} collective-permute-done((bf16[2,64,256]{2,1,0:T(8,128)(2,1)S(1)}, bf16[2,64,256]{2,1,0:T(8,128)(2,1)S(1)}, u32[]{:S(2)}, u32[]{:S(2)}) %collective-permute-start.8) | collective-permute-done | bytes 65568 | tf_op jit(solution)/shard_map/ppermute | solution.py:20
  164.4 1.8 copy.204
  166.2 6.2 %all-to-all-start.3 = ((f32[8,32,256]{2,1,0:T(8,128)}), f32[8,32,256]{2,1,0:T(8,128)S(1)}, u32[]{:S(2)}, u32[]{:S(2)}) async-start(f32[8,32,256]{2,1,0:T(8,128)} %bitcast.47), calls=%async_computation.4 | async-start | bytes 524288 | tf_op jit(solution)/shard_map/all_to_all | solution.py:43
  172.5 0.7 slice_bitcast_fusion
  173.2 9.7 %all-to-all-done.3 = f32[8,32,256]{2,1,0:T(8,128)S(1)} async-done(((f32[8,32,256]{2,1,0:T(8,128)}), f32[8,32,256]{2,1,0:T(8,128)S(1)}, u32[]{:S(2)}, u32[]{:S(2)}) %all-to-all-start.3) | async-done | bytes 262176 | tf_op jit(solution)/shard_map/all_to_all | solution.py:43
  182.9 0.6 reduce_sum.109
  (95 shorter events, 2.3 us)
Async XLA Ops:
  14.7 10.1 %copy-start.3 = (bf16[128,256]{1,0:T(8,128)(2,1)S(1)}, bf16[128,256]{1,0:T(8,128)(2,1)}, u32[]{:S(2)}) copy-start(bf16[128,256]{1,0:T(8,128)(2,1)} %param.8) | copy-start | bytes 196612
  14.8 10.1 %copy-start = (bf16[128,256]{1,0:T(8,128)(2,1)S(1)}, bf16[128,256]{1,0:T(8,128)(2,1)}, u32[]{:S(2)}) copy-start(bf16[128,256]{1,0:T(8,128)(2,1)} %param.6) | copy-start | bytes 196612
  15.2 9.8 %copy-start.1 = (bf16[128,256]{1,0:T(8,128)(2,1)S(1)}, bf16[128,256]{1,0:T(8,128)(2,1)}, u32[]{:S(2)}) copy-start(bf16[128,256]{1,0:T(8,128)(2,1)} %param.7) | copy-start | bytes 196612
  17.7 27.1 %all-to-all-start = ((bf16[8,2,78,256]{3,1,2,0:T(2,128)(2,1)}), bf16[8,2,78,256]{3,1,2,0:T(2,128)(2,1)S(1)}, u32[]{:S(2)}, u32[]{:S(2)}) async-start(bf16[8,2,78,256]{3,1,2,0:T(2,128)(2,1)} %pad_maximum_fusion), calls=%async_computation | async-start | bytes 1277952 | tf_op jit(solution)/shard_map/all_to_all | solution.py:119
  45.6 13.4 %copy-start.4 = (bf16[32,256]{1,0:T(8,128)(2,1)S(1)}, bf16[32,256]{1,0:T(8,128)(2,1)}, u32[]{:S(2)}) copy-start(bf16[32,256]{1,0:T(8,128)(2,1)} %param.9) | copy-start | bytes 49156
  45.6 13.4 %all-to-all-start.1 = ((bf16[8,128,256]{1,2,0:T(8,128)(2,1)}), bf16[8,128,256]{1,2,0:T(8,128)(2,1)S(1)}, u32[]{:S(2)}, u32[]{:S(2)}) async-start(bf16[8,128,256]{1,2,0:T(8,128)(2,1)} %broadcast_in_dim.43), calls=%async_computation.1 | async-start | bytes 1048576 | tf_op jit(solution)/shard_map/all_to_all | solution.py:31
  51.2 7.7 %collective-permute-start = (bf16[2,112,256]{2,1,0:T(8,128)(2,1)S(1)}, bf16[2,112,256]{2,1,0:T(8,128)(2,1)S(1)}, u32[]{:S(2)}, u32[]{:S(2)}) collective-permute-start(bf16[2,112,256]{2,1,0:T(8,128)(2,1)S(1)} %pad_maximum_fusion.2), channel_id=1, source_target_pairs={{0,64},{64,0},{128,192},{192,128},{256,320},{320,256},{384,448},{4... | collective-permute-start | bytes 344072 | tf_op jit(solution)/shard_map/ppermute | solution.py:90
  59.0 52.4 %copy-start.2 = (bf16[128,256]{1,0:T(8,128)(2,1)S(1)}, bf16[128,256]{1,0:T(8,128)(2,1)}, u32[]{:S(2)}) copy-start(bf16[128,256]{1,0:T(8,128)(2,1)} %param.5) | copy-start | bytes 196612
  60.2 52.4 %all-to-all-start.2 = ((bf16[64,32,256]{2,1,0:T(8,128)(2,1)}), bf16[64,32,256]{2,1,0:T(8,128)(2,1)S(1)}, u32[]{:S(2)}, u32[]{:S(2)}) async-start(bf16[64,32,256]{2,1,0:T(8,128)(2,1)} %broadcast_in_dim.44), calls=%async_computation.2 | async-start | bytes 2097152 | tf_op jit(solution)/shard_map/all_to_all | solution.py:31
  71.2 93.2 %reduce-scatter.2.cloned.1.call-start = ((), (), s32[]{:S(2)}) async-start(), calls=%async_computation.5 | async-start | bytes 2359296 | tf_op jit(solution)/shard_map/reduce_scatter | solution.py:40
  71.3 29.3 %collective-permute-start.1 = (bf16[2,96,256]{2,1,0:T(8,128)(2,1)S(1)}, bf16[2,96,256]{2,1,0:T(8,128)(2,1)S(1)}, u32[]{:S(2)}, u32[]{:S(2)}) collective-permute-start(bf16[2,96,256]{2,1,0:T(8,128)(2,1)S(1)} %pad_maximum_fusion.3), channel_id=1, source_target_pairs={{0,128},{64,192},{128,0},{192,64},{256,384},{320,448},{384,256},{4... | collective-permute-start | bytes 294920 | tf_op jit(solution)/shard_map/ppermute | solution.py:90
  100.6 10.8 %collective-permute-start.2 = (bf16[2,64,256]{2,1,0:T(8,128)(2,1)S(1)}, bf16[2,64,256]{2,1,0:T(8,128)(2,1)S(1)}, u32[]{:S(2)}, u32[]{:S(2)}) collective-permute-start(bf16[2,64,256]{2,1,0:T(8,128)(2,1)S(1)} %maximum_select_fusion.1), channel_id=1, source_target_pairs={{0,256},{64,320},{128,384},{192,448},{256,0},{320,64},{384,128},{4... | collective-permute-start | bytes 196616 | tf_op jit(solution)/shard_map/ppermute | solution.py:90
  114.4 10.4 %collective-permute-start.3 = (bf16[2,64,256]{2,1,0:T(8,128)(2,1)S(1)}, bf16[2,64,256]{2,1,0:T(8,128)(2,1)S(1)}, u32[]{:S(2)}, u32[]{:S(2)}) collective-permute-start(bf16[2,64,256]{2,1,0:T(8,128)(2,1)S(1)} %fusion.17), channel_id=1, source_target_pairs={{0,256},{256,0},{8,264},{264,8},{16,272},{272,16},{24,280},{280,24... | collective-permute-start | bytes 196616 | tf_op jit(solution)/shard_map/ppermute | solution.py:20
  125.0 7.1 %collective-permute-start.4 = (bf16[2,64,256]{2,1,0:T(8,128)(2,1)S(1)}, bf16[2,64,256]{2,1,0:T(8,128)(2,1)S(1)}, u32[]{:S(2)}, u32[]{:S(2)}) collective-permute-start(bf16[2,64,256]{2,1,0:T(8,128)(2,1)S(1)} %fusion.20), channel_id=1, source_target_pairs={{0,128},{128,0},{8,136},{136,8},{16,144},{144,16},{24,152},{152,24... | collective-permute-start | bytes 196616 | tf_op jit(solution)/shard_map/ppermute | solution.py:20
  132.4 6.6 %collective-permute-start.5 = (bf16[2,64,256]{2,1,0:T(8,128)(2,1)S(1)}, bf16[2,64,256]{2,1,0:T(8,128)(2,1)S(1)}, u32[]{:S(2)}, u32[]{:S(2)}) collective-permute-start(bf16[2,64,256]{2,1,0:T(8,128)(2,1)S(1)} %fusion.23), channel_id=1, source_target_pairs={{0,64},{64,0},{8,72},{72,8},{16,80},{80,16},{24,88},{88,24},{32,96... | collective-permute-start | bytes 196616 | tf_op jit(solution)/shard_map/ppermute | solution.py:20
  139.3 10.1 %collective-permute-start.6 = (bf16[2,64,256]{2,1,0:T(8,128)(2,1)S(1)}, bf16[2,64,256]{2,1,0:T(8,128)(2,1)S(1)}, u32[]{:S(2)}, u32[]{:S(2)}) collective-permute-start(bf16[2,64,256]{2,1,0:T(8,128)(2,1)S(1)} %fusion.26), channel_id=1, source_target_pairs={{0,32},{32,0},{8,40},{40,8},{16,48},{48,16},{24,56},{56,24},{64,96... | collective-permute-start | bytes 196616 | tf_op jit(solution)/shard_map/ppermute | solution.py:20
  149.6 8.2 %collective-permute-start.7 = (bf16[2,64,256]{2,1,0:T(8,128)(2,1)S(1)}, bf16[2,64,256]{2,1,0:T(8,128)(2,1)S(1)}, u32[]{:S(2)}, u32[]{:S(2)}) collective-permute-start(bf16[2,64,256]{2,1,0:T(8,128)(2,1)S(1)} %fusion.15), channel_id=1, source_target_pairs={{0,16},{16,0},{8,24},{24,8},{32,48},{48,32},{40,56},{56,40},{64,80... | collective-permute-start | bytes 196616 | tf_op jit(solution)/shard_map/ppermute | solution.py:20
  158.1 6.2 %collective-permute-start.8 = (bf16[2,64,256]{2,1,0:T(8,128)(2,1)S(1)}, bf16[2,64,256]{2,1,0:T(8,128)(2,1)S(1)}, u32[]{:S(2)}, u32[]{:S(2)}) collective-permute-start(bf16[2,64,256]{2,1,0:T(8,128)(2,1)S(1)} %fusion.28), channel_id=1, source_target_pairs={{0,8},{8,0},{16,24},{24,16},{32,40},{40,32},{48,56},{56,48},{64,72... | collective-permute-start | bytes 196616 | tf_op jit(solution)/shard_map/ppermute | solution.py:20
  166.2 16.7 %all-to-all-start.3 = ((f32[8,32,256]{2,1,0:T(8,128)}), f32[8,32,256]{2,1,0:T(8,128)S(1)}, u32[]{:S(2)}, u32[]{:S(2)}) async-start(f32[8,32,256]{2,1,0:T(8,128)} %bitcast.47), calls=%async_computation.4 | async-start | bytes 524288 | tf_op jit(solution)/shard_map/all_to_all | solution.py:43
Sparse Core Ops, SparseCore 0:
  121.1 42.6 reduce-scatter.1

commit v4 on v3

--- a/solution.py
+++ b/solution.py
@@ -104,7 +104,11 @@
     minor_pos = lax.axis_index(minor)
     major_pos = lax.axis_index(major)
     table = jnp.stack([keys, values]).astype(jnp.float32)
-    means = [pooled(table, 2 << m).astype(jnp.bfloat16) for m in range(depth)]
+    means = []
+    running = table
+    for m in range(depth):
+        running = pair_mean(running)
+        means.append(running.astype(jnp.bfloat16))
     peers = jnp.arange(n_minor, dtype=jnp.int32)
     near_level = top_bit(minor_pos ^ peers)
     near_kv = pick_level(
@@ -116,7 +120,15 @@
     near_send = jnp.concatenate(
         [near_kv, jnp.broadcast_to(upper[None], (n_minor,) + upper.shape)], axis=2
     )
-    near_recv = lax.all_to_all(near_send, minor, 0, 0, tiled=True)
+    kv_rows = near_send.shape[2]
+    w_rows = out_weight.shape[0]
+    near_send = jnp.concatenate(
+        [near_send.reshape(n_minor, 2 * kv_rows, width), jnp.broadcast_to(out_weight[None], (n_minor, w_rows, width))],
+        axis=1,
+    )
+    near_all = lax.all_to_all(near_send, minor, 0, 0, tiled=True)
+    near_recv = near_all[:, : 2 * kv_rows].reshape(n_minor, 2, kv_rows, width)
+    weight_rows = near_all[:, 2 * kv_rows :].reshape(n_minor * w_rows, width)
     levels_kv = []
     for m in range(minor_depth):
         start = ((minor_pos >> m) ^ 1) << m
@@ -129,9 +141,19 @@
         slices.append(part.reshape(2, n_minor * rows, width))
         offset += rows
     for r in range(depth - minor_depth):
-        got = swap_major(jnp.concatenate(slices, axis=1), major, r)
+        kv_all = jnp.concatenate(slices, axis=1)
+        kv_count = kv_all.shape[1]
+        payload = jnp.concatenate([kv_all.reshape(2 * kv_count, width), weight_rows], axis=0)
+        arrived = swap_major(payload, major, r)
+        got = arrived[: 2 * kv_count].reshape(2, kv_count, width)
+        far_weight = arrived[2 * kv_count :]
         levels_kv.append(got[:, :coarse])
         lower_half = (major_pos >> r) & 1 == 0
+        weight_rows = jnp.where(
+            lower_half,
+            jnp.concatenate([weight_rows, far_weight], 0),
+            jnp.concatenate([far_weight, weight_rows], 0),
+        )
         joined = []
         used = coarse
         for own in slices[1:]:
@@ -144,7 +166,7 @@
     key_set = jnp.concatenate([keys] + [lv[0] for lv in levels_kv], axis=0)
     value_set = jnp.concatenate([values] + [lv[1] for lv in levels_kv], axis=0)
     full_cot = gathered_copies(cotangent, "dp", 1)
-    full_weight = gathered_copies(out_weight, SEQ, 0)
+    full_weight = weight_rows
     grad_attended = jnp.dot(full_cot, full_weight, preferred_element_type=jnp.float32).astype(
         jnp.bfloat16
     )

time: 192 us -> 193 us (level)
  waiting for transfers between devices: 83.6 us -> 107 us
  starting transfers between devices: 67.3 us -> 51.3 us
  other arithmetic: 8.03 us -> 3.45 us
    ppermute x3, waiting for transfers between devices: 33.4 us -> 47.2 us  [swap_major(): return lax.ppermute(block, axis, [(i, i ^ 1 << bit) for i in range(count)])]
    all_to_all x2 -> x1, starting transfers between devices: 16 us -> 4.78 us  [from_everyone(): return lax.all_to_all(copies, axis, split_axis=0, concat_axis=0, tiled=True)]
    ppermute x6, waiting for transfers between devices: 20.8 us -> 27.7 us  [from_partner(): return lax.ppermute(block, axis, route)]
    ppermute x6, starting transfers between devices: 23.9 us -> 17.2 us  [from_partner(): return lax.ppermute(block, axis, route)]
    ppermute x3, starting transfers between devices: 14.1 us -> 18.8 us  [swap_major(): return lax.ppermute(block, axis, [(i, i ^ 1 << bit) for i in range(count)])]
    reduce_sum x6 -> x0, other arithmetic: 4.22 us -> none  [pooled(): table.reshape(table.shape[0], table.shape[1] // factor, factor, table.sha...]
    all_to_all x1, waiting for transfers between devices: 19.8 us -> 22.9 us  [on_device(): near_all = lax.all_to_all(near_send, minor, 0, 0, tiled=True)]
    all_to_all x1, starting transfers between devices: 6.2 us -> 3.41 us  [own_rows(): return jnp.sum(lax.all_to_all(parts, last, 0, 0, tiled=True), axis=0)]
  transfers between devices with their start and end apart: 14 -> 13, of which waited for: 11 -> 11; matrix products, arithmetic and copies ran while one was open for 4% -> 4% of each run, Pallas kernels for 0% -> 0%
where the time goes in v4:
time: 193 us; the launch traced here: 192 us
  waiting for transfers between devices  107 us (55%)
  starting transfers between devices  51.3 us (27%)
  between operations  15.1 us (8%)
  local copies, waits for them, and re-layouts  10.4 us (5%)
  matrix products  4.81 us (2%)
  other arithmetic  3.45 us (2%)
    ppermute x3, waiting for transfers between devices, swap_major(): return lax.ppermute(block, axis, [(i, i ^ 1 << bit) for i in range(count)])  47.2 us
    ppermute x6, waiting for transfers between devices, from_partner(): return lax.ppermute(block, axis, route)  27.7 us
    all_to_all x1, waiting for transfers between devices, on_device(): near_all = lax.all_to_all(near_send, minor, 0, 0, tiled=True)  22.9 us
    ppermute x3, starting transfers between devices, swap_major(): return lax.ppermute(block, axis, [(i, i ^ 1 << bit) for i in range(count)])  18.8 us
    ppermute x6, starting transfers between devices, from_partner(): return lax.ppermute(block, axis, route)  17.2 us
    all_to_all x1, waiting for transfers between devices, own_rows(): return jnp.sum(lax.all_to_all(parts, last, 0, 0, tiled=True), axis=0)  9.61 us
    all_to_all x1, starting transfers between devices, on_device(): near_all = lax.all_to_all(near_send, minor, 0, 0, tiled=True)  7.1 us
    all_to_all x1, starting transfers between devices, from_everyone(): return lax.all_to_all(copies, axis, split_axis=0, concat_axis=0, tiled=True)  4.78 us
  transfers between devices with their start and end apart: 13, of which 11 were waited for; matrix products, arithmetic and copies ran while one was open for 4% of the time, Pallas kernels for 0%

profile of v4, /device:TPU:6, one launch (start us, length us, event | category | flops | bytes accessed | tf_op | source)
XLA Modules:
  0.0 192.5 jit_solution(11165793225986219109)
XLA Ops:
  7.2 0.9 stack.18
  8.1 0.9 stack.19
  8.9 0.2 maximum_convert_fusion
  9.1 0.2 fusion.84
  9.4 0.3 reduce.4
  10.2 0.2 select_select_fusion
  10.7 1.0 copy.222
  11.7 7.1 %all-to-all-start = ((bf16[8,188,256]{2,1,0:T(8,128)(2,1)}), bf16[8,188,256]{2,1,0:T(8,128)(2,1)S(1)}, u32[]{:S(2)}, u32[]{:S(2)}) async-start(bf16[8,188,256]{2,1,0:T(8,128)(2,1)} %copy.222), calls=%async_computation | async-start | bytes 1572864 | tf_op jit(solution)/shard_map/all_to_all | solution.py:129
  18.8 0.1 copy.238
  19.0 22.9 %all-to-all-done = bf16[8,188,256]{2,1,0:T(8,128)(2,1)S(1)} async-done(((bf16[8,188,256]{2,1,0:T(8,128)(2,1)}), bf16[8,188,256]{2,1,0:T(8,128)(2,1)S(1)}, u32[]{:S(2)}, u32[]{:S(2)}) %all-to-all-start) | async-done | bytes 770080 | tf_op jit(solution)/shard_map/all_to_all | solution.py:129
  41.9 0.9 broadcast_in_dim.44
  42.8 4.8 %all-to-all-start.1 = ((bf16[8,128,256]{1,2,0:T(8,128)(2,1)}), bf16[8,128,256]{1,2,0:T(8,128)(2,1)S(1)}, u32[]{:S(2)}, u32[]{:S(2)}) async-start(bf16[8,128,256]{1,2,0:T(8,128)(2,1)} %broadcast_in_dim.44), calls=%async_computation.1 | async-start | bytes 1048576 | tf_op jit(solution)/shard_map/all_to_all | solution.py:31
  47.6 0.4 copy.285
  48.4 4.3 %collective-permute-start = (bf16[480,256]{1,0:T(8,128)(2,1)S(1)}, bf16[480,256]{1,0:T(8,128)(2,1)S(1)}, u32[]{:S(2)}, u32[]{:S(2)}) collective-permute-start(bf16[480,256]{1,0:T(8,128)(2,1)S(1)} %pad_maximum_fusion.4), channel_id=1, source_target_pairs={{0,64},{64,0},{128,192},{192,128},{256,320},{320,256},{384,448},{4... | collective-permute-start | bytes 737288 | tf_op jit(solution)/shard_map/ppermute | solution.py:90
  52.7 0.1 constant_dynamic-slice_fusion
  52.9 6.0 %collective-permute-done = bf16[480,256]{1,0:T(8,128)(2,1)S(1)} collective-permute-done((bf16[480,256]{1,0:T(8,128)(2,1)S(1)}, bf16[480,256]{1,0:T(8,128)(2,1)S(1)}, u32[]{:S(2)}, u32[]{:S(2)}) %collective-permute-start) | collective-permute-done | bytes 245792 | tf_op jit(solution)/shard_map/ppermute | solution.py:90
  59.0 0.1 maximum_select_fusion.3
  59.1 0.2 broadcast_select_fusion.1
  59.4 0.1 pad_maximum_fusion.7
  59.6 6.1 %collective-permute-start.1 = (bf16[704,256]{1,0:T(8,128)(2,1)S(1)}, bf16[704,256]{1,0:T(8,128)(2,1)S(1)}, u32[]{:S(2)}, u32[]{:S(2)}) collective-permute-start(bf16[704,256]{1,0:T(8,128)(2,1)S(1)} %pad_maximum_fusion.3), channel_id=1, source_target_pairs={{0,128},{64,192},{128,0},{192,64},{256,384},{320,448},{384,256},{4... | collective-permute-start | bytes 1081352 | tf_op jit(solution)/shard_map/ppermute | solution.py:90
  65.7 15.8 %collective-permute-done.1 = bf16[704,256]{1,0:T(8,128)(2,1)S(1)} collective-permute-done((bf16[704,256]{1,0:T(8,128)(2,1)S(1)}, bf16[704,256]{1,0:T(8,128)(2,1)S(1)}, u32[]{:S(2)}, u32[]{:S(2)}) %collective-permute-start.1) | collective-permute-done | bytes 360480 | tf_op jit(solution)/shard_map/ppermute | solution.py:90
  81.7 0.2 maximum_select_fusion.2
  81.9 0.2 broadcast_select_fusion
  82.1 8.4 %collective-permute-start.2 = (bf16[1152,256]{1,0:T(8,128)(2,1)S(1)}, bf16[1152,256]{1,0:T(8,128)(2,1)S(1)}, u32[]{:S(2)}, u32[]{:S(2)}) collective-permute-start(bf16[1152,256]{1,0:T(8,128)(2,1)S(1)} %pad_maximum_fusion.2), channel_id=1, source_target_pairs={{0,256},{64,320},{128,384},{192,448},{256,0},{320,64},{384,128},{4... | collective-permute-start | bytes 1769480 | tf_op jit(solution)/shard_map/ppermute | solution.py:90
  90.6 25.3 %collective-permute-done.2 = bf16[1152,256]{1,0:T(8,128)(2,1)S(1)} collective-permute-done((bf16[1152,256]{1,0:T(8,128)(2,1)S(1)}, bf16[1152,256]{1,0:T(8,128)(2,1)S(1)}, u32[]{:S(2)}, u32[]{:S(2)}) %collective-permute-start.2) | collective-permute-done | bytes 589856 | tf_op jit(solution)/shard_map/ppermute | solution.py:90
  116.0 0.2 fusion.99
  116.4 0.2 convolution_convert_fusion.3
  116.6 0.5 fusion
  117.1 0.2 fusion.48
  117.3 0.2 fusion.10
  117.5 0.2 fusion.100
  117.8 0.2 convolution_convert_fusion.4
  118.1 0.2 fusion.13
  118.3 0.2 fusion.47
  118.6 0.2 fusion.59
  118.8 0.2 fusion.62
  119.1 4.7 %collective-permute-start.3 = (bf16[2,64,256]{2,1,0:T(8,128)(2,1)S(1)}, bf16[2,64,256]{2,1,0:T(8,128)(2,1)S(1)}, u32[]{:S(2)}, u32[]{:S(2)}) collective-permute-start(bf16[2,64,256]{2,1,0:T(8,128)(2,1)S(1)} %fusion.24), channel_id=1, source_target_pairs={{0,256},{256,0},{8,264},{264,8},{16,272},{272,16},{24,280},{280,24... | collective-permute-start | bytes 196616 | tf_op jit(solution)/shard_map/ppermute | solution.py:20
  123.8 1.8 convolution_bitcast_fusion
  125.6 3.6 %collective-permute-done.3 = bf16[2,64,256]{2,1,0:T(8,128)(2,1)S(1)} collective-permute-done((bf16[2,64,256]{2,1,0:T(8,128)(2,1)S(1)}, bf16[2,64,256]{2,1,0:T(8,128)(2,1)S(1)}, u32[]{:S(2)}, u32[]{:S(2)}) %collective-permute-start.3) | collective-permute-done | bytes 65568 | tf_op jit(solution)/shard_map/ppermute | solution.py:20
  129.2 0.1 copy.247
  129.4 1.9 collective-permute-start.4
  131.4 5.1 %collective-permute-done.4 = bf16[2,64,256]{2,1,0:T(8,128)(2,1)S(1)} collective-permute-done((bf16[2,64,256]{2,1,0:T(8,128)(2,1)S(1)}, bf16[2,64,256]{2,1,0:T(8,128)(2,1)S(1)}, u32[]{:S(2)}, u32[]{:S(2)}) %collective-permute-start.4) | collective-permute-done | bytes 65568 | tf_op jit(solution)/shard_map/ppermute | solution.py:20
  136.5 0.1 copy.250
  136.8 4.5 %collective-permute-start.5 = (bf16[2,64,256]{2,1,0:T(8,128)(2,1)S(1)}, bf16[2,64,256]{2,1,0:T(8,128)(2,1)S(1)}, u32[]{:S(2)}, u32[]{:S(2)}) collective-permute-start(bf16[2,64,256]{2,1,0:T(8,128)(2,1)S(1)} %fusion.30), channel_id=1, source_target_pairs={{0,64},{64,0},{8,72},{72,8},{16,80},{80,16},{24,88},{88,24},{32,96... | collective-permute-start | bytes 196616 | tf_op jit(solution)/shard_map/ppermute | solution.py:20
  141.3 0.2 convolution_convert_fusion.1
  141.6 2.9 %collective-permute-done.5 = bf16[2,64,256]{2,1,0:T(8,128)(2,1)S(1)} collective-permute-done((bf16[2,64,256]{2,1,0:T(8,128)(2,1)S(1)}, bf16[2,64,256]{2,1,0:T(8,128)(2,1)S(1)}, u32[]{:S(2)}, u32[]{:S(2)}) %collective-permute-start.5) | collective-permute-done | bytes 65568 | tf_op jit(solution)/shard_map/ppermute | solution.py:20
  144.5 0.1 copy.253
  144.7 2.1 %collective-permute-start.6 = (bf16[2,64,256]{2,1,0:T(8,128)(2,1)S(1)}, bf16[2,64,256]{2,1,0:T(8,128)(2,1)S(1)}, u32[]{:S(2)}, u32[]{:S(2)}) collective-permute-start(bf16[2,64,256]{2,1,0:T(8,128)(2,1)S(1)} %fusion.33), channel_id=1, source_target_pairs={{0,32},{32,0},{8,40},{40,8},{16,48},{48,16},{24,56},{56,24},{64,96... | collective-permute-start | bytes 196616 | tf_op jit(solution)/shard_map/ppermute | solution.py:20
  146.8 0.2 convolution_convert_fusion.2
  147.0 7.8 %collective-permute-done.6 = bf16[2,64,256]{2,1,0:T(8,128)(2,1)S(1)} collective-permute-done((bf16[2,64,256]{2,1,0:T(8,128)(2,1)S(1)}, bf16[2,64,256]{2,1,0:T(8,128)(2,1)S(1)}, u32[]{:S(2)}, u32[]{:S(2)}) %collective-permute-start.6) | collective-permute-done | bytes 65568 | tf_op jit(solution)/shard_map/ppermute | solution.py:20
  154.8 0.1 copy.256
  155.1 2.0 %collective-permute-start.7 = (bf16[2,64,256]{2,1,0:T(8,128)(2,1)S(1)}, bf16[2,64,256]{2,1,0:T(8,128)(2,1)S(1)}, u32[]{:S(2)}, u32[]{:S(2)}) collective-permute-start(bf16[2,64,256]{2,1,0:T(8,128)(2,1)S(1)} %fusion.22), channel_id=1, source_target_pairs={{0,16},{16,0},{8,24},{24,8},{32,48},{48,32},{40,56},{56,40},{64,80... | collective-permute-start | bytes 196616 | tf_op jit(solution)/shard_map/ppermute | solution.py:20
  157.1 0.7 copy.266
  157.9 5.0 %collective-permute-done.7 = bf16[2,64,256]{2,1,0:T(8,128)(2,1)S(1)} collective-permute-done((bf16[2,64,256]{2,1,0:T(8,128)(2,1)S(1)}, bf16[2,64,256]{2,1,0:T(8,128)(2,1)S(1)}, u32[]{:S(2)}, u32[]{:S(2)}) %collective-permute-start.7) | collective-permute-done | bytes 65568 | tf_op jit(solution)/shard_map/ppermute | solution.py:20
  162.9 0.1 copy.259
  163.1 2.0 %collective-permute-start.8 = (bf16[2,64,256]{2,1,0:T(8,128)(2,1)S(1)}, bf16[2,64,256]{2,1,0:T(8,128)(2,1)S(1)}, u32[]{:S(2)}, u32[]{:S(2)}) collective-permute-start(bf16[2,64,256]{2,1,0:T(8,128)(2,1)S(1)} %fusion.35), channel_id=1, source_target_pairs={{0,8},{8,0},{16,24},{24,16},{32,40},{40,32},{48,56},{56,48},{64,72... | collective-permute-start | bytes 196616 | tf_op jit(solution)/shard_map/ppermute | solution.py:20
  165.1 0.7 copy.265
  165.9 3.4 %collective-permute-done.8 = bf16[2,64,256]{2,1,0:T(8,128)(2,1)S(1)} collective-permute-done((bf16[2,64,256]{2,1,0:T(8,128)(2,1)S(1)}, bf16[2,64,256]{2,1,0:T(8,128)(2,1)S(1)}, u32[]{:S(2)}, u32[]{:S(2)}) %collective-permute-start.8) | collective-permute-done | bytes 65568 | tf_op jit(solution)/shard_map/ppermute | solution.py:20
  169.3 0.1 copy.262
  169.4 1.8 copy.264
  171.2 3.4 %all-to-all-start.2 = ((f32[8,32,256]{2,1,0:T(8,128)}), f32[8,32,256]{2,1,0:T(8,128)S(1)}, u32[]{:S(2)}, u32[]{:S(2)}) async-start(f32[8,32,256]{2,1,0:T(8,128)} %bitcast.49), calls=%async_computation.3 | async-start | bytes 524288 | tf_op jit(solution)/shard_map/all_to_all | solution.py:43
  174.8 0.7 slice_bitcast_fusion
  175.4 9.6 %all-to-all-done.2 = f32[8,32,256]{2,1,0:T(8,128)S(1)} async-done(((f32[8,32,256]{2,1,0:T(8,128)}), f32[8,32,256]{2,1,0:T(8,128)S(1)}, u32[]{:S(2)}, u32[]{:S(2)}) %all-to-all-start.2) | async-done | bytes 262176 | tf_op jit(solution)/shard_map/all_to_all | solution.py:43
  185.0 0.6 reduce_sum.49
  (114 shorter events, 2.8 us)
Async XLA Ops:
  9.3 1.2 copy-start.4
  10.5 8.3 %copy-start.3 = (bf16[128,256]{1,0:T(8,128)(2,1)S(1)}, bf16[128,256]{1,0:T(8,128)(2,1)}, u32[]{:S(2)}) copy-start(bf16[128,256]{1,0:T(8,128)(2,1)} %param.8) | copy-start | bytes 196612
  10.6 8.4 %copy-start = (bf16[128,256]{1,0:T(8,128)(2,1)S(1)}, bf16[128,256]{1,0:T(8,128)(2,1)}, u32[]{:S(2)}) copy-start(bf16[128,256]{1,0:T(8,128)(2,1)} %param.6) | copy-start | bytes 196612
  10.6 8.3 %copy-start.1 = (bf16[128,256]{1,0:T(8,128)(2,1)S(1)}, bf16[128,256]{1,0:T(8,128)(2,1)}, u32[]{:S(2)}) copy-start(bf16[128,256]{1,0:T(8,128)(2,1)} %param.7) | copy-start | bytes 196612
  11.7 30.2 %all-to-all-start = ((bf16[8,188,256]{2,1,0:T(8,128)(2,1)}), bf16[8,188,256]{2,1,0:T(8,128)(2,1)S(1)}, u32[]{:S(2)}, u32[]{:S(2)}) async-start(bf16[8,188,256]{2,1,0:T(8,128)(2,1)} %copy.222), calls=%async_computation | async-start | bytes 1572864 | tf_op jit(solution)/shard_map/all_to_all | solution.py:129
  42.8 73.8 %all-to-all-start.1 = ((bf16[8,128,256]{1,2,0:T(8,128)(2,1)}), bf16[8,128,256]{1,2,0:T(8,128)(2,1)S(1)}, u32[]{:S(2)}, u32[]{:S(2)}) async-start(bf16[8,128,256]{1,2,0:T(8,128)(2,1)} %broadcast_in_dim.44), calls=%async_computation.1 | async-start | bytes 1048576 | tf_op jit(solution)/shard_map/all_to_all | solution.py:31
  47.5 121.9 %reduce-scatter.2.cloned.1.call-start = ((), (), s32[]{:S(2)}) async-start(), calls=%async_computation.4 | async-start | bytes 2359296 | tf_op jit(solution)/shard_map/reduce_scatter | solution.py:40
  48.4 10.5 %collective-permute-start = (bf16[480,256]{1,0:T(8,128)(2,1)S(1)}, bf16[480,256]{1,0:T(8,128)(2,1)S(1)}, u32[]{:S(2)}, u32[]{:S(2)}) collective-permute-start(bf16[480,256]{1,0:T(8,128)(2,1)S(1)} %pad_maximum_fusion.4), channel_id=1, source_target_pairs={{0,64},{64,0},{128,192},{192,128},{256,320},{320,256},{384,448},{4... | collective-permute-start | bytes 737288 | tf_op jit(solution)/shard_map/ppermute | solution.py:90
  59.6 22.0 %collective-permute-start.1 = (bf16[704,256]{1,0:T(8,128)(2,1)S(1)}, bf16[704,256]{1,0:T(8,128)(2,1)S(1)}, u32[]{:S(2)}, u32[]{:S(2)}) collective-permute-start(bf16[704,256]{1,0:T(8,128)(2,1)S(1)} %pad_maximum_fusion.3), channel_id=1, source_target_pairs={{0,128},{64,192},{128,0},{192,64},{256,384},{320,448},{384,256},{4... | collective-permute-start | bytes 1081352 | tf_op jit(solution)/shard_map/ppermute | solution.py:90
  65.7 50.3 %copy-start.2 = (bf16[128,256]{1,0:T(8,128)(2,1)S(1)}, bf16[128,256]{1,0:T(8,128)(2,1)}, u32[]{:S(2)}) copy-start(bf16[128,256]{1,0:T(8,128)(2,1)} %param.5) | copy-start | bytes 196612
  82.1 33.8 %collective-permute-start.2 = (bf16[1152,256]{1,0:T(8,128)(2,1)S(1)}, bf16[1152,256]{1,0:T(8,128)(2,1)S(1)}, u32[]{:S(2)}, u32[]{:S(2)}) collective-permute-start(bf16[1152,256]{1,0:T(8,128)(2,1)S(1)} %pad_maximum_fusion.2), channel_id=1, source_target_pairs={{0,256},{64,320},{128,384},{192,448},{256,0},{320,64},{384,128},{4... | collective-permute-start | bytes 1769480 | tf_op jit(solution)/shard_map/ppermute | solution.py:90
  119.1 10.1 %collective-permute-start.3 = (bf16[2,64,256]{2,1,0:T(8,128)(2,1)S(1)}, bf16[2,64,256]{2,1,0:T(8,128)(2,1)S(1)}, u32[]{:S(2)}, u32[]{:S(2)}) collective-permute-start(bf16[2,64,256]{2,1,0:T(8,128)(2,1)S(1)} %fusion.24), channel_id=1, source_target_pairs={{0,256},{256,0},{8,264},{264,8},{16,272},{272,16},{24,280},{280,24... | collective-permute-start | bytes 196616 | tf_op jit(solution)/shard_map/ppermute | solution.py:20
  129.4 7.1 %collective-permute-start.4 = (bf16[2,64,256]{2,1,0:T(8,128)(2,1)S(1)}, bf16[2,64,256]{2,1,0:T(8,128)(2,1)S(1)}, u32[]{:S(2)}, u32[]{:S(2)}) collective-permute-start(bf16[2,64,256]{2,1,0:T(8,128)(2,1)S(1)} %fusion.27), channel_id=1, source_target_pairs={{0,128},{128,0},{8,136},{136,8},{16,144},{144,16},{24,152},{152,24... | collective-permute-start | bytes 196616 | tf_op jit(solution)/shard_map/ppermute | solution.py:20
  136.8 7.6 %collective-permute-start.5 = (bf16[2,64,256]{2,1,0:T(8,128)(2,1)S(1)}, bf16[2,64,256]{2,1,0:T(8,128)(2,1)S(1)}, u32[]{:S(2)}, u32[]{:S(2)}) collective-permute-start(bf16[2,64,256]{2,1,0:T(8,128)(2,1)S(1)} %fusion.30), channel_id=1, source_target_pairs={{0,64},{64,0},{8,72},{72,8},{16,80},{80,16},{24,88},{88,24},{32,96... | collective-permute-start | bytes 196616 | tf_op jit(solution)/shard_map/ppermute | solution.py:20
  144.7 10.1 %collective-permute-start.6 = (bf16[2,64,256]{2,1,0:T(8,128)(2,1)S(1)}, bf16[2,64,256]{2,1,0:T(8,128)(2,1)S(1)}, u32[]{:S(2)}, u32[]{:S(2)}) collective-permute-start(bf16[2,64,256]{2,1,0:T(8,128)(2,1)S(1)} %fusion.33), channel_id=1, source_target_pairs={{0,32},{32,0},{8,40},{40,8},{16,48},{48,16},{24,56},{56,24},{64,96... | collective-permute-start | bytes 196616 | tf_op jit(solution)/shard_map/ppermute | solution.py:20
  155.1 7.8 %collective-permute-start.7 = (bf16[2,64,256]{2,1,0:T(8,128)(2,1)S(1)}, bf16[2,64,256]{2,1,0:T(8,128)(2,1)S(1)}, u32[]{:S(2)}, u32[]{:S(2)}) collective-permute-start(bf16[2,64,256]{2,1,0:T(8,128)(2,1)S(1)} %fusion.22), channel_id=1, source_target_pairs={{0,16},{16,0},{8,24},{24,8},{32,48},{48,32},{40,56},{56,40},{64,80... | collective-permute-start | bytes 196616 | tf_op jit(solution)/shard_map/ppermute | solution.py:20
  163.1 6.2 %collective-permute-start.8 = (bf16[2,64,256]{2,1,0:T(8,128)(2,1)S(1)}, bf16[2,64,256]{2,1,0:T(8,128)(2,1)S(1)}, u32[]{:S(2)}, u32[]{:S(2)}) collective-permute-start(bf16[2,64,256]{2,1,0:T(8,128)(2,1)S(1)} %fusion.35), channel_id=1, source_target_pairs={{0,8},{8,0},{16,24},{24,16},{32,40},{40,32},{48,56},{56,48},{64,72... | collective-permute-start | bytes 196616 | tf_op jit(solution)/shard_map/ppermute | solution.py:20
  171.2 13.8 %all-to-all-start.2 = ((f32[8,32,256]{2,1,0:T(8,128)}), f32[8,32,256]{2,1,0:T(8,128)S(1)}, u32[]{:S(2)}, u32[]{:S(2)}) async-start(f32[8,32,256]{2,1,0:T(8,128)} %bitcast.49), calls=%async_computation.3 | async-start | bytes 524288 | tf_op jit(solution)/shard_map/all_to_all | solution.py:43
Sparse Core Ops, SparseCore 0:
  125.7 40.2 reduce-scatter.1

commit v5 on v0

--- a/solution.py
+++ b/solution.py
@@ -36,9 +36,9 @@
 
 
 def own_rows(running, axes):
-    for axis in axes:
-        running = lax.psum_scatter(running, axis, scatter_dimension=0, tiled=True)
-    return running
+    count = lax.axis_size(axes)
+    parts = running.astype(jnp.bfloat16).reshape(count, running.shape[0] // count, running.shape[1])
+    return jnp.sum(lax.all_to_all(parts, axes, 0, 0, tiled=True).astype(jnp.float32), axis=0)
 
 
 def pair_mean(table):

time: 209 us -> 172 us (0.82)
  waiting for transfers between devices: 111 us -> 80.2 us
  between operations: 14.8 us -> 1.45 us
  starting transfers between devices: 64.6 us -> 72.1 us
  other arithmetic: 1.14 us -> 3.37 us
    unnamed x3 -> x0, waiting for transfers between devices: 37.8 us -> none
    ppermute x12, waiting for transfers between devices: 70.4 us -> 80.2 us  [from_partner(): return lax.ppermute(block, axis, route)]
    all_to_all x0 -> x1, starting transfers between devices: none -> 8.36 us  [own_rows(): lax.all_to_all(parts, axes, 0, 0, tiled=True).astype(jnp.float32)]
    reduce_scatter x1 -> x0, waiting for transfers between devices: 3.24 us -> none  [own_rows(): running = lax.psum_scatter(running, axis, scatter_dimension=0, tiled=True)]
    unnamed x18 -> x23, local copies, waits for them, and re-layouts: 4.29 us -> 2.46 us
  transfers between devices with their start and end apart: 16 -> 15, of which waited for: 12 -> 9; matrix products, arithmetic and copies ran while one was open for 6% -> 6% of each run, Pallas kernels for 0% -> 0%
where the time goes in v5:
time: 172 us; the launch traced here: 171 us
  waiting for transfers between devices  80.2 us (47%)
  starting transfers between devices  72.1 us (42%)
  local copies, waits for them, and re-layouts  10.6 us (6%)
  other arithmetic  3.37 us (2%)
  matrix products  3.36 us (2%)
    ppermute x12, waiting for transfers between devices, from_partner(): return lax.ppermute(block, axis, route)  80.2 us
    ppermute x12, starting transfers between devices, from_partner(): return lax.ppermute(block, axis, route)  44.9 us
    all_to_all x2, starting transfers between devices, from_everyone(): return lax.all_to_all(copies, axis, split_axis=0, concat_axis=0, tiled=True)  18.9 us
    all_to_all x1, starting transfers between devices, own_rows(): lax.all_to_all(parts, axes, 0, 0, tiled=True).astype(jnp.float32)  8.36 us
  transfers between devices with their start and end apart: 15, of which 9 were waited for; matrix products, arithmetic and copies ran while one was open for 6% of the time, Pallas kernels for 0%

profile of v5, /device:TPU:6, one launch (start us, length us, event | category | flops | bytes accessed | tf_op | source)
XLA Modules:
  0.0 171.1 jit_solution(4324878269061192461)
XLA Ops:
  0.6 0.9 stack.18
  1.6 0.9 stack.19
  2.5 3.6 %collective-permute-start = (f32[2,64,256]{2,1,0:T(8,128)S(1)}, f32[2,64,256]{2,1,0:T(8,128)S(1)}, u32[]{:S(2)}, u32[]{:S(2)}) collective-permute-start(f32[2,64,256]{2,1,0:T(8,128)S(1)} %fusion.31), channel_id=1, source_target_pairs={{0,8},{8,0},{16,24},{24,16},{32,40},{40,32},{48,56},{56,48},{64,72... | collective-permute-start | bytes 393224 | tf_op jit(solution)/shard_map/ppermute | solution.py:20
  6.2 0.1 copy.107
  6.3 0.9 broadcast_in_dim.16
  7.2 7.7 %all-to-all-start = ((bf16[8,128,256]{1,2,0:T(8,128)(2,1)}), bf16[8,128,256]{1,2,0:T(8,128)(2,1)S(1)}, u32[]{:S(2)}, u32[]{:S(2)}) async-start(bf16[8,128,256]{1,2,0:T(8,128)(2,1)} %broadcast_in_dim.16), calls=%async_computation | async-start | bytes 1048576 | tf_op jit(solution)/shard_map/all_to_all | solution.py:31
  15.0 0.2 copy.92
  15.3 1.9 %collective-permute-start.1 = (f32[2,64,256]{2,1,0:T(8,128)S(1)}, f32[2,64,256]{2,1,0:T(8,128)S(1)}, u32[]{:S(2)}, u32[]{:S(2)}) collective-permute-start(f32[2,64,256]{2,1,0:T(8,128)S(1)} %fusion.41), channel_id=1, source_target_pairs={{0,16},{16,0},{8,24},{24,8},{32,48},{48,32},{40,56},{56,40},{64,80... | collective-permute-start | bytes 393224 | tf_op jit(solution)/shard_map/ppermute | solution.py:20
  17.2 9.2 %collective-permute-done.1 = f32[2,64,256]{2,1,0:T(8,128)S(1)} collective-permute-done((f32[2,64,256]{2,1,0:T(8,128)S(1)}, f32[2,64,256]{2,1,0:T(8,128)S(1)}, u32[]{:S(2)}, u32[]{:S(2)}) %collective-permute-start.1) | collective-permute-done | bytes 131104 | tf_op jit(solution)/shard_map/ppermute | solution.py:20
  26.5 0.2 copy.95
  26.8 3.9 %collective-permute-start.2 = (f32[2,64,256]{2,1,0:T(8,128)S(1)}, f32[2,64,256]{2,1,0:T(8,128)S(1)}, u32[]{:S(2)}, u32[]{:S(2)}) collective-permute-start(f32[2,64,256]{2,1,0:T(8,128)S(1)} %fusion.39), channel_id=1, source_target_pairs={{0,32},{32,0},{8,40},{40,8},{16,48},{48,16},{24,56},{56,24},{64,96... | collective-permute-start | bytes 393224 | tf_op jit(solution)/shard_map/ppermute | solution.py:20
  30.7 8.0 %collective-permute-done.2 = f32[2,64,256]{2,1,0:T(8,128)S(1)} collective-permute-done((f32[2,64,256]{2,1,0:T(8,128)S(1)}, f32[2,64,256]{2,1,0:T(8,128)S(1)}, u32[]{:S(2)}, u32[]{:S(2)}) %collective-permute-start.2) | collective-permute-done | bytes 131104 | tf_op jit(solution)/shard_map/ppermute | solution.py:20
  38.8 0.2 copy.98
  39.1 3.3 %collective-permute-start.3 = (f32[2,64,256]{2,1,0:T(8,128)S(1)}, f32[2,64,256]{2,1,0:T(8,128)S(1)}, u32[]{:S(2)}, u32[]{:S(2)}) collective-permute-start(f32[2,64,256]{2,1,0:T(8,128)S(1)} %fusion.37), channel_id=1, source_target_pairs={{0,64},{64,0},{8,72},{72,8},{16,80},{80,16},{24,88},{88,24},{32,96... | collective-permute-start | bytes 393224 | tf_op jit(solution)/shard_map/ppermute | solution.py:20
  42.5 3.6 %collective-permute-done.3 = f32[2,64,256]{2,1,0:T(8,128)S(1)} collective-permute-done((f32[2,64,256]{2,1,0:T(8,128)S(1)}, f32[2,64,256]{2,1,0:T(8,128)S(1)}, u32[]{:S(2)}, u32[]{:S(2)}) %collective-permute-start.3) | collective-permute-done | bytes 131104 | tf_op jit(solution)/shard_map/ppermute | solution.py:20
  46.2 0.2 copy.101
  46.5 5.4 %collective-permute-start.4 = (f32[2,64,256]{2,1,0:T(8,128)S(1)}, f32[2,64,256]{2,1,0:T(8,128)S(1)}, u32[]{:S(2)}, u32[]{:S(2)}) collective-permute-start(f32[2,64,256]{2,1,0:T(8,128)S(1)} %fusion.35), channel_id=1, source_target_pairs={{0,128},{128,0},{8,136},{136,8},{16,144},{144,16},{24,152},{152,24... | collective-permute-start | bytes 393224 | tf_op jit(solution)/shard_map/ppermute | solution.py:20
  51.9 1.1 broadcast_in_dim.17
  53.0 11.1 %all-to-all-start.1 = ((bf16[64,32,256]{2,1,0:T(8,128)(2,1)}), bf16[64,32,256]{2,1,0:T(8,128)(2,1)S(1)}, u32[]{:S(2)}, u32[]{:S(2)}) async-start(bf16[64,32,256]{2,1,0:T(8,128)(2,1)} %broadcast_in_dim.17), calls=%async_computation.1 | async-start | bytes 2097152 | tf_op jit(solution)/shard_map/all_to_all | solution.py:31
  64.2 0.2 copy.104
  64.5 7.5 %collective-permute-start.5 = (bf16[2,64,256]{2,1,0:T(8,128)(2,1)S(1)}, bf16[2,64,256]{2,1,0:T(8,128)(2,1)S(1)}, u32[]{:S(2)}, u32[]{:S(2)}) collective-permute-start(bf16[2,64,256]{2,1,0:T(8,128)(2,1)S(1)} %fusion.33), channel_id=1, source_target_pairs={{0,256},{256,0},{8,264},{264,8},{16,272},{272,16},{24,280},{280,24... | collective-permute-start | bytes 196616 | tf_op jit(solution)/shard_map/ppermute | solution.py:20
  72.0 22.3 %collective-permute-done.5 = bf16[2,64,256]{2,1,0:T(8,128)(2,1)S(1)} collective-permute-done((bf16[2,64,256]{2,1,0:T(8,128)(2,1)S(1)}, bf16[2,64,256]{2,1,0:T(8,128)(2,1)S(1)}, u32[]{:S(2)}, u32[]{:S(2)}) %collective-permute-start.5) | collective-permute-done | bytes 65568 | tf_op jit(solution)/shard_map/ppermute | solution.py:20
  94.3 0.2 fusion.90
  94.6 0.1 fusion.13
  94.7 0.2 fusion.91
  94.9 0.1 fusion.11
  95.0 0.2 convolution_convert_fusion.4
  95.3 0.4 convolution_convert_fusion.1
  95.6 0.2 fusion.53
  95.8 0.2 fusion.4
  96.1 0.2 fusion.52
  96.2 0.8 copy-done.6
  97.0 0.2 fusion.7
  97.3 0.2 fusion.73
  97.6 0.2 fusion.70
  97.9 2.5 %collective-permute-start.6 = (bf16[2,64,256]{2,1,0:T(8,128)(2,1)S(1)}, bf16[2,64,256]{2,1,0:T(8,128)(2,1)S(1)}, u32[]{:S(2)}, u32[]{:S(2)}) collective-permute-start(bf16[2,64,256]{2,1,0:T(8,128)(2,1)S(1)} %fusion.18), channel_id=1, source_target_pairs={{0,256},{256,0},{8,264},{264,8},{16,272},{272,16},{24,280},{280,24... | collective-permute-start | bytes 196616 | tf_op jit(solution)/shard_map/ppermute | solution.py:20
  100.3 0.2 convolution_convert_fusion.5
  100.6 7.5 %collective-permute-done.6 = bf16[2,64,256]{2,1,0:T(8,128)(2,1)S(1)} collective-permute-done((bf16[2,64,256]{2,1,0:T(8,128)(2,1)S(1)}, bf16[2,64,256]{2,1,0:T(8,128)(2,1)S(1)}, u32[]{:S(2)}, u32[]{:S(2)}) %collective-permute-start.6) | collective-permute-done | bytes 65568 | tf_op jit(solution)/shard_map/ppermute | solution.py:20
  108.1 0.1 copy.116
  108.3 2.4 %collective-permute-start.7 = (bf16[2,64,256]{2,1,0:T(8,128)(2,1)S(1)}, bf16[2,64,256]{2,1,0:T(8,128)(2,1)S(1)}, u32[]{:S(2)}, u32[]{:S(2)}) collective-permute-start(bf16[2,64,256]{2,1,0:T(8,128)(2,1)S(1)} %fusion.21), channel_id=1, source_target_pairs={{0,128},{128,0},{8,136},{136,8},{16,144},{144,16},{24,152},{152,24... | collective-permute-start | bytes 196616 | tf_op jit(solution)/shard_map/ppermute | solution.py:20
  110.7 0.4 fusion
  111.1 4.6 %collective-permute-done.7 = bf16[2,64,256]{2,1,0:T(8,128)(2,1)S(1)} collective-permute-done((bf16[2,64,256]{2,1,0:T(8,128)(2,1)S(1)}, bf16[2,64,256]{2,1,0:T(8,128)(2,1)S(1)}, u32[]{:S(2)}, u32[]{:S(2)}) %collective-permute-start.7) | collective-permute-done | bytes 65568 | tf_op jit(solution)/shard_map/ppermute | solution.py:20
  115.7 0.1 copy.119
  115.9 0.7 fusion.24
  116.6 1.9 %collective-permute-start.8 = (bf16[2,64,256]{2,1,0:T(8,128)(2,1)}, bf16[2,64,256]{2,1,0:T(8,128)(2,1)}, u32[]{:S(2)}, u32[]{:S(2)}) collective-permute-start(bf16[2,64,256]{2,1,0:T(8,128)(2,1)} %fusion.24), channel_id=1, source_target_pairs={{0,64},{64,0},{8,72},{72,8},{16,80},{80,16},{24,88},{88,24},{32,96... | collective-permute-start | bytes 196616 | tf_op jit(solution)/shard_map/ppermute | solution.py:20
  118.5 0.7 copy.134
  119.3 1.3 copy.133
  120.6 8.4 %all-to-all-start.2 = ((bf16[64,32,256]{2,1,0:T(8,128)(2,1)}), bf16[64,32,256]{2,1,0:T(8,128)(2,1)S(1)}, u32[]{:S(2)}, u32[]{:S(2)}) async-start(bf16[64,32,256]{2,1,0:T(8,128)(2,1)} %bitcast.40), calls=%async_computation.2 | async-start | bytes 2097152 | tf_op jit(solution)/shard_map/all_to_all | solution.py:41
  129.0 0.9 add_multiply_fusion.3
  129.8 0.1 copy.122
  130.1 7.4 %collective-permute-start.9 = (bf16[2,64,256]{2,1,0:T(8,128)(2,1)S(1)}, bf16[2,64,256]{2,1,0:T(8,128)(2,1)S(1)}, u32[]{:S(2)}, u32[]{:S(2)}) collective-permute-start(bf16[2,64,256]{2,1,0:T(8,128)(2,1)S(1)} %fusion.27), channel_id=1, source_target_pairs={{0,32},{32,0},{8,40},{40,8},{16,48},{48,16},{24,56},{56,24},{64,96... | collective-permute-start | bytes 196616 | tf_op jit(solution)/shard_map/ppermute | solution.py:20
  137.5 0.2 convolution_convert_fusion.2
  137.7 17.8 %collective-permute-done.9 = bf16[2,64,256]{2,1,0:T(8,128)(2,1)S(1)} collective-permute-done((bf16[2,64,256]{2,1,0:T(8,128)(2,1)S(1)}, bf16[2,64,256]{2,1,0:T(8,128)(2,1)S(1)}, u32[]{:S(2)}, u32[]{:S(2)}) %collective-permute-start.9) | collective-permute-done | bytes 65568 | tf_op jit(solution)/shard_map/ppermute | solution.py:20
  155.6 0.1 copy.125
  155.8 2.1 %collective-permute-start.10 = (bf16[2,64,256]{2,1,0:T(8,128)(2,1)S(1)}, bf16[2,64,256]{2,1,0:T(8,128)(2,1)S(1)}, u32[]{:S(2)}, u32[]{:S(2)}) collective-permute-start(bf16[2,64,256]{2,1,0:T(8,128)(2,1)S(1)} %fusion.16), channel_id=1, source_target_pairs={{0,16},{16,0},{8,24},{24,8},{32,48},{48,32},{40,56},{56,40},{64,80... | collective-permute-start | bytes 196616 | tf_op jit(solution)/shard_map/ppermute | solution.py:20
  158.0 0.2 convolution_convert_fusion.3
  158.2 4.8 %collective-permute-done.10 = bf16[2,64,256]{2,1,0:T(8,128)(2,1)S(1)} collective-permute-done((bf16[2,64,256]{2,1,0:T(8,128)(2,1)S(1)}, bf16[2,64,256]{2,1,0:T(8,128)(2,1)S(1)}, u32[]{:S(2)}, u32[]{:S(2)}) %collective-permute-start.10) | collective-permute-done | bytes 65568 | tf_op jit(solution)/shard_map/ppermute | solution.py:20
  163.0 0.1 copy.128
  163.3 3.1 %collective-permute-start.11 = (bf16[2,64,256]{2,1,0:T(8,128)(2,1)S(1)}, bf16[2,64,256]{2,1,0:T(8,128)(2,1)S(1)}, u32[]{:S(2)}, u32[]{:S(2)}) collective-permute-start(bf16[2,64,256]{2,1,0:T(8,128)(2,1)S(1)} %fusion.29), channel_id=1, source_target_pairs={{0,8},{8,0},{16,24},{24,16},{32,40},{40,32},{48,56},{56,48},{64,72... | collective-permute-start | bytes 196616 | tf_op jit(solution)/shard_map/ppermute | solution.py:20
  166.4 0.7 copy.135
  167.1 2.3 %collective-permute-done.11 = bf16[2,64,256]{2,1,0:T(8,128)(2,1)S(1)} collective-permute-done((bf16[2,64,256]{2,1,0:T(8,128)(2,1)S(1)}, bf16[2,64,256]{2,1,0:T(8,128)(2,1)S(1)}, u32[]{:S(2)}, u32[]{:S(2)}) %collective-permute-start.11) | collective-permute-done | bytes 65568 | tf_op jit(solution)/shard_map/ppermute | solution.py:20
  169.5 0.1 copy.131
  169.7 0.7 slice_bitcast_fusion
  170.3 0.8 convert_reduce_fusion
  (78 shorter events, 1.8 us)
Async XLA Ops:
  0.6 5.5 %copy-start.3 = (bf16[128,256]{1,0:T(8,128)(2,1)S(1)}, bf16[128,256]{1,0:T(8,128)(2,1)}, u32[]{:S(2)}) copy-start(bf16[128,256]{1,0:T(8,128)(2,1)} %param.8) | copy-start | bytes 196612
  2.5 12.4 %copy-start = (bf16[128,256]{1,0:T(8,128)(2,1)S(1)}, bf16[128,256]{1,0:T(8,128)(2,1)}, u32[]{:S(2)}) copy-start(bf16[128,256]{1,0:T(8,128)(2,1)} %param.6) | copy-start | bytes 196612
  2.5 12.4 %copy-start.1 = (bf16[128,256]{1,0:T(8,128)(2,1)S(1)}, bf16[128,256]{1,0:T(8,128)(2,1)}, u32[]{:S(2)}) copy-start(bf16[128,256]{1,0:T(8,128)(2,1)} %param.7) | copy-start | bytes 196612
  2.5 12.4 %collective-permute-start = (f32[2,64,256]{2,1,0:T(8,128)S(1)}, f32[2,64,256]{2,1,0:T(8,128)S(1)}, u32[]{:S(2)}, u32[]{:S(2)}) collective-permute-start(f32[2,64,256]{2,1,0:T(8,128)S(1)} %fusion.31), channel_id=1, source_target_pairs={{0,8},{8,0},{16,24},{24,16},{32,40},{40,32},{48,56},{56,48},{64,72... | collective-permute-start | bytes 393224 | tf_op jit(solution)/shard_map/ppermute | solution.py:20
  7.2 44.7 %all-to-all-start = ((bf16[8,128,256]{1,2,0:T(8,128)(2,1)}), bf16[8,128,256]{1,2,0:T(8,128)(2,1)S(1)}, u32[]{:S(2)}, u32[]{:S(2)}) async-start(bf16[8,128,256]{1,2,0:T(8,128)(2,1)} %broadcast_in_dim.16), calls=%async_computation | async-start | bytes 1048576 | tf_op jit(solution)/shard_map/all_to_all | solution.py:31
  15.3 11.2 %collective-permute-start.1 = (f32[2,64,256]{2,1,0:T(8,128)S(1)}, f32[2,64,256]{2,1,0:T(8,128)S(1)}, u32[]{:S(2)}, u32[]{:S(2)}) collective-permute-start(f32[2,64,256]{2,1,0:T(8,128)S(1)} %fusion.41), channel_id=1, source_target_pairs={{0,16},{16,0},{8,24},{24,8},{32,48},{48,32},{40,56},{56,40},{64,80... | collective-permute-start | bytes 393224 | tf_op jit(solution)/shard_map/ppermute | solution.py:20
  26.8 12.0 %collective-permute-start.2 = (f32[2,64,256]{2,1,0:T(8,128)S(1)}, f32[2,64,256]{2,1,0:T(8,128)S(1)}, u32[]{:S(2)}, u32[]{:S(2)}) collective-permute-start(f32[2,64,256]{2,1,0:T(8,128)S(1)} %fusion.39), channel_id=1, source_target_pairs={{0,32},{32,0},{8,40},{40,8},{16,48},{48,16},{24,56},{56,24},{64,96... | collective-permute-start | bytes 393224 | tf_op jit(solution)/shard_map/ppermute | solution.py:20
  39.1 7.0 %collective-permute-start.3 = (f32[2,64,256]{2,1,0:T(8,128)S(1)}, f32[2,64,256]{2,1,0:T(8,128)S(1)}, u32[]{:S(2)}, u32[]{:S(2)}) collective-permute-start(f32[2,64,256]{2,1,0:T(8,128)S(1)} %fusion.37), channel_id=1, source_target_pairs={{0,64},{64,0},{8,72},{72,8},{16,80},{80,16},{24,88},{88,24},{32,96... | collective-permute-start | bytes 393224 | tf_op jit(solution)/shard_map/ppermute | solution.py:20
  46.1 5.7 %copy-start.4 = (bf16[32,256]{1,0:T(8,128)(2,1)S(1)}, bf16[32,256]{1,0:T(8,128)(2,1)}, u32[]{:S(2)}) copy-start(bf16[32,256]{1,0:T(8,128)(2,1)} %param.9) | copy-start | bytes 49156
  46.5 17.7 %collective-permute-start.4 = (f32[2,64,256]{2,1,0:T(8,128)S(1)}, f32[2,64,256]{2,1,0:T(8,128)S(1)}, u32[]{:S(2)}, u32[]{:S(2)}) collective-permute-start(f32[2,64,256]{2,1,0:T(8,128)S(1)} %fusion.35), channel_id=1, source_target_pairs={{0,128},{128,0},{8,136},{136,8},{16,144},{144,16},{24,152},{152,24... | collective-permute-start | bytes 393224 | tf_op jit(solution)/shard_map/ppermute | solution.py:20
  53.0 42.3 %all-to-all-start.1 = ((bf16[64,32,256]{2,1,0:T(8,128)(2,1)}), bf16[64,32,256]{2,1,0:T(8,128)(2,1)S(1)}, u32[]{:S(2)}, u32[]{:S(2)}) async-start(bf16[64,32,256]{2,1,0:T(8,128)(2,1)} %broadcast_in_dim.17), calls=%async_computation.1 | async-start | bytes 2097152 | tf_op jit(solution)/shard_map/all_to_all | solution.py:31
  64.2 30.2 %copy-start.2 = (bf16[128,256]{1,0:T(8,128)(2,1)S(1)}, bf16[128,256]{1,0:T(8,128)(2,1)}, u32[]{:S(2)}) copy-start(bf16[128,256]{1,0:T(8,128)(2,1)} %param.5) | copy-start | bytes 196612
  64.5 29.8 %collective-permute-start.5 = (bf16[2,64,256]{2,1,0:T(8,128)(2,1)S(1)}, bf16[2,64,256]{2,1,0:T(8,128)(2,1)S(1)}, u32[]{:S(2)}, u32[]{:S(2)}) collective-permute-start(bf16[2,64,256]{2,1,0:T(8,128)(2,1)S(1)} %fusion.33), channel_id=1, source_target_pairs={{0,256},{256,0},{8,264},{264,8},{16,272},{272,16},{24,280},{280,24... | collective-permute-start | bytes 196616 | tf_op jit(solution)/shard_map/ppermute | solution.py:20
  94.3 1.5 copy-start.5
  96.1 1.0 copy-start.6
  97.9 10.2 %collective-permute-start.6 = (bf16[2,64,256]{2,1,0:T(8,128)(2,1)S(1)}, bf16[2,64,256]{2,1,0:T(8,128)(2,1)S(1)}, u32[]{:S(2)}, u32[]{:S(2)}) collective-permute-start(bf16[2,64,256]{2,1,0:T(8,128)(2,1)S(1)} %fusion.18), channel_id=1, source_target_pairs={{0,256},{256,0},{8,264},{264,8},{16,272},{272,16},{24,280},{280,24... | collective-permute-start | bytes 196616 | tf_op jit(solution)/shard_map/ppermute | solution.py:20
  108.3 7.4 %collective-permute-start.7 = (bf16[2,64,256]{2,1,0:T(8,128)(2,1)S(1)}, bf16[2,64,256]{2,1,0:T(8,128)(2,1)S(1)}, u32[]{:S(2)}, u32[]{:S(2)}) collective-permute-start(bf16[2,64,256]{2,1,0:T(8,128)(2,1)S(1)} %fusion.21), channel_id=1, source_target_pairs={{0,128},{128,0},{8,136},{136,8},{16,144},{144,16},{24,152},{152,24... | collective-permute-start | bytes 196616 | tf_op jit(solution)/shard_map/ppermute | solution.py:20
  116.6 12.4 %collective-permute-start.8 = (bf16[2,64,256]{2,1,0:T(8,128)(2,1)}, bf16[2,64,256]{2,1,0:T(8,128)(2,1)}, u32[]{:S(2)}, u32[]{:S(2)}) collective-permute-start(bf16[2,64,256]{2,1,0:T(8,128)(2,1)} %fusion.24), channel_id=1, source_target_pairs={{0,64},{64,0},{8,72},{72,8},{16,80},{80,16},{24,88},{88,24},{32,96... | collective-permute-start | bytes 196616 | tf_op jit(solution)/shard_map/ppermute | solution.py:20
  120.6 49.8 %all-to-all-start.2 = ((bf16[64,32,256]{2,1,0:T(8,128)(2,1)}), bf16[64,32,256]{2,1,0:T(8,128)(2,1)S(1)}, u32[]{:S(2)}, u32[]{:S(2)}) async-start(bf16[64,32,256]{2,1,0:T(8,128)(2,1)} %bitcast.40), calls=%async_computation.2 | async-start | bytes 2097152 | tf_op jit(solution)/shard_map/all_to_all | solution.py:41
  130.1 25.5 %collective-permute-start.9 = (bf16[2,64,256]{2,1,0:T(8,128)(2,1)S(1)}, bf16[2,64,256]{2,1,0:T(8,128)(2,1)S(1)}, u32[]{:S(2)}, u32[]{:S(2)}) collective-permute-start(bf16[2,64,256]{2,1,0:T(8,128)(2,1)S(1)} %fusion.27), channel_id=1, source_target_pairs={{0,32},{32,0},{8,40},{40,8},{16,48},{48,16},{24,56},{56,24},{64,96... | collective-permute-start | bytes 196616 | tf_op jit(solution)/shard_map/ppermute | solution.py:20
  155.8 7.2 %collective-permute-start.10 = (bf16[2,64,256]{2,1,0:T(8,128)(2,1)S(1)}, bf16[2,64,256]{2,1,0:T(8,128)(2,1)S(1)}, u32[]{:S(2)}, u32[]{:S(2)}) collective-permute-start(bf16[2,64,256]{2,1,0:T(8,128)(2,1)S(1)} %fusion.16), channel_id=1, source_target_pairs={{0,16},{16,0},{8,24},{24,8},{32,48},{48,32},{40,56},{56,40},{64,80... | collective-permute-start | bytes 196616 | tf_op jit(solution)/shard_map/ppermute | solution.py:20
  163.3 6.2 %collective-permute-start.11 = (bf16[2,64,256]{2,1,0:T(8,128)(2,1)S(1)}, bf16[2,64,256]{2,1,0:T(8,128)(2,1)S(1)}, u32[]{:S(2)}, u32[]{:S(2)}) collective-permute-start(bf16[2,64,256]{2,1,0:T(8,128)(2,1)S(1)} %fusion.29), channel_id=1, source_target_pairs={{0,8},{8,0},{16,24},{24,16},{32,40},{40,32},{48,56},{56,48},{64,72... | collective-permute-start | bytes 196616 | tf_op jit(solution)/shard_map/ppermute | solution.py:20

commit v6 on v3

--- a/solution.py
+++ b/solution.py
@@ -36,11 +36,9 @@
 
 
 def own_rows(running, axes):
-    first, last = axes
-    running = lax.psum_scatter(running, first, scatter_dimension=0, tiled=True)
-    count = lax.axis_size(last)
-    parts = running.reshape(count, running.shape[0] // count, running.shape[1])
-    return jnp.sum(lax.all_to_all(parts, last, 0, 0, tiled=True), axis=0)
+    count = lax.axis_size(axes)
+    parts = running.astype(jnp.bfloat16).reshape(count, running.shape[0] // count, running.shape[1])
+    return jnp.sum(lax.all_to_all(parts, axes, 0, 0, tiled=True).astype(jnp.float32), axis=0)
 
 
 def pair_mean(table):
@@ -104,7 +102,11 @@
     minor_pos = lax.axis_index(minor)
     major_pos = lax.axis_index(major)
     table = jnp.stack([keys, values]).astype(jnp.float32)
-    means = [pooled(table, 2 << m).astype(jnp.bfloat16) for m in range(depth)]
+    means = []
+    running = table
+    for m in range(depth):
+        running = pair_mean(running)
+        means.append(running.astype(jnp.bfloat16))
     peers = jnp.arange(n_minor, dtype=jnp.int32)
     near_level = top_bit(minor_pos ^ peers)
     near_kv = pick_level(

time: 192 us -> 182 us (0.948)
  between operations: 14.9 us -> 1.49 us
  starting transfers between devices: 67.3 us -> 74.9 us
  other arithmetic: 8.03 us -> 5.97 us
    all_to_all x1, waiting for transfers between devices: 9.71 us -> 0.01 us  [own_rows(): lax.all_to_all(parts, axes, 0, 0, tiled=True).astype(jnp.float32)]
    ppermute x6, waiting for transfers between devices: 20.8 us -> 29.6 us  [from_partner(): return lax.ppermute(block, axis, route)]
    all_to_all x1, starting transfers between devices: 6.2 us -> 11.2 us  [own_rows(): lax.all_to_all(parts, axes, 0, 0, tiled=True).astype(jnp.float32)]
    reduce_sum x7 -> x1, other arithmetic: 4.85 us -> 0.79 us  [own_rows(): jnp.sum(lax.all_to_all(parts, axes, 0, 0, tiled=True).astype(jnp.float32)...]
    ppermute x6, starting transfers between devices: 23.9 us -> 26.1 us  [from_partner(): return lax.ppermute(block, axis, route)]
  transfers between devices with their start and end apart: 14 -> 13, of which waited for: 11 -> 10; matrix products, arithmetic and copies ran while one was open for 4% -> 5% of each run, Pallas kernels for 0% -> 0%
where the time goes in v6:
time: 182 us; the launch traced here: 179 us
  waiting for transfers between devices  82.5 us (45%)
  starting transfers between devices  74.9 us (41%)
  local copies, waits for them, and re-layouts  10.4 us (6%)
  other arithmetic  5.97 us (3%)
  matrix products  3.35 us (2%)
    ppermute x3, waiting for transfers between devices, swap_major(): return lax.ppermute(block, axis, [(i, i ^ 1 << bit) for i in range(count)])  32.8 us
    ppermute x6, waiting for transfers between devices, from_partner(): return lax.ppermute(block, axis, route)  29.6 us
    ppermute x6, starting transfers between devices, from_partner(): return lax.ppermute(block, axis, route)  26.1 us
    all_to_all x1, waiting for transfers between devices, on_device(): near_recv = lax.all_to_all(near_send, minor, 0, 0, tiled=True)  19.7 us
    all_to_all x2, starting transfers between devices, from_everyone(): return lax.all_to_all(copies, axis, split_axis=0, concat_axis=0, tiled=True)  16.2 us
    ppermute x3, starting transfers between devices, swap_major(): return lax.ppermute(block, axis, [(i, i ^ 1 << bit) for i in range(count)])  14.1 us
    all_to_all x1, starting transfers between devices, own_rows(): lax.all_to_all(parts, axes, 0, 0, tiled=True).astype(jnp.float32)  11.2 us
    all_to_all x1, starting transfers between devices, on_device(): near_recv = lax.all_to_all(near_send, minor, 0, 0, tiled=True)  7.23 us
  transfers between devices with their start and end apart: 13, of which 10 were waited for; matrix products, arithmetic and copies ran while one was open for 5% of the time, Pallas kernels for 0%

profile of v6, /device:TPU:6, one launch (start us, length us, event | category | flops | bytes accessed | tf_op | source)
XLA Modules:
  0.0 178.6 jit_solution(7470962651981421132)
XLA Ops:
  0.7 0.9 stack.18
  1.5 0.1 copy.144
  1.6 0.9 stack.19
  2.5 0.1 copy.145
  2.6 0.3 maximum_convert_fusion
  2.9 0.1 convert_bitcast_fusion
  3.3 0.7 broadcast_select_fusion
  4.1 1.7 pad_maximum_fusion
  5.8 7.2 %all-to-all-start = ((bf16[8,2,78,256]{3,1,2,0:T(2,128)(2,1)}), bf16[8,2,78,256]{3,1,2,0:T(2,128)(2,1)S(1)}, u32[]{:S(2)}, u32[]{:S(2)}) async-start(bf16[8,2,78,256]{3,1,2,0:T(2,128)(2,1)} %pad_maximum_fusion), calls=%async_computation | async-start | bytes 1277952 | tf_op jit(solution)/shard_map/all_to_all | solution.py:121
  13.0 0.1 copy.158
  13.2 19.7 %all-to-all-done = bf16[8,2,78,256]{3,1,2,0:T(2,128)(2,1)S(1)} async-done(((bf16[8,2,78,256]{3,1,2,0:T(2,128)(2,1)}), bf16[8,2,78,256]{3,1,2,0:T(2,128)(2,1)S(1)}, u32[]{:S(2)}, u32[]{:S(2)}) %all-to-all-start) | async-done | bytes 639008 | tf_op jit(solution)/shard_map/all_to_all | solution.py:121
  33.0 0.9 broadcast_in_dim.43
  33.8 4.8 %all-to-all-start.1 = ((bf16[8,128,256]{1,2,0:T(8,128)(2,1)}), bf16[8,128,256]{1,2,0:T(8,128)(2,1)S(1)}, u32[]{:S(2)}, u32[]{:S(2)}) async-start(bf16[8,128,256]{1,2,0:T(8,128)(2,1)} %broadcast_in_dim.43), calls=%async_computation.1 | async-start | bytes 1048576 | tf_op jit(solution)/shard_map/all_to_all | solution.py:31
  38.8 4.3 %collective-permute-start = (bf16[2,112,256]{2,1,0:T(8,128)(2,1)S(1)}, bf16[2,112,256]{2,1,0:T(8,128)(2,1)S(1)}, u32[]{:S(2)}, u32[]{:S(2)}) collective-permute-start(bf16[2,112,256]{2,1,0:T(8,128)(2,1)S(1)} %pad_maximum_fusion.2), channel_id=1, source_target_pairs={{0,64},{64,0},{128,192},{192,128},{256,320},{320,256},{384,448},{4... | collective-permute-start | bytes 344072 | tf_op jit(solution)/shard_map/ppermute | solution.py:88
  43.1 0.4 slice.269
  43.6 0.1 constant_dynamic-slice_fusion
  43.8 2.7 %collective-permute-done = bf16[2,112,256]{2,1,0:T(8,128)(2,1)S(1)} collective-permute-done((bf16[2,112,256]{2,1,0:T(8,128)(2,1)S(1)}, bf16[2,112,256]{2,1,0:T(8,128)(2,1)S(1)}, u32[]{:S(2)}, u32[]{:S(2)}) %collective-permute-start) | collective-permute-done | bytes 114720 | tf_op jit(solution)/shard_map/ppermute | solution.py:88
  46.5 0.4 all-to-all-done.1
  46.9 1.1 broadcast_in_dim.44
  48.0 11.5 %all-to-all-start.2 = ((bf16[64,32,256]{2,1,0:T(8,128)(2,1)}), bf16[64,32,256]{2,1,0:T(8,128)(2,1)S(1)}, u32[]{:S(2)}, u32[]{:S(2)}) async-start(bf16[64,32,256]{2,1,0:T(8,128)(2,1)} %broadcast_in_dim.44), calls=%async_computation.2 | async-start | bytes 2097152 | tf_op jit(solution)/shard_map/all_to_all | solution.py:31
  59.5 4.4 %collective-permute-start.1 = (bf16[2,96,256]{2,1,0:T(8,128)(2,1)S(1)}, bf16[2,96,256]{2,1,0:T(8,128)(2,1)S(1)}, u32[]{:S(2)}, u32[]{:S(2)}) collective-permute-start(bf16[2,96,256]{2,1,0:T(8,128)(2,1)S(1)} %pad_maximum_fusion.3), channel_id=1, source_target_pairs={{0,128},{64,192},{128,0},{192,64},{256,384},{320,448},{384,256},{4... | collective-permute-start | bytes 294920 | tf_op jit(solution)/shard_map/ppermute | solution.py:88
  64.0 24.9 %collective-permute-done.1 = bf16[2,96,256]{2,1,0:T(8,128)(2,1)S(1)} collective-permute-done((bf16[2,96,256]{2,1,0:T(8,128)(2,1)S(1)}, bf16[2,96,256]{2,1,0:T(8,128)(2,1)S(1)}, u32[]{:S(2)}, u32[]{:S(2)}) %collective-permute-start.1) | collective-permute-done | bytes 98336 | tf_op jit(solution)/shard_map/ppermute | solution.py:88
  88.9 5.5 %collective-permute-start.2 = (bf16[2,64,256]{2,1,0:T(8,128)(2,1)S(1)}, bf16[2,64,256]{2,1,0:T(8,128)(2,1)S(1)}, u32[]{:S(2)}, u32[]{:S(2)}) collective-permute-start(bf16[2,64,256]{2,1,0:T(8,128)(2,1)S(1)} %maximum_select_fusion.1), channel_id=1, source_target_pairs={{0,256},{64,320},{128,384},{192,448},{256,0},{320,64},{384,128},{4... | collective-permute-start | bytes 196616 | tf_op jit(solution)/shard_map/ppermute | solution.py:88
  94.4 5.3 %collective-permute-done.2 = bf16[2,64,256]{2,1,0:T(8,128)(2,1)S(1)} collective-permute-done((bf16[2,64,256]{2,1,0:T(8,128)(2,1)S(1)}, bf16[2,64,256]{2,1,0:T(8,128)(2,1)S(1)}, u32[]{:S(2)}, u32[]{:S(2)}) %collective-permute-start.2) | collective-permute-done | bytes 65568 | tf_op jit(solution)/shard_map/ppermute | solution.py:88
  99.7 0.2 fusion.94
  100.0 0.2 fusion.93
  100.3 0.2 convolution_convert_fusion.5
  100.6 0.4 convolution_convert_fusion.1
  101.0 0.2 fusion.41
  101.1 0.2 fusion.7
  101.4 0.2 fusion.42
  101.6 0.8 copy-done.6
  102.3 0.2 fusion.4
  102.7 0.2 fusion.60
  102.9 0.2 fusion.57
  103.2 4.8 %collective-permute-start.3 = (bf16[2,64,256]{2,1,0:T(8,128)(2,1)S(1)}, bf16[2,64,256]{2,1,0:T(8,128)(2,1)S(1)}, u32[]{:S(2)}, u32[]{:S(2)}) collective-permute-start(bf16[2,64,256]{2,1,0:T(8,128)(2,1)S(1)} %fusion.18), channel_id=1, source_target_pairs={{0,256},{256,0},{8,264},{264,8},{16,272},{272,16},{24,280},{280,24... | collective-permute-start | bytes 196616 | tf_op jit(solution)/shard_map/ppermute | solution.py:20
  108.0 0.2 convolution_convert_fusion.4
  108.2 5.4 %collective-permute-done.3 = bf16[2,64,256]{2,1,0:T(8,128)(2,1)S(1)} collective-permute-done((bf16[2,64,256]{2,1,0:T(8,128)(2,1)S(1)}, bf16[2,64,256]{2,1,0:T(8,128)(2,1)S(1)}, u32[]{:S(2)}, u32[]{:S(2)}) %collective-permute-start.3) | collective-permute-done | bytes 65568 | tf_op jit(solution)/shard_map/ppermute | solution.py:20
  113.6 0.1 copy.167
  113.8 0.7 fusion.21
  114.5 1.9 %collective-permute-start.4 = (bf16[2,64,256]{2,1,0:T(8,128)(2,1)}, bf16[2,64,256]{2,1,0:T(8,128)(2,1)}, u32[]{:S(2)}, u32[]{:S(2)}) collective-permute-start(bf16[2,64,256]{2,1,0:T(8,128)(2,1)} %fusion.21), channel_id=1, source_target_pairs={{0,128},{128,0},{8,136},{136,8},{16,144},{144,16},{24,152},{152,24... | collective-permute-start | bytes 196616 | tf_op jit(solution)/shard_map/ppermute | solution.py:20
  116.4 0.4 fusion
  116.8 1.3 copy.184
  118.1 11.2 %all-to-all-start.3 = ((bf16[64,32,256]{2,1,0:T(8,128)(2,1)}), bf16[64,32,256]{2,1,0:T(8,128)(2,1)S(1)}, u32[]{:S(2)}, u32[]{:S(2)}) async-start(bf16[64,32,256]{2,1,0:T(8,128)(2,1)} %bitcast.50), calls=%async_computation.3 | async-start | bytes 2097152 | tf_op jit(solution)/shard_map/all_to_all | solution.py:41
  129.3 0.9 add_multiply_fusion.4
  130.2 0.1 copy.170
  130.5 3.5 %collective-permute-start.5 = (bf16[2,64,256]{2,1,0:T(8,128)(2,1)S(1)}, bf16[2,64,256]{2,1,0:T(8,128)(2,1)S(1)}, u32[]{:S(2)}, u32[]{:S(2)}) collective-permute-start(bf16[2,64,256]{2,1,0:T(8,128)(2,1)S(1)} %fusion.24), channel_id=1, source_target_pairs={{0,64},{64,0},{8,72},{72,8},{16,80},{80,16},{24,88},{88,24},{32,96... | collective-permute-start | bytes 196616 | tf_op jit(solution)/shard_map/ppermute | solution.py:20
  134.0 0.7 copy.185
  134.7 16.6 %collective-permute-done.5 = bf16[2,64,256]{2,1,0:T(8,128)(2,1)S(1)} collective-permute-done((bf16[2,64,256]{2,1,0:T(8,128)(2,1)S(1)}, bf16[2,64,256]{2,1,0:T(8,128)(2,1)S(1)}, u32[]{:S(2)}, u32[]{:S(2)}) %collective-permute-start.5) | collective-permute-done | bytes 65568 | tf_op jit(solution)/shard_map/ppermute | solution.py:20
  151.3 0.1 copy.173
  151.5 9.0 %collective-permute-start.6 = (bf16[2,64,256]{2,1,0:T(8,128)(2,1)S(1)}, bf16[2,64,256]{2,1,0:T(8,128)(2,1)S(1)}, u32[]{:S(2)}, u32[]{:S(2)}) collective-permute-start(bf16[2,64,256]{2,1,0:T(8,128)(2,1)S(1)} %fusion.27), channel_id=1, source_target_pairs={{0,32},{32,0},{8,40},{40,8},{16,48},{48,16},{24,56},{56,24},{64,96... | collective-permute-start | bytes 196616 | tf_op jit(solution)/shard_map/ppermute | solution.py:20
  160.5 0.2 convolution_convert_fusion.3
  160.8 2.2 %collective-permute-done.6 = bf16[2,64,256]{2,1,0:T(8,128)(2,1)S(1)} collective-permute-done((bf16[2,64,256]{2,1,0:T(8,128)(2,1)S(1)}, bf16[2,64,256]{2,1,0:T(8,128)(2,1)S(1)}, u32[]{:S(2)}, u32[]{:S(2)}) %collective-permute-start.6) | collective-permute-done | bytes 65568 | tf_op jit(solution)/shard_map/ppermute | solution.py:20
  163.0 0.1 copy.176
  163.3 5.0 %collective-permute-start.7 = (bf16[2,64,256]{2,1,0:T(8,128)(2,1)S(1)}, bf16[2,64,256]{2,1,0:T(8,128)(2,1)S(1)}, u32[]{:S(2)}, u32[]{:S(2)}) collective-permute-start(bf16[2,64,256]{2,1,0:T(8,128)(2,1)S(1)} %fusion.16), channel_id=1, source_target_pairs={{0,16},{16,0},{8,24},{24,8},{32,48},{48,32},{40,56},{56,40},{64,80... | collective-permute-start | bytes 196616 | tf_op jit(solution)/shard_map/ppermute | solution.py:20
  168.3 0.2 convolution_convert_fusion.2
  168.5 2.0 %collective-permute-done.7 = bf16[2,64,256]{2,1,0:T(8,128)(2,1)S(1)} collective-permute-done((bf16[2,64,256]{2,1,0:T(8,128)(2,1)S(1)}, bf16[2,64,256]{2,1,0:T(8,128)(2,1)S(1)}, u32[]{:S(2)}, u32[]{:S(2)}) %collective-permute-start.7) | collective-permute-done | bytes 65568 | tf_op jit(solution)/shard_map/ppermute | solution.py:20
  170.5 0.1 copy.179
  170.8 1.9 %collective-permute-start.8 = (bf16[2,64,256]{2,1,0:T(8,128)(2,1)S(1)}, bf16[2,64,256]{2,1,0:T(8,128)(2,1)S(1)}, u32[]{:S(2)}, u32[]{:S(2)}) collective-permute-start(bf16[2,64,256]{2,1,0:T(8,128)(2,1)S(1)} %fusion.29), channel_id=1, source_target_pairs={{0,8},{8,0},{16,24},{24,16},{32,40},{40,32},{48,56},{56,48},{64,72... | collective-permute-start | bytes 196616 | tf_op jit(solution)/shard_map/ppermute | solution.py:20
  172.7 0.7 copy.186
  173.5 3.5 %collective-permute-done.8 = bf16[2,64,256]{2,1,0:T(8,128)(2,1)S(1)} collective-permute-done((bf16[2,64,256]{2,1,0:T(8,128)(2,1)S(1)}, bf16[2,64,256]{2,1,0:T(8,128)(2,1)S(1)}, u32[]{:S(2)}, u32[]{:S(2)}) %collective-permute-start.8) | collective-permute-done | bytes 65568 | tf_op jit(solution)/shard_map/ppermute | solution.py:20
  177.0 0.1 copy.182
  177.2 0.7 slice_bitcast_fusion
  177.9 0.8 convert_reduce_fusion
  (87 shorter events, 1.9 us)
Async XLA Ops:
  4.1 8.9 %copy-start.3 = (bf16[128,256]{1,0:T(8,128)(2,1)S(1)}, bf16[128,256]{1,0:T(8,128)(2,1)}, u32[]{:S(2)}) copy-start(bf16[128,256]{1,0:T(8,128)(2,1)} %param.8) | copy-start | bytes 196612
  5.8 7.4 %copy-start = (bf16[128,256]{1,0:T(8,128)(2,1)S(1)}, bf16[128,256]{1,0:T(8,128)(2,1)}, u32[]{:S(2)}) copy-start(bf16[128,256]{1,0:T(8,128)(2,1)} %param.7) | copy-start | bytes 196612
  5.8 7.4 %copy-start.1 = (bf16[128,256]{1,0:T(8,128)(2,1)S(1)}, bf16[128,256]{1,0:T(8,128)(2,1)}, u32[]{:S(2)}) copy-start(bf16[128,256]{1,0:T(8,128)(2,1)} %param.6) | copy-start | bytes 196612
  5.8 27.2 %all-to-all-start = ((bf16[8,2,78,256]{3,1,2,0:T(2,128)(2,1)}), bf16[8,2,78,256]{3,1,2,0:T(2,128)(2,1)S(1)}, u32[]{:S(2)}, u32[]{:S(2)}) async-start(bf16[8,2,78,256]{3,1,2,0:T(2,128)(2,1)} %pad_maximum_fusion), calls=%async_computation | async-start | bytes 1277952 | tf_op jit(solution)/shard_map/all_to_all | solution.py:121
  33.8 13.1 %all-to-all-start.1 = ((bf16[8,128,256]{1,2,0:T(8,128)(2,1)}), bf16[8,128,256]{1,2,0:T(8,128)(2,1)S(1)}, u32[]{:S(2)}, u32[]{:S(2)}) async-start(bf16[8,128,256]{1,2,0:T(8,128)(2,1)} %broadcast_in_dim.43), calls=%async_computation.1 | async-start | bytes 1048576 | tf_op jit(solution)/shard_map/all_to_all | solution.py:31
  38.8 7.7 %collective-permute-start = (bf16[2,112,256]{2,1,0:T(8,128)(2,1)S(1)}, bf16[2,112,256]{2,1,0:T(8,128)(2,1)S(1)}, u32[]{:S(2)}, u32[]{:S(2)}) collective-permute-start(bf16[2,112,256]{2,1,0:T(8,128)(2,1)S(1)} %pad_maximum_fusion.2), channel_id=1, source_target_pairs={{0,64},{64,0},{128,192},{192,128},{256,320},{320,256},{384,448},{4... | collective-permute-start | bytes 344072 | tf_op jit(solution)/shard_map/ppermute | solution.py:88
  43.4 3.5 %copy-start.4 = (bf16[32,256]{1,0:T(8,128)(2,1)S(1)}, bf16[32,256]{1,0:T(8,128)(2,1)}, u32[]{:S(2)}) copy-start(bf16[32,256]{1,0:T(8,128)(2,1)} %param.9) | copy-start | bytes 49156
  48.0 51.6 %copy-start.2 = (bf16[128,256]{1,0:T(8,128)(2,1)S(1)}, bf16[128,256]{1,0:T(8,128)(2,1)}, u32[]{:S(2)}) copy-start(bf16[128,256]{1,0:T(8,128)(2,1)} %param.5) | copy-start | bytes 196612
  48.0 52.5 %all-to-all-start.2 = ((bf16[64,32,256]{2,1,0:T(8,128)(2,1)}), bf16[64,32,256]{2,1,0:T(8,128)(2,1)S(1)}, u32[]{:S(2)}, u32[]{:S(2)}) async-start(bf16[64,32,256]{2,1,0:T(8,128)(2,1)} %broadcast_in_dim.44), calls=%async_computation.2 | async-start | bytes 2097152 | tf_op jit(solution)/shard_map/all_to_all | solution.py:31
  59.5 29.3 %collective-permute-start.1 = (bf16[2,96,256]{2,1,0:T(8,128)(2,1)S(1)}, bf16[2,96,256]{2,1,0:T(8,128)(2,1)S(1)}, u32[]{:S(2)}, u32[]{:S(2)}) collective-permute-start(bf16[2,96,256]{2,1,0:T(8,128)(2,1)S(1)} %pad_maximum_fusion.3), channel_id=1, source_target_pairs={{0,128},{64,192},{128,0},{192,64},{256,384},{320,448},{384,256},{4... | collective-permute-start | bytes 294920 | tf_op jit(solution)/shard_map/ppermute | solution.py:88
  88.9 10.8 %collective-permute-start.2 = (bf16[2,64,256]{2,1,0:T(8,128)(2,1)S(1)}, bf16[2,64,256]{2,1,0:T(8,128)(2,1)S(1)}, u32[]{:S(2)}, u32[]{:S(2)}) collective-permute-start(bf16[2,64,256]{2,1,0:T(8,128)(2,1)S(1)} %maximum_select_fusion.1), channel_id=1, source_target_pairs={{0,256},{64,320},{128,384},{192,448},{256,0},{320,64},{384,128},{4... | collective-permute-start | bytes 196616 | tf_op jit(solution)/shard_map/ppermute | solution.py:88
  99.6 1.5 copy-start.5
  101.4 1.0 copy-start.6
  103.2 10.4 %collective-permute-start.3 = (bf16[2,64,256]{2,1,0:T(8,128)(2,1)S(1)}, bf16[2,64,256]{2,1,0:T(8,128)(2,1)S(1)}, u32[]{:S(2)}, u32[]{:S(2)}) collective-permute-start(bf16[2,64,256]{2,1,0:T(8,128)(2,1)S(1)} %fusion.18), channel_id=1, source_target_pairs={{0,256},{256,0},{8,264},{264,8},{16,272},{272,16},{24,280},{280,24... | collective-permute-start | bytes 196616 | tf_op jit(solution)/shard_map/ppermute | solution.py:20
  114.5 14.9 %collective-permute-start.4 = (bf16[2,64,256]{2,1,0:T(8,128)(2,1)}, bf16[2,64,256]{2,1,0:T(8,128)(2,1)}, u32[]{:S(2)}, u32[]{:S(2)}) collective-permute-start(bf16[2,64,256]{2,1,0:T(8,128)(2,1)} %fusion.21), channel_id=1, source_target_pairs={{0,128},{128,0},{8,136},{136,8},{16,144},{144,16},{24,152},{152,24... | collective-permute-start | bytes 196616 | tf_op jit(solution)/shard_map/ppermute | solution.py:20
  118.1 59.7 %all-to-all-start.3 = ((bf16[64,32,256]{2,1,0:T(8,128)(2,1)}), bf16[64,32,256]{2,1,0:T(8,128)(2,1)S(1)}, u32[]{:S(2)}, u32[]{:S(2)}) async-start(bf16[64,32,256]{2,1,0:T(8,128)(2,1)} %bitcast.50), calls=%async_computation.3 | async-start | bytes 2097152 | tf_op jit(solution)/shard_map/all_to_all | solution.py:41
  130.5 20.8 %collective-permute-start.5 = (bf16[2,64,256]{2,1,0:T(8,128)(2,1)S(1)}, bf16[2,64,256]{2,1,0:T(8,128)(2,1)S(1)}, u32[]{:S(2)}, u32[]{:S(2)}) collective-permute-start(bf16[2,64,256]{2,1,0:T(8,128)(2,1)S(1)} %fusion.24), channel_id=1, source_target_pairs={{0,64},{64,0},{8,72},{72,8},{16,80},{80,16},{24,88},{88,24},{32,96... | collective-permute-start | bytes 196616 | tf_op jit(solution)/shard_map/ppermute | solution.py:20
  151.5 11.4 %collective-permute-start.6 = (bf16[2,64,256]{2,1,0:T(8,128)(2,1)S(1)}, bf16[2,64,256]{2,1,0:T(8,128)(2,1)S(1)}, u32[]{:S(2)}, u32[]{:S(2)}) collective-permute-start(bf16[2,64,256]{2,1,0:T(8,128)(2,1)S(1)} %fusion.27), channel_id=1, source_target_pairs={{0,32},{32,0},{8,40},{40,8},{16,48},{48,16},{24,56},{56,24},{64,96... | collective-permute-start | bytes 196616 | tf_op jit(solution)/shard_map/ppermute | solution.py:20
  163.3 7.2 %collective-permute-start.7 = (bf16[2,64,256]{2,1,0:T(8,128)(2,1)S(1)}, bf16[2,64,256]{2,1,0:T(8,128)(2,1)S(1)}, u32[]{:S(2)}, u32[]{:S(2)}) collective-permute-start(bf16[2,64,256]{2,1,0:T(8,128)(2,1)S(1)} %fusion.16), channel_id=1, source_target_pairs={{0,16},{16,0},{8,24},{24,8},{32,48},{48,32},{40,56},{56,40},{64,80... | collective-permute-start | bytes 196616 | tf_op jit(solution)/shard_map/ppermute | solution.py:20
  170.8 6.2 %collective-permute-start.8 = (bf16[2,64,256]{2,1,0:T(8,128)(2,1)S(1)}, bf16[2,64,256]{2,1,0:T(8,128)(2,1)S(1)}, u32[]{:S(2)}, u32[]{:S(2)}) collective-permute-start(bf16[2,64,256]{2,1,0:T(8,128)(2,1)S(1)} %fusion.29), channel_id=1, source_target_pairs={{0,8},{8,0},{16,24},{24,16},{32,40},{40,32},{48,56},{56,48},{64,72... | collective-permute-start | bytes 196616 | tf_op jit(solution)/shard_map/ppermute | solution.py:20

commit v7 on v5

--- a/solution.py
+++ b/solution.py
@@ -51,6 +51,25 @@
         table[:, :, None], (table.shape[0], table.shape[1], 2, table.shape[2])
     )
     return doubled.reshape(table.shape[0], table.shape[1] * 2, table.shape[2])
+
+
+def top_bit(d):
+    total = jnp.zeros_like(d) - 1
+    for k in range(0, 7):
+        total = total + (d >= (1 << k)).astype(d.dtype)
+    return total
+
+
+def pad_rows(x, rows):
+    return jnp.pad(x, ((0, 0), (0, rows - x.shape[1]), (0, 0)))
+
+
+def pick_level(level_of, tables, lo):
+    out = tables[-1]
+    for i in range(len(tables) - 2, -1, -1):
+        mask = (level_of == lo + i).reshape((-1,) + (1,) * (tables[i].ndim - 1))
+        out = jnp.where(mask, tables[i], out)
+    return out
 
 
 def on_device(queries, keys, values, cotangent, out_weight):
@@ -126,31 +145,64 @@
     grad_sets = jnp.stack(
         [jnp.concatenate(grad_key_parts, axis=1), jnp.concatenate(grad_value_parts, axis=1)]
     )
-    carried = jnp.zeros((2, coarse, width), jnp.float32)
-    for layer_bit in reversed(range(depth)):
-        first = tokens + layer_bit * coarse
-        outgoing = grad_sets[:, first : first + coarse]
-        kept = jnp.zeros((2, coarse, width), jnp.float32)
-        if layer_bit + 1 < depth:
-            lower_half = position >> layer_bit & 1 == 0
-            spread = spread_rows(carried * 0.5)
-            low_part = spread[:, :coarse]
-            high_part = spread[:, coarse:]
-            kept = jnp.where(lower_half, low_part, high_part)
-            outgoing = outgoing + jnp.where(lower_half, high_part, low_part)
-        incoming = from_partner(outgoing.astype(jnp.bfloat16), SEQ, layer_bit).astype(
-            outgoing.dtype
-        )
-        carried = kept + incoming
-    own_grads = grad_sets[:, :tokens] + spread_rows(carried * 0.5)
+    major, minor = SEQ
+    n_minor = lax.axis_size(minor)
+    n_seq = lax.axis_size(SEQ)
+    minor_depth = n_minor.bit_length() - 1
+    far_rows = coarse >> minor_depth
+    near_level = top_bit(lax.axis_index(minor) ^ jnp.arange(n_minor, dtype=jnp.int32))
+    far_level = top_bit(position ^ jnp.arange(n_seq, dtype=jnp.int32))
+    level_grads = []
+    for m in range(depth):
+        first = tokens + m * coarse
+        part = grad_sets[:, first : first + coarse].astype(jnp.bfloat16)
+        level_grads.append(part.reshape(2, 1 << m, coarse >> m, width))
+    near_back = pick_level(
+        near_level,
+        [
+            jnp.stack([pad_rows(level_grads[m][:, k & ((1 << m) - 1)], coarse) for k in range(n_minor)])
+            for m in range(minor_depth)
+        ],
+        0,
+    )
+    near_got = lax.all_to_all(near_back, minor, 0, 0, tiled=True).astype(jnp.float32)
+    far_back = pick_level(
+        far_level,
+        [
+            jnp.stack([pad_rows(level_grads[m][:, c & ((1 << m) - 1)], far_rows) for c in range(n_seq)])
+            for m in range(minor_depth, depth)
+        ],
+        minor_depth,
+    )
+    weight_grad = lax.dot_general(
+        full_cot, attended, (((0,), (0,)), ((), ())), preferred_element_type=jnp.float32
+    )
+    w_rows = weight_grad.shape[0] // n_seq
+    far_send = jnp.concatenate(
+        [
+            far_back.reshape(n_seq, 2 * far_rows, width),
+            weight_grad.astype(jnp.bfloat16).reshape(n_seq, w_rows, width),
+        ],
+        axis=1,
+    )
+    far_all = lax.all_to_all(far_send, SEQ, 0, 0, tiled=True).astype(jnp.float32)
+    far_got = far_all[:, : 2 * far_rows].reshape(n_seq, 2, far_rows, width)
+    grad_out_weight = jnp.sum(far_all[:, 2 * far_rows :], axis=0)
+
+    own_grads = grad_sets[:, :tokens]
+    for m in range(depth):
+        rows = coarse >> m
+        if m < minor_depth:
+            got, level_of = near_got, near_level
+        else:
+            got, level_of = far_got, far_level
+        mask = (level_of == m).reshape(-1, 1, 1, 1)
+        summed = jnp.sum(jnp.where(mask, got[:, :, :rows], 0.0), axis=0)
+        factor = 2 << m
+        spread = jnp.broadcast_to((summed / factor)[:, :, None], (2, rows, factor, width))
+        own_grads = own_grads + spread.reshape(2, tokens, width)
     grad_keys = own_grads[0].astype(jnp.bfloat16)
     grad_values = own_grads[1].astype(jnp.bfloat16)
-    grad_out_weight = own_rows(
-        lax.dot_general(
-            full_cot, attended, (((0,), (0,)), ((), ())), preferred_element_type=jnp.float32
-        ),
-        SEQ,
-    )
     return (attended, grad_queries, grad_keys, grad_values, grad_out_weight)
 
 

time: 172 us -> 187 us (1.087)
  starting transfers between devices: 72.1 us -> 55.8 us
  waiting for transfers between devices: 80.2 us -> 92.5 us
  other arithmetic: 3.37 us -> 11 us
  local copies, waits for them, and re-layouts: 10.6 us -> 16.4 us
  matrix products: 3.36 us -> 6.36 us
  between operations: 1.45 us -> 3.51 us
    all_to_all x1 -> x2, waiting for transfers between devices: 0.01 us -> 43.9 us  [the longest x1 31.7 us: on_device(): lax.all_to_all(far_send, SEQ, 0, 0, tiled=True).astype(jnp.float32)]
    ppermute x12 -> x6, waiting for transfers between devices: 80.2 us -> 48.6 us  [from_partner(): return lax.ppermute(block, axis, route)]
    ppermute x12 -> x6, starting transfers between devices: 44.9 us -> 25.5 us  [from_partner(): return lax.ppermute(block, axis, route)]
    unnamed x23 -> x252, local copies, waits for them, and re-layouts: 2.46 us -> 6.89 us
    all_to_all x1 -> x2, starting transfers between devices: 8.36 us -> 11.3 us  [the longest x1 6.42 us: on_device(): lax.all_to_all(near_back, minor, 0, 0, tiled=True).astype(jnp.float32)]
    reduce_sum x1 -> x7, other arithmetic: 0.79 us -> 3.65 us  [the longest x6 2.89 us: on_device(): summed = jnp.sum(jnp.where(mask, got[:, :, :rows], 0.0), axis=0)]
  transfers between devices with their start and end apart: 15 -> 10, of which waited for: 9 -> 7; matrix products, arithmetic and copies ran while one was open for 6% -> 11% of each run, Pallas kernels for 0% -> 0%
where the time goes in v7:
time: 187 us; the launch traced here: 186 us
  waiting for transfers between devices  92.5 us (49%)
  starting transfers between devices  55.8 us (30%)
  local copies, waits for them, and re-layouts  16.4 us (9%)
  other arithmetic  11 us (6%)
  matrix products  6.36 us (3%)
  between operations  3.51 us (2%)
    ppermute x6, waiting for transfers between devices, from_partner(): return lax.ppermute(block, axis, route)  48.6 us
    all_to_all x1, waiting for transfers between devices, on_device(): lax.all_to_all(far_send, SEQ, 0, 0, tiled=True).astype(jnp.float32)  31.7 us
    ppermute x6, starting transfers between devices, from_partner(): return lax.ppermute(block, axis, route)  25.5 us
    all_to_all x2, starting transfers between devices, from_everyone(): return lax.all_to_all(copies, axis, split_axis=0, concat_axis=0, tiled=True)  19.1 us
    all_to_all x1, waiting for transfers between devices, on_device(): lax.all_to_all(near_back, minor, 0, 0, tiled=True).astype(jnp.float32)  12.2 us
    unnamed x252, local copies, waits for them, and re-layouts  6.89 us
    all_to_all x1, starting transfers between devices, on_device(): lax.all_to_all(near_back, minor, 0, 0, tiled=True).astype(jnp.float32)  6.42 us
    all_to_all x1, starting transfers between devices, on_device(): lax.all_to_all(far_send, SEQ, 0, 0, tiled=True).astype(jnp.float32)  4.85 us
  transfers between devices with their start and end apart: 10, of which 7 were waited for; matrix products, arithmetic and copies ran while one was open for 11% of the time, Pallas kernels for 0%

profile of v7, /device:TPU:6, one launch (start us, length us, event | category | flops | bytes accessed | tf_op | source)
XLA Modules:
  0.0 185.6 jit_solution(10629670721931857465)
XLA Ops:
  0.7 0.9 stack.148
  1.6 0.9 stack.149
  2.8 3.5 %collective-permute-start = (f32[2,64,256]{2,1,0:T(8,128)S(1)}, f32[2,64,256]{2,1,0:T(8,128)S(1)}, u32[]{:S(2)}, u32[]{:S(2)}) collective-permute-start(f32[2,64,256]{2,1,0:T(8,128)S(1)} %bitcast.740), channel_id=1, source_target_pairs={{0,8},{8,0},{16,24},{24,16},{32,40},{40,32},{48,56},{56,48},{64,72... | collective-permute-start | bytes 393224 | tf_op jit(solution)/shard_map/ppermute | solution.py:20
  6.3 1.0 copy.123
  7.3 0.9 broadcast_in_dim.142
  8.1 7.7 %all-to-all-start = ((bf16[8,128,256]{1,2,0:T(8,128)(2,1)}), bf16[8,128,256]{1,2,0:T(8,128)(2,1)S(1)}, u32[]{:S(2)}, u32[]{:S(2)}) async-start(bf16[8,128,256]{1,2,0:T(8,128)(2,1)} %broadcast_in_dim.142), calls=%async_computation | async-start | bytes 1048576 | tf_op jit(solution)/shard_map/all_to_all | solution.py:31
  15.9 0.5 broadcast_compare_fusion
  16.6 0.2 copy.111
  16.8 0.2 fusion.29
  17.1 1.9 %collective-permute-start.1 = (f32[2,64,256]{2,1,0:T(8,128)S(1)}, f32[2,64,256]{2,1,0:T(8,128)S(1)}, u32[]{:S(2)}, u32[]{:S(2)}) collective-permute-start(f32[2,64,256]{2,1,0:T(8,128)S(1)} %bitcast.741), channel_id=1, source_target_pairs={{0,16},{16,0},{8,24},{24,8},{32,48},{48,32},{40,56},{56,40},{64,80... | collective-permute-start | bytes 393224 | tf_op jit(solution)/shard_map/ppermute | solution.py:20
  19.0 9.2 %collective-permute-done.1 = f32[2,64,256]{2,1,0:T(8,128)S(1)} collective-permute-done((f32[2,64,256]{2,1,0:T(8,128)S(1)}, f32[2,64,256]{2,1,0:T(8,128)S(1)}, u32[]{:S(2)}, u32[]{:S(2)}) %collective-permute-start.1) | collective-permute-done | bytes 131104 | tf_op jit(solution)/shard_map/ppermute | solution.py:20
  28.3 0.2 copy.114
  28.6 0.2 fusion.28
  28.8 3.9 %collective-permute-start.2 = (f32[2,64,256]{2,1,0:T(8,128)S(1)}, f32[2,64,256]{2,1,0:T(8,128)S(1)}, u32[]{:S(2)}, u32[]{:S(2)}) collective-permute-start(f32[2,64,256]{2,1,0:T(8,128)S(1)} %bitcast.742), channel_id=1, source_target_pairs={{0,32},{32,0},{8,40},{40,8},{16,48},{48,16},{24,56},{56,24},{64,96... | collective-permute-start | bytes 393224 | tf_op jit(solution)/shard_map/ppermute | solution.py:20
  32.7 8.0 %collective-permute-done.2 = f32[2,64,256]{2,1,0:T(8,128)S(1)} collective-permute-done((f32[2,64,256]{2,1,0:T(8,128)S(1)}, f32[2,64,256]{2,1,0:T(8,128)S(1)}, u32[]{:S(2)}, u32[]{:S(2)}) %collective-permute-start.2) | collective-permute-done | bytes 131104 | tf_op jit(solution)/shard_map/ppermute | solution.py:20
  40.8 0.2 copy.117
  41.1 0.2 fusion.27
  41.3 3.3 %collective-permute-start.3 = (f32[2,64,256]{2,1,0:T(8,128)S(1)}, f32[2,64,256]{2,1,0:T(8,128)S(1)}, u32[]{:S(2)}, u32[]{:S(2)}) collective-permute-start(f32[2,64,256]{2,1,0:T(8,128)S(1)} %bitcast.743), channel_id=1, source_target_pairs={{0,64},{64,0},{8,72},{72,8},{16,80},{80,16},{24,88},{88,24},{32,96... | collective-permute-start | bytes 393224 | tf_op jit(solution)/shard_map/ppermute | solution.py:20
  44.7 3.6 %collective-permute-done.3 = f32[2,64,256]{2,1,0:T(8,128)S(1)} collective-permute-done((f32[2,64,256]{2,1,0:T(8,128)S(1)}, f32[2,64,256]{2,1,0:T(8,128)S(1)}, u32[]{:S(2)}, u32[]{:S(2)}) %collective-permute-start.3) | collective-permute-done | bytes 131104 | tf_op jit(solution)/shard_map/ppermute | solution.py:20
  48.4 0.2 copy.120
  48.7 0.2 fusion.26
  48.9 5.4 %collective-permute-start.4 = (f32[2,64,256]{2,1,0:T(8,128)S(1)}, f32[2,64,256]{2,1,0:T(8,128)S(1)}, u32[]{:S(2)}, u32[]{:S(2)}) collective-permute-start(f32[2,64,256]{2,1,0:T(8,128)S(1)} %bitcast.744), channel_id=1, source_target_pairs={{0,128},{128,0},{8,136},{136,8},{16,144},{144,16},{24,152},{152,24... | collective-permute-start | bytes 393224 | tf_op jit(solution)/shard_map/ppermute | solution.py:20
  54.3 4.8 %collective-permute-done.4 = f32[2,64,256]{2,1,0:T(8,128)S(1)} collective-permute-done((f32[2,64,256]{2,1,0:T(8,128)S(1)}, f32[2,64,256]{2,1,0:T(8,128)S(1)}, u32[]{:S(2)}, u32[]{:S(2)}) %collective-permute-start.4) | collective-permute-done | bytes 131104 | tf_op jit(solution)/shard_map/ppermute | solution.py:20
  59.3 1.1 broadcast_in_dim.143
  60.4 11.4 %all-to-all-start.1 = ((bf16[64,32,256]{2,1,0:T(8,128)(2,1)}), bf16[64,32,256]{2,1,0:T(8,128)(2,1)S(1)}, u32[]{:S(2)}, u32[]{:S(2)}) async-start(bf16[64,32,256]{2,1,0:T(8,128)(2,1)} %broadcast_in_dim.143), calls=%async_computation.1 | async-start | bytes 2097152 | tf_op jit(solution)/shard_map/all_to_all | solution.py:31
  72.0 7.5 %collective-permute-start.5 = (bf16[2,64,256]{2,1,0:T(8,128)(2,1)S(1)}, bf16[2,64,256]{2,1,0:T(8,128)(2,1)S(1)}, u32[]{:S(2)}, u32[]{:S(2)}) collective-permute-start(bf16[2,64,256]{2,1,0:T(8,128)(2,1)S(1)} %bitcast.809), channel_id=1, source_target_pairs={{0,256},{256,0},{8,264},{264,8},{16,272},{272,16},{24,280},{280,24... | collective-permute-start | bytes 196616 | tf_op jit(solution)/shard_map/ppermute | solution.py:20
  79.5 22.9 %collective-permute-done.5 = bf16[2,64,256]{2,1,0:T(8,128)(2,1)S(1)} collective-permute-done((bf16[2,64,256]{2,1,0:T(8,128)(2,1)S(1)}, bf16[2,64,256]{2,1,0:T(8,128)(2,1)S(1)}, u32[]{:S(2)}, u32[]{:S(2)}) %collective-permute-start.5) | collective-permute-done | bytes 65568 | tf_op jit(solution)/shard_map/ppermute | solution.py:20
  102.5 0.2 fusion.78
  102.8 0.2 fusion.79
  103.2 0.2 convolution_convert_fusion.4
  103.4 0.2 convolution_convert_fusion.5
  103.7 0.3 copy-done.9
  104.0 0.2 copy-done.11
  104.3 1.4 fusion
  105.7 1.5 copy.191
  107.2 0.4 convolution_convert_fusion.1
  107.5 0.2 fusion.40
  107.8 0.2 fusion.41
  108.0 0.2 fusion.14
  108.2 0.2 fusion.17
  108.6 0.2 fusion.49
  108.8 0.4 copy-done.1
  109.3 0.6 copy-done.3
  109.9 0.2 fusion.46
  112.1 1.0 select_select_fusion.1
  113.1 6.4 %all-to-all-start.2 = ((bf16[8,2,64,256]{3,2,1,0:T(8,128)(2,1)}), bf16[8,2,64,256]{3,2,1,0:T(8,128)(2,1)S(1)}, u32[]{:S(2)}, u32[]{:S(2)}) async-start(bf16[8,2,64,256]{3,2,1,0:T(8,128)(2,1)} %select_select_fusion.1), calls=%async_computation.2 | async-start | bytes 1048576 | tf_op jit(solution)/shard_map/all_to_all | solution.py:168
  122.0 0.2 select_select_fusion
  122.2 1.3 pad_maximum_fusion
  123.5 12.2 %all-to-all-done.2 = bf16[8,2,64,256]{3,2,1,0:T(8,128)(2,1)S(1)} async-done(((bf16[8,2,64,256]{3,2,1,0:T(8,128)(2,1)}), bf16[8,2,64,256]{3,2,1,0:T(8,128)(2,1)S(1)}, u32[]{:S(2)}, u32[]{:S(2)}) %all-to-all-start.2) | async-done | bytes 524320 | tf_op jit(solution)/shard_map/all_to_all | solution.py:168
  135.7 4.9 %all-to-all-start.3 = ((bf16[64,48,256]{2,1,0:T(8,128)(2,1)}), bf16[64,48,256]{2,1,0:T(8,128)(2,1)S(1)}, u32[]{:S(2)}, u32[]{:S(2)}) async-start(bf16[64,48,256]{2,1,0:T(8,128)(2,1)} %pad_maximum_fusion), calls=%async_computation.3 | async-start | bytes 3145728 | tf_op jit(solution)/shard_map/all_to_all | solution.py:188
  140.6 0.6 broadcast_compare_fusion.4
  141.2 0.7 copy.195
  141.9 1.1 convolution_convert_fusion.2
  143.1 1.1 convolution_convert_fusion.3
  144.2 0.7 copy.196
  145.4 0.9 copy.136
  146.2 1.1 convert_element_type.464
  147.3 1.2 fusion.3
  148.8 1.0 fusion.13
  150.0 31.7 %all-to-all-done.3 = bf16[64,48,256]{2,1,0:T(8,128)(2,1)S(1)} async-done(((bf16[64,48,256]{2,1,0:T(8,128)(2,1)}), bf16[64,48,256]{2,1,0:T(8,128)(2,1)S(1)}, u32[]{:S(2)}, u32[]{:S(2)}) %all-to-all-start.3) | async-done | bytes 1572896 | tf_op jit(solution)/shard_map/all_to_all | solution.py:188
  181.7 0.4 convert_element_type.474
  182.1 0.8 slice_reduce_fusion
  184.1 0.7 copy.198
  184.8 0.7 copy.197
  (366 shorter events, 6.0 us)
Async XLA Ops:
  0.6 15.8 %copy-start.6 = (bf16[128,256]{1,0:T(8,128)(2,1)S(1)}, bf16[128,256]{1,0:T(8,128)(2,1)}, u32[]{:S(2)}) copy-start(bf16[128,256]{1,0:T(8,128)(2,1)} %param.6) | copy-start | bytes 196612
  0.6 15.8 %copy-start.7 = (bf16[128,256]{1,0:T(8,128)(2,1)S(1)}, bf16[128,256]{1,0:T(8,128)(2,1)}, u32[]{:S(2)}) copy-start(bf16[128,256]{1,0:T(8,128)(2,1)} %param.7) | copy-start | bytes 196612
  2.8 13.7 %collective-permute-start = (f32[2,64,256]{2,1,0:T(8,128)S(1)}, f32[2,64,256]{2,1,0:T(8,128)S(1)}, u32[]{:S(2)}, u32[]{:S(2)}) collective-permute-start(f32[2,64,256]{2,1,0:T(8,128)S(1)} %bitcast.740), channel_id=1, source_target_pairs={{0,8},{8,0},{16,24},{24,16},{32,40},{40,32},{48,56},{56,48},{64,72... | collective-permute-start | bytes 393224 | tf_op jit(solution)/shard_map/ppermute | solution.py:20
  8.1 51.2 %all-to-all-start = ((bf16[8,128,256]{1,2,0:T(8,128)(2,1)}), bf16[8,128,256]{1,2,0:T(8,128)(2,1)S(1)}, u32[]{:S(2)}, u32[]{:S(2)}) async-start(bf16[8,128,256]{1,2,0:T(8,128)(2,1)} %broadcast_in_dim.142), calls=%async_computation | async-start | bytes 1048576 | tf_op jit(solution)/shard_map/all_to_all | solution.py:31
  17.1 11.2 %collective-permute-start.1 = (f32[2,64,256]{2,1,0:T(8,128)S(1)}, f32[2,64,256]{2,1,0:T(8,128)S(1)}, u32[]{:S(2)}, u32[]{:S(2)}) collective-permute-start(f32[2,64,256]{2,1,0:T(8,128)S(1)} %bitcast.741), channel_id=1, source_target_pairs={{0,16},{16,0},{8,24},{24,8},{32,48},{48,32},{40,56},{56,40},{64,80... | collective-permute-start | bytes 393224 | tf_op jit(solution)/shard_map/ppermute | solution.py:20
  28.8 12.0 %collective-permute-start.2 = (f32[2,64,256]{2,1,0:T(8,128)S(1)}, f32[2,64,256]{2,1,0:T(8,128)S(1)}, u32[]{:S(2)}, u32[]{:S(2)}) collective-permute-start(f32[2,64,256]{2,1,0:T(8,128)S(1)} %bitcast.742), channel_id=1, source_target_pairs={{0,32},{32,0},{8,40},{40,8},{16,48},{48,16},{24,56},{56,24},{64,96... | collective-permute-start | bytes 393224 | tf_op jit(solution)/shard_map/ppermute | solution.py:20
  41.3 7.0 %collective-permute-start.3 = (f32[2,64,256]{2,1,0:T(8,128)S(1)}, f32[2,64,256]{2,1,0:T(8,128)S(1)}, u32[]{:S(2)}, u32[]{:S(2)}) collective-permute-start(f32[2,64,256]{2,1,0:T(8,128)S(1)} %bitcast.743), channel_id=1, source_target_pairs={{0,64},{64,0},{8,72},{72,8},{16,80},{80,16},{24,88},{88,24},{32,96... | collective-permute-start | bytes 393224 | tf_op jit(solution)/shard_map/ppermute | solution.py:20
  48.4 10.9 %copy-start.13 = (bf16[32,256]{1,0:T(8,128)(2,1)S(1)}, bf16[32,256]{1,0:T(8,128)(2,1)}, u32[]{:S(2)}) copy-start(bf16[32,256]{1,0:T(8,128)(2,1)} %param.9) | copy-start | bytes 49156
  48.9 10.1 %collective-permute-start.4 = (f32[2,64,256]{2,1,0:T(8,128)S(1)}, f32[2,64,256]{2,1,0:T(8,128)S(1)}, u32[]{:S(2)}, u32[]{:S(2)}) collective-permute-start(f32[2,64,256]{2,1,0:T(8,128)S(1)} %bitcast.744), channel_id=1, source_target_pairs={{0,128},{128,0},{8,136},{136,8},{16,144},{144,16},{24,152},{152,24... | collective-permute-start | bytes 393224 | tf_op jit(solution)/shard_map/ppermute | solution.py:20
  59.3 43.2 %copy-start.8 = (bf16[128,256]{1,0:T(8,128)(2,1)S(1)}, bf16[128,256]{1,0:T(8,128)(2,1)}, u32[]{:S(2)}) copy-start(bf16[128,256]{1,0:T(8,128)(2,1)} %param.5) | copy-start | bytes 196612
  60.4 46.7 %all-to-all-start.1 = ((bf16[64,32,256]{2,1,0:T(8,128)(2,1)}), bf16[64,32,256]{2,1,0:T(8,128)(2,1)S(1)}, u32[]{:S(2)}, u32[]{:S(2)}) async-start(bf16[64,32,256]{2,1,0:T(8,128)(2,1)} %broadcast_in_dim.143), calls=%async_computation.1 | async-start | bytes 2097152 | tf_op jit(solution)/shard_map/all_to_all | solution.py:31
  72.0 30.4 %collective-permute-start.5 = (bf16[2,64,256]{2,1,0:T(8,128)(2,1)S(1)}, bf16[2,64,256]{2,1,0:T(8,128)(2,1)S(1)}, u32[]{:S(2)}, u32[]{:S(2)}) collective-permute-start(bf16[2,64,256]{2,1,0:T(8,128)(2,1)S(1)} %bitcast.809), channel_id=1, source_target_pairs={{0,256},{256,0},{8,264},{264,8},{16,272},{272,16},{24,280},{280,24... | collective-permute-start | bytes 196616 | tf_op jit(solution)/shard_map/ppermute | solution.py:20
  102.5 1.2 copy-start.5
  103.4 0.6 copy-start.9
  103.6 0.6 copy-start.11
  108.6 0.7 copy-start.1
  109.3 0.6 copy-start.3
  113.1 22.6 %all-to-all-start.2 = ((bf16[8,2,64,256]{3,2,1,0:T(8,128)(2,1)}), bf16[8,2,64,256]{3,2,1,0:T(8,128)(2,1)S(1)}, u32[]{:S(2)}, u32[]{:S(2)}) async-start(bf16[8,2,64,256]{3,2,1,0:T(8,128)(2,1)} %select_select_fusion.1), calls=%async_computation.2 | async-start | bytes 1048576 | tf_op jit(solution)/shard_map/all_to_all | solution.py:168
  123.5 17.7 %copy-start.10 = (bf16[128,128]{0,1:T(8,128)(2,1)S(1)}, bf16[128,128]{0,1:T(8,128)(2,1)}, u32[]{:S(2)}) copy-start(bf16[128,128]{0,1:T(8,128)(2,1)} %copy-done.9) | copy-start | bytes 98308
  123.5 17.7 %copy-start.12 = (bf16[128,128]{0,1:T(8,128)(2,1)S(1)}, bf16[128,128]{0,1:T(8,128)(2,1)}, u32[]{:S(2)}) copy-start(bf16[128,128]{0,1:T(8,128)(2,1)} %copy-done.11) | copy-start | bytes 98308
  123.5 18.4 %copy-start.4 = (bf16[128,512]{0,1:T(8,128)(2,1)S(1)}, bf16[128,512]{0,1:T(8,128)(2,1)}, u32[]{:S(2)}) copy-start(bf16[128,512]{0,1:T(8,128)(2,1)} %copy-done.3) | copy-start | bytes 393220
  123.5 19.6 %copy-start.2 = (bf16[128,512]{0,1:T(8,128)(2,1)S(1)}, bf16[128,512]{0,1:T(8,128)(2,1)}, u32[]{:S(2)}) copy-start(bf16[128,512]{0,1:T(8,128)(2,1)} %copy-done.1) | copy-start | bytes 393220
  135.7 46.0 %all-to-all-start.3 = ((bf16[64,48,256]{2,1,0:T(8,128)(2,1)}), bf16[64,48,256]{2,1,0:T(8,128)(2,1)S(1)}, u32[]{:S(2)}, u32[]{:S(2)}) async-start(bf16[64,48,256]{2,1,0:T(8,128)(2,1)} %pad_maximum_fusion), calls=%async_computation.3 | async-start | bytes 3145728 | tf_op jit(solution)/shard_map/all_to_all | solution.py:188
  145.3 3.5 %copy-start.15 = (pred[8]{0:T(512)(128)(4,1)S(1)}, pred[8]{0:T(512)(128)(4,1)}, u32[]{:S(2)}) copy-start(pred[8]{0:T(512)(128)(4,1)} %broadcast_compare_fusion.4) | copy-start | bytes 28
  182.1 1.1 copy-start.14
  183.0 1.0 copy-start

commit v8 on v5

--- a/solution.py
+++ b/solution.py
@@ -46,6 +46,10 @@
     return (paired[:, :, 0] + paired[:, :, 1]) * 0.5
 
 
+def pair_mean_rows(table, factor):
+    return table.reshape(table.shape[0], table.shape[1] // factor, factor, table.shape[2]).mean(axis=2)
+
+
 def spread_rows(table):
     doubled = jnp.broadcast_to(
         table[:, :, None], (table.shape[0], table.shape[1], 2, table.shape[2])
@@ -64,7 +68,28 @@
     own_table = pair_mean(jnp.stack([keys, values]).astype(jnp.float32))
     far_keys = []
     far_values = []
+    top = depth - 1
+    top_rows = pair_mean_rows(jnp.stack([keys, values]).astype(jnp.float32), 2 << top).astype(jnp.bfloat16)
+    n_seq = lax.axis_size(SEQ)
+    w_rows = out_weight.shape[0]
+    top_count = top_rows.shape[1]
+    send = jnp.concatenate(
+        [
+            jnp.broadcast_to(out_weight[None], (n_seq, w_rows, width)),
+            jnp.broadcast_to(top_rows.reshape(1, 2 * top_count, width), (n_seq, 2 * top_count, width)),
+        ],
+        axis=1,
+    )
+    arrived = lax.all_to_all(send, SEQ, 0, 0, tiled=True)
+    full_weight = arrived[:, :w_rows].reshape(n_seq * w_rows, width)
+    first = ((position >> top) ^ 1) << top
+    top_far = lax.dynamic_slice_in_dim(arrived[:, w_rows:], first, 1 << top, axis=0)
+    top_far = top_far.reshape(1 << top, 2, top_count, width)
     for layer_bit in range(depth):
+        if layer_bit == top:
+            far_keys.append(top_far[:, 0].reshape(-1, width))
+            far_values.append(top_far[:, 1].reshape(-1, width))
+            continue
         far_table = from_partner(own_table, SEQ, layer_bit)
         far_keys.append(far_table[0].astype(jnp.bfloat16))
         far_values.append(far_table[1].astype(jnp.bfloat16))
@@ -81,7 +106,6 @@
     key_set = jnp.concatenate([keys] + far_keys, axis=0)
     value_set = jnp.concatenate([values] + far_values, axis=0)
     full_cot = gathered_copies(cotangent, "dp", 1)
-    full_weight = gathered_copies(out_weight, SEQ, 0)
     grad_attended = jnp.dot(full_cot, full_weight, preferred_element_type=jnp.float32).astype(
         jnp.bfloat16
     )

time: 172 us -> 180 us (1.047)
  starting transfers between devices: 72.1 us -> 80.5 us
  waiting for transfers between devices: 80.2 us -> 78.3 us
    all_to_all x0 -> x1, starting transfers between devices: none -> 15.8 us  [on_device(): arrived = lax.all_to_all(send, SEQ, 0, 0, tiled=True)]
    all_to_all x2 -> x1, starting transfers between devices: 18.9 us -> 4.78 us  [from_everyone(): return lax.all_to_all(copies, axis, split_axis=0, concat_axis=0, tiled=True)]
    ppermute x12 -> x11, waiting for transfers between devices: 80.2 us -> 71.1 us  [from_partner(): return lax.ppermute(block, axis, route)]
    all_to_all x2 -> x1, waiting for transfers between devices: 0.01 us -> 7.16 us  [from_everyone(): return lax.all_to_all(copies, axis, split_axis=0, concat_axis=0, tiled=True)]
    all_to_all x1, starting transfers between devices: 8.36 us -> 11.7 us  [own_rows(): lax.all_to_all(parts, axes, 0, 0, tiled=True).astype(jnp.float32)]
    ppermute x12 -> x11, starting transfers between devices: 44.9 us -> 48.2 us  [from_partner(): return lax.ppermute(block, axis, route)]
  transfers between devices with their start and end apart: 15 -> 14, of which waited for: 9 -> 10; matrix products, arithmetic and copies ran while one was open for 6% -> 6% of each run, Pallas kernels for 0% -> 0%
where the time goes in v8:
time: 180 us; the launch traced here: 178 us
  starting transfers between devices  80.5 us (45%)
  waiting for transfers between devices  78.3 us (44%)
  local copies, waits for them, and re-layouts  8.87 us (5%)
  matrix products  4.69 us (3%)
  other arithmetic  3.93 us (2%)
    ppermute x11, waiting for transfers between devices, from_partner(): return lax.ppermute(block, axis, route)  71.1 us
    ppermute x11, starting transfers between devices, from_partner(): return lax.ppermute(block, axis, route)  48.2 us
    all_to_all x1, starting transfers between devices, on_device(): arrived = lax.all_to_all(send, SEQ, 0, 0, tiled=True)  15.8 us
    all_to_all x1, starting transfers between devices, own_rows(): lax.all_to_all(parts, axes, 0, 0, tiled=True).astype(jnp.float32)  11.7 us
    all_to_all x1, waiting for transfers between devices, from_everyone(): return lax.all_to_all(copies, axis, split_axis=0, concat_axis=0, tiled=True)  7.16 us
    all_to_all x1, starting transfers between devices, from_everyone(): return lax.all_to_all(copies, axis, split_axis=0, concat_axis=0, tiled=True)  4.78 us
  transfers between devices with their start and end apart: 14, of which 10 were waited for; matrix products, arithmetic and copies ran while one was open for 6% of the time, Pallas kernels for 0%

profile of v8, /device:TPU:6, one launch (start us, length us, event | category | flops | bytes accessed | tf_op | source)
XLA Modules:
  0.0 177.9 jit_solution(16683005198477446456)
XLA Ops:
  0.7 0.9 stack.28
  1.6 0.9 stack.27
  2.5 3.5 %collective-permute-start = (f32[2,64,256]{2,1,0:T(8,128)S(1)}, f32[2,64,256]{2,1,0:T(8,128)S(1)}, u32[]{:S(2)}, u32[]{:S(2)}) collective-permute-start(f32[2,64,256]{2,1,0:T(8,128)S(1)} %fusion.32), channel_id=1, source_target_pairs={{0,8},{8,0},{16,24},{24,16},{32,40},{40,32},{48,56},{56,48},{64,72... | collective-permute-start | bytes 393224 | tf_op jit(solution)/shard_map/ppermute | solution.py:20
  6.2 0.1 broadcast_in_dim.18
  6.3 1.2 pad_maximum_fusion
  7.5 15.8 %all-to-all-start = ((bf16[64,36,256]{2,1,0:T(8,128)(2,1)}), bf16[64,36,256]{2,1,0:T(8,128)(2,1)S(1)}, u32[]{:S(2)}, u32[]{:S(2)}) async-start(bf16[64,36,256]{2,1,0:T(8,128)(2,1)} %pad_maximum_fusion), calls=%async_computation | async-start | bytes 2621440 | tf_op jit(solution)/shard_map/all_to_all | solution.py:83
  23.4 0.1 copy.208
  23.6 0.2 copy.193
  23.9 4.4 %collective-permute-start.1 = (f32[2,64,256]{2,1,0:T(8,128)S(1)}, f32[2,64,256]{2,1,0:T(8,128)S(1)}, u32[]{:S(2)}, u32[]{:S(2)}) collective-permute-start(f32[2,64,256]{2,1,0:T(8,128)S(1)} %fusion.40), channel_id=1, source_target_pairs={{0,16},{16,0},{8,24},{24,8},{32,48},{48,32},{40,56},{56,40},{64,80... | collective-permute-start | bytes 393224 | tf_op jit(solution)/shard_map/ppermute | solution.py:20
  28.3 30.9 %collective-permute-done.1 = f32[2,64,256]{2,1,0:T(8,128)S(1)} collective-permute-done((f32[2,64,256]{2,1,0:T(8,128)S(1)}, f32[2,64,256]{2,1,0:T(8,128)S(1)}, u32[]{:S(2)}, u32[]{:S(2)}) %collective-permute-start.1) | collective-permute-done | bytes 131104 | tf_op jit(solution)/shard_map/ppermute | solution.py:20
  59.3 0.2 copy.196
  59.6 5.5 %collective-permute-start.2 = (f32[2,64,256]{2,1,0:T(8,128)S(1)}, f32[2,64,256]{2,1,0:T(8,128)S(1)}, u32[]{:S(2)}, u32[]{:S(2)}) collective-permute-start(f32[2,64,256]{2,1,0:T(8,128)S(1)} %fusion.38), channel_id=1, source_target_pairs={{0,32},{32,0},{8,40},{40,8},{16,48},{48,16},{24,56},{56,24},{64,96... | collective-permute-start | bytes 393224 | tf_op jit(solution)/shard_map/ppermute | solution.py:20
  65.1 7.3 %collective-permute-done.2 = f32[2,64,256]{2,1,0:T(8,128)S(1)} collective-permute-done((f32[2,64,256]{2,1,0:T(8,128)S(1)}, f32[2,64,256]{2,1,0:T(8,128)S(1)}, u32[]{:S(2)}, u32[]{:S(2)}) %collective-permute-start.2) | collective-permute-done | bytes 131104 | tf_op jit(solution)/shard_map/ppermute | solution.py:20
  72.5 0.2 copy.199
  72.8 3.4 %collective-permute-start.3 = (f32[2,64,256]{2,1,0:T(8,128)S(1)}, f32[2,64,256]{2,1,0:T(8,128)S(1)}, u32[]{:S(2)}, u32[]{:S(2)}) collective-permute-start(f32[2,64,256]{2,1,0:T(8,128)S(1)} %fusion.36), channel_id=1, source_target_pairs={{0,64},{64,0},{8,72},{72,8},{16,80},{80,16},{24,88},{88,24},{32,96... | collective-permute-start | bytes 393224 | tf_op jit(solution)/shard_map/ppermute | solution.py:20
  76.2 3.5 %collective-permute-done.3 = f32[2,64,256]{2,1,0:T(8,128)S(1)} collective-permute-done((f32[2,64,256]{2,1,0:T(8,128)S(1)}, f32[2,64,256]{2,1,0:T(8,128)S(1)}, u32[]{:S(2)}, u32[]{:S(2)}) %collective-permute-start.3) | collective-permute-done | bytes 131104 | tf_op jit(solution)/shard_map/ppermute | solution.py:20
  79.7 0.2 copy.202
  80.0 4.3 %collective-permute-start.4 = (bf16[2,64,256]{2,1,0:T(8,128)(2,1)S(1)}, bf16[2,64,256]{2,1,0:T(8,128)(2,1)S(1)}, u32[]{:S(2)}, u32[]{:S(2)}) collective-permute-start(bf16[2,64,256]{2,1,0:T(8,128)(2,1)S(1)} %fusion.34), channel_id=1, source_target_pairs={{0,128},{128,0},{8,136},{136,8},{16,144},{144,16},{24,152},{152,24... | collective-permute-start | bytes 196616 | tf_op jit(solution)/shard_map/ppermute | solution.py:20
  84.3 2.8 %collective-permute-done.4 = bf16[2,64,256]{2,1,0:T(8,128)(2,1)S(1)} collective-permute-done((bf16[2,64,256]{2,1,0:T(8,128)(2,1)S(1)}, bf16[2,64,256]{2,1,0:T(8,128)(2,1)S(1)}, u32[]{:S(2)}, u32[]{:S(2)}) %collective-permute-start.4) | collective-permute-done | bytes 65568 | tf_op jit(solution)/shard_map/ppermute | solution.py:20
  87.1 0.9 broadcast_in_dim.20
  87.9 4.8 %all-to-all-start.1 = ((bf16[8,128,256]{1,2,0:T(8,128)(2,1)}), bf16[8,128,256]{1,2,0:T(8,128)(2,1)S(1)}, u32[]{:S(2)}, u32[]{:S(2)}) async-start(bf16[8,128,256]{1,2,0:T(8,128)(2,1)} %broadcast_in_dim.20), calls=%async_computation.1 | async-start | bytes 1048576 | tf_op jit(solution)/shard_map/all_to_all | solution.py:31
  93.0 0.2 fusion.87
  93.3 0.1 fusion.14
  93.4 0.2 fusion.88
  93.6 0.2 convolution_convert_fusion.4
  93.8 7.2 %all-to-all-done.1 = bf16[8,128,256]{1,2,0:T(8,128)(2,1)S(1)} async-done(((bf16[8,128,256]{1,2,0:T(8,128)(2,1)}), bf16[8,128,256]{1,2,0:T(8,128)(2,1)S(1)}, u32[]{:S(2)}, u32[]{:S(2)}) %all-to-all-start.1) | async-done | bytes 524320 | tf_op jit(solution)/shard_map/all_to_all | solution.py:31
  101.0 0.5 fusion.1
  101.5 0.2 fusion.5
  101.7 0.2 fusion.52
  101.9 0.1 fusion.12
  102.0 0.2 fusion.8
  102.2 0.2 fusion.51
  102.4 0.1 fusion.7
  102.5 0.2 fusion.67
  102.7 0.1 fusion.10
  102.7 0.2 fusion.70
  103.0 8.1 %collective-permute-start.5 = (bf16[2,64,256]{2,1,0:T(8,128)(2,1)S(1)}, bf16[2,64,256]{2,1,0:T(8,128)(2,1)S(1)}, u32[]{:S(2)}, u32[]{:S(2)}) collective-permute-start(bf16[2,64,256]{2,1,0:T(8,128)(2,1)S(1)} %fusion.19), channel_id=1, source_target_pairs={{0,256},{256,0},{8,264},{264,8},{16,272},{272,16},{24,280},{280,24... | collective-permute-start | bytes 196616 | tf_op jit(solution)/shard_map/ppermute | solution.py:20
  111.1 0.2 convolution_convert_fusion.5
  111.4 2.1 %collective-permute-done.5 = bf16[2,64,256]{2,1,0:T(8,128)(2,1)S(1)} collective-permute-done((bf16[2,64,256]{2,1,0:T(8,128)(2,1)S(1)}, bf16[2,64,256]{2,1,0:T(8,128)(2,1)S(1)}, u32[]{:S(2)}, u32[]{:S(2)}) %collective-permute-start.5) | collective-permute-done | bytes 65568 | tf_op jit(solution)/shard_map/ppermute | solution.py:20
  113.5 0.1 copy.217
  113.8 4.8 %collective-permute-start.6 = (bf16[2,64,256]{2,1,0:T(8,128)(2,1)S(1)}, bf16[2,64,256]{2,1,0:T(8,128)(2,1)S(1)}, u32[]{:S(2)}, u32[]{:S(2)}) collective-permute-start(bf16[2,64,256]{2,1,0:T(8,128)(2,1)S(1)} %fusion.22), channel_id=1, source_target_pairs={{0,128},{128,0},{8,136},{136,8},{16,144},{144,16},{24,152},{152,24... | collective-permute-start | bytes 196616 | tf_op jit(solution)/shard_map/ppermute | solution.py:20
  118.6 0.4 fusion
  119.0 1.8 %collective-permute-done.6 = bf16[2,64,256]{2,1,0:T(8,128)(2,1)S(1)} collective-permute-done((bf16[2,64,256]{2,1,0:T(8,128)(2,1)S(1)}, bf16[2,64,256]{2,1,0:T(8,128)(2,1)S(1)}, u32[]{:S(2)}, u32[]{:S(2)}) %collective-permute-start.6) | collective-permute-done | bytes 65568 | tf_op jit(solution)/shard_map/ppermute | solution.py:20
  120.9 0.1 copy.220
  121.1 3.5 %collective-permute-start.7 = (bf16[2,64,256]{2,1,0:T(8,128)(2,1)S(1)}, bf16[2,64,256]{2,1,0:T(8,128)(2,1)S(1)}, u32[]{:S(2)}, u32[]{:S(2)}) collective-permute-start(bf16[2,64,256]{2,1,0:T(8,128)(2,1)S(1)} %fusion.25), channel_id=1, source_target_pairs={{0,64},{64,0},{8,72},{72,8},{16,80},{80,16},{24,88},{88,24},{32,96... | collective-permute-start | bytes 196616 | tf_op jit(solution)/shard_map/ppermute | solution.py:20
  124.6 0.8 convolution_convert_fusion.2
  125.5 1.8 %collective-permute-done.7 = bf16[2,64,256]{2,1,0:T(8,128)(2,1)S(1)} collective-permute-done((bf16[2,64,256]{2,1,0:T(8,128)(2,1)S(1)}, bf16[2,64,256]{2,1,0:T(8,128)(2,1)S(1)}, u32[]{:S(2)}, u32[]{:S(2)}) %collective-permute-start.7) | collective-permute-done | bytes 65568 | tf_op jit(solution)/shard_map/ppermute | solution.py:20
  127.3 0.1 copy.223
  127.6 4.5 %collective-permute-start.8 = (bf16[2,64,256]{2,1,0:T(8,128)(2,1)S(1)}, bf16[2,64,256]{2,1,0:T(8,128)(2,1)}, u32[]{:S(2)}, u32[]{:S(2)}) collective-permute-start(bf16[2,64,256]{2,1,0:T(8,128)(2,1)S(1)} %fusion.28), channel_id=1, source_target_pairs={{0,32},{32,0},{8,40},{40,8},{16,48},{48,16},{24,56},{56,24},{64,96... | collective-permute-start | bytes 196616 | tf_op jit(solution)/shard_map/ppermute | solution.py:20
  132.1 0.8 convolution_convert_fusion.3
  132.9 1.3 copy.234
  134.3 11.7 %all-to-all-start.2 = ((bf16[64,32,256]{2,1,0:T(8,128)(2,1)}), bf16[64,32,256]{2,1,0:T(8,128)(2,1)S(1)}, u32[]{:S(2)}, u32[]{:S(2)}) async-start(bf16[64,32,256]{2,1,0:T(8,128)(2,1)} %bitcast.40), calls=%async_computation.2 | async-start | bytes 2097152 | tf_op jit(solution)/shard_map/all_to_all | solution.py:41
  145.9 0.9 add_multiply_fusion.2
  146.8 0.1 copy.226
  147.1 4.4 %collective-permute-start.9 = (bf16[2,64,256]{2,1,0:T(8,128)(2,1)S(1)}, bf16[2,64,256]{2,1,0:T(8,128)(2,1)S(1)}, u32[]{:S(2)}, u32[]{:S(2)}) collective-permute-start(bf16[2,64,256]{2,1,0:T(8,128)(2,1)S(1)} %fusion.17), channel_id=1, source_target_pairs={{0,16},{16,0},{8,24},{24,8},{32,48},{48,32},{40,56},{56,40},{64,80... | collective-permute-start | bytes 196616 | tf_op jit(solution)/shard_map/ppermute | solution.py:20
  151.5 0.7 copy.235
  152.2 17.5 %collective-permute-done.9 = bf16[2,64,256]{2,1,0:T(8,128)(2,1)S(1)} collective-permute-done((bf16[2,64,256]{2,1,0:T(8,128)(2,1)S(1)}, bf16[2,64,256]{2,1,0:T(8,128)(2,1)S(1)}, u32[]{:S(2)}, u32[]{:S(2)}) %collective-permute-start.9) | collective-permute-done | bytes 65568 | tf_op jit(solution)/shard_map/ppermute | solution.py:20
  169.7 0.1 copy.229
  170.0 1.9 %collective-permute-start.10 = (bf16[2,64,256]{2,1,0:T(8,128)(2,1)S(1)}, bf16[2,64,256]{2,1,0:T(8,128)(2,1)S(1)}, u32[]{:S(2)}, u32[]{:S(2)}) collective-permute-start(bf16[2,64,256]{2,1,0:T(8,128)(2,1)S(1)} %fusion.30), channel_id=1, source_target_pairs={{0,8},{8,0},{16,24},{24,16},{32,40},{40,32},{48,56},{56,48},{64,72... | collective-permute-start | bytes 196616 | tf_op jit(solution)/shard_map/ppermute | solution.py:20
  171.9 0.7 copy.236
  172.7 3.5 %collective-permute-done.10 = bf16[2,64,256]{2,1,0:T(8,128)(2,1)S(1)} collective-permute-done((bf16[2,64,256]{2,1,0:T(8,128)(2,1)S(1)}, bf16[2,64,256]{2,1,0:T(8,128)(2,1)S(1)}, u32[]{:S(2)}, u32[]{:S(2)}) %collective-permute-start.10) | collective-permute-done | bytes 65568 | tf_op jit(solution)/shard_map/ppermute | solution.py:20
  176.2 0.1 copy.232
  176.4 0.7 slice_bitcast_fusion
  177.1 0.8 convert_reduce_fusion
  (93 shorter events, 1.8 us)
Async XLA Ops:
  0.6 5.4 %copy-start.2 = (bf16[128,256]{1,0:T(8,128)(2,1)S(1)}, bf16[128,256]{1,0:T(8,128)(2,1)}, u32[]{:S(2)}) copy-start(bf16[128,256]{1,0:T(8,128)(2,1)} %param.7) | copy-start | bytes 196612
  0.6 5.4 %copy-start.1 = (bf16[128,256]{1,0:T(8,128)(2,1)S(1)}, bf16[128,256]{1,0:T(8,128)(2,1)}, u32[]{:S(2)}) copy-start(bf16[128,256]{1,0:T(8,128)(2,1)} %param.6) | copy-start | bytes 196612
  0.7 5.5 %copy-start.7 = (bf16[32,256]{1,0:T(8,128)(2,1)S(1)}, bf16[32,256]{1,0:T(8,128)(2,1)}, u32[]{:S(2)}) copy-start(bf16[32,256]{1,0:T(8,128)(2,1)} %param.9) | copy-start | bytes 49156
  2.5 21.0 %collective-permute-start = (f32[2,64,256]{2,1,0:T(8,128)S(1)}, f32[2,64,256]{2,1,0:T(8,128)S(1)}, u32[]{:S(2)}, u32[]{:S(2)}) collective-permute-start(f32[2,64,256]{2,1,0:T(8,128)S(1)} %fusion.32), channel_id=1, source_target_pairs={{0,8},{8,0},{16,24},{24,16},{32,40},{40,32},{48,56},{56,48},{64,72... | collective-permute-start | bytes 393224 | tf_op jit(solution)/shard_map/ppermute | solution.py:20
  7.5 15.9 %copy-start.4 = (bf16[128,256]{1,0:T(8,128)(2,1)S(1)}, bf16[128,256]{1,0:T(8,128)(2,1)}, u32[]{:S(2)}) copy-start(bf16[128,256]{1,0:T(8,128)(2,1)} %param.8) | copy-start | bytes 196612
  7.5 79.5 %all-to-all-start = ((bf16[64,36,256]{2,1,0:T(8,128)(2,1)}), bf16[64,36,256]{2,1,0:T(8,128)(2,1)S(1)}, u32[]{:S(2)}, u32[]{:S(2)}) async-start(bf16[64,36,256]{2,1,0:T(8,128)(2,1)} %pad_maximum_fusion), calls=%async_computation | async-start | bytes 2621440 | tf_op jit(solution)/shard_map/all_to_all | solution.py:83
  23.9 35.3 %collective-permute-start.1 = (f32[2,64,256]{2,1,0:T(8,128)S(1)}, f32[2,64,256]{2,1,0:T(8,128)S(1)}, u32[]{:S(2)}, u32[]{:S(2)}) collective-permute-start(f32[2,64,256]{2,1,0:T(8,128)S(1)} %fusion.40), channel_id=1, source_target_pairs={{0,16},{16,0},{8,24},{24,8},{32,48},{48,32},{40,56},{56,40},{64,80... | collective-permute-start | bytes 393224 | tf_op jit(solution)/shard_map/ppermute | solution.py:20
  59.6 12.8 %collective-permute-start.2 = (f32[2,64,256]{2,1,0:T(8,128)S(1)}, f32[2,64,256]{2,1,0:T(8,128)S(1)}, u32[]{:S(2)}, u32[]{:S(2)}) collective-permute-start(f32[2,64,256]{2,1,0:T(8,128)S(1)} %fusion.38), channel_id=1, source_target_pairs={{0,32},{32,0},{8,40},{40,8},{16,48},{48,16},{24,56},{56,24},{64,96... | collective-permute-start | bytes 393224 | tf_op jit(solution)/shard_map/ppermute | solution.py:20
  72.8 6.9 %collective-permute-start.3 = (f32[2,64,256]{2,1,0:T(8,128)S(1)}, f32[2,64,256]{2,1,0:T(8,128)S(1)}, u32[]{:S(2)}, u32[]{:S(2)}) collective-permute-start(f32[2,64,256]{2,1,0:T(8,128)S(1)} %fusion.36), channel_id=1, source_target_pairs={{0,64},{64,0},{8,72},{72,8},{16,80},{80,16},{24,88},{88,24},{32,96... | collective-permute-start | bytes 393224 | tf_op jit(solution)/shard_map/ppermute | solution.py:20
  80.0 7.1 %collective-permute-start.4 = (bf16[2,64,256]{2,1,0:T(8,128)(2,1)S(1)}, bf16[2,64,256]{2,1,0:T(8,128)(2,1)S(1)}, u32[]{:S(2)}, u32[]{:S(2)}) collective-permute-start(bf16[2,64,256]{2,1,0:T(8,128)(2,1)S(1)} %fusion.34), channel_id=1, source_target_pairs={{0,128},{128,0},{8,136},{136,8},{16,144},{144,16},{24,152},{152,24... | collective-permute-start | bytes 196616 | tf_op jit(solution)/shard_map/ppermute | solution.py:20
  87.0 6.0 %copy-start.3 = (bf16[128,256]{1,0:T(8,128)(2,1)S(1)}, bf16[128,256]{1,0:T(8,128)(2,1)}, u32[]{:S(2)}) copy-start(bf16[128,256]{1,0:T(8,128)(2,1)} %param.5) | copy-start | bytes 196612
  87.1 6.3 %copy-start = (bf16[64,36,256]{2,1,0:T(8,128)(2,1)}, bf16[64,36,256]{2,1,0:T(8,128)(2,1)S(1)}, u32[]{:S(2)}) copy-start(bf16[64,36,256]{2,1,0:T(8,128)(2,1)S(1)} %all-to-all-done) | copy-start | bytes 3538948
  87.9 13.1 %all-to-all-start.1 = ((bf16[8,128,256]{1,2,0:T(8,128)(2,1)}), bf16[8,128,256]{1,2,0:T(8,128)(2,1)S(1)}, u32[]{:S(2)}, u32[]{:S(2)}) async-start(bf16[8,128,256]{1,2,0:T(8,128)(2,1)} %broadcast_in_dim.20), calls=%async_computation.1 | async-start | bytes 1048576 | tf_op jit(solution)/shard_map/all_to_all | solution.py:31
  93.0 9.0 %copy-start.8 = (bf16[512,256]{1,0:T(8,128)(2,1)}, bf16[512,256]{1,0:T(8,128)(2,1)S(1)}, u32[]{:S(2)}) copy-start(bf16[512,256]{1,0:T(8,128)(2,1)S(1)} %constant_dynamic-update-slice_fusion.2) | copy-start | bytes 786436
  93.4 7.6 %slice-start = ((bf16[64,36,256]{2,1,0:T(8,128)(2,1)}), bf16[64,32,256]{2,1,0:T(8,128)(2,1)S(1)}, s32[]{:S(2)}) async-start(bf16[64,36,256]{2,1,0:T(8,128)(2,1)} %copy-done), calls=%async_computation.3 | async-start | bytes 2097152 | tf_op jit(solution)/shard_map/slice | solution.py:84
  103.0 8.2 %copy-start.9 = (bf16[512,256]{1,0:T(8,128)(2,1)S(1)}, bf16[512,256]{1,0:T(8,128)(2,1)}, u32[]{:S(2)}) copy-start(bf16[512,256]{1,0:T(8,128)(2,1)} %copy-done.8) | copy-start | bytes 786436
  103.0 10.5 %collective-permute-start.5 = (bf16[2,64,256]{2,1,0:T(8,128)(2,1)S(1)}, bf16[2,64,256]{2,1,0:T(8,128)(2,1)S(1)}, u32[]{:S(2)}, u32[]{:S(2)}) collective-permute-start(bf16[2,64,256]{2,1,0:T(8,128)(2,1)S(1)} %fusion.19), channel_id=1, source_target_pairs={{0,256},{256,0},{8,264},{264,8},{16,272},{272,16},{24,280},{280,24... | collective-permute-start | bytes 196616 | tf_op jit(solution)/shard_map/ppermute | solution.py:20
  113.8 7.1 %collective-permute-start.6 = (bf16[2,64,256]{2,1,0:T(8,128)(2,1)S(1)}, bf16[2,64,256]{2,1,0:T(8,128)(2,1)S(1)}, u32[]{:S(2)}, u32[]{:S(2)}) collective-permute-start(bf16[2,64,256]{2,1,0:T(8,128)(2,1)S(1)} %fusion.22), channel_id=1, source_target_pairs={{0,128},{128,0},{8,136},{136,8},{16,144},{144,16},{24,152},{152,24... | collective-permute-start | bytes 196616 | tf_op jit(solution)/shard_map/ppermute | solution.py:20
  121.1 6.2 %collective-permute-start.7 = (bf16[2,64,256]{2,1,0:T(8,128)(2,1)S(1)}, bf16[2,64,256]{2,1,0:T(8,128)(2,1)S(1)}, u32[]{:S(2)}, u32[]{:S(2)}) collective-permute-start(bf16[2,64,256]{2,1,0:T(8,128)(2,1)S(1)} %fusion.25), channel_id=1, source_target_pairs={{0,64},{64,0},{8,72},{72,8},{16,80},{80,16},{24,88},{88,24},{32,96... | collective-permute-start | bytes 196616 | tf_op jit(solution)/shard_map/ppermute | solution.py:20
  127.6 18.4 %collective-permute-start.8 = (bf16[2,64,256]{2,1,0:T(8,128)(2,1)S(1)}, bf16[2,64,256]{2,1,0:T(8,128)(2,1)}, u32[]{:S(2)}, u32[]{:S(2)}) collective-permute-start(bf16[2,64,256]{2,1,0:T(8,128)(2,1)S(1)} %fusion.28), channel_id=1, source_target_pairs={{0,32},{32,0},{8,40},{40,8},{16,48},{48,16},{24,56},{56,24},{64,96... | collective-permute-start | bytes 196616 | tf_op jit(solution)/shard_map/ppermute | solution.py:20
  134.3 42.8 %all-to-all-start.2 = ((bf16[64,32,256]{2,1,0:T(8,128)(2,1)}), bf16[64,32,256]{2,1,0:T(8,128)(2,1)S(1)}, u32[]{:S(2)}, u32[]{:S(2)}) async-start(bf16[64,32,256]{2,1,0:T(8,128)(2,1)} %bitcast.40), calls=%async_computation.2 | async-start | bytes 2097152 | tf_op jit(solution)/shard_map/all_to_all | solution.py:41
  147.1 22.6 %collective-permute-start.9 = (bf16[2,64,256]{2,1,0:T(8,128)(2,1)S(1)}, bf16[2,64,256]{2,1,0:T(8,128)(2,1)S(1)}, u32[]{:S(2)}, u32[]{:S(2)}) collective-permute-start(bf16[2,64,256]{2,1,0:T(8,128)(2,1)S(1)} %fusion.17), channel_id=1, source_target_pairs={{0,16},{16,0},{8,24},{24,8},{32,48},{48,32},{40,56},{56,40},{64,80... | collective-permute-start | bytes 196616 | tf_op jit(solution)/shard_map/ppermute | solution.py:20
  169.7 2.2 %copy-start.5 = (bf16[128,128]{0,1:T(8,128)(2,1)S(1)}, bf16[128,128]{0,1:T(8,128)(2,1)}, u32[]{:S(2)}) copy-start(bf16[128,128]{0,1:T(8,128)(2,1)} %convolution_convert_fusion.2) | copy-start | bytes 98308
  169.7 2.2 %copy-start.6 = (bf16[128,128]{0,1:T(8,128)(2,1)S(1)}, bf16[128,128]{0,1:T(8,128)(2,1)}, u32[]{:S(2)}) copy-start(bf16[128,128]{0,1:T(8,128)(2,1)} %convolution_convert_fusion.3) | copy-start | bytes 98308
  170.0 6.2 %collective-permute-start.10 = (bf16[2,64,256]{2,1,0:T(8,128)(2,1)S(1)}, bf16[2,64,256]{2,1,0:T(8,128)(2,1)S(1)}, u32[]{:S(2)}, u32[]{:S(2)}) collective-permute-start(bf16[2,64,256]{2,1,0:T(8,128)(2,1)S(1)} %fusion.30), channel_id=1, source_target_pairs={{0,8},{8,0},{16,24},{24,16},{32,40},{40,32},{48,56},{56,48},{64,72... | collective-permute-start | bytes 196616 | tf_op jit(solution)/shard_map/ppermute | solution.py:20

commit v9 on v5

--- a/solution.py
+++ b/solution.py
@@ -61,7 +61,9 @@
     scale = 1.0 / math.sqrt(HEAD)
     depth = lax.axis_size(SEQ).bit_length() - 1
     position = lax.axis_index(SEQ)
-    own_table = pair_mean(jnp.stack([keys, values]).astype(jnp.float32))
+    own_table = jnp.stack(
+        [pair_mean(keys[None].astype(jnp.float32))[0], pair_mean(values[None].astype(jnp.float32))[0]]
+    )
     far_keys = []
     far_values = []
     for layer_bit in range(depth):
@@ -147,7 +149,7 @@
     grad_values = own_grads[1].astype(jnp.bfloat16)
     grad_out_weight = own_rows(
         lax.dot_general(
-            full_cot, attended, (((0,), (0,)), ((), ())), preferred_element_type=jnp.float32
+            full_cot, attended, (((0,), (0,)), ((), ())), preferred_element_type=jnp.bfloat16
         ),
         SEQ,
     )

time: 172 us -> 172 us (level)
    reshape x0 -> x2, local copies, waits for them, and re-layouts: none -> 1.84 us  [pair_mean(): table.reshape(table.shape[0], table.shape[1] // 2, 2, table.shape[2])]
    another operation x4 -> x0, local copies, waits for them, and re-layouts: 1.8 us -> none  [on_device(): own_table = pair_mean(jnp.stack([keys, values]).astype(jnp.float32))]
where the time goes in v9:
time: 172 us; the launch traced here: 171 us
  waiting for transfers between devices  80.2 us (47%)
  starting transfers between devices  72.2 us (42%)
  local copies, waits for them, and re-layouts  10.9 us (6%)
  other arithmetic  3.37 us (2%)
  matrix products  3.35 us (2%)
    ppermute x12, waiting for transfers between devices, from_partner(): return lax.ppermute(block, axis, route)  80.2 us
    ppermute x12, starting transfers between devices, from_partner(): return lax.ppermute(block, axis, route)  44.9 us
    all_to_all x2, starting transfers between devices, from_everyone(): return lax.all_to_all(copies, axis, split_axis=0, concat_axis=0, tiled=True)  18.9 us
    all_to_all x1, starting transfers between devices, own_rows(): lax.all_to_all(parts, axes, 0, 0, tiled=True).astype(jnp.float32)  8.36 us
  transfers between devices with their start and end apart: 15, of which 9 were waited for; matrix products, arithmetic and copies ran while one was open for 6% of the time, Pallas kernels for 0%

profile of v9, /device:TPU:6, one launch (start us, length us, event | category | flops | bytes accessed | tf_op | source)
XLA Modules:
  0.0 171.4 jit_solution(10053707169174047155)
XLA Ops:
  0.6 0.9 reshape.182
  1.6 0.1 fusion.91
  1.7 0.9 reshape.184
  2.6 0.1 fusion.92
  2.8 3.6 %collective-permute-start = (f32[2,64,256]{2,1,0:T(8,128)S(1)}, f32[2,64,256]{2,1,0:T(8,128)S(1)}, u32[]{:S(2)}, u32[]{:S(2)}) collective-permute-start(f32[2,64,256]{2,1,0:T(8,128)S(1)} %pad_maximum_fusion.6), channel_id=1, source_target_pairs={{0,8},{8,0},{16,24},{24,16},{32,40},{40,32},{48,56},{56,48},{64,72... | collective-permute-start | bytes 393224 | tf_op jit(solution)/shard_map/ppermute | solution.py:20
  6.4 0.1 copy.109
  6.5 0.9 broadcast_in_dim.16
  7.4 7.7 %all-to-all-start = ((bf16[8,128,256]{1,2,0:T(8,128)(2,1)}), bf16[8,128,256]{1,2,0:T(8,128)(2,1)S(1)}, u32[]{:S(2)}, u32[]{:S(2)}) async-start(bf16[8,128,256]{1,2,0:T(8,128)(2,1)} %broadcast_in_dim.16), calls=%async_computation | async-start | bytes 1048576 | tf_op jit(solution)/shard_map/all_to_all | solution.py:31
  15.2 0.2 copy.94
  15.5 1.9 %collective-permute-start.1 = (f32[2,64,256]{2,1,0:T(8,128)S(1)}, f32[2,64,256]{2,1,0:T(8,128)S(1)}, u32[]{:S(2)}, u32[]{:S(2)}) collective-permute-start(f32[2,64,256]{2,1,0:T(8,128)S(1)} %fusion.38), channel_id=1, source_target_pairs={{0,16},{16,0},{8,24},{24,8},{32,48},{48,32},{40,56},{56,40},{64,80... | collective-permute-start | bytes 393224 | tf_op jit(solution)/shard_map/ppermute | solution.py:20
  17.5 9.2 %collective-permute-done.1 = f32[2,64,256]{2,1,0:T(8,128)S(1)} collective-permute-done((f32[2,64,256]{2,1,0:T(8,128)S(1)}, f32[2,64,256]{2,1,0:T(8,128)S(1)}, u32[]{:S(2)}, u32[]{:S(2)}) %collective-permute-start.1) | collective-permute-done | bytes 131104 | tf_op jit(solution)/shard_map/ppermute | solution.py:20
  26.7 0.2 copy.97
  27.0 3.9 %collective-permute-start.2 = (f32[2,64,256]{2,1,0:T(8,128)S(1)}, f32[2,64,256]{2,1,0:T(8,128)S(1)}, u32[]{:S(2)}, u32[]{:S(2)}) collective-permute-start(f32[2,64,256]{2,1,0:T(8,128)S(1)} %fusion.36), channel_id=1, source_target_pairs={{0,32},{32,0},{8,40},{40,8},{16,48},{48,16},{24,56},{56,24},{64,96... | collective-permute-start | bytes 393224 | tf_op jit(solution)/shard_map/ppermute | solution.py:20
  30.9 8.0 %collective-permute-done.2 = f32[2,64,256]{2,1,0:T(8,128)S(1)} collective-permute-done((f32[2,64,256]{2,1,0:T(8,128)S(1)}, f32[2,64,256]{2,1,0:T(8,128)S(1)}, u32[]{:S(2)}, u32[]{:S(2)}) %collective-permute-start.2) | collective-permute-done | bytes 131104 | tf_op jit(solution)/shard_map/ppermute | solution.py:20
  39.0 0.2 copy.100
  39.3 3.3 %collective-permute-start.3 = (f32[2,64,256]{2,1,0:T(8,128)S(1)}, f32[2,64,256]{2,1,0:T(8,128)S(1)}, u32[]{:S(2)}, u32[]{:S(2)}) collective-permute-start(f32[2,64,256]{2,1,0:T(8,128)S(1)} %fusion.34), channel_id=1, source_target_pairs={{0,64},{64,0},{8,72},{72,8},{16,80},{80,16},{24,88},{88,24},{32,96... | collective-permute-start | bytes 393224 | tf_op jit(solution)/shard_map/ppermute | solution.py:20
  42.7 3.6 %collective-permute-done.3 = f32[2,64,256]{2,1,0:T(8,128)S(1)} collective-permute-done((f32[2,64,256]{2,1,0:T(8,128)S(1)}, f32[2,64,256]{2,1,0:T(8,128)S(1)}, u32[]{:S(2)}, u32[]{:S(2)}) %collective-permute-start.3) | collective-permute-done | bytes 131104 | tf_op jit(solution)/shard_map/ppermute | solution.py:20
  46.4 0.2 copy.103
  46.7 5.4 %collective-permute-start.4 = (f32[2,64,256]{2,1,0:T(8,128)S(1)}, f32[2,64,256]{2,1,0:T(8,128)S(1)}, u32[]{:S(2)}, u32[]{:S(2)}) collective-permute-start(f32[2,64,256]{2,1,0:T(8,128)S(1)} %fusion.32), channel_id=1, source_target_pairs={{0,128},{128,0},{8,136},{136,8},{16,144},{144,16},{24,152},{152,24... | collective-permute-start | bytes 393224 | tf_op jit(solution)/shard_map/ppermute | solution.py:20
  52.1 1.1 broadcast_in_dim.17
  53.2 11.1 %all-to-all-start.1 = ((bf16[64,32,256]{2,1,0:T(8,128)(2,1)}), bf16[64,32,256]{2,1,0:T(8,128)(2,1)S(1)}, u32[]{:S(2)}, u32[]{:S(2)}) async-start(bf16[64,32,256]{2,1,0:T(8,128)(2,1)} %broadcast_in_dim.17), calls=%async_computation.1 | async-start | bytes 2097152 | tf_op jit(solution)/shard_map/all_to_all | solution.py:31
  64.4 0.2 copy.106
  64.7 7.5 %collective-permute-start.5 = (bf16[2,64,256]{2,1,0:T(8,128)(2,1)S(1)}, bf16[2,64,256]{2,1,0:T(8,128)(2,1)S(1)}, u32[]{:S(2)}, u32[]{:S(2)}) collective-permute-start(bf16[2,64,256]{2,1,0:T(8,128)(2,1)S(1)} %fusion.30), channel_id=1, source_target_pairs={{0,256},{256,0},{8,264},{264,8},{16,272},{272,16},{24,280},{280,24... | collective-permute-start | bytes 196616 | tf_op jit(solution)/shard_map/ppermute | solution.py:20
  72.2 22.3 %collective-permute-done.5 = bf16[2,64,256]{2,1,0:T(8,128)(2,1)S(1)} collective-permute-done((bf16[2,64,256]{2,1,0:T(8,128)(2,1)S(1)}, bf16[2,64,256]{2,1,0:T(8,128)(2,1)S(1)}, u32[]{:S(2)}, u32[]{:S(2)}) %collective-permute-start.5) | collective-permute-done | bytes 65568 | tf_op jit(solution)/shard_map/ppermute | solution.py:20
  94.6 0.2 fusion.93
  94.9 0.2 fusion.94
  95.2 0.2 convolution_convert_fusion.3
  95.5 0.4 convolution_convert_fusion
  95.9 0.2 fusion.50
  96.1 0.2 fusion.3
  96.3 0.2 fusion.49
  96.5 0.8 copy-done.6
  97.2 0.2 fusion.6
  97.6 0.2 fusion.74
  97.8 0.2 fusion.71
  98.1 2.5 %collective-permute-start.6 = (bf16[2,64,256]{2,1,0:T(8,128)(2,1)S(1)}, bf16[2,64,256]{2,1,0:T(8,128)(2,1)S(1)}, u32[]{:S(2)}, u32[]{:S(2)}) collective-permute-start(bf16[2,64,256]{2,1,0:T(8,128)(2,1)S(1)} %fusion.17), channel_id=1, source_target_pairs={{0,256},{256,0},{8,264},{264,8},{16,272},{272,16},{24,280},{280,24... | collective-permute-start | bytes 196616 | tf_op jit(solution)/shard_map/ppermute | solution.py:20
  100.6 0.2 convolution_convert_fusion.4
  100.8 7.5 %collective-permute-done.6 = bf16[2,64,256]{2,1,0:T(8,128)(2,1)S(1)} collective-permute-done((bf16[2,64,256]{2,1,0:T(8,128)(2,1)S(1)}, bf16[2,64,256]{2,1,0:T(8,128)(2,1)S(1)}, u32[]{:S(2)}, u32[]{:S(2)}) %collective-permute-start.6) | collective-permute-done | bytes 65568 | tf_op jit(solution)/shard_map/ppermute | solution.py:20
  108.3 0.1 copy.118
  108.5 2.4 %collective-permute-start.7 = (bf16[2,64,256]{2,1,0:T(8,128)(2,1)S(1)}, bf16[2,64,256]{2,1,0:T(8,128)(2,1)S(1)}, u32[]{:S(2)}, u32[]{:S(2)}) collective-permute-start(bf16[2,64,256]{2,1,0:T(8,128)(2,1)S(1)} %fusion.20), channel_id=1, source_target_pairs={{0,128},{128,0},{8,136},{136,8},{16,144},{144,16},{24,152},{152,24... | collective-permute-start | bytes 196616 | tf_op jit(solution)/shard_map/ppermute | solution.py:20
  110.9 0.4 convolution_bitcast_fusion
  111.4 4.6 %collective-permute-done.7 = bf16[2,64,256]{2,1,0:T(8,128)(2,1)S(1)} collective-permute-done((bf16[2,64,256]{2,1,0:T(8,128)(2,1)S(1)}, bf16[2,64,256]{2,1,0:T(8,128)(2,1)S(1)}, u32[]{:S(2)}, u32[]{:S(2)}) %collective-permute-start.7) | collective-permute-done | bytes 65568 | tf_op jit(solution)/shard_map/ppermute | solution.py:20
  115.9 0.1 copy.121
  116.2 0.7 fusion.23
  116.8 1.9 %collective-permute-start.8 = (bf16[2,64,256]{2,1,0:T(8,128)(2,1)}, bf16[2,64,256]{2,1,0:T(8,128)(2,1)}, u32[]{:S(2)}, u32[]{:S(2)}) collective-permute-start(bf16[2,64,256]{2,1,0:T(8,128)(2,1)} %fusion.23), channel_id=1, source_target_pairs={{0,64},{64,0},{8,72},{72,8},{16,80},{80,16},{24,88},{88,24},{32,96... | collective-permute-start | bytes 196616 | tf_op jit(solution)/shard_map/ppermute | solution.py:20
  118.7 0.7 copy.136
  119.5 1.3 copy.135
  120.8 8.4 %all-to-all-start.2 = ((bf16[64,32,256]{2,1,0:T(8,128)(2,1)}), bf16[64,32,256]{2,1,0:T(8,128)(2,1)S(1)}, u32[]{:S(2)}, u32[]{:S(2)}) async-start(bf16[64,32,256]{2,1,0:T(8,128)(2,1)} %bitcast.41), calls=%async_computation.2 | async-start | bytes 2097152 | tf_op jit(solution)/shard_map/all_to_all | solution.py:41
  129.2 0.9 add_multiply_fusion.3
  130.0 0.1 copy.124
  130.3 7.4 %collective-permute-start.9 = (bf16[2,64,256]{2,1,0:T(8,128)(2,1)S(1)}, bf16[2,64,256]{2,1,0:T(8,128)(2,1)S(1)}, u32[]{:S(2)}, u32[]{:S(2)}) collective-permute-start(bf16[2,64,256]{2,1,0:T(8,128)(2,1)S(1)} %fusion.26), channel_id=1, source_target_pairs={{0,32},{32,0},{8,40},{40,8},{16,48},{48,16},{24,56},{56,24},{64,96... | collective-permute-start | bytes 196616 | tf_op jit(solution)/shard_map/ppermute | solution.py:20
  137.7 0.2 convolution_convert_fusion.1
  137.9 17.8 %collective-permute-done.9 = bf16[2,64,256]{2,1,0:T(8,128)(2,1)S(1)} collective-permute-done((bf16[2,64,256]{2,1,0:T(8,128)(2,1)S(1)}, bf16[2,64,256]{2,1,0:T(8,128)(2,1)S(1)}, u32[]{:S(2)}, u32[]{:S(2)}) %collective-permute-start.9) | collective-permute-done | bytes 65568 | tf_op jit(solution)/shard_map/ppermute | solution.py:20
  155.8 0.1 copy.127
  156.0 2.1 %collective-permute-start.10 = (bf16[2,64,256]{2,1,0:T(8,128)(2,1)S(1)}, bf16[2,64,256]{2,1,0:T(8,128)(2,1)S(1)}, u32[]{:S(2)}, u32[]{:S(2)}) collective-permute-start(bf16[2,64,256]{2,1,0:T(8,128)(2,1)S(1)} %fusion.15), channel_id=1, source_target_pairs={{0,16},{16,0},{8,24},{24,8},{32,48},{48,32},{40,56},{56,40},{64,80... | collective-permute-start | bytes 196616 | tf_op jit(solution)/shard_map/ppermute | solution.py:20
  158.2 0.2 convolution_convert_fusion.2
  158.4 4.8 %collective-permute-done.10 = bf16[2,64,256]{2,1,0:T(8,128)(2,1)S(1)} collective-permute-done((bf16[2,64,256]{2,1,0:T(8,128)(2,1)S(1)}, bf16[2,64,256]{2,1,0:T(8,128)(2,1)S(1)}, u32[]{:S(2)}, u32[]{:S(2)}) %collective-permute-start.10) | collective-permute-done | bytes 65568 | tf_op jit(solution)/shard_map/ppermute | solution.py:20
  163.2 0.1 copy.130
  163.5 3.1 %collective-permute-start.11 = (bf16[2,64,256]{2,1,0:T(8,128)(2,1)S(1)}, bf16[2,64,256]{2,1,0:T(8,128)(2,1)S(1)}, u32[]{:S(2)}, u32[]{:S(2)}) collective-permute-start(bf16[2,64,256]{2,1,0:T(8,128)(2,1)S(1)} %fusion.28), channel_id=1, source_target_pairs={{0,8},{8,0},{16,24},{24,16},{32,40},{40,32},{48,56},{56,48},{64,72... | collective-permute-start | bytes 196616 | tf_op jit(solution)/shard_map/ppermute | solution.py:20
  166.6 0.7 copy.137
  167.3 2.3 %collective-permute-done.11 = bf16[2,64,256]{2,1,0:T(8,128)(2,1)S(1)} collective-permute-done((bf16[2,64,256]{2,1,0:T(8,128)(2,1)S(1)}, bf16[2,64,256]{2,1,0:T(8,128)(2,1)S(1)}, u32[]{:S(2)}, u32[]{:S(2)}) %collective-permute-start.11) | collective-permute-done | bytes 65568 | tf_op jit(solution)/shard_map/ppermute | solution.py:20
  169.7 0.1 copy.133
  169.9 0.7 slice_bitcast_fusion
  170.6 0.8 convert_reduce_fusion
  (78 shorter events, 1.9 us)
Async XLA Ops:
  0.6 5.8 %copy-start.3 = (bf16[128,256]{1,0:T(8,128)(2,1)S(1)}, bf16[128,256]{1,0:T(8,128)(2,1)}, u32[]{:S(2)}) copy-start(bf16[128,256]{1,0:T(8,128)(2,1)} %param.8) | copy-start | bytes 196612
  2.7 12.4 %copy-start = (bf16[128,256]{1,0:T(8,128)(2,1)S(1)}, bf16[128,256]{1,0:T(8,128)(2,1)}, u32[]{:S(2)}) copy-start(bf16[128,256]{1,0:T(8,128)(2,1)} %param.6) | copy-start | bytes 196612
  2.8 12.4 %copy-start.1 = (bf16[128,256]{1,0:T(8,128)(2,1)S(1)}, bf16[128,256]{1,0:T(8,128)(2,1)}, u32[]{:S(2)}) copy-start(bf16[128,256]{1,0:T(8,128)(2,1)} %param.7) | copy-start | bytes 196612
  2.8 12.4 %collective-permute-start = (f32[2,64,256]{2,1,0:T(8,128)S(1)}, f32[2,64,256]{2,1,0:T(8,128)S(1)}, u32[]{:S(2)}, u32[]{:S(2)}) collective-permute-start(f32[2,64,256]{2,1,0:T(8,128)S(1)} %pad_maximum_fusion.6), channel_id=1, source_target_pairs={{0,8},{8,0},{16,24},{24,16},{32,40},{40,32},{48,56},{56,48},{64,72... | collective-permute-start | bytes 393224 | tf_op jit(solution)/shard_map/ppermute | solution.py:20
  7.4 44.7 %all-to-all-start = ((bf16[8,128,256]{1,2,0:T(8,128)(2,1)}), bf16[8,128,256]{1,2,0:T(8,128)(2,1)S(1)}, u32[]{:S(2)}, u32[]{:S(2)}) async-start(bf16[8,128,256]{1,2,0:T(8,128)(2,1)} %broadcast_in_dim.16), calls=%async_computation | async-start | bytes 1048576 | tf_op jit(solution)/shard_map/all_to_all | solution.py:31
  15.5 11.2 %collective-permute-start.1 = (f32[2,64,256]{2,1,0:T(8,128)S(1)}, f32[2,64,256]{2,1,0:T(8,128)S(1)}, u32[]{:S(2)}, u32[]{:S(2)}) collective-permute-start(f32[2,64,256]{2,1,0:T(8,128)S(1)} %fusion.38), channel_id=1, source_target_pairs={{0,16},{16,0},{8,24},{24,8},{32,48},{48,32},{40,56},{56,40},{64,80... | collective-permute-start | bytes 393224 | tf_op jit(solution)/shard_map/ppermute | solution.py:20
  27.0 12.0 %collective-permute-start.2 = (f32[2,64,256]{2,1,0:T(8,128)S(1)}, f32[2,64,256]{2,1,0:T(8,128)S(1)}, u32[]{:S(2)}, u32[]{:S(2)}) collective-permute-start(f32[2,64,256]{2,1,0:T(8,128)S(1)} %fusion.36), channel_id=1, source_target_pairs={{0,32},{32,0},{8,40},{40,8},{16,48},{48,16},{24,56},{56,24},{64,96... | collective-permute-start | bytes 393224 | tf_op jit(solution)/shard_map/ppermute | solution.py:20
  39.3 7.0 %collective-permute-start.3 = (f32[2,64,256]{2,1,0:T(8,128)S(1)}, f32[2,64,256]{2,1,0:T(8,128)S(1)}, u32[]{:S(2)}, u32[]{:S(2)}) collective-permute-start(f32[2,64,256]{2,1,0:T(8,128)S(1)} %fusion.34), channel_id=1, source_target_pairs={{0,64},{64,0},{8,72},{72,8},{16,80},{80,16},{24,88},{88,24},{32,96... | collective-permute-start | bytes 393224 | tf_op jit(solution)/shard_map/ppermute | solution.py:20
  46.4 5.7 %copy-start.4 = (bf16[32,256]{1,0:T(8,128)(2,1)S(1)}, bf16[32,256]{1,0:T(8,128)(2,1)}, u32[]{:S(2)}) copy-start(bf16[32,256]{1,0:T(8,128)(2,1)} %param.9) | copy-start | bytes 49156
  46.7 17.7 %collective-permute-start.4 = (f32[2,64,256]{2,1,0:T(8,128)S(1)}, f32[2,64,256]{2,1,0:T(8,128)S(1)}, u32[]{:S(2)}, u32[]{:S(2)}) collective-permute-start(f32[2,64,256]{2,1,0:T(8,128)S(1)} %fusion.32), channel_id=1, source_target_pairs={{0,128},{128,0},{8,136},{136,8},{16,144},{144,16},{24,152},{152,24... | collective-permute-start | bytes 393224 | tf_op jit(solution)/shard_map/ppermute | solution.py:20
  53.2 42.3 %all-to-all-start.1 = ((bf16[64,32,256]{2,1,0:T(8,128)(2,1)}), bf16[64,32,256]{2,1,0:T(8,128)(2,1)S(1)}, u32[]{:S(2)}, u32[]{:S(2)}) async-start(bf16[64,32,256]{2,1,0:T(8,128)(2,1)} %broadcast_in_dim.17), calls=%async_computation.1 | async-start | bytes 2097152 | tf_op jit(solution)/shard_map/all_to_all | solution.py:31
  64.4 30.2 %copy-start.2 = (bf16[128,256]{1,0:T(8,128)(2,1)S(1)}, bf16[128,256]{1,0:T(8,128)(2,1)}, u32[]{:S(2)}) copy-start(bf16[128,256]{1,0:T(8,128)(2,1)} %param.5) | copy-start | bytes 196612
  64.7 29.8 %collective-permute-start.5 = (bf16[2,64,256]{2,1,0:T(8,128)(2,1)S(1)}, bf16[2,64,256]{2,1,0:T(8,128)(2,1)S(1)}, u32[]{:S(2)}, u32[]{:S(2)}) collective-permute-start(bf16[2,64,256]{2,1,0:T(8,128)(2,1)S(1)} %fusion.30), channel_id=1, source_target_pairs={{0,256},{256,0},{8,264},{264,8},{16,272},{272,16},{24,280},{280,24... | collective-permute-start | bytes 196616 | tf_op jit(solution)/shard_map/ppermute | solution.py:20
  94.6 1.5 copy-start.5
  96.3 1.0 copy-start.6
  98.1 10.2 %collective-permute-start.6 = (bf16[2,64,256]{2,1,0:T(8,128)(2,1)S(1)}, bf16[2,64,256]{2,1,0:T(8,128)(2,1)S(1)}, u32[]{:S(2)}, u32[]{:S(2)}) collective-permute-start(bf16[2,64,256]{2,1,0:T(8,128)(2,1)S(1)} %fusion.17), channel_id=1, source_target_pairs={{0,256},{256,0},{8,264},{264,8},{16,272},{272,16},{24,280},{280,24... | collective-permute-start | bytes 196616 | tf_op jit(solution)/shard_map/ppermute | solution.py:20
  108.5 7.4 %collective-permute-start.7 = (bf16[2,64,256]{2,1,0:T(8,128)(2,1)S(1)}, bf16[2,64,256]{2,1,0:T(8,128)(2,1)S(1)}, u32[]{:S(2)}, u32[]{:S(2)}) collective-permute-start(bf16[2,64,256]{2,1,0:T(8,128)(2,1)S(1)} %fusion.20), channel_id=1, source_target_pairs={{0,128},{128,0},{8,136},{136,8},{16,144},{144,16},{24,152},{152,24... | collective-permute-start | bytes 196616 | tf_op jit(solution)/shard_map/ppermute | solution.py:20
  116.8 12.3 %collective-permute-start.8 = (bf16[2,64,256]{2,1,0:T(8,128)(2,1)}, bf16[2,64,256]{2,1,0:T(8,128)(2,1)}, u32[]{:S(2)}, u32[]{:S(2)}) collective-permute-start(bf16[2,64,256]{2,1,0:T(8,128)(2,1)} %fusion.23), channel_id=1, source_target_pairs={{0,64},{64,0},{8,72},{72,8},{16,80},{80,16},{24,88},{88,24},{32,96... | collective-permute-start | bytes 196616 | tf_op jit(solution)/shard_map/ppermute | solution.py:20
  120.8 49.8 %all-to-all-start.2 = ((bf16[64,32,256]{2,1,0:T(8,128)(2,1)}), bf16[64,32,256]{2,1,0:T(8,128)(2,1)S(1)}, u32[]{:S(2)}, u32[]{:S(2)}) async-start(bf16[64,32,256]{2,1,0:T(8,128)(2,1)} %bitcast.41), calls=%async_computation.2 | async-start | bytes 2097152 | tf_op jit(solution)/shard_map/all_to_all | solution.py:41
  130.3 25.5 %collective-permute-start.9 = (bf16[2,64,256]{2,1,0:T(8,128)(2,1)S(1)}, bf16[2,64,256]{2,1,0:T(8,128)(2,1)S(1)}, u32[]{:S(2)}, u32[]{:S(2)}) collective-permute-start(bf16[2,64,256]{2,1,0:T(8,128)(2,1)S(1)} %fusion.26), channel_id=1, source_target_pairs={{0,32},{32,0},{8,40},{40,8},{16,48},{48,16},{24,56},{56,24},{64,96... | collective-permute-start | bytes 196616 | tf_op jit(solution)/shard_map/ppermute | solution.py:20
  156.0 7.2 %collective-permute-start.10 = (bf16[2,64,256]{2,1,0:T(8,128)(2,1)S(1)}, bf16[2,64,256]{2,1,0:T(8,128)(2,1)S(1)}, u32[]{:S(2)}, u32[]{:S(2)}) collective-permute-start(bf16[2,64,256]{2,1,0:T(8,128)(2,1)S(1)} %fusion.15), channel_id=1, source_target_pairs={{0,16},{16,0},{8,24},{24,8},{32,48},{48,32},{40,56},{56,40},{64,80... | collective-permute-start | bytes 196616 | tf_op jit(solution)/shard_map/ppermute | solution.py:20
  163.5 6.2 %collective-permute-start.11 = (bf16[2,64,256]{2,1,0:T(8,128)(2,1)S(1)}, bf16[2,64,256]{2,1,0:T(8,128)(2,1)S(1)}, u32[]{:S(2)}, u32[]{:S(2)}) collective-permute-start(bf16[2,64,256]{2,1,0:T(8,128)(2,1)S(1)} %fusion.28), channel_id=1, source_target_pairs={{0,8},{8,0},{16,24},{24,16},{32,40},{40,32},{48,56},{56,48},{64,72... | collective-permute-start | bytes 196616 | tf_op jit(solution)/shard_map/ppermute | solution.py:20

commit v10 on v8

--- a/solution.py
+++ b/solution.py
@@ -80,17 +80,20 @@
         ],
         axis=1,
     )
-    arrived = lax.all_to_all(send, SEQ, 0, 0, tiled=True)
-    full_weight = arrived[:, :w_rows].reshape(n_seq * w_rows, width)
     first = ((position >> top) ^ 1) << top
-    top_far = lax.dynamic_slice_in_dim(arrived[:, w_rows:], first, 1 << top, axis=0)
-    top_far = top_far.reshape(1 << top, 2, top_count, width)
+    tie = max(top - 2, 0)
     for layer_bit in range(depth):
         if layer_bit == top:
             far_keys.append(top_far[:, 0].reshape(-1, width))
             far_values.append(top_far[:, 1].reshape(-1, width))
             continue
         far_table = from_partner(own_table, SEQ, layer_bit)
+        if layer_bit == tie:
+            send, far_table = lax.optimization_barrier((send, far_table))
+            arrived = lax.all_to_all(send, SEQ, 0, 0, tiled=True)
+            full_weight = arrived[:, :w_rows].reshape(n_seq * w_rows, width)
+            top_far = lax.dynamic_slice_in_dim(arrived[:, w_rows:], first, 1 << top, axis=0)
+            top_far = top_far.reshape(1 << top, 2, top_count, width)
         far_keys.append(far_table[0].astype(jnp.bfloat16))
         far_values.append(far_table[1].astype(jnp.bfloat16))
         if layer_bit + 1 < depth:

time: 180 us -> 180 us (level)
  starting transfers between devices: 80.5 us -> 73.9 us
  waiting for transfers between devices: 78.3 us -> 84.7 us
    all_to_all x1, starting transfers between devices: 11.7 us -> 6.97 us  [own_rows(): lax.all_to_all(parts, axes, 0, 0, tiled=True).astype(jnp.float32)]
    ppermute x11, waiting for transfers between devices: 71.1 us -> 75.6 us  [from_partner(): return lax.ppermute(block, axis, route)]
    all_to_all x1, waiting for transfers between devices: 0.01 us -> 1.91 us  [on_device(): arrived = lax.all_to_all(send, SEQ, 0, 0, tiled=True)]
  transfers between devices with their start and end apart: 14 -> 14, of which waited for: 10 -> 12; matrix products, arithmetic and copies ran while one was open for 6% -> 6% of each run, Pallas kernels for 0% -> 0%
where the time goes in v10:
time: 180 us; the launch traced here: 178 us
  waiting for transfers between devices  84.7 us (47%)
  starting transfers between devices  73.9 us (41%)
  local copies, waits for them, and re-layouts  8.92 us (5%)
  matrix products  4.68 us (3%)
  other arithmetic  3.93 us (2%)
    ppermute x11, waiting for transfers between devices, from_partner(): return lax.ppermute(block, axis, route)  75.6 us
    ppermute x11, starting transfers between devices, from_partner(): return lax.ppermute(block, axis, route)  48.1 us
    all_to_all x1, starting transfers between devices, on_device(): arrived = lax.all_to_all(send, SEQ, 0, 0, tiled=True)  14.1 us
    all_to_all x1, waiting for transfers between devices, from_everyone(): return lax.all_to_all(copies, axis, split_axis=0, concat_axis=0, tiled=True)  7.16 us
    all_to_all x1, starting transfers between devices, own_rows(): lax.all_to_all(parts, axes, 0, 0, tiled=True).astype(jnp.float32)  6.97 us
    all_to_all x1, starting transfers between devices, from_everyone(): return lax.all_to_all(copies, axis, split_axis=0, concat_axis=0, tiled=True)  4.78 us
  transfers between devices with their start and end apart: 14, of which 12 were waited for; matrix products, arithmetic and copies ran while one was open for 6% of the time, Pallas kernels for 0%

profile of v10, /device:TPU:6, one launch (start us, length us, event | category | flops | bytes accessed | tf_op | source)
XLA Modules:
  0.0 177.7 jit_solution(10752066497214079358)
XLA Ops:
  0.6 0.9 stack.28
  1.5 0.9 stack.27
  2.5 3.5 %collective-permute-start = (f32[2,64,256]{2,1,0:T(8,128)S(1)}, f32[2,64,256]{2,1,0:T(8,128)S(1)}, u32[]{:S(2)}, u32[]{:S(2)}) collective-permute-start(f32[2,64,256]{2,1,0:T(8,128)S(1)} %fusion.32), channel_id=1, source_target_pairs={{0,8},{8,0},{16,24},{24,16},{32,40},{40,32},{48,56},{56,48},{64,72... | collective-permute-start | bytes 393224 | tf_op jit(solution)/shard_map/ppermute | solution.py:20
  6.0 3.6 %collective-permute-done = f32[2,64,256]{2,1,0:T(8,128)S(1)} collective-permute-done((f32[2,64,256]{2,1,0:T(8,128)S(1)}, f32[2,64,256]{2,1,0:T(8,128)S(1)}, u32[]{:S(2)}, u32[]{:S(2)}) %collective-permute-start) | collective-permute-done | bytes 131104 | tf_op jit(solution)/shard_map/ppermute | solution.py:20
  9.7 0.2 copy.193
  10.0 4.5 %collective-permute-start.1 = (f32[2,64,256]{2,1,0:T(8,128)S(1)}, f32[2,64,256]{2,1,0:T(8,128)S(1)}, u32[]{:S(2)}, u32[]{:S(2)}) collective-permute-start(f32[2,64,256]{2,1,0:T(8,128)S(1)} %fusion.40), channel_id=1, source_target_pairs={{0,16},{16,0},{8,24},{24,8},{32,48},{48,32},{40,56},{56,40},{64,80... | collective-permute-start | bytes 393224 | tf_op jit(solution)/shard_map/ppermute | solution.py:20
  14.5 5.4 %collective-permute-done.1 = f32[2,64,256]{2,1,0:T(8,128)S(1)} collective-permute-done((f32[2,64,256]{2,1,0:T(8,128)S(1)}, f32[2,64,256]{2,1,0:T(8,128)S(1)}, u32[]{:S(2)}, u32[]{:S(2)}) %collective-permute-start.1) | collective-permute-done | bytes 131104 | tf_op jit(solution)/shard_map/ppermute | solution.py:20
  20.0 0.2 copy.196
  20.3 7.7 %collective-permute-start.2 = (f32[2,64,256]{2,1,0:T(8,128)S(1)}, f32[2,64,256]{2,1,0:T(8,128)S(1)}, u32[]{:S(2)}, u32[]{:S(2)}) collective-permute-start(f32[2,64,256]{2,1,0:T(8,128)S(1)} %fusion.38), channel_id=1, source_target_pairs={{0,32},{32,0},{8,40},{40,8},{16,48},{48,16},{24,56},{56,24},{64,96... | collective-permute-start | bytes 393224 | tf_op jit(solution)/shard_map/ppermute | solution.py:20
  28.1 5.9 %collective-permute-done.2 = f32[2,64,256]{2,1,0:T(8,128)S(1)} collective-permute-done((f32[2,64,256]{2,1,0:T(8,128)S(1)}, f32[2,64,256]{2,1,0:T(8,128)S(1)}, u32[]{:S(2)}, u32[]{:S(2)}) %collective-permute-start.2) | collective-permute-done | bytes 131104 | tf_op jit(solution)/shard_map/ppermute | solution.py:20
  34.0 0.2 copy.199
  34.3 4.3 %collective-permute-start.3 = (f32[2,64,256]{2,1,0:T(8,128)S(1)}, f32[2,64,256]{2,1,0:T(8,128)S(1)}, u32[]{:S(2)}, u32[]{:S(2)}) collective-permute-start(f32[2,64,256]{2,1,0:T(8,128)S(1)} %fusion.36), channel_id=1, source_target_pairs={{0,64},{64,0},{8,72},{72,8},{16,80},{80,16},{24,88},{88,24},{32,96... | collective-permute-start | bytes 393224 | tf_op jit(solution)/shard_map/ppermute | solution.py:20
  38.7 0.1 broadcast_in_dim.18
  38.8 1.2 pad_maximum_fusion
  40.0 1.5 collective-permute-done.3
  41.5 14.1 %all-to-all-start = ((bf16[64,36,256]{2,1,0:T(8,128)(2,1)}), bf16[64,36,256]{2,1,0:T(8,128)(2,1)S(1)}, u32[]{:S(2)}, u32[]{:S(2)}) async-start(bf16[64,36,256]{2,1,0:T(8,128)(2,1)} %pad_maximum_fusion), calls=%async_computation | async-start | bytes 2621440 | tf_op jit(solution)/shard_map/all_to_all | solution.py:93
  55.6 0.1 copy.208
  55.9 0.2 copy.202
  56.2 4.4 %collective-permute-start.4 = (bf16[2,64,256]{2,1,0:T(8,128)(2,1)S(1)}, bf16[2,64,256]{2,1,0:T(8,128)(2,1)S(1)}, u32[]{:S(2)}, u32[]{:S(2)}) collective-permute-start(bf16[2,64,256]{2,1,0:T(8,128)(2,1)S(1)} %fusion.34), channel_id=1, source_target_pairs={{0,128},{128,0},{8,136},{136,8},{16,144},{144,16},{24,152},{152,24... | collective-permute-start | bytes 196616 | tf_op jit(solution)/shard_map/ppermute | solution.py:20
  60.6 26.9 %collective-permute-done.4 = bf16[2,64,256]{2,1,0:T(8,128)(2,1)S(1)} collective-permute-done((bf16[2,64,256]{2,1,0:T(8,128)(2,1)S(1)}, bf16[2,64,256]{2,1,0:T(8,128)(2,1)S(1)}, u32[]{:S(2)}, u32[]{:S(2)}) %collective-permute-start.4) | collective-permute-done | bytes 65568 | tf_op jit(solution)/shard_map/ppermute | solution.py:20
  87.5 1.9 %all-to-all-done = bf16[64,36,256]{2,1,0:T(8,128)(2,1)S(1)} async-done(((bf16[64,36,256]{2,1,0:T(8,128)(2,1)}), bf16[64,36,256]{2,1,0:T(8,128)(2,1)S(1)}, u32[]{:S(2)}, u32[]{:S(2)}) %all-to-all-start) | async-done | bytes 1179680 | tf_op jit(solution)/shard_map/all_to_all | solution.py:93
  89.4 1.0 broadcast_in_dim.20
  90.4 4.8 %all-to-all-start.1 = ((bf16[8,128,256]{1,2,0:T(8,128)(2,1)}), bf16[8,128,256]{1,2,0:T(8,128)(2,1)S(1)}, u32[]{:S(2)}, u32[]{:S(2)}) async-start(bf16[8,128,256]{1,2,0:T(8,128)(2,1)} %broadcast_in_dim.20), calls=%async_computation.1 | async-start | bytes 1048576 | tf_op jit(solution)/shard_map/all_to_all | solution.py:31
  95.5 0.2 fusion.87
  95.7 0.1 fusion.14
  95.8 0.2 fusion.88
  96.0 0.2 convolution_convert_fusion.4
  96.3 7.2 %all-to-all-done.1 = bf16[8,128,256]{1,2,0:T(8,128)(2,1)S(1)} async-done(((bf16[8,128,256]{1,2,0:T(8,128)(2,1)}), bf16[8,128,256]{1,2,0:T(8,128)(2,1)S(1)}, u32[]{:S(2)}, u32[]{:S(2)}) %all-to-all-start.1) | async-done | bytes 524320 | tf_op jit(solution)/shard_map/all_to_all | solution.py:31
  103.4 0.5 fusion.1
  103.9 0.2 fusion.5
  104.1 0.2 fusion.52
  104.3 0.1 fusion.12
  104.4 0.2 fusion.8
  104.7 0.2 fusion.51
  104.9 0.2 fusion.67
  105.2 0.2 fusion.70
  105.5 4.7 %collective-permute-start.5 = (bf16[2,64,256]{2,1,0:T(8,128)(2,1)S(1)}, bf16[2,64,256]{2,1,0:T(8,128)(2,1)S(1)}, u32[]{:S(2)}, u32[]{:S(2)}) collective-permute-start(bf16[2,64,256]{2,1,0:T(8,128)(2,1)S(1)} %fusion.19), channel_id=1, source_target_pairs={{0,256},{256,0},{8,264},{264,8},{16,272},{272,16},{24,280},{280,24... | collective-permute-start | bytes 196616 | tf_op jit(solution)/shard_map/ppermute | solution.py:20
  110.2 0.2 convolution_convert_fusion.5
  110.5 5.5 %collective-permute-done.5 = bf16[2,64,256]{2,1,0:T(8,128)(2,1)S(1)} collective-permute-done((bf16[2,64,256]{2,1,0:T(8,128)(2,1)S(1)}, bf16[2,64,256]{2,1,0:T(8,128)(2,1)S(1)}, u32[]{:S(2)}, u32[]{:S(2)}) %collective-permute-start.5) | collective-permute-done | bytes 65568 | tf_op jit(solution)/shard_map/ppermute | solution.py:20
  116.0 0.1 copy.217
  116.3 4.6 %collective-permute-start.6 = (bf16[2,64,256]{2,1,0:T(8,128)(2,1)S(1)}, bf16[2,64,256]{2,1,0:T(8,128)(2,1)S(1)}, u32[]{:S(2)}, u32[]{:S(2)}) collective-permute-start(bf16[2,64,256]{2,1,0:T(8,128)(2,1)S(1)} %fusion.22), channel_id=1, source_target_pairs={{0,128},{128,0},{8,136},{136,8},{16,144},{144,16},{24,152},{152,24... | collective-permute-start | bytes 196616 | tf_op jit(solution)/shard_map/ppermute | solution.py:20
  120.9 0.4 fusion
  121.3 2.4 %collective-permute-done.6 = bf16[2,64,256]{2,1,0:T(8,128)(2,1)S(1)} collective-permute-done((bf16[2,64,256]{2,1,0:T(8,128)(2,1)S(1)}, bf16[2,64,256]{2,1,0:T(8,128)(2,1)S(1)}, u32[]{:S(2)}, u32[]{:S(2)}) %collective-permute-start.6) | collective-permute-done | bytes 65568 | tf_op jit(solution)/shard_map/ppermute | solution.py:20
  123.7 0.1 copy.220
  123.9 1.9 %collective-permute-start.7 = (bf16[2,64,256]{2,1,0:T(8,128)(2,1)S(1)}, bf16[2,64,256]{2,1,0:T(8,128)(2,1)S(1)}, u32[]{:S(2)}, u32[]{:S(2)}) collective-permute-start(bf16[2,64,256]{2,1,0:T(8,128)(2,1)S(1)} %fusion.25), channel_id=1, source_target_pairs={{0,64},{64,0},{8,72},{72,8},{16,80},{80,16},{24,88},{88,24},{32,96... | collective-permute-start | bytes 196616 | tf_op jit(solution)/shard_map/ppermute | solution.py:20
  125.9 0.8 convolution_convert_fusion.2
  126.7 3.4 %collective-permute-done.7 = bf16[2,64,256]{2,1,0:T(8,128)(2,1)S(1)} collective-permute-done((bf16[2,64,256]{2,1,0:T(8,128)(2,1)S(1)}, bf16[2,64,256]{2,1,0:T(8,128)(2,1)S(1)}, u32[]{:S(2)}, u32[]{:S(2)}) %collective-permute-start.7) | collective-permute-done | bytes 65568 | tf_op jit(solution)/shard_map/ppermute | solution.py:20
  130.1 0.1 copy.223
  130.4 6.1 %collective-permute-start.8 = (bf16[2,64,256]{2,1,0:T(8,128)(2,1)S(1)}, bf16[2,64,256]{2,1,0:T(8,128)(2,1)}, u32[]{:S(2)}, u32[]{:S(2)}) collective-permute-start(bf16[2,64,256]{2,1,0:T(8,128)(2,1)S(1)} %fusion.28), channel_id=1, source_target_pairs={{0,32},{32,0},{8,40},{40,8},{16,48},{48,16},{24,56},{56,24},{64,96... | collective-permute-start | bytes 196616 | tf_op jit(solution)/shard_map/ppermute | solution.py:20
  136.5 0.8 convolution_convert_fusion.3
  137.4 1.3 copy.234
  138.7 7.0 %all-to-all-start.2 = ((bf16[64,32,256]{2,1,0:T(8,128)(2,1)}), bf16[64,32,256]{2,1,0:T(8,128)(2,1)S(1)}, u32[]{:S(2)}, u32[]{:S(2)}) async-start(bf16[64,32,256]{2,1,0:T(8,128)(2,1)} %bitcast.40), calls=%async_computation.2 | async-start | bytes 2097152 | tf_op jit(solution)/shard_map/all_to_all | solution.py:41
  145.7 0.9 add_multiply_fusion.2
  146.6 0.1 copy.226
  146.8 4.4 %collective-permute-start.9 = (bf16[2,64,256]{2,1,0:T(8,128)(2,1)S(1)}, bf16[2,64,256]{2,1,0:T(8,128)(2,1)S(1)}, u32[]{:S(2)}, u32[]{:S(2)}) collective-permute-start(bf16[2,64,256]{2,1,0:T(8,128)(2,1)S(1)} %fusion.17), channel_id=1, source_target_pairs={{0,16},{16,0},{8,24},{24,8},{32,48},{48,32},{40,56},{56,40},{64,80... | collective-permute-start | bytes 196616 | tf_op jit(solution)/shard_map/ppermute | solution.py:20
  151.2 0.7 copy.235
  151.9 17.6 %collective-permute-done.9 = bf16[2,64,256]{2,1,0:T(8,128)(2,1)S(1)} collective-permute-done((bf16[2,64,256]{2,1,0:T(8,128)(2,1)S(1)}, bf16[2,64,256]{2,1,0:T(8,128)(2,1)S(1)}, u32[]{:S(2)}, u32[]{:S(2)}) %collective-permute-start.9) | collective-permute-done | bytes 65568 | tf_op jit(solution)/shard_map/ppermute | solution.py:20
  169.6 0.1 copy.229
  169.8 1.9 %collective-permute-start.10 = (bf16[2,64,256]{2,1,0:T(8,128)(2,1)S(1)}, bf16[2,64,256]{2,1,0:T(8,128)(2,1)S(1)}, u32[]{:S(2)}, u32[]{:S(2)}) collective-permute-start(bf16[2,64,256]{2,1,0:T(8,128)(2,1)S(1)} %fusion.30), channel_id=1, source_target_pairs={{0,8},{8,0},{16,24},{24,16},{32,40},{40,32},{48,56},{56,48},{64,72... | collective-permute-start | bytes 196616 | tf_op jit(solution)/shard_map/ppermute | solution.py:20
  171.8 0.7 copy.236
  172.5 3.5 %collective-permute-done.10 = bf16[2,64,256]{2,1,0:T(8,128)(2,1)S(1)} collective-permute-done((bf16[2,64,256]{2,1,0:T(8,128)(2,1)S(1)}, bf16[2,64,256]{2,1,0:T(8,128)(2,1)S(1)}, u32[]{:S(2)}, u32[]{:S(2)}) %collective-permute-start.10) | collective-permute-done | bytes 65568 | tf_op jit(solution)/shard_map/ppermute | solution.py:20
  176.0 0.1 copy.232
  176.2 0.7 slice_bitcast_fusion
  176.9 0.8 convert_reduce_fusion
  (93 shorter events, 2.0 us)
Async XLA Ops:
  2.5 7.1 %collective-permute-start = (f32[2,64,256]{2,1,0:T(8,128)S(1)}, f32[2,64,256]{2,1,0:T(8,128)S(1)}, u32[]{:S(2)}, u32[]{:S(2)}) collective-permute-start(f32[2,64,256]{2,1,0:T(8,128)S(1)} %fusion.32), channel_id=1, source_target_pairs={{0,8},{8,0},{16,24},{24,16},{32,40},{40,32},{48,56},{56,48},{64,72... | collective-permute-start | bytes 393224 | tf_op jit(solution)/shard_map/ppermute | solution.py:20
  6.0 8.5 %copy-start.1 = (bf16[128,256]{1,0:T(8,128)(2,1)S(1)}, bf16[128,256]{1,0:T(8,128)(2,1)}, u32[]{:S(2)}) copy-start(bf16[128,256]{1,0:T(8,128)(2,1)} %param.6) | copy-start | bytes 196612
  6.0 8.5 %copy-start.2 = (bf16[128,256]{1,0:T(8,128)(2,1)S(1)}, bf16[128,256]{1,0:T(8,128)(2,1)}, u32[]{:S(2)}) copy-start(bf16[128,256]{1,0:T(8,128)(2,1)} %param.7) | copy-start | bytes 196612
  10.0 10.0 %collective-permute-start.1 = (f32[2,64,256]{2,1,0:T(8,128)S(1)}, f32[2,64,256]{2,1,0:T(8,128)S(1)}, u32[]{:S(2)}, u32[]{:S(2)}) collective-permute-start(f32[2,64,256]{2,1,0:T(8,128)S(1)} %fusion.40), channel_id=1, source_target_pairs={{0,16},{16,0},{8,24},{24,8},{32,48},{48,32},{40,56},{56,40},{64,80... | collective-permute-start | bytes 393224 | tf_op jit(solution)/shard_map/ppermute | solution.py:20
  20.3 13.7 %collective-permute-start.2 = (f32[2,64,256]{2,1,0:T(8,128)S(1)}, f32[2,64,256]{2,1,0:T(8,128)S(1)}, u32[]{:S(2)}, u32[]{:S(2)}) collective-permute-start(f32[2,64,256]{2,1,0:T(8,128)S(1)} %fusion.38), channel_id=1, source_target_pairs={{0,32},{32,0},{8,40},{40,8},{16,48},{48,16},{24,56},{56,24},{64,96... | collective-permute-start | bytes 393224 | tf_op jit(solution)/shard_map/ppermute | solution.py:20
  28.0 10.6 %copy-start.7 = (bf16[32,256]{1,0:T(8,128)(2,1)S(1)}, bf16[32,256]{1,0:T(8,128)(2,1)}, u32[]{:S(2)}) copy-start(bf16[32,256]{1,0:T(8,128)(2,1)} %param.9) | copy-start | bytes 49156
  34.3 7.2 %collective-permute-start.3 = (f32[2,64,256]{2,1,0:T(8,128)S(1)}, f32[2,64,256]{2,1,0:T(8,128)S(1)}, u32[]{:S(2)}, u32[]{:S(2)}) collective-permute-start(f32[2,64,256]{2,1,0:T(8,128)S(1)} %fusion.36), channel_id=1, source_target_pairs={{0,64},{64,0},{8,72},{72,8},{16,80},{80,16},{24,88},{88,24},{32,96... | collective-permute-start | bytes 393224 | tf_op jit(solution)/shard_map/ppermute | solution.py:20
  40.0 15.6 %copy-start.4 = (bf16[128,256]{1,0:T(8,128)(2,1)S(1)}, bf16[128,256]{1,0:T(8,128)(2,1)}, u32[]{:S(2)}) copy-start(bf16[128,256]{1,0:T(8,128)(2,1)} %param.8) | copy-start | bytes 196612
  41.5 47.9 %all-to-all-start = ((bf16[64,36,256]{2,1,0:T(8,128)(2,1)}), bf16[64,36,256]{2,1,0:T(8,128)(2,1)S(1)}, u32[]{:S(2)}, u32[]{:S(2)}) async-start(bf16[64,36,256]{2,1,0:T(8,128)(2,1)} %pad_maximum_fusion), calls=%async_computation | async-start | bytes 2621440 | tf_op jit(solution)/shard_map/all_to_all | solution.py:93
  56.2 31.3 %collective-permute-start.4 = (bf16[2,64,256]{2,1,0:T(8,128)(2,1)S(1)}, bf16[2,64,256]{2,1,0:T(8,128)(2,1)S(1)}, u32[]{:S(2)}, u32[]{:S(2)}) collective-permute-start(bf16[2,64,256]{2,1,0:T(8,128)(2,1)S(1)} %fusion.34), channel_id=1, source_target_pairs={{0,128},{128,0},{8,136},{136,8},{16,144},{144,16},{24,152},{152,24... | collective-permute-start | bytes 196616 | tf_op jit(solution)/shard_map/ppermute | solution.py:20
  87.5 7.9 %copy-start.3 = (bf16[128,256]{1,0:T(8,128)(2,1)S(1)}, bf16[128,256]{1,0:T(8,128)(2,1)}, u32[]{:S(2)}) copy-start(bf16[128,256]{1,0:T(8,128)(2,1)} %param.5) | copy-start | bytes 196612
  89.4 6.4 %copy-start = (bf16[64,36,256]{2,1,0:T(8,128)(2,1)}, bf16[64,36,256]{2,1,0:T(8,128)(2,1)S(1)}, u32[]{:S(2)}) copy-start(bf16[64,36,256]{2,1,0:T(8,128)(2,1)S(1)} %all-to-all-done) | copy-start | bytes 3538948
  90.4 13.1 %all-to-all-start.1 = ((bf16[8,128,256]{1,2,0:T(8,128)(2,1)}), bf16[8,128,256]{1,2,0:T(8,128)(2,1)S(1)}, u32[]{:S(2)}, u32[]{:S(2)}) async-start(bf16[8,128,256]{1,2,0:T(8,128)(2,1)} %broadcast_in_dim.20), calls=%async_computation.1 | async-start | bytes 1048576 | tf_op jit(solution)/shard_map/all_to_all | solution.py:31
  95.4 9.0 %copy-start.8 = (bf16[512,256]{1,0:T(8,128)(2,1)}, bf16[512,256]{1,0:T(8,128)(2,1)S(1)}, u32[]{:S(2)}) copy-start(bf16[512,256]{1,0:T(8,128)(2,1)S(1)} %constant_dynamic-update-slice_fusion.2) | copy-start | bytes 786436
  95.8 7.6 %slice-start = ((bf16[64,36,256]{2,1,0:T(8,128)(2,1)}), bf16[64,32,256]{2,1,0:T(8,128)(2,1)S(1)}, s32[]{:S(2)}) async-start(bf16[64,36,256]{2,1,0:T(8,128)(2,1)} %copy-done), calls=%async_computation.3 | async-start | bytes 2097152 | tf_op jit(solution)/shard_map/slice | solution.py:94
  105.4 4.8 %copy-start.9 = (bf16[512,256]{1,0:T(8,128)(2,1)S(1)}, bf16[512,256]{1,0:T(8,128)(2,1)}, u32[]{:S(2)}) copy-start(bf16[512,256]{1,0:T(8,128)(2,1)} %copy-done.8) | copy-start | bytes 786436
  105.5 10.5 %collective-permute-start.5 = (bf16[2,64,256]{2,1,0:T(8,128)(2,1)S(1)}, bf16[2,64,256]{2,1,0:T(8,128)(2,1)S(1)}, u32[]{:S(2)}, u32[]{:S(2)}) collective-permute-start(bf16[2,64,256]{2,1,0:T(8,128)(2,1)S(1)} %fusion.19), channel_id=1, source_target_pairs={{0,256},{256,0},{8,264},{264,8},{16,272},{272,16},{24,280},{280,24... | collective-permute-start | bytes 196616 | tf_op jit(solution)/shard_map/ppermute | solution.py:20
  116.3 7.4 %collective-permute-start.6 = (bf16[2,64,256]{2,1,0:T(8,128)(2,1)S(1)}, bf16[2,64,256]{2,1,0:T(8,128)(2,1)S(1)}, u32[]{:S(2)}, u32[]{:S(2)}) collective-permute-start(bf16[2,64,256]{2,1,0:T(8,128)(2,1)S(1)} %fusion.22), channel_id=1, source_target_pairs={{0,128},{128,0},{8,136},{136,8},{16,144},{144,16},{24,152},{152,24... | collective-permute-start | bytes 196616 | tf_op jit(solution)/shard_map/ppermute | solution.py:20
  123.9 6.2 %collective-permute-start.7 = (bf16[2,64,256]{2,1,0:T(8,128)(2,1)S(1)}, bf16[2,64,256]{2,1,0:T(8,128)(2,1)S(1)}, u32[]{:S(2)}, u32[]{:S(2)}) collective-permute-start(bf16[2,64,256]{2,1,0:T(8,128)(2,1)S(1)} %fusion.25), channel_id=1, source_target_pairs={{0,64},{64,0},{8,72},{72,8},{16,80},{80,16},{24,88},{88,24},{32,96... | collective-permute-start | bytes 196616 | tf_op jit(solution)/shard_map/ppermute | solution.py:20
  130.4 15.3 %collective-permute-start.8 = (bf16[2,64,256]{2,1,0:T(8,128)(2,1)S(1)}, bf16[2,64,256]{2,1,0:T(8,128)(2,1)}, u32[]{:S(2)}, u32[]{:S(2)}) collective-permute-start(bf16[2,64,256]{2,1,0:T(8,128)(2,1)S(1)} %fusion.28), channel_id=1, source_target_pairs={{0,32},{32,0},{8,40},{40,8},{16,48},{48,16},{24,56},{56,24},{64,96... | collective-permute-start | bytes 196616 | tf_op jit(solution)/shard_map/ppermute | solution.py:20
  138.7 38.2 %all-to-all-start.2 = ((bf16[64,32,256]{2,1,0:T(8,128)(2,1)}), bf16[64,32,256]{2,1,0:T(8,128)(2,1)S(1)}, u32[]{:S(2)}, u32[]{:S(2)}) async-start(bf16[64,32,256]{2,1,0:T(8,128)(2,1)} %bitcast.40), calls=%async_computation.2 | async-start | bytes 2097152 | tf_op jit(solution)/shard_map/all_to_all | solution.py:41
  146.8 22.7 %collective-permute-start.9 = (bf16[2,64,256]{2,1,0:T(8,128)(2,1)S(1)}, bf16[2,64,256]{2,1,0:T(8,128)(2,1)S(1)}, u32[]{:S(2)}, u32[]{:S(2)}) collective-permute-start(bf16[2,64,256]{2,1,0:T(8,128)(2,1)S(1)} %fusion.17), channel_id=1, source_target_pairs={{0,16},{16,0},{8,24},{24,8},{32,48},{48,32},{40,56},{56,40},{64,80... | collective-permute-start | bytes 196616 | tf_op jit(solution)/shard_map/ppermute | solution.py:20
  169.5 2.2 %copy-start.5 = (bf16[128,128]{0,1:T(8,128)(2,1)S(1)}, bf16[128,128]{0,1:T(8,128)(2,1)}, u32[]{:S(2)}) copy-start(bf16[128,128]{0,1:T(8,128)(2,1)} %convolution_convert_fusion.2) | copy-start | bytes 98308
  169.5 2.2 %copy-start.6 = (bf16[128,128]{0,1:T(8,128)(2,1)S(1)}, bf16[128,128]{0,1:T(8,128)(2,1)}, u32[]{:S(2)}) copy-start(bf16[128,128]{0,1:T(8,128)(2,1)} %convolution_convert_fusion.3) | copy-start | bytes 98308
  169.8 6.2 %collective-permute-start.10 = (bf16[2,64,256]{2,1,0:T(8,128)(2,1)S(1)}, bf16[2,64,256]{2,1,0:T(8,128)(2,1)S(1)}, u32[]{:S(2)}, u32[]{:S(2)}) collective-permute-start(bf16[2,64,256]{2,1,0:T(8,128)(2,1)S(1)} %fusion.30), channel_id=1, source_target_pairs={{0,8},{8,0},{16,24},{24,16},{32,40},{40,32},{48,56},{56,48},{64,72... | collective-permute-start | bytes 196616 | tf_op jit(solution)/shard_map/ppermute | solution.py:20

commit v11 on v9

--- a/solution.py
+++ b/solution.py
@@ -67,7 +67,7 @@
     far_keys = []
     far_values = []
     for layer_bit in range(depth):
-        far_table = from_partner(own_table, SEQ, layer_bit)
+        far_table = from_partner(own_table.astype(jnp.bfloat16), SEQ, layer_bit).astype(jnp.float32)
         far_keys.append(far_table[0].astype(jnp.bfloat16))
         far_values.append(far_table[1].astype(jnp.bfloat16))
         if layer_bit + 1 < depth:

time: 172 us -> 167 us (0.971)
  waiting for transfers between devices: 80.2 us -> 70.6 us
  starting transfers between devices: 72.2 us -> 75.7 us
    ppermute x12, waiting for transfers between devices: 80.2 us -> 70.6 us  [from_partner(): return lax.ppermute(block, axis, route)]
    all_to_all x2, starting transfers between devices: 18.9 us -> 22 us  [from_everyone(): return lax.all_to_all(copies, axis, split_axis=0, concat_axis=0, tiled=True)]
  transfers between devices with their start and end apart: 15 -> 15, of which waited for: 9 -> 9; matrix products, arithmetic and copies ran while one was open for 6% -> 7% of each run, Pallas kernels for 0% -> 0%
where the time goes in v11:
time: 167 us; the launch traced here: 165 us
  starting transfers between devices  75.7 us (45%)
  waiting for transfers between devices  70.6 us (42%)
  local copies, waits for them, and re-layouts  10.9 us (7%)
  other arithmetic  3.37 us (2%)
  matrix products  3.36 us (2%)
    ppermute x12, waiting for transfers between devices, from_partner(): return lax.ppermute(block, axis, route)  70.6 us
    ppermute x12, starting transfers between devices, from_partner(): return lax.ppermute(block, axis, route)  45.2 us
    all_to_all x2, starting transfers between devices, from_everyone(): return lax.all_to_all(copies, axis, split_axis=0, concat_axis=0, tiled=True)  22 us
    all_to_all x1, starting transfers between devices, own_rows(): lax.all_to_all(parts, axes, 0, 0, tiled=True).astype(jnp.float32)  8.49 us
  transfers between devices with their start and end apart: 15, of which 9 were waited for; matrix products, arithmetic and copies ran while one was open for 7% of the time, Pallas kernels for 0%

profile of v11, /device:TPU:6, one launch (start us, length us, event | category | flops | bytes accessed | tf_op | source)
XLA Modules:
  0.0 165.3 jit_solution(6730001463248313017)
XLA Ops:
  0.6 0.9 reshape.183
  1.6 0.1 fusion.97
  1.7 0.9 reshape.185
  2.6 0.1 fusion.98
  2.8 3.6 %collective-permute-start = (bf16[2,64,256]{2,1,0:T(8,128)(2,1)S(1)}, bf16[2,64,256]{2,1,0:T(8,128)(2,1)S(1)}, u32[]{:S(2)}, u32[]{:S(2)}) collective-permute-start(bf16[2,64,256]{2,1,0:T(8,128)(2,1)S(1)} %fusion.49), channel_id=1, source_target_pairs={{0,8},{8,0},{16,24},{24,16},{32,40},{40,32},{48,56},{56,48},{64,72... | collective-permute-start | bytes 196616 | tf_op jit(solution)/shard_map/ppermute | solution.py:20
  6.4 0.1 copy.109
  6.5 0.9 broadcast_in_dim.16
  7.4 7.7 %all-to-all-start = ((bf16[8,128,256]{1,2,0:T(8,128)(2,1)}), bf16[8,128,256]{1,2,0:T(8,128)(2,1)S(1)}, u32[]{:S(2)}, u32[]{:S(2)}) async-start(bf16[8,128,256]{1,2,0:T(8,128)(2,1)} %broadcast_in_dim.16), calls=%async_computation | async-start | bytes 1048576 | tf_op jit(solution)/shard_map/all_to_all | solution.py:31
  15.2 0.2 copy.94
  15.5 1.9 %collective-permute-start.1 = (bf16[2,64,256]{2,1,0:T(8,128)(2,1)S(1)}, bf16[2,64,256]{2,1,0:T(8,128)(2,1)S(1)}, u32[]{:S(2)}, u32[]{:S(2)}) collective-permute-start(bf16[2,64,256]{2,1,0:T(8,128)(2,1)S(1)} %fusion.79), channel_id=1, source_target_pairs={{0,16},{16,0},{8,24},{24,8},{32,48},{48,32},{40,56},{56,40},{64,80... | collective-permute-start | bytes 196616 | tf_op jit(solution)/shard_map/ppermute | solution.py:20
  17.5 5.1 %collective-permute-done.1 = bf16[2,64,256]{2,1,0:T(8,128)(2,1)S(1)} collective-permute-done((bf16[2,64,256]{2,1,0:T(8,128)(2,1)S(1)}, bf16[2,64,256]{2,1,0:T(8,128)(2,1)S(1)}, u32[]{:S(2)}, u32[]{:S(2)}) %collective-permute-start.1) | collective-permute-done | bytes 65568 | tf_op jit(solution)/shard_map/ppermute | solution.py:20
  22.6 0.2 copy.97
  22.9 5.3 %collective-permute-start.2 = (bf16[2,64,256]{2,1,0:T(8,128)(2,1)S(1)}, bf16[2,64,256]{2,1,0:T(8,128)(2,1)S(1)}, u32[]{:S(2)}, u32[]{:S(2)}) collective-permute-start(bf16[2,64,256]{2,1,0:T(8,128)(2,1)S(1)} %fusion.80), channel_id=1, source_target_pairs={{0,32},{32,0},{8,40},{40,8},{16,48},{48,16},{24,56},{56,24},{64,96... | collective-permute-start | bytes 196616 | tf_op jit(solution)/shard_map/ppermute | solution.py:20
  28.2 5.5 %collective-permute-done.2 = bf16[2,64,256]{2,1,0:T(8,128)(2,1)S(1)} collective-permute-done((bf16[2,64,256]{2,1,0:T(8,128)(2,1)S(1)}, bf16[2,64,256]{2,1,0:T(8,128)(2,1)S(1)}, u32[]{:S(2)}, u32[]{:S(2)}) %collective-permute-start.2) | collective-permute-done | bytes 65568 | tf_op jit(solution)/shard_map/ppermute | solution.py:20
  33.8 0.2 copy.100
  34.1 2.3 %collective-permute-start.3 = (bf16[2,64,256]{2,1,0:T(8,128)(2,1)S(1)}, bf16[2,64,256]{2,1,0:T(8,128)(2,1)S(1)}, u32[]{:S(2)}, u32[]{:S(2)}) collective-permute-start(bf16[2,64,256]{2,1,0:T(8,128)(2,1)S(1)} %fusion.81), channel_id=1, source_target_pairs={{0,64},{64,0},{8,72},{72,8},{16,80},{80,16},{24,88},{88,24},{32,96... | collective-permute-start | bytes 196616 | tf_op jit(solution)/shard_map/ppermute | solution.py:20
  36.3 3.9 %collective-permute-done.3 = bf16[2,64,256]{2,1,0:T(8,128)(2,1)S(1)} collective-permute-done((bf16[2,64,256]{2,1,0:T(8,128)(2,1)S(1)}, bf16[2,64,256]{2,1,0:T(8,128)(2,1)S(1)}, u32[]{:S(2)}, u32[]{:S(2)}) %collective-permute-start.3) | collective-permute-done | bytes 65568 | tf_op jit(solution)/shard_map/ppermute | solution.py:20
  40.3 0.2 copy.103
  40.6 4.4 %collective-permute-start.4 = (bf16[2,64,256]{2,1,0:T(8,128)(2,1)S(1)}, bf16[2,64,256]{2,1,0:T(8,128)(2,1)S(1)}, u32[]{:S(2)}, u32[]{:S(2)}) collective-permute-start(bf16[2,64,256]{2,1,0:T(8,128)(2,1)S(1)} %fusion.82), channel_id=1, source_target_pairs={{0,128},{128,0},{8,136},{136,8},{16,144},{144,16},{24,152},{152,24... | collective-permute-start | bytes 196616 | tf_op jit(solution)/shard_map/ppermute | solution.py:20
  45.1 1.1 broadcast_in_dim.17
  46.2 14.3 %all-to-all-start.1 = ((bf16[64,32,256]{2,1,0:T(8,128)(2,1)}), bf16[64,32,256]{2,1,0:T(8,128)(2,1)S(1)}, u32[]{:S(2)}, u32[]{:S(2)}) async-start(bf16[64,32,256]{2,1,0:T(8,128)(2,1)} %broadcast_in_dim.17), calls=%async_computation.1 | async-start | bytes 2097152 | tf_op jit(solution)/shard_map/all_to_all | solution.py:31
  60.6 0.2 copy.106
  60.9 7.5 %collective-permute-start.5 = (bf16[2,64,256]{2,1,0:T(8,128)(2,1)S(1)}, bf16[2,64,256]{2,1,0:T(8,128)(2,1)S(1)}, u32[]{:S(2)}, u32[]{:S(2)}) collective-permute-start(bf16[2,64,256]{2,1,0:T(8,128)(2,1)S(1)} %fusion.50), channel_id=1, source_target_pairs={{0,256},{256,0},{8,264},{264,8},{16,272},{272,16},{24,280},{280,24... | collective-permute-start | bytes 196616 | tf_op jit(solution)/shard_map/ppermute | solution.py:20
  68.4 19.8 %collective-permute-done.5 = bf16[2,64,256]{2,1,0:T(8,128)(2,1)S(1)} collective-permute-done((bf16[2,64,256]{2,1,0:T(8,128)(2,1)S(1)}, bf16[2,64,256]{2,1,0:T(8,128)(2,1)S(1)}, u32[]{:S(2)}, u32[]{:S(2)}) %collective-permute-start.5) | collective-permute-done | bytes 65568 | tf_op jit(solution)/shard_map/ppermute | solution.py:20
  88.2 0.2 fusion.99
  88.5 0.2 fusion.100
  88.8 0.2 convolution_convert_fusion.3
  89.1 0.4 convolution_convert_fusion
  89.5 0.2 fusion.52
  89.6 0.2 fusion.3
  89.9 0.2 fusion.51
  90.1 0.8 copy-done.6
  90.8 0.2 fusion.6
  91.2 0.2 fusion.76
  91.4 0.2 fusion.73
  91.7 3.3 %collective-permute-start.6 = (bf16[2,64,256]{2,1,0:T(8,128)(2,1)S(1)}, bf16[2,64,256]{2,1,0:T(8,128)(2,1)S(1)}, u32[]{:S(2)}, u32[]{:S(2)}) collective-permute-start(bf16[2,64,256]{2,1,0:T(8,128)(2,1)S(1)} %fusion.17), channel_id=1, source_target_pairs={{0,256},{256,0},{8,264},{264,8},{16,272},{272,16},{24,280},{280,24... | collective-permute-start | bytes 196616 | tf_op jit(solution)/shard_map/ppermute | solution.py:20
  95.0 0.2 convolution_convert_fusion.4
  95.2 7.1 %collective-permute-done.6 = bf16[2,64,256]{2,1,0:T(8,128)(2,1)S(1)} collective-permute-done((bf16[2,64,256]{2,1,0:T(8,128)(2,1)S(1)}, bf16[2,64,256]{2,1,0:T(8,128)(2,1)S(1)}, u32[]{:S(2)}, u32[]{:S(2)}) %collective-permute-start.6) | collective-permute-done | bytes 65568 | tf_op jit(solution)/shard_map/ppermute | solution.py:20
  102.3 0.1 copy.118
  102.6 2.0 %collective-permute-start.7 = (bf16[2,64,256]{2,1,0:T(8,128)(2,1)S(1)}, bf16[2,64,256]{2,1,0:T(8,128)(2,1)S(1)}, u32[]{:S(2)}, u32[]{:S(2)}) collective-permute-start(bf16[2,64,256]{2,1,0:T(8,128)(2,1)S(1)} %fusion.20), channel_id=1, source_target_pairs={{0,128},{128,0},{8,136},{136,8},{16,144},{144,16},{24,152},{152,24... | collective-permute-start | bytes 196616 | tf_op jit(solution)/shard_map/ppermute | solution.py:20
  104.6 0.7 copy.136
  105.3 4.4 %collective-permute-done.7 = bf16[2,64,256]{2,1,0:T(8,128)(2,1)S(1)} collective-permute-done((bf16[2,64,256]{2,1,0:T(8,128)(2,1)S(1)}, bf16[2,64,256]{2,1,0:T(8,128)(2,1)S(1)}, u32[]{:S(2)}, u32[]{:S(2)}) %collective-permute-start.7) | collective-permute-done | bytes 65568 | tf_op jit(solution)/shard_map/ppermute | solution.py:20
  109.7 0.1 copy.121
  109.9 0.7 fusion.23
  110.6 1.9 %collective-permute-start.8 = (bf16[2,64,256]{2,1,0:T(8,128)(2,1)}, bf16[2,64,256]{2,1,0:T(8,128)(2,1)}, u32[]{:S(2)}, u32[]{:S(2)}) collective-permute-start(bf16[2,64,256]{2,1,0:T(8,128)(2,1)} %fusion.23), channel_id=1, source_target_pairs={{0,64},{64,0},{8,72},{72,8},{16,80},{80,16},{24,88},{88,24},{32,96... | collective-permute-start | bytes 196616 | tf_op jit(solution)/shard_map/ppermute | solution.py:20
  112.5 0.4 convolution_bitcast_fusion
  112.9 1.3 copy.135
  114.3 8.5 %all-to-all-start.2 = ((bf16[64,32,256]{2,1,0:T(8,128)(2,1)}), bf16[64,32,256]{2,1,0:T(8,128)(2,1)S(1)}, u32[]{:S(2)}, u32[]{:S(2)}) async-start(bf16[64,32,256]{2,1,0:T(8,128)(2,1)} %bitcast.41), calls=%async_computation.2 | async-start | bytes 2097152 | tf_op jit(solution)/shard_map/all_to_all | solution.py:41
  122.8 0.9 add_multiply_fusion.3
  123.6 0.1 copy.124
  123.9 7.4 %collective-permute-start.9 = (bf16[2,64,256]{2,1,0:T(8,128)(2,1)S(1)}, bf16[2,64,256]{2,1,0:T(8,128)(2,1)S(1)}, u32[]{:S(2)}, u32[]{:S(2)}) collective-permute-start(bf16[2,64,256]{2,1,0:T(8,128)(2,1)S(1)} %fusion.26), channel_id=1, source_target_pairs={{0,32},{32,0},{8,40},{40,8},{16,48},{48,16},{24,56},{56,24},{64,96... | collective-permute-start | bytes 196616 | tf_op jit(solution)/shard_map/ppermute | solution.py:20
  131.3 0.2 convolution_convert_fusion.1
  131.5 18.2 %collective-permute-done.9 = bf16[2,64,256]{2,1,0:T(8,128)(2,1)S(1)} collective-permute-done((bf16[2,64,256]{2,1,0:T(8,128)(2,1)S(1)}, bf16[2,64,256]{2,1,0:T(8,128)(2,1)S(1)}, u32[]{:S(2)}, u32[]{:S(2)}) %collective-permute-start.9) | collective-permute-done | bytes 65568 | tf_op jit(solution)/shard_map/ppermute | solution.py:20
  149.8 0.1 copy.127
  150.0 2.1 %collective-permute-start.10 = (bf16[2,64,256]{2,1,0:T(8,128)(2,1)S(1)}, bf16[2,64,256]{2,1,0:T(8,128)(2,1)S(1)}, u32[]{:S(2)}, u32[]{:S(2)}) collective-permute-start(bf16[2,64,256]{2,1,0:T(8,128)(2,1)S(1)} %fusion.15), channel_id=1, source_target_pairs={{0,16},{16,0},{8,24},{24,8},{32,48},{48,32},{40,56},{56,40},{64,80... | collective-permute-start | bytes 196616 | tf_op jit(solution)/shard_map/ppermute | solution.py:20
  152.2 0.2 convolution_convert_fusion.2
  152.4 4.8 %collective-permute-done.10 = bf16[2,64,256]{2,1,0:T(8,128)(2,1)S(1)} collective-permute-done((bf16[2,64,256]{2,1,0:T(8,128)(2,1)S(1)}, bf16[2,64,256]{2,1,0:T(8,128)(2,1)S(1)}, u32[]{:S(2)}, u32[]{:S(2)}) %collective-permute-start.10) | collective-permute-done | bytes 65568 | tf_op jit(solution)/shard_map/ppermute | solution.py:20
  157.2 0.1 copy.130
  157.5 3.5 %collective-permute-start.11 = (bf16[2,64,256]{2,1,0:T(8,128)(2,1)S(1)}, bf16[2,64,256]{2,1,0:T(8,128)(2,1)S(1)}, u32[]{:S(2)}, u32[]{:S(2)}) collective-permute-start(bf16[2,64,256]{2,1,0:T(8,128)(2,1)S(1)} %fusion.28), channel_id=1, source_target_pairs={{0,8},{8,0},{16,24},{24,16},{32,40},{40,32},{48,56},{56,48},{64,72... | collective-permute-start | bytes 196616 | tf_op jit(solution)/shard_map/ppermute | solution.py:20
  161.0 0.7 copy.137
  161.8 1.8 %collective-permute-done.11 = bf16[2,64,256]{2,1,0:T(8,128)(2,1)S(1)} collective-permute-done((bf16[2,64,256]{2,1,0:T(8,128)(2,1)S(1)}, bf16[2,64,256]{2,1,0:T(8,128)(2,1)S(1)}, u32[]{:S(2)}, u32[]{:S(2)}) %collective-permute-start.11) | collective-permute-done | bytes 65568 | tf_op jit(solution)/shard_map/ppermute | solution.py:20
  163.7 0.1 copy.133
  163.9 0.7 slice_bitcast_fusion
  164.6 0.8 convert_reduce_fusion
  (78 shorter events, 1.9 us)
Async XLA Ops:
  0.6 5.8 %copy-start.3 = (bf16[128,256]{1,0:T(8,128)(2,1)S(1)}, bf16[128,256]{1,0:T(8,128)(2,1)}, u32[]{:S(2)}) copy-start(bf16[128,256]{1,0:T(8,128)(2,1)} %param.8) | copy-start | bytes 196612
  2.7 12.4 %copy-start = (bf16[128,256]{1,0:T(8,128)(2,1)S(1)}, bf16[128,256]{1,0:T(8,128)(2,1)}, u32[]{:S(2)}) copy-start(bf16[128,256]{1,0:T(8,128)(2,1)} %param.6) | copy-start | bytes 196612
  2.8 12.4 %copy-start.1 = (bf16[128,256]{1,0:T(8,128)(2,1)S(1)}, bf16[128,256]{1,0:T(8,128)(2,1)}, u32[]{:S(2)}) copy-start(bf16[128,256]{1,0:T(8,128)(2,1)} %param.7) | copy-start | bytes 196612
  2.8 12.4 %collective-permute-start = (bf16[2,64,256]{2,1,0:T(8,128)(2,1)S(1)}, bf16[2,64,256]{2,1,0:T(8,128)(2,1)S(1)}, u32[]{:S(2)}, u32[]{:S(2)}) collective-permute-start(bf16[2,64,256]{2,1,0:T(8,128)(2,1)S(1)} %fusion.49), channel_id=1, source_target_pairs={{0,8},{8,0},{16,24},{24,16},{32,40},{40,32},{48,56},{56,48},{64,72... | collective-permute-start | bytes 196616 | tf_op jit(solution)/shard_map/ppermute | solution.py:20
  7.4 37.6 %all-to-all-start = ((bf16[8,128,256]{1,2,0:T(8,128)(2,1)}), bf16[8,128,256]{1,2,0:T(8,128)(2,1)S(1)}, u32[]{:S(2)}, u32[]{:S(2)}) async-start(bf16[8,128,256]{1,2,0:T(8,128)(2,1)} %broadcast_in_dim.16), calls=%async_computation | async-start | bytes 1048576 | tf_op jit(solution)/shard_map/all_to_all | solution.py:31
  15.5 7.1 %collective-permute-start.1 = (bf16[2,64,256]{2,1,0:T(8,128)(2,1)S(1)}, bf16[2,64,256]{2,1,0:T(8,128)(2,1)S(1)}, u32[]{:S(2)}, u32[]{:S(2)}) collective-permute-start(bf16[2,64,256]{2,1,0:T(8,128)(2,1)S(1)} %fusion.79), channel_id=1, source_target_pairs={{0,16},{16,0},{8,24},{24,8},{32,48},{48,32},{40,56},{56,40},{64,80... | collective-permute-start | bytes 196616 | tf_op jit(solution)/shard_map/ppermute | solution.py:20
  22.9 10.8 %collective-permute-start.2 = (bf16[2,64,256]{2,1,0:T(8,128)(2,1)S(1)}, bf16[2,64,256]{2,1,0:T(8,128)(2,1)S(1)}, u32[]{:S(2)}, u32[]{:S(2)}) collective-permute-start(bf16[2,64,256]{2,1,0:T(8,128)(2,1)S(1)} %fusion.80), channel_id=1, source_target_pairs={{0,32},{32,0},{8,40},{40,8},{16,48},{48,16},{24,56},{56,24},{64,96... | collective-permute-start | bytes 196616 | tf_op jit(solution)/shard_map/ppermute | solution.py:20
  34.1 6.2 %collective-permute-start.3 = (bf16[2,64,256]{2,1,0:T(8,128)(2,1)S(1)}, bf16[2,64,256]{2,1,0:T(8,128)(2,1)S(1)}, u32[]{:S(2)}, u32[]{:S(2)}) collective-permute-start(bf16[2,64,256]{2,1,0:T(8,128)(2,1)S(1)} %fusion.81), channel_id=1, source_target_pairs={{0,64},{64,0},{8,72},{72,8},{16,80},{80,16},{24,88},{88,24},{32,96... | collective-permute-start | bytes 196616 | tf_op jit(solution)/shard_map/ppermute | solution.py:20
  40.3 4.8 %copy-start.4 = (bf16[32,256]{1,0:T(8,128)(2,1)S(1)}, bf16[32,256]{1,0:T(8,128)(2,1)}, u32[]{:S(2)}) copy-start(bf16[32,256]{1,0:T(8,128)(2,1)} %param.9) | copy-start | bytes 49156
  40.6 19.9 %collective-permute-start.4 = (bf16[2,64,256]{2,1,0:T(8,128)(2,1)S(1)}, bf16[2,64,256]{2,1,0:T(8,128)(2,1)S(1)}, u32[]{:S(2)}, u32[]{:S(2)}) collective-permute-start(bf16[2,64,256]{2,1,0:T(8,128)(2,1)S(1)} %fusion.82), channel_id=1, source_target_pairs={{0,128},{128,0},{8,136},{136,8},{16,144},{144,16},{24,152},{152,24... | collective-permute-start | bytes 196616 | tf_op jit(solution)/shard_map/ppermute | solution.py:20
  46.2 42.9 %all-to-all-start.1 = ((bf16[64,32,256]{2,1,0:T(8,128)(2,1)}), bf16[64,32,256]{2,1,0:T(8,128)(2,1)S(1)}, u32[]{:S(2)}, u32[]{:S(2)}) async-start(bf16[64,32,256]{2,1,0:T(8,128)(2,1)} %broadcast_in_dim.17), calls=%async_computation.1 | async-start | bytes 2097152 | tf_op jit(solution)/shard_map/all_to_all | solution.py:31
  60.5 27.6 %copy-start.2 = (bf16[128,256]{1,0:T(8,128)(2,1)S(1)}, bf16[128,256]{1,0:T(8,128)(2,1)}, u32[]{:S(2)}) copy-start(bf16[128,256]{1,0:T(8,128)(2,1)} %param.5) | copy-start | bytes 196612
  60.9 27.3 %collective-permute-start.5 = (bf16[2,64,256]{2,1,0:T(8,128)(2,1)S(1)}, bf16[2,64,256]{2,1,0:T(8,128)(2,1)S(1)}, u32[]{:S(2)}, u32[]{:S(2)}) collective-permute-start(bf16[2,64,256]{2,1,0:T(8,128)(2,1)S(1)} %fusion.50), channel_id=1, source_target_pairs={{0,256},{256,0},{8,264},{264,8},{16,272},{272,16},{24,280},{280,24... | collective-permute-start | bytes 196616 | tf_op jit(solution)/shard_map/ppermute | solution.py:20
  88.1 1.5 copy-start.5
  89.9 1.0 copy-start.6
  91.7 10.6 %collective-permute-start.6 = (bf16[2,64,256]{2,1,0:T(8,128)(2,1)S(1)}, bf16[2,64,256]{2,1,0:T(8,128)(2,1)S(1)}, u32[]{:S(2)}, u32[]{:S(2)}) collective-permute-start(bf16[2,64,256]{2,1,0:T(8,128)(2,1)S(1)} %fusion.17), channel_id=1, source_target_pairs={{0,256},{256,0},{8,264},{264,8},{16,272},{272,16},{24,280},{280,24... | collective-permute-start | bytes 196616 | tf_op jit(solution)/shard_map/ppermute | solution.py:20
  102.6 7.1 %collective-permute-start.7 = (bf16[2,64,256]{2,1,0:T(8,128)(2,1)S(1)}, bf16[2,64,256]{2,1,0:T(8,128)(2,1)S(1)}, u32[]{:S(2)}, u32[]{:S(2)}) collective-permute-start(bf16[2,64,256]{2,1,0:T(8,128)(2,1)S(1)} %fusion.20), channel_id=1, source_target_pairs={{0,128},{128,0},{8,136},{136,8},{16,144},{144,16},{24,152},{152,24... | collective-permute-start | bytes 196616 | tf_op jit(solution)/shard_map/ppermute | solution.py:20
  110.6 12.2 %collective-permute-start.8 = (bf16[2,64,256]{2,1,0:T(8,128)(2,1)}, bf16[2,64,256]{2,1,0:T(8,128)(2,1)}, u32[]{:S(2)}, u32[]{:S(2)}) collective-permute-start(bf16[2,64,256]{2,1,0:T(8,128)(2,1)} %fusion.23), channel_id=1, source_target_pairs={{0,64},{64,0},{8,72},{72,8},{16,80},{80,16},{24,88},{88,24},{32,96... | collective-permute-start | bytes 196616 | tf_op jit(solution)/shard_map/ppermute | solution.py:20
  114.3 50.3 %all-to-all-start.2 = ((bf16[64,32,256]{2,1,0:T(8,128)(2,1)}), bf16[64,32,256]{2,1,0:T(8,128)(2,1)S(1)}, u32[]{:S(2)}, u32[]{:S(2)}) async-start(bf16[64,32,256]{2,1,0:T(8,128)(2,1)} %bitcast.41), calls=%async_computation.2 | async-start | bytes 2097152 | tf_op jit(solution)/shard_map/all_to_all | solution.py:41
  123.9 25.9 %collective-permute-start.9 = (bf16[2,64,256]{2,1,0:T(8,128)(2,1)S(1)}, bf16[2,64,256]{2,1,0:T(8,128)(2,1)S(1)}, u32[]{:S(2)}, u32[]{:S(2)}) collective-permute-start(bf16[2,64,256]{2,1,0:T(8,128)(2,1)S(1)} %fusion.26), channel_id=1, source_target_pairs={{0,32},{32,0},{8,40},{40,8},{16,48},{48,16},{24,56},{56,24},{64,96... | collective-permute-start | bytes 196616 | tf_op jit(solution)/shard_map/ppermute | solution.py:20
  150.0 7.2 %collective-permute-start.10 = (bf16[2,64,256]{2,1,0:T(8,128)(2,1)S(1)}, bf16[2,64,256]{2,1,0:T(8,128)(2,1)S(1)}, u32[]{:S(2)}, u32[]{:S(2)}) collective-permute-start(bf16[2,64,256]{2,1,0:T(8,128)(2,1)S(1)} %fusion.15), channel_id=1, source_target_pairs={{0,16},{16,0},{8,24},{24,8},{32,48},{48,32},{40,56},{56,40},{64,80... | collective-permute-start | bytes 196616 | tf_op jit(solution)/shard_map/ppermute | solution.py:20
  157.5 6.2 %collective-permute-start.11 = (bf16[2,64,256]{2,1,0:T(8,128)(2,1)S(1)}, bf16[2,64,256]{2,1,0:T(8,128)(2,1)S(1)}, u32[]{:S(2)}, u32[]{:S(2)}) collective-permute-start(bf16[2,64,256]{2,1,0:T(8,128)(2,1)S(1)} %fusion.28), channel_id=1, source_target_pairs={{0,8},{8,0},{16,24},{24,16},{32,40},{40,32},{48,56},{56,48},{64,72... | collective-permute-start | bytes 196616 | tf_op jit(solution)/shard_map/ppermute | solution.py:20

commit v12 on v11

--- a/solution.py
+++ b/solution.py
@@ -61,8 +61,14 @@
     scale = 1.0 / math.sqrt(HEAD)
     depth = lax.axis_size(SEQ).bit_length() - 1
     position = lax.axis_index(SEQ)
+    rows = lax.broadcasted_iota(jnp.int32, (tokens // 2, tokens), 0)
+    cols = lax.broadcasted_iota(jnp.int32, (tokens // 2, tokens), 1)
+    pool = jnp.where(cols // 2 == rows, 0.5, 0.0).astype(jnp.bfloat16)
     own_table = jnp.stack(
-        [pair_mean(keys[None].astype(jnp.float32))[0], pair_mean(values[None].astype(jnp.float32))[0]]
+        [
+            jnp.dot(pool, keys, preferred_element_type=jnp.float32),
+            jnp.dot(pool, values, preferred_element_type=jnp.float32),
+        ]
     )
     far_keys = []
     far_values = []

time: 167 us -> 169 us (1.012)
  matrix products: 3.36 us -> 5.37 us
    dot_general x0 -> x2, matrix products: none -> 2.01 us  [the longest x1 1.04 us: on_device(): jnp.dot(pool, values, preferred_element_type=jnp.float32)]
  transfers between devices with their start and end apart: 15 -> 15, of which waited for: 9 -> 9; matrix products, arithmetic and copies ran while one was open for 7% -> 8% of each run, Pallas kernels for 0% -> 0%
where the time goes in v12:
time: 169 us; the launch traced here: 167 us
  starting transfers between devices  75.6 us (45%)
  waiting for transfers between devices  70.5 us (42%)
  local copies, waits for them, and re-layouts  10.6 us (6%)
  matrix products  5.37 us (3%)
  other arithmetic  3.36 us (2%)
    ppermute x12, waiting for transfers between devices, from_partner(): return lax.ppermute(block, axis, route)  70.5 us
    ppermute x12, starting transfers between devices, from_partner(): return lax.ppermute(block, axis, route)  45.1 us
    all_to_all x2, starting transfers between devices, from_everyone(): return lax.all_to_all(copies, axis, split_axis=0, concat_axis=0, tiled=True)  22 us
    all_to_all x1, starting transfers between devices, own_rows(): lax.all_to_all(parts, axes, 0, 0, tiled=True).astype(jnp.float32)  8.51 us
  transfers between devices with their start and end apart: 15, of which 9 were waited for; matrix products, arithmetic and copies ran while one was open for 8% of the time, Pallas kernels for 0%

profile of v12, /device:TPU:6, one launch (start us, length us, event | category | flops | bytes accessed | tf_op | source)
XLA Modules:
  0.0 166.8 jit_solution(14965709304919897963)
XLA Ops:
  0.7 1.0 convolution_bitcast_fusion.2
  1.6 1.0 convolution_bitcast_fusion.1
  2.7 3.5 %collective-permute-start = (bf16[2,64,256]{2,1,0:T(8,128)(2,1)S(1)}, bf16[2,64,256]{2,1,0:T(8,128)(2,1)S(1)}, u32[]{:S(2)}, u32[]{:S(2)}) collective-permute-start(bf16[2,64,256]{2,1,0:T(8,128)(2,1)S(1)} %fusion.49), channel_id=1, source_target_pairs={{0,8},{8,0},{16,24},{24,16},{32,40},{40,32},{48,56},{56,48},{64,72... | collective-permute-start | bytes 196616 | tf_op jit(solution)/shard_map/ppermute | solution.py:20
  6.2 1.0 copy.39
  7.2 0.9 broadcast_in_dim.26
  8.0 7.7 %all-to-all-start = ((bf16[8,128,256]{1,2,0:T(8,128)(2,1)}), bf16[8,128,256]{1,2,0:T(8,128)(2,1)S(1)}, u32[]{:S(2)}, u32[]{:S(2)}) async-start(bf16[8,128,256]{1,2,0:T(8,128)(2,1)} %broadcast_in_dim.26), calls=%async_computation | async-start | bytes 1048576 | tf_op jit(solution)/shard_map/all_to_all | solution.py:31
  15.8 0.1 reshape.94
  16.0 0.2 fusion.101
  16.2 1.9 %collective-permute-start.1 = (bf16[2,64,256]{2,1,0:T(8,128)(2,1)S(1)}, bf16[2,64,256]{2,1,0:T(8,128)(2,1)S(1)}, u32[]{:S(2)}, u32[]{:S(2)}) collective-permute-start(bf16[2,64,256]{2,1,0:T(8,128)(2,1)S(1)} %fusion.89), channel_id=1, source_target_pairs={{0,16},{16,0},{8,24},{24,8},{32,48},{48,32},{40,56},{56,40},{64,80... | collective-permute-start | bytes 196616 | tf_op jit(solution)/shard_map/ppermute | solution.py:20
  18.2 5.1 %collective-permute-done.1 = bf16[2,64,256]{2,1,0:T(8,128)(2,1)S(1)} collective-permute-done((bf16[2,64,256]{2,1,0:T(8,128)(2,1)S(1)}, bf16[2,64,256]{2,1,0:T(8,128)(2,1)S(1)}, u32[]{:S(2)}, u32[]{:S(2)}) %collective-permute-start.1) | collective-permute-done | bytes 65568 | tf_op jit(solution)/shard_map/ppermute | solution.py:20
  23.4 0.1 reshape.95
  23.5 0.2 fusion.100
  23.8 5.3 %collective-permute-start.2 = (bf16[2,64,256]{2,1,0:T(8,128)(2,1)S(1)}, bf16[2,64,256]{2,1,0:T(8,128)(2,1)S(1)}, u32[]{:S(2)}, u32[]{:S(2)}) collective-permute-start(bf16[2,64,256]{2,1,0:T(8,128)(2,1)S(1)} %fusion.90), channel_id=1, source_target_pairs={{0,32},{32,0},{8,40},{40,8},{16,48},{48,16},{24,56},{56,24},{64,96... | collective-permute-start | bytes 196616 | tf_op jit(solution)/shard_map/ppermute | solution.py:20
  29.0 5.5 %collective-permute-done.2 = bf16[2,64,256]{2,1,0:T(8,128)(2,1)S(1)} collective-permute-done((bf16[2,64,256]{2,1,0:T(8,128)(2,1)S(1)}, bf16[2,64,256]{2,1,0:T(8,128)(2,1)S(1)}, u32[]{:S(2)}, u32[]{:S(2)}) %collective-permute-start.2) | collective-permute-done | bytes 65568 | tf_op jit(solution)/shard_map/ppermute | solution.py:20
  34.7 0.2 fusion.99
  35.0 2.3 %collective-permute-start.3 = (bf16[2,64,256]{2,1,0:T(8,128)(2,1)S(1)}, bf16[2,64,256]{2,1,0:T(8,128)(2,1)S(1)}, u32[]{:S(2)}, u32[]{:S(2)}) collective-permute-start(bf16[2,64,256]{2,1,0:T(8,128)(2,1)S(1)} %fusion.91), channel_id=1, source_target_pairs={{0,64},{64,0},{8,72},{72,8},{16,80},{80,16},{24,88},{88,24},{32,96... | collective-permute-start | bytes 196616 | tf_op jit(solution)/shard_map/ppermute | solution.py:20
  37.3 3.9 %collective-permute-done.3 = bf16[2,64,256]{2,1,0:T(8,128)(2,1)S(1)} collective-permute-done((bf16[2,64,256]{2,1,0:T(8,128)(2,1)S(1)}, bf16[2,64,256]{2,1,0:T(8,128)(2,1)S(1)}, u32[]{:S(2)}, u32[]{:S(2)}) %collective-permute-start.3) | collective-permute-done | bytes 65568 | tf_op jit(solution)/shard_map/ppermute | solution.py:20
  41.4 0.2 fusion.98
  41.6 4.4 %collective-permute-start.4 = (bf16[2,64,256]{2,1,0:T(8,128)(2,1)S(1)}, bf16[2,64,256]{2,1,0:T(8,128)(2,1)S(1)}, u32[]{:S(2)}, u32[]{:S(2)}) collective-permute-start(bf16[2,64,256]{2,1,0:T(8,128)(2,1)S(1)} %fusion.92), channel_id=1, source_target_pairs={{0,128},{128,0},{8,136},{136,8},{16,144},{144,16},{24,152},{152,24... | collective-permute-start | bytes 196616 | tf_op jit(solution)/shard_map/ppermute | solution.py:20
  46.1 1.1 broadcast_in_dim.27
  47.2 14.3 %all-to-all-start.1 = ((bf16[64,32,256]{2,1,0:T(8,128)(2,1)}), bf16[64,32,256]{2,1,0:T(8,128)(2,1)S(1)}, u32[]{:S(2)}, u32[]{:S(2)}) async-start(bf16[64,32,256]{2,1,0:T(8,128)(2,1)} %broadcast_in_dim.27), calls=%async_computation.1 | async-start | bytes 2097152 | tf_op jit(solution)/shard_map/all_to_all | solution.py:31
  61.6 0.2 copy.36
  61.9 7.5 %collective-permute-start.5 = (bf16[2,64,256]{2,1,0:T(8,128)(2,1)S(1)}, bf16[2,64,256]{2,1,0:T(8,128)(2,1)S(1)}, u32[]{:S(2)}, u32[]{:S(2)}) collective-permute-start(bf16[2,64,256]{2,1,0:T(8,128)(2,1)S(1)} %fusion.50), channel_id=1, source_target_pairs={{0,256},{256,0},{8,264},{264,8},{16,272},{272,16},{24,280},{280,24... | collective-permute-start | bytes 196616 | tf_op jit(solution)/shard_map/ppermute | solution.py:20
  69.4 19.8 %collective-permute-done.5 = bf16[2,64,256]{2,1,0:T(8,128)(2,1)S(1)} collective-permute-done((bf16[2,64,256]{2,1,0:T(8,128)(2,1)S(1)}, bf16[2,64,256]{2,1,0:T(8,128)(2,1)S(1)}, u32[]{:S(2)}, u32[]{:S(2)}) %collective-permute-start.5) | collective-permute-done | bytes 65568 | tf_op jit(solution)/shard_map/ppermute | solution.py:20
  89.2 0.2 fusion.102
  89.6 0.2 fusion.103
  89.9 0.2 convolution_convert_fusion.3
  90.1 0.4 convolution_convert_fusion
  90.5 0.2 fusion.52
  90.7 0.2 fusion.3
  90.9 0.2 fusion.51
  91.1 0.8 copy-done.5
  91.9 0.2 fusion.6
  92.2 0.2 fusion.72
  92.5 0.2 fusion.69
  92.8 3.2 %collective-permute-start.6 = (bf16[2,64,256]{2,1,0:T(8,128)(2,1)S(1)}, bf16[2,64,256]{2,1,0:T(8,128)(2,1)S(1)}, u32[]{:S(2)}, u32[]{:S(2)}) collective-permute-start(bf16[2,64,256]{2,1,0:T(8,128)(2,1)S(1)} %fusion.17), channel_id=1, source_target_pairs={{0,256},{256,0},{8,264},{264,8},{16,272},{272,16},{24,280},{280,24... | collective-permute-start | bytes 196616 | tf_op jit(solution)/shard_map/ppermute | solution.py:20
  96.0 0.2 convolution_convert_fusion.4
  96.2 7.1 %collective-permute-done.6 = bf16[2,64,256]{2,1,0:T(8,128)(2,1)S(1)} collective-permute-done((bf16[2,64,256]{2,1,0:T(8,128)(2,1)S(1)}, bf16[2,64,256]{2,1,0:T(8,128)(2,1)S(1)}, u32[]{:S(2)}, u32[]{:S(2)}) %collective-permute-start.6) | collective-permute-done | bytes 65568 | tf_op jit(solution)/shard_map/ppermute | solution.py:20
  103.5 0.2 reshape.101
  103.7 2.0 %collective-permute-start.7 = (bf16[2,64,256]{2,1,0:T(8,128)(2,1)S(1)}, bf16[2,64,256]{2,1,0:T(8,128)(2,1)S(1)}, u32[]{:S(2)}, u32[]{:S(2)}) collective-permute-start(bf16[2,64,256]{2,1,0:T(8,128)(2,1)S(1)} %fusion.20), channel_id=1, source_target_pairs={{0,128},{128,0},{8,136},{136,8},{16,144},{144,16},{24,152},{152,24... | collective-permute-start | bytes 196616 | tf_op jit(solution)/shard_map/ppermute | solution.py:20
  105.7 0.7 copy.49
  106.5 4.4 %collective-permute-done.7 = bf16[2,64,256]{2,1,0:T(8,128)(2,1)S(1)} collective-permute-done((bf16[2,64,256]{2,1,0:T(8,128)(2,1)S(1)}, bf16[2,64,256]{2,1,0:T(8,128)(2,1)S(1)}, u32[]{:S(2)}, u32[]{:S(2)}) %collective-permute-start.7) | collective-permute-done | bytes 65568 | tf_op jit(solution)/shard_map/ppermute | solution.py:20
  110.9 0.2 reshape.102
  111.1 0.7 fusion.23
  111.8 1.9 %collective-permute-start.8 = (bf16[2,64,256]{2,1,0:T(8,128)(2,1)}, bf16[2,64,256]{2,1,0:T(8,128)(2,1)}, u32[]{:S(2)}, u32[]{:S(2)}) collective-permute-start(bf16[2,64,256]{2,1,0:T(8,128)(2,1)} %fusion.23), channel_id=1, source_target_pairs={{0,64},{64,0},{8,72},{72,8},{16,80},{80,16},{24,88},{88,24},{32,96... | collective-permute-start | bytes 196616 | tf_op jit(solution)/shard_map/ppermute | solution.py:20
  113.7 0.4 convolution_bitcast_fusion
  114.1 1.3 copy.48
  115.5 8.5 %all-to-all-start.2 = ((bf16[64,32,256]{2,1,0:T(8,128)(2,1)}), bf16[64,32,256]{2,1,0:T(8,128)(2,1)S(1)}, u32[]{:S(2)}, u32[]{:S(2)}) async-start(bf16[64,32,256]{2,1,0:T(8,128)(2,1)} %bitcast.31), calls=%async_computation.2 | async-start | bytes 2097152 | tf_op jit(solution)/shard_map/all_to_all | solution.py:41
  124.0 0.9 add_multiply_fusion.3
  125.0 0.2 reshape.103
  125.2 7.4 %collective-permute-start.9 = (bf16[2,64,256]{2,1,0:T(8,128)(2,1)S(1)}, bf16[2,64,256]{2,1,0:T(8,128)(2,1)S(1)}, u32[]{:S(2)}, u32[]{:S(2)}) collective-permute-start(bf16[2,64,256]{2,1,0:T(8,128)(2,1)S(1)} %fusion.26), channel_id=1, source_target_pairs={{0,32},{32,0},{8,40},{40,8},{16,48},{48,16},{24,56},{56,24},{64,96... | collective-permute-start | bytes 196616 | tf_op jit(solution)/shard_map/ppermute | solution.py:20
  132.6 0.2 convolution_convert_fusion.1
  132.8 18.1 %collective-permute-done.9 = bf16[2,64,256]{2,1,0:T(8,128)(2,1)S(1)} collective-permute-done((bf16[2,64,256]{2,1,0:T(8,128)(2,1)S(1)}, bf16[2,64,256]{2,1,0:T(8,128)(2,1)S(1)}, u32[]{:S(2)}, u32[]{:S(2)}) %collective-permute-start.9) | collective-permute-done | bytes 65568 | tf_op jit(solution)/shard_map/ppermute | solution.py:20
  151.1 0.2 reshape.104
  151.3 2.1 %collective-permute-start.10 = (bf16[2,64,256]{2,1,0:T(8,128)(2,1)S(1)}, bf16[2,64,256]{2,1,0:T(8,128)(2,1)S(1)}, u32[]{:S(2)}, u32[]{:S(2)}) collective-permute-start(bf16[2,64,256]{2,1,0:T(8,128)(2,1)S(1)} %fusion.15), channel_id=1, source_target_pairs={{0,16},{16,0},{8,24},{24,8},{32,48},{48,32},{40,56},{56,40},{64,80... | collective-permute-start | bytes 196616 | tf_op jit(solution)/shard_map/ppermute | solution.py:20
  153.4 0.2 convolution_convert_fusion.2
  153.7 4.8 %collective-permute-done.10 = bf16[2,64,256]{2,1,0:T(8,128)(2,1)S(1)} collective-permute-done((bf16[2,64,256]{2,1,0:T(8,128)(2,1)S(1)}, bf16[2,64,256]{2,1,0:T(8,128)(2,1)S(1)}, u32[]{:S(2)}, u32[]{:S(2)}) %collective-permute-start.10) | collective-permute-done | bytes 65568 | tf_op jit(solution)/shard_map/ppermute | solution.py:20
  158.6 0.2 reshape.105
  158.8 3.6 %collective-permute-start.11 = (bf16[2,64,256]{2,1,0:T(8,128)(2,1)S(1)}, bf16[2,64,256]{2,1,0:T(8,128)(2,1)S(1)}, u32[]{:S(2)}, u32[]{:S(2)}) collective-permute-start(bf16[2,64,256]{2,1,0:T(8,128)(2,1)S(1)} %fusion.28), channel_id=1, source_target_pairs={{0,8},{8,0},{16,24},{24,16},{32,40},{40,32},{48,56},{56,48},{64,72... | collective-permute-start | bytes 196616 | tf_op jit(solution)/shard_map/ppermute | solution.py:20
  162.4 0.7 copy.50
  163.2 1.8 %collective-permute-done.11 = bf16[2,64,256]{2,1,0:T(8,128)(2,1)S(1)} collective-permute-done((bf16[2,64,256]{2,1,0:T(8,128)(2,1)S(1)}, bf16[2,64,256]{2,1,0:T(8,128)(2,1)S(1)}, u32[]{:S(2)}, u32[]{:S(2)}) %collective-permute-start.11) | collective-permute-done | bytes 65568 | tf_op jit(solution)/shard_map/ppermute | solution.py:20
  165.1 0.2 reshape.106
  165.3 0.7 slice_bitcast_fusion
  166.0 0.8 convert_reduce_fusion
  (70 shorter events, 2.0 us)
Async XLA Ops:
  1.6 14.1 %copy-start = (bf16[128,256]{1,0:T(8,128)(2,1)S(1)}, bf16[128,256]{1,0:T(8,128)(2,1)}, u32[]{:S(2)}) copy-start(bf16[128,256]{1,0:T(8,128)(2,1)} %param.6) | copy-start | bytes 196612
  1.6 14.1 %copy-start.1 = (bf16[128,256]{1,0:T(8,128)(2,1)S(1)}, bf16[128,256]{1,0:T(8,128)(2,1)}, u32[]{:S(2)}) copy-start(bf16[128,256]{1,0:T(8,128)(2,1)} %param.7) | copy-start | bytes 196612
  2.7 13.1 %collective-permute-start = (bf16[2,64,256]{2,1,0:T(8,128)(2,1)S(1)}, bf16[2,64,256]{2,1,0:T(8,128)(2,1)S(1)}, u32[]{:S(2)}, u32[]{:S(2)}) collective-permute-start(bf16[2,64,256]{2,1,0:T(8,128)(2,1)S(1)} %fusion.49), channel_id=1, source_target_pairs={{0,8},{8,0},{16,24},{24,16},{32,40},{40,32},{48,56},{56,48},{64,72... | collective-permute-start | bytes 196616 | tf_op jit(solution)/shard_map/ppermute | solution.py:20
  8.0 38.0 %all-to-all-start = ((bf16[8,128,256]{1,2,0:T(8,128)(2,1)}), bf16[8,128,256]{1,2,0:T(8,128)(2,1)S(1)}, u32[]{:S(2)}, u32[]{:S(2)}) async-start(bf16[8,128,256]{1,2,0:T(8,128)(2,1)} %broadcast_in_dim.26), calls=%async_computation | async-start | bytes 1048576 | tf_op jit(solution)/shard_map/all_to_all | solution.py:31
  16.2 7.1 %collective-permute-start.1 = (bf16[2,64,256]{2,1,0:T(8,128)(2,1)S(1)}, bf16[2,64,256]{2,1,0:T(8,128)(2,1)S(1)}, u32[]{:S(2)}, u32[]{:S(2)}) collective-permute-start(bf16[2,64,256]{2,1,0:T(8,128)(2,1)S(1)} %fusion.89), channel_id=1, source_target_pairs={{0,16},{16,0},{8,24},{24,8},{32,48},{48,32},{40,56},{56,40},{64,80... | collective-permute-start | bytes 196616 | tf_op jit(solution)/shard_map/ppermute | solution.py:20
  23.8 10.8 %collective-permute-start.2 = (bf16[2,64,256]{2,1,0:T(8,128)(2,1)S(1)}, bf16[2,64,256]{2,1,0:T(8,128)(2,1)S(1)}, u32[]{:S(2)}, u32[]{:S(2)}) collective-permute-start(bf16[2,64,256]{2,1,0:T(8,128)(2,1)S(1)} %fusion.90), channel_id=1, source_target_pairs={{0,32},{32,0},{8,40},{40,8},{16,48},{48,16},{24,56},{56,24},{64,96... | collective-permute-start | bytes 196616 | tf_op jit(solution)/shard_map/ppermute | solution.py:20
  35.0 6.2 %collective-permute-start.3 = (bf16[2,64,256]{2,1,0:T(8,128)(2,1)S(1)}, bf16[2,64,256]{2,1,0:T(8,128)(2,1)S(1)}, u32[]{:S(2)}, u32[]{:S(2)}) collective-permute-start(bf16[2,64,256]{2,1,0:T(8,128)(2,1)S(1)} %fusion.91), channel_id=1, source_target_pairs={{0,64},{64,0},{8,72},{72,8},{16,80},{80,16},{24,88},{88,24},{32,96... | collective-permute-start | bytes 196616 | tf_op jit(solution)/shard_map/ppermute | solution.py:20
  41.2 4.9 %copy-start.3 = (bf16[32,256]{1,0:T(8,128)(2,1)S(1)}, bf16[32,256]{1,0:T(8,128)(2,1)}, u32[]{:S(2)}) copy-start(bf16[32,256]{1,0:T(8,128)(2,1)} %param.9) | copy-start | bytes 49156
  41.6 19.9 %collective-permute-start.4 = (bf16[2,64,256]{2,1,0:T(8,128)(2,1)S(1)}, bf16[2,64,256]{2,1,0:T(8,128)(2,1)S(1)}, u32[]{:S(2)}, u32[]{:S(2)}) collective-permute-start(bf16[2,64,256]{2,1,0:T(8,128)(2,1)S(1)} %fusion.92), channel_id=1, source_target_pairs={{0,128},{128,0},{8,136},{136,8},{16,144},{144,16},{24,152},{152,24... | collective-permute-start | bytes 196616 | tf_op jit(solution)/shard_map/ppermute | solution.py:20
  47.2 42.9 %all-to-all-start.1 = ((bf16[64,32,256]{2,1,0:T(8,128)(2,1)}), bf16[64,32,256]{2,1,0:T(8,128)(2,1)S(1)}, u32[]{:S(2)}, u32[]{:S(2)}) async-start(bf16[64,32,256]{2,1,0:T(8,128)(2,1)} %broadcast_in_dim.27), calls=%async_computation.1 | async-start | bytes 2097152 | tf_op jit(solution)/shard_map/all_to_all | solution.py:31
  61.6 27.6 %copy-start.2 = (bf16[128,256]{1,0:T(8,128)(2,1)S(1)}, bf16[128,256]{1,0:T(8,128)(2,1)}, u32[]{:S(2)}) copy-start(bf16[128,256]{1,0:T(8,128)(2,1)} %param.5) | copy-start | bytes 196612
  61.9 27.3 %collective-permute-start.5 = (bf16[2,64,256]{2,1,0:T(8,128)(2,1)S(1)}, bf16[2,64,256]{2,1,0:T(8,128)(2,1)S(1)}, u32[]{:S(2)}, u32[]{:S(2)}) collective-permute-start(bf16[2,64,256]{2,1,0:T(8,128)(2,1)S(1)} %fusion.50), channel_id=1, source_target_pairs={{0,256},{256,0},{8,264},{264,8},{16,272},{272,16},{24,280},{280,24... | collective-permute-start | bytes 196616 | tf_op jit(solution)/shard_map/ppermute | solution.py:20
  89.2 1.5 copy-start.4
  90.9 1.0 copy-start.5
  92.8 10.6 %collective-permute-start.6 = (bf16[2,64,256]{2,1,0:T(8,128)(2,1)S(1)}, bf16[2,64,256]{2,1,0:T(8,128)(2,1)S(1)}, u32[]{:S(2)}, u32[]{:S(2)}) collective-permute-start(bf16[2,64,256]{2,1,0:T(8,128)(2,1)S(1)} %fusion.17), channel_id=1, source_target_pairs={{0,256},{256,0},{8,264},{264,8},{16,272},{272,16},{24,280},{280,24... | collective-permute-start | bytes 196616 | tf_op jit(solution)/shard_map/ppermute | solution.py:20
  103.7 7.1 %collective-permute-start.7 = (bf16[2,64,256]{2,1,0:T(8,128)(2,1)S(1)}, bf16[2,64,256]{2,1,0:T(8,128)(2,1)S(1)}, u32[]{:S(2)}, u32[]{:S(2)}) collective-permute-start(bf16[2,64,256]{2,1,0:T(8,128)(2,1)S(1)} %fusion.20), channel_id=1, source_target_pairs={{0,128},{128,0},{8,136},{136,8},{16,144},{144,16},{24,152},{152,24... | collective-permute-start | bytes 196616 | tf_op jit(solution)/shard_map/ppermute | solution.py:20
  111.8 12.2 %collective-permute-start.8 = (bf16[2,64,256]{2,1,0:T(8,128)(2,1)}, bf16[2,64,256]{2,1,0:T(8,128)(2,1)}, u32[]{:S(2)}, u32[]{:S(2)}) collective-permute-start(bf16[2,64,256]{2,1,0:T(8,128)(2,1)} %fusion.23), channel_id=1, source_target_pairs={{0,64},{64,0},{8,72},{72,8},{16,80},{80,16},{24,88},{88,24},{32,96... | collective-permute-start | bytes 196616 | tf_op jit(solution)/shard_map/ppermute | solution.py:20
  115.5 50.5 %all-to-all-start.2 = ((bf16[64,32,256]{2,1,0:T(8,128)(2,1)}), bf16[64,32,256]{2,1,0:T(8,128)(2,1)S(1)}, u32[]{:S(2)}, u32[]{:S(2)}) async-start(bf16[64,32,256]{2,1,0:T(8,128)(2,1)} %bitcast.31), calls=%async_computation.2 | async-start | bytes 2097152 | tf_op jit(solution)/shard_map/all_to_all | solution.py:41
  125.2 25.8 %collective-permute-start.9 = (bf16[2,64,256]{2,1,0:T(8,128)(2,1)S(1)}, bf16[2,64,256]{2,1,0:T(8,128)(2,1)S(1)}, u32[]{:S(2)}, u32[]{:S(2)}) collective-permute-start(bf16[2,64,256]{2,1,0:T(8,128)(2,1)S(1)} %fusion.26), channel_id=1, source_target_pairs={{0,32},{32,0},{8,40},{40,8},{16,48},{48,16},{24,56},{56,24},{64,96... | collective-permute-start | bytes 196616 | tf_op jit(solution)/shard_map/ppermute | solution.py:20
  151.3 7.2 %collective-permute-start.10 = (bf16[2,64,256]{2,1,0:T(8,128)(2,1)S(1)}, bf16[2,64,256]{2,1,0:T(8,128)(2,1)S(1)}, u32[]{:S(2)}, u32[]{:S(2)}) collective-permute-start(bf16[2,64,256]{2,1,0:T(8,128)(2,1)S(1)} %fusion.15), channel_id=1, source_target_pairs={{0,16},{16,0},{8,24},{24,8},{32,48},{48,32},{40,56},{56,40},{64,80... | collective-permute-start | bytes 196616 | tf_op jit(solution)/shard_map/ppermute | solution.py:20
  158.8 6.2 %collective-permute-start.11 = (bf16[2,64,256]{2,1,0:T(8,128)(2,1)S(1)}, bf16[2,64,256]{2,1,0:T(8,128)(2,1)S(1)}, u32[]{:S(2)}, u32[]{:S(2)}) collective-permute-start(bf16[2,64,256]{2,1,0:T(8,128)(2,1)S(1)} %fusion.28), channel_id=1, source_target_pairs={{0,8},{8,0},{16,24},{24,16},{32,40},{40,32},{48,56},{56,48},{64,72... | collective-permute-start | bytes 196616 | tf_op jit(solution)/shard_map/ppermute | solution.py:20

commit v13 on v11

--- a/solution.py
+++ b/solution.py
@@ -66,8 +66,26 @@
     )
     far_keys = []
     far_values = []
+    major, minor = SEQ
+    minor_depth = lax.axis_size(minor).bit_length() - 1
+    slice_weight = out_weight
+    table_rows = 2 * coarse
     for layer_bit in range(depth):
-        far_table = from_partner(own_table.astype(jnp.bfloat16), SEQ, layer_bit).astype(jnp.float32)
+        if layer_bit < minor_depth:
+            payload = jnp.concatenate(
+                [own_table.astype(jnp.bfloat16).reshape(table_rows, width), slice_weight], axis=0
+            )
+            got = from_partner(payload, SEQ, layer_bit)
+            far_table = got[:table_rows].reshape(2, coarse, width).astype(jnp.float32)
+            far_weight = got[table_rows:]
+            weight_low = position >> layer_bit & 1 == 0
+            slice_weight = jnp.where(
+                weight_low,
+                jnp.concatenate([slice_weight, far_weight], axis=0),
+                jnp.concatenate([far_weight, slice_weight], axis=0),
+            )
+        else:
+            far_table = from_partner(own_table.astype(jnp.bfloat16), SEQ, layer_bit).astype(jnp.float32)
         far_keys.append(far_table[0].astype(jnp.bfloat16))
         far_values.append(far_table[1].astype(jnp.bfloat16))
         if layer_bit + 1 < depth:
@@ -83,7 +101,7 @@
     key_set = jnp.concatenate([keys] + far_keys, axis=0)
     value_set = jnp.concatenate([values] + far_values, axis=0)
     full_cot = gathered_copies(cotangent, "dp", 1)
-    full_weight = gathered_copies(out_weight, SEQ, 0)
+    full_weight = gathered_copies(slice_weight, major, 0)
     grad_attended = jnp.dot(full_cot, full_weight, preferred_element_type=jnp.float32).astype(
         jnp.bfloat16
     )

time: 167 us -> 163 us (0.976)
  starting transfers between devices: 75.7 us -> 70 us
  waiting for transfers between devices: 70.6 us -> 73 us
    all_to_all x2, starting transfers between devices: 22 us -> 13.4 us  [from_everyone(): return lax.all_to_all(copies, axis, split_axis=0, concat_axis=0, tiled=True)]
    ppermute x12, starting transfers between devices: 45.2 us -> 52 us  [from_partner(): return lax.ppermute(block, axis, route)]
    all_to_all x1, starting transfers between devices: 8.49 us -> 4.65 us  [own_rows(): lax.all_to_all(parts, axes, 0, 0, tiled=True).astype(jnp.float32)]
    ppermute x12, waiting for transfers between devices: 70.6 us -> 73 us  [from_partner(): return lax.ppermute(block, axis, route)]
  transfers between devices with their start and end apart: 15 -> 15, of which waited for: 9 -> 10; matrix products, arithmetic and copies ran while one was open for 7% -> 5% of each run, Pallas kernels for 0% -> 0%
where the time goes in v13:
time: 163 us; the launch traced here: 160 us
  waiting for transfers between devices  73 us (45%)
  starting transfers between devices  70 us (43%)
  local copies, waits for them, and re-layouts  10.3 us (6%)
  matrix products  3.4 us (2%)
  other arithmetic  2.01 us (1%)
    ppermute x12, waiting for transfers between devices, from_partner(): return lax.ppermute(block, axis, route)  73 us
    ppermute x12, starting transfers between devices, from_partner(): return lax.ppermute(block, axis, route)  52 us
    all_to_all x2, starting transfers between devices, from_everyone(): return lax.all_to_all(copies, axis, split_axis=0, concat_axis=0, tiled=True)  13.4 us
    all_to_all x1, starting transfers between devices, own_rows(): lax.all_to_all(parts, axes, 0, 0, tiled=True).astype(jnp.float32)  4.65 us
  transfers between devices with their start and end apart: 15, of which 10 were waited for; matrix products, arithmetic and copies ran while one was open for 5% of the time, Pallas kernels for 0%

profile of v13, /device:TPU:6, one launch (start us, length us, event | category | flops | bytes accessed | tf_op | source)
XLA Modules:
  0.0 160.2 jit_solution(11536313864948129242)
XLA Ops:
  0.7 1.0 reshape.226
  1.6 0.1 fusion.95
  1.7 0.9 reshape.224
  2.6 0.1 fusion.94
  2.8 3.5 %collective-permute-start = (bf16[160,256]{1,0:T(8,128)(2,1)S(1)}, bf16[160,256]{1,0:T(8,128)(2,1)S(1)}, u32[]{:S(2)}, u32[]{:S(2)}) collective-permute-start(bf16[160,256]{1,0:T(8,128)(2,1)S(1)} %pad_maximum_fusion.10), channel_id=1, source_target_pairs={{0,8},{8,0},{16,24},{24,16},{32,40},{40,32},{48,56},{56,48},{64,72... | collective-permute-start | bytes 245768 | tf_op jit(solution)/shard_map/ppermute | solution.py:20
  6.4 2.8 %collective-permute-done = bf16[160,256]{1,0:T(8,128)(2,1)S(1)} collective-permute-done((bf16[160,256]{1,0:T(8,128)(2,1)S(1)}, bf16[160,256]{1,0:T(8,128)(2,1)S(1)}, u32[]{:S(2)}, u32[]{:S(2)}) %collective-permute-start) | collective-permute-done | bytes 81952 | tf_op jit(solution)/shard_map/ppermute | solution.py:20
  9.2 0.2 copy.93
  9.6 4.5 %collective-permute-start.1 = (bf16[192,256]{1,0:T(8,128)(2,1)S(1)}, bf16[192,256]{1,0:T(8,128)(2,1)S(1)}, u32[]{:S(2)}, u32[]{:S(2)}) collective-permute-start(bf16[192,256]{1,0:T(8,128)(2,1)S(1)} %pad_maximum_fusion.9), channel_id=1, source_target_pairs={{0,16},{16,0},{8,24},{24,8},{32,48},{48,32},{40,56},{56,40},{64,80... | collective-permute-start | bytes 294920 | tf_op jit(solution)/shard_map/ppermute | solution.py:20
  14.1 2.9 %collective-permute-done.1 = bf16[192,256]{1,0:T(8,128)(2,1)S(1)} collective-permute-done((bf16[192,256]{1,0:T(8,128)(2,1)S(1)}, bf16[192,256]{1,0:T(8,128)(2,1)S(1)}, u32[]{:S(2)}, u32[]{:S(2)}) %collective-permute-start.1) | collective-permute-done | bytes 98336 | tf_op jit(solution)/shard_map/ppermute | solution.py:20
  17.1 0.2 copy.96
  17.4 8.8 %collective-permute-start.2 = (bf16[256,256]{1,0:T(8,128)(2,1)S(1)}, bf16[256,256]{1,0:T(8,128)(2,1)S(1)}, u32[]{:S(2)}, u32[]{:S(2)}) collective-permute-start(bf16[256,256]{1,0:T(8,128)(2,1)S(1)} %pad_maximum_fusion.6), channel_id=1, source_target_pairs={{0,32},{32,0},{8,40},{40,8},{16,48},{48,16},{24,56},{56,24},{64,96... | collective-permute-start | bytes 393224 | tf_op jit(solution)/shard_map/ppermute | solution.py:20
  26.2 0.8 broadcast_in_dim.17
  27.0 4.8 %all-to-all-start.1 = ((bf16[8,128,256]{2,1,0:T(8,128)(2,1)}), bf16[8,128,256]{2,1,0:T(8,128)(2,1)S(1)}, u32[]{:S(2)}, u32[]{:S(2)}) async-start(bf16[8,128,256]{2,1,0:T(8,128)(2,1)} %broadcast_in_dim.17), calls=%async_computation.1 | async-start | bytes 1048576 | tf_op jit(solution)/shard_map/all_to_all | solution.py:31
  31.9 0.2 copy.99
  32.2 4.3 %collective-permute-start.3 = (bf16[2,64,256]{2,1,0:T(8,128)(2,1)S(1)}, bf16[2,64,256]{2,1,0:T(8,128)(2,1)S(1)}, u32[]{:S(2)}, u32[]{:S(2)}) collective-permute-start(bf16[2,64,256]{2,1,0:T(8,128)(2,1)S(1)} %fusion.77), channel_id=1, source_target_pairs={{0,64},{64,0},{8,72},{72,8},{16,80},{80,16},{24,88},{88,24},{32,96... | collective-permute-start | bytes 196616 | tf_op jit(solution)/shard_map/ppermute | solution.py:20
  36.5 0.1 copy.108
  36.6 2.2 %collective-permute-done.3 = bf16[2,64,256]{2,1,0:T(8,128)(2,1)S(1)} collective-permute-done((bf16[2,64,256]{2,1,0:T(8,128)(2,1)S(1)}, bf16[2,64,256]{2,1,0:T(8,128)(2,1)S(1)}, u32[]{:S(2)}, u32[]{:S(2)}) %collective-permute-start.3) | collective-permute-done | bytes 65568 | tf_op jit(solution)/shard_map/ppermute | solution.py:20
  38.9 0.2 copy.102
  39.2 6.1 %collective-permute-start.4 = (bf16[2,64,256]{2,1,0:T(8,128)(2,1)S(1)}, bf16[2,64,256]{2,1,0:T(8,128)(2,1)S(1)}, u32[]{:S(2)}, u32[]{:S(2)}) collective-permute-start(bf16[2,64,256]{2,1,0:T(8,128)(2,1)S(1)} %fusion.78), channel_id=1, source_target_pairs={{0,128},{128,0},{8,136},{136,8},{16,144},{144,16},{24,152},{152,24... | collective-permute-start | bytes 196616 | tf_op jit(solution)/shard_map/ppermute | solution.py:20
  45.3 2.8 %collective-permute-done.4 = bf16[2,64,256]{2,1,0:T(8,128)(2,1)S(1)} collective-permute-done((bf16[2,64,256]{2,1,0:T(8,128)(2,1)S(1)}, bf16[2,64,256]{2,1,0:T(8,128)(2,1)S(1)}, u32[]{:S(2)}, u32[]{:S(2)}) %collective-permute-start.4) | collective-permute-done | bytes 65568 | tf_op jit(solution)/shard_map/ppermute | solution.py:20
  48.2 0.2 copy.105
  48.4 1.0 broadcast_in_dim.16
  49.5 8.6 %all-to-all-start = ((bf16[8,256,256]{1,2,0:T(8,128)(2,1)}), bf16[8,256,256]{1,2,0:T(8,128)(2,1)S(1)}, u32[]{:S(2)}, u32[]{:S(2)}) async-start(bf16[8,256,256]{1,2,0:T(8,128)(2,1)} %broadcast_in_dim.16), calls=%async_computation | async-start | bytes 2097152 | tf_op jit(solution)/shard_map/all_to_all | solution.py:31
  58.2 7.8 %collective-permute-start.5 = (bf16[2,64,256]{2,1,0:T(8,128)(2,1)S(1)}, bf16[2,64,256]{2,1,0:T(8,128)(2,1)S(1)}, u32[]{:S(2)}, u32[]{:S(2)}) collective-permute-start(bf16[2,64,256]{2,1,0:T(8,128)(2,1)S(1)} %fusion.51), channel_id=1, source_target_pairs={{0,256},{256,0},{8,264},{264,8},{16,272},{272,16},{24,280},{280,24... | collective-permute-start | bytes 196616 | tf_op jit(solution)/shard_map/ppermute | solution.py:20
  66.0 0.3 copy.134
  66.3 21.6 %collective-permute-done.5 = bf16[2,64,256]{2,1,0:T(8,128)(2,1)S(1)} collective-permute-done((bf16[2,64,256]{2,1,0:T(8,128)(2,1)S(1)}, bf16[2,64,256]{2,1,0:T(8,128)(2,1)S(1)}, u32[]{:S(2)}, u32[]{:S(2)}) %collective-permute-start.5) | collective-permute-done | bytes 65568 | tf_op jit(solution)/shard_map/ppermute | solution.py:20
  88.0 0.2 fusion.96
  88.2 0.1 fusion.14
  88.3 0.2 fusion.97
  88.6 0.2 convolution_convert_fusion.2
  88.9 0.4 fusion.1
  89.3 0.2 fusion.5
  89.5 0.2 fusion.53
  89.7 0.2 fusion.8
  89.9 0.2 fusion.52
  90.2 0.2 fusion.68
  90.5 0.2 fusion.71
  90.8 1.9 %collective-permute-start.6 = (bf16[2,64,256]{2,1,0:T(8,128)(2,1)S(1)}, bf16[2,64,256]{2,1,0:T(8,128)(2,1)S(1)}, u32[]{:S(2)}, u32[]{:S(2)}) collective-permute-start(bf16[2,64,256]{2,1,0:T(8,128)(2,1)S(1)} %fusion.20), channel_id=1, source_target_pairs={{0,256},{256,0},{8,264},{264,8},{16,272},{272,16},{24,280},{280,24... | collective-permute-start | bytes 196616 | tf_op jit(solution)/shard_map/ppermute | solution.py:20
  92.7 0.2 convolution_convert_fusion.3
  92.9 8.6 %collective-permute-done.6 = bf16[2,64,256]{2,1,0:T(8,128)(2,1)S(1)} collective-permute-done((bf16[2,64,256]{2,1,0:T(8,128)(2,1)S(1)}, bf16[2,64,256]{2,1,0:T(8,128)(2,1)S(1)}, u32[]{:S(2)}, u32[]{:S(2)}) %collective-permute-start.6) | collective-permute-done | bytes 65568 | tf_op jit(solution)/shard_map/ppermute | solution.py:20
  101.5 0.1 copy.117
  101.8 1.9 %collective-permute-start.7 = (bf16[2,64,256]{2,1,0:T(8,128)(2,1)S(1)}, bf16[2,64,256]{2,1,0:T(8,128)(2,1)S(1)}, u32[]{:S(2)}, u32[]{:S(2)}) collective-permute-start(bf16[2,64,256]{2,1,0:T(8,128)(2,1)S(1)} %fusion.23), channel_id=1, source_target_pairs={{0,128},{128,0},{8,136},{136,8},{16,144},{144,16},{24,152},{152,24... | collective-permute-start | bytes 196616 | tf_op jit(solution)/shard_map/ppermute | solution.py:20
  103.7 0.4 convolution_bitcast_fusion
  104.2 4.7 %collective-permute-done.7 = bf16[2,64,256]{2,1,0:T(8,128)(2,1)S(1)} collective-permute-done((bf16[2,64,256]{2,1,0:T(8,128)(2,1)S(1)}, bf16[2,64,256]{2,1,0:T(8,128)(2,1)S(1)}, u32[]{:S(2)}, u32[]{:S(2)}) %collective-permute-start.7) | collective-permute-done | bytes 65568 | tf_op jit(solution)/shard_map/ppermute | solution.py:20
  108.9 0.1 copy.120
  109.2 1.9 %collective-permute-start.8 = (bf16[2,64,256]{2,1,0:T(8,128)(2,1)S(1)}, bf16[2,64,256]{2,1,0:T(8,128)(2,1)S(1)}, u32[]{:S(2)}, u32[]{:S(2)}) collective-permute-start(bf16[2,64,256]{2,1,0:T(8,128)(2,1)S(1)} %fusion.26), channel_id=1, source_target_pairs={{0,64},{64,0},{8,72},{72,8},{16,80},{80,16},{24,88},{88,24},{32,96... | collective-permute-start | bytes 196616 | tf_op jit(solution)/shard_map/ppermute | solution.py:20
  111.1 0.7 copy.136
  111.8 1.3 copy.135
  113.2 4.7 %all-to-all-start.2 = ((bf16[64,32,256]{2,1,0:T(8,128)(2,1)}), bf16[64,32,256]{2,1,0:T(8,128)(2,1)S(1)}, u32[]{:S(2)}, u32[]{:S(2)}) async-start(bf16[64,32,256]{2,1,0:T(8,128)(2,1)} %bitcast.44), calls=%async_computation.2 | async-start | bytes 2097152 | tf_op jit(solution)/shard_map/all_to_all | solution.py:41
  117.9 0.1 copy.123
  118.1 7.4 %collective-permute-start.9 = (bf16[2,64,256]{2,1,0:T(8,128)(2,1)S(1)}, bf16[2,64,256]{2,1,0:T(8,128)(2,1)S(1)}, u32[]{:S(2)}, u32[]{:S(2)}) collective-permute-start(bf16[2,64,256]{2,1,0:T(8,128)(2,1)S(1)} %fusion.29), channel_id=1, source_target_pairs={{0,32},{32,0},{8,40},{40,8},{16,48},{48,16},{24,56},{56,24},{64,96... | collective-permute-start | bytes 196616 | tf_op jit(solution)/shard_map/ppermute | solution.py:20
  125.5 0.2 convolution_convert_fusion
  125.7 18.2 %collective-permute-done.9 = bf16[2,64,256]{2,1,0:T(8,128)(2,1)S(1)} collective-permute-done((bf16[2,64,256]{2,1,0:T(8,128)(2,1)S(1)}, bf16[2,64,256]{2,1,0:T(8,128)(2,1)S(1)}, u32[]{:S(2)}, u32[]{:S(2)}) %collective-permute-start.9) | collective-permute-done | bytes 65568 | tf_op jit(solution)/shard_map/ppermute | solution.py:20
  144.0 0.1 copy.126
  144.3 1.9 %collective-permute-start.10 = (bf16[2,64,256]{2,1,0:T(8,128)(2,1)S(1)}, bf16[2,64,256]{2,1,0:T(8,128)(2,1)S(1)}, u32[]{:S(2)}, u32[]{:S(2)}) collective-permute-start(bf16[2,64,256]{2,1,0:T(8,128)(2,1)S(1)} %fusion.18), channel_id=1, source_target_pairs={{0,16},{16,0},{8,24},{24,8},{32,48},{48,32},{40,56},{56,40},{64,80... | collective-permute-start | bytes 196616 | tf_op jit(solution)/shard_map/ppermute | solution.py:20
  146.2 0.2 convolution_convert_fusion.1
  146.4 5.6 %collective-permute-done.10 = bf16[2,64,256]{2,1,0:T(8,128)(2,1)S(1)} collective-permute-done((bf16[2,64,256]{2,1,0:T(8,128)(2,1)S(1)}, bf16[2,64,256]{2,1,0:T(8,128)(2,1)S(1)}, u32[]{:S(2)}, u32[]{:S(2)}) %collective-permute-start.10) | collective-permute-done | bytes 65568 | tf_op jit(solution)/shard_map/ppermute | solution.py:20
  152.0 0.1 copy.129
  152.3 2.0 %collective-permute-start.11 = (bf16[2,64,256]{2,1,0:T(8,128)(2,1)S(1)}, bf16[2,64,256]{2,1,0:T(8,128)(2,1)S(1)}, u32[]{:S(2)}, u32[]{:S(2)}) collective-permute-start(bf16[2,64,256]{2,1,0:T(8,128)(2,1)S(1)} %fusion.31), channel_id=1, source_target_pairs={{0,8},{8,0},{16,24},{24,16},{32,40},{40,32},{48,56},{56,48},{64,72... | collective-permute-start | bytes 196616 | tf_op jit(solution)/shard_map/ppermute | solution.py:20
  154.3 0.7 copy.137
  155.0 3.4 %collective-permute-done.11 = bf16[2,64,256]{2,1,0:T(8,128)(2,1)S(1)} collective-permute-done((bf16[2,64,256]{2,1,0:T(8,128)(2,1)S(1)}, bf16[2,64,256]{2,1,0:T(8,128)(2,1)S(1)}, u32[]{:S(2)}, u32[]{:S(2)}) %collective-permute-start.11) | collective-permute-done | bytes 65568 | tf_op jit(solution)/shard_map/ppermute | solution.py:20
  158.5 0.1 copy.132
  158.7 0.7 slice_bitcast_fusion
  159.4 0.8 convert_reduce_fusion
  (85 shorter events, 2.0 us)
Async XLA Ops:
  0.6 5.7 %copy-start.1 = (bf16[128,256]{1,0:T(8,128)(2,1)S(1)}, bf16[128,256]{1,0:T(8,128)(2,1)}, u32[]{:S(2)}) copy-start(bf16[128,256]{1,0:T(8,128)(2,1)} %param.7) | copy-start | bytes 196612
  0.6 5.7 %copy-start = (bf16[128,256]{1,0:T(8,128)(2,1)S(1)}, bf16[128,256]{1,0:T(8,128)(2,1)}, u32[]{:S(2)}) copy-start(bf16[128,256]{1,0:T(8,128)(2,1)} %param.6) | copy-start | bytes 196612
  0.7 2.1 %copy-start.4 = (bf16[32,256]{1,0:T(8,128)(2,1)S(1)}, bf16[32,256]{1,0:T(8,128)(2,1)}, u32[]{:S(2)}) copy-start(bf16[32,256]{1,0:T(8,128)(2,1)} %param.9) | copy-start | bytes 49156
  2.8 6.3 %collective-permute-start = (bf16[160,256]{1,0:T(8,128)(2,1)S(1)}, bf16[160,256]{1,0:T(8,128)(2,1)S(1)}, u32[]{:S(2)}, u32[]{:S(2)}) collective-permute-start(bf16[160,256]{1,0:T(8,128)(2,1)S(1)} %pad_maximum_fusion.10), channel_id=1, source_target_pairs={{0,8},{8,0},{16,24},{24,16},{32,40},{40,32},{48,56},{56,48},{64,72... | collective-permute-start | bytes 245768 | tf_op jit(solution)/shard_map/ppermute | solution.py:20
  9.6 7.4 %collective-permute-start.1 = (bf16[192,256]{1,0:T(8,128)(2,1)S(1)}, bf16[192,256]{1,0:T(8,128)(2,1)S(1)}, u32[]{:S(2)}, u32[]{:S(2)}) collective-permute-start(bf16[192,256]{1,0:T(8,128)(2,1)S(1)} %pad_maximum_fusion.9), channel_id=1, source_target_pairs={{0,16},{16,0},{8,24},{24,8},{32,48},{48,32},{40,56},{56,40},{64,80... | collective-permute-start | bytes 294920 | tf_op jit(solution)/shard_map/ppermute | solution.py:20
  17.1 9.1 %copy-start.3 = (bf16[128,256]{1,0:T(8,128)(2,1)S(1)}, bf16[128,256]{1,0:T(8,128)(2,1)}, u32[]{:S(2)}) copy-start(bf16[128,256]{1,0:T(8,128)(2,1)} %param.8) | copy-start | bytes 196612
  17.4 14.4 %collective-permute-start.2 = (bf16[256,256]{1,0:T(8,128)(2,1)S(1)}, bf16[256,256]{1,0:T(8,128)(2,1)S(1)}, u32[]{:S(2)}, u32[]{:S(2)}) collective-permute-start(bf16[256,256]{1,0:T(8,128)(2,1)S(1)} %pad_maximum_fusion.6), channel_id=1, source_target_pairs={{0,32},{32,0},{8,40},{40,8},{16,48},{48,16},{24,56},{56,24},{64,96... | collective-permute-start | bytes 393224 | tf_op jit(solution)/shard_map/ppermute | solution.py:20
  27.0 21.4 %all-to-all-start.1 = ((bf16[8,128,256]{2,1,0:T(8,128)(2,1)}), bf16[8,128,256]{2,1,0:T(8,128)(2,1)S(1)}, u32[]{:S(2)}, u32[]{:S(2)}) async-start(bf16[8,128,256]{2,1,0:T(8,128)(2,1)} %broadcast_in_dim.17), calls=%async_computation.1 | async-start | bytes 1048576 | tf_op jit(solution)/shard_map/all_to_all | solution.py:31
  32.2 6.7 %collective-permute-start.3 = (bf16[2,64,256]{2,1,0:T(8,128)(2,1)S(1)}, bf16[2,64,256]{2,1,0:T(8,128)(2,1)S(1)}, u32[]{:S(2)}, u32[]{:S(2)}) collective-permute-start(bf16[2,64,256]{2,1,0:T(8,128)(2,1)S(1)} %fusion.77), channel_id=1, source_target_pairs={{0,64},{64,0},{8,72},{72,8},{16,80},{80,16},{24,88},{88,24},{32,96... | collective-permute-start | bytes 196616 | tf_op jit(solution)/shard_map/ppermute | solution.py:20
  39.2 8.9 %collective-permute-start.4 = (bf16[2,64,256]{2,1,0:T(8,128)(2,1)S(1)}, bf16[2,64,256]{2,1,0:T(8,128)(2,1)S(1)}, u32[]{:S(2)}, u32[]{:S(2)}) collective-permute-start(bf16[2,64,256]{2,1,0:T(8,128)(2,1)S(1)} %fusion.78), channel_id=1, source_target_pairs={{0,128},{128,0},{8,136},{136,8},{16,144},{144,16},{24,152},{152,24... | collective-permute-start | bytes 196616 | tf_op jit(solution)/shard_map/ppermute | solution.py:20
  49.5 39.4 %all-to-all-start = ((bf16[8,256,256]{1,2,0:T(8,128)(2,1)}), bf16[8,256,256]{1,2,0:T(8,128)(2,1)S(1)}, u32[]{:S(2)}, u32[]{:S(2)}) async-start(bf16[8,256,256]{1,2,0:T(8,128)(2,1)} %broadcast_in_dim.16), calls=%async_computation | async-start | bytes 2097152 | tf_op jit(solution)/shard_map/all_to_all | solution.py:31
  58.1 29.9 %copy-start.2 = (bf16[128,256]{1,0:T(8,128)(2,1)S(1)}, bf16[128,256]{1,0:T(8,128)(2,1)}, u32[]{:S(2)}) copy-start(bf16[128,256]{1,0:T(8,128)(2,1)} %param.5) | copy-start | bytes 196612
  58.2 29.8 %collective-permute-start.5 = (bf16[2,64,256]{2,1,0:T(8,128)(2,1)S(1)}, bf16[2,64,256]{2,1,0:T(8,128)(2,1)S(1)}, u32[]{:S(2)}, u32[]{:S(2)}) collective-permute-start(bf16[2,64,256]{2,1,0:T(8,128)(2,1)S(1)} %fusion.51), channel_id=1, source_target_pairs={{0,256},{256,0},{8,264},{264,8},{16,272},{272,16},{24,280},{280,24... | collective-permute-start | bytes 196616 | tf_op jit(solution)/shard_map/ppermute | solution.py:20
  90.8 10.8 %collective-permute-start.6 = (bf16[2,64,256]{2,1,0:T(8,128)(2,1)S(1)}, bf16[2,64,256]{2,1,0:T(8,128)(2,1)S(1)}, u32[]{:S(2)}, u32[]{:S(2)}) collective-permute-start(bf16[2,64,256]{2,1,0:T(8,128)(2,1)S(1)} %fusion.20), channel_id=1, source_target_pairs={{0,256},{256,0},{8,264},{264,8},{16,272},{272,16},{24,280},{280,24... | collective-permute-start | bytes 196616 | tf_op jit(solution)/shard_map/ppermute | solution.py:20
  101.8 7.1 %collective-permute-start.7 = (bf16[2,64,256]{2,1,0:T(8,128)(2,1)S(1)}, bf16[2,64,256]{2,1,0:T(8,128)(2,1)S(1)}, u32[]{:S(2)}, u32[]{:S(2)}) collective-permute-start(bf16[2,64,256]{2,1,0:T(8,128)(2,1)S(1)} %fusion.23), channel_id=1, source_target_pairs={{0,128},{128,0},{8,136},{136,8},{16,144},{144,16},{24,152},{152,24... | collective-permute-start | bytes 196616 | tf_op jit(solution)/shard_map/ppermute | solution.py:20
  109.2 8.7 %collective-permute-start.8 = (bf16[2,64,256]{2,1,0:T(8,128)(2,1)S(1)}, bf16[2,64,256]{2,1,0:T(8,128)(2,1)S(1)}, u32[]{:S(2)}, u32[]{:S(2)}) collective-permute-start(bf16[2,64,256]{2,1,0:T(8,128)(2,1)S(1)} %fusion.26), channel_id=1, source_target_pairs={{0,64},{64,0},{8,72},{72,8},{16,80},{80,16},{24,88},{88,24},{32,96... | collective-permute-start | bytes 196616 | tf_op jit(solution)/shard_map/ppermute | solution.py:20
  113.2 46.2 %all-to-all-start.2 = ((bf16[64,32,256]{2,1,0:T(8,128)(2,1)}), bf16[64,32,256]{2,1,0:T(8,128)(2,1)S(1)}, u32[]{:S(2)}, u32[]{:S(2)}) async-start(bf16[64,32,256]{2,1,0:T(8,128)(2,1)} %bitcast.44), calls=%async_computation.2 | async-start | bytes 2097152 | tf_op jit(solution)/shard_map/all_to_all | solution.py:41
  118.1 25.9 %collective-permute-start.9 = (bf16[2,64,256]{2,1,0:T(8,128)(2,1)S(1)}, bf16[2,64,256]{2,1,0:T(8,128)(2,1)S(1)}, u32[]{:S(2)}, u32[]{:S(2)}) collective-permute-start(bf16[2,64,256]{2,1,0:T(8,128)(2,1)S(1)} %fusion.29), channel_id=1, source_target_pairs={{0,32},{32,0},{8,40},{40,8},{16,48},{48,16},{24,56},{56,24},{64,96... | collective-permute-start | bytes 196616 | tf_op jit(solution)/shard_map/ppermute | solution.py:20
  144.3 7.8 %collective-permute-start.10 = (bf16[2,64,256]{2,1,0:T(8,128)(2,1)S(1)}, bf16[2,64,256]{2,1,0:T(8,128)(2,1)S(1)}, u32[]{:S(2)}, u32[]{:S(2)}) collective-permute-start(bf16[2,64,256]{2,1,0:T(8,128)(2,1)S(1)} %fusion.18), channel_id=1, source_target_pairs={{0,16},{16,0},{8,24},{24,8},{32,48},{48,32},{40,56},{56,40},{64,80... | collective-permute-start | bytes 196616 | tf_op jit(solution)/shard_map/ppermute | solution.py:20
  152.3 6.2 %collective-permute-start.11 = (bf16[2,64,256]{2,1,0:T(8,128)(2,1)S(1)}, bf16[2,64,256]{2,1,0:T(8,128)(2,1)S(1)}, u32[]{:S(2)}, u32[]{:S(2)}) collective-permute-start(bf16[2,64,256]{2,1,0:T(8,128)(2,1)S(1)} %fusion.31), channel_id=1, source_target_pairs={{0,8},{8,0},{16,24},{24,16},{32,40},{40,32},{48,56},{56,48},{64,72... | collective-permute-start | bytes 196616 | tf_op jit(solution)/shard_map/ppermute | solution.py:20

commit v14 on v13

--- a/solution.py
+++ b/solution.py
@@ -146,6 +146,14 @@
     grad_sets = jnp.stack(
         [jnp.concatenate(grad_key_parts, axis=1), jnp.concatenate(grad_value_parts, axis=1)]
     )
+    weight_grad = lax.dot_general(
+        full_cot, attended, (((0,), (0,)), ((), ())), preferred_element_type=jnp.bfloat16
+    )
+    n_major = lax.axis_size(major)
+    weight_grad = lax.all_to_all(
+        weight_grad.reshape(n_major, weight_grad.shape[0] // n_major, width), major, 0, 0, tiled=True
+    )
+    weight_sum = jnp.sum(weight_grad.astype(jnp.float32), axis=0)
     carried = jnp.zeros((2, coarse, width), jnp.float32)
     for layer_bit in reversed(range(depth)):
         first = tokens + layer_bit * coarse
@@ -158,19 +166,26 @@
             high_part = spread[:, coarse:]
             kept = jnp.where(lower_half, low_part, high_part)
             outgoing = outgoing + jnp.where(lower_half, high_part, low_part)
-        incoming = from_partner(outgoing.astype(jnp.bfloat16), SEQ, layer_bit).astype(
-            outgoing.dtype
-        )
+        if layer_bit < minor_depth:
+            half = weight_sum.shape[0] // 2
+            weight_low = position >> layer_bit & 1 == 0
+            keep_w = jnp.where(weight_low, weight_sum[:half], weight_sum[half:])
+            send_w = jnp.where(weight_low, weight_sum[half:], weight_sum[:half])
+            payload = jnp.concatenate(
+                [outgoing.astype(jnp.bfloat16).reshape(2 * coarse, width), send_w.astype(jnp.bfloat16)], axis=0
+            )
+            got = from_partner(payload, SEQ, layer_bit)
+            incoming = got[: 2 * coarse].reshape(2, coarse, width).astype(outgoing.dtype)
+            weight_sum = keep_w + got[2 * coarse :].astype(jnp.float32)
+        else:
+            incoming = from_partner(outgoing.astype(jnp.bfloat16), SEQ, layer_bit).astype(
+                outgoing.dtype
+            )
         carried = kept + incoming
     own_grads = grad_sets[:, :tokens] + spread_rows(carried * 0.5)
     grad_keys = own_grads[0].astype(jnp.bfloat16)
     grad_values = own_grads[1].astype(jnp.bfloat16)
-    grad_out_weight = own_rows(
-        lax.dot_general(
-            full_cot, attended, (((0,), (0,)), ((), ())), preferred_element_type=jnp.bfloat16
-        ),
-        SEQ,
-    )
+    grad_out_weight = weight_sum
     return (attended, grad_queries, grad_keys, grad_values, grad_out_weight)
 
 

time: 163 us -> 171 us (1.049)
  local copies, waits for them, and re-layouts: 10.3 us -> 16 us
  matrix products: 3.4 us -> 7.01 us
  starting transfers between devices: 70 us -> 67.2 us
  waiting for transfers between devices: 73 us -> 75.4 us
    all_to_all x2, waiting for transfers between devices: 0.01 us -> 20.8 us  [from_everyone(): return lax.all_to_all(copies, axis, split_axis=0, concat_axis=0, tiled=True)]
    ppermute x12, waiting for transfers between devices: 73 us -> 54.6 us  [from_partner(): return lax.ppermute(block, axis, route)]
    unnamed x18 -> x27, local copies, waits for them, and re-layouts: 1.56 us -> 6.39 us
    all_to_all x2, starting transfers between devices: 13.4 us -> 10 us  [from_everyone(): return lax.all_to_all(copies, axis, split_axis=0, concat_axis=0, tiled=True)]
    dot_general x2, matrix products: 0.46 us -> 2.27 us  [on_device(): jnp.dot(weights, value_head, preferred_element_type=jnp.float32)]
    dot_general x2, matrix products: 0.45 us -> 2.25 us  [on_device(): jnp.einsum('ta,ka->tk', grad_head, value_head, preferred_element_type=jnp...]
  transfers between devices with their start and end apart: 15 -> 15, of which waited for: 10 -> 11; matrix products, arithmetic and copies ran while one was open for 5% -> 10% of each run, Pallas kernels for 0% -> 0%
where the time goes in v14:
time: 171 us; the launch traced here: 169 us
  waiting for transfers between devices  75.4 us (44%)
  starting transfers between devices  67.2 us (39%)
  local copies, waits for them, and re-layouts  16 us (9%)
  matrix products  7.01 us (4%)
  other arithmetic  1.87 us (1%)
    ppermute x12, waiting for transfers between devices, from_partner(): return lax.ppermute(block, axis, route)  54.6 us
    ppermute x12, starting transfers between devices, from_partner(): return lax.ppermute(block, axis, route)  53.6 us
    all_to_all x2, waiting for transfers between devices, from_everyone(): return lax.all_to_all(copies, axis, split_axis=0, concat_axis=0, tiled=True)  20.8 us
    all_to_all x2, starting transfers between devices, from_everyone(): return lax.all_to_all(copies, axis, split_axis=0, concat_axis=0, tiled=True)  10 us
    unnamed x27, local copies, waits for them, and re-layouts  6.39 us
    all_to_all x1, starting transfers between devices, on_device(): lax.all_to_all(weight_grad.reshape(n_major, weight_grad.shape[0] // n_maj...  3.56 us
  transfers between devices with their start and end apart: 15, of which 11 were waited for; matrix products, arithmetic and copies ran while one was open for 10% of the time, Pallas kernels for 0%

profile of v14, /device:TPU:6, one launch (start us, length us, event | category | flops | bytes accessed | tf_op | source)
XLA Modules:
  0.0 169.1 jit_solution(4682101843701888147)
XLA Ops:
  0.7 1.0 reshape.247
  1.7 0.9 reshape.245
  2.8 3.5 %collective-permute-start = (bf16[160,256]{1,0:T(8,128)(2,1)S(1)}, bf16[160,256]{1,0:T(8,128)(2,1)S(1)}, u32[]{:S(2)}, u32[]{:S(2)}) collective-permute-start(bf16[160,256]{1,0:T(8,128)(2,1)S(1)} %pad_maximum_fusion.13), channel_id=1, source_target_pairs={{0,8},{8,0},{16,24},{24,16},{32,40},{40,32},{48,56},{56,48},{64,72... | collective-permute-start | bytes 245768 | tf_op jit(solution)/shard_map/ppermute | solution.py:20
  6.3 0.6 constant_dynamic-update-slice_fusion
  7.0 2.2 %collective-permute-done = bf16[160,256]{1,0:T(8,128)(2,1)S(1)} collective-permute-done((bf16[160,256]{1,0:T(8,128)(2,1)S(1)}, bf16[160,256]{1,0:T(8,128)(2,1)S(1)}, u32[]{:S(2)}, u32[]{:S(2)}) %collective-permute-start) | collective-permute-done | bytes 81952 | tf_op jit(solution)/shard_map/ppermute | solution.py:20
  9.2 0.2 copy.174
  9.6 4.5 %collective-permute-start.1 = (bf16[192,256]{1,0:T(8,128)(2,1)S(1)}, bf16[192,256]{1,0:T(8,128)(2,1)S(1)}, u32[]{:S(2)}, u32[]{:S(2)}) collective-permute-start(bf16[192,256]{1,0:T(8,128)(2,1)S(1)} %pad_maximum_fusion.12), channel_id=1, source_target_pairs={{0,16},{16,0},{8,24},{24,8},{32,48},{48,32},{40,56},{56,40},{64,80... | collective-permute-start | bytes 294920 | tf_op jit(solution)/shard_map/ppermute | solution.py:20
  14.1 0.6 slice_dynamic-update-slice_fusion.5
  14.7 2.3 %collective-permute-done.1 = bf16[192,256]{1,0:T(8,128)(2,1)S(1)} collective-permute-done((bf16[192,256]{1,0:T(8,128)(2,1)S(1)}, bf16[192,256]{1,0:T(8,128)(2,1)S(1)}, u32[]{:S(2)}, u32[]{:S(2)}) %collective-permute-start.1) | collective-permute-done | bytes 98336 | tf_op jit(solution)/shard_map/ppermute | solution.py:20
  17.0 0.6 slice_dynamic-update-slice_fusion.4
  17.7 0.2 copy.177
  18.0 8.8 %collective-permute-start.2 = (bf16[256,256]{1,0:T(8,128)(2,1)S(1)}, bf16[256,256]{1,0:T(8,128)(2,1)S(1)}, u32[]{:S(2)}, u32[]{:S(2)}) collective-permute-start(bf16[256,256]{1,0:T(8,128)(2,1)S(1)} %pad_maximum_fusion.6), channel_id=1, source_target_pairs={{0,32},{32,0},{8,40},{40,8},{16,48},{48,16},{24,56},{56,24},{64,96... | collective-permute-start | bytes 393224 | tf_op jit(solution)/shard_map/ppermute | solution.py:20
  26.8 0.8 broadcast_in_dim.17
  27.6 4.8 %all-to-all-start.1 = ((bf16[8,128,256]{2,1,0:T(8,128)(2,1)}), bf16[8,128,256]{2,1,0:T(8,128)(2,1)S(1)}, u32[]{:S(2)}, u32[]{:S(2)}) async-start(bf16[8,128,256]{2,1,0:T(8,128)(2,1)} %broadcast_in_dim.17), calls=%async_computation.1 | async-start | bytes 1048576 | tf_op jit(solution)/shard_map/all_to_all | solution.py:31
  32.5 0.2 copy.180
  32.8 4.3 %collective-permute-start.3 = (bf16[2,64,256]{2,1,0:T(8,128)(2,1)S(1)}, bf16[2,64,256]{2,1,0:T(8,128)(2,1)S(1)}, u32[]{:S(2)}, u32[]{:S(2)}) collective-permute-start(bf16[2,64,256]{2,1,0:T(8,128)(2,1)S(1)} %fusion.78), channel_id=1, source_target_pairs={{0,64},{64,0},{8,72},{72,8},{16,80},{80,16},{24,88},{88,24},{32,96... | collective-permute-start | bytes 196616 | tf_op jit(solution)/shard_map/ppermute | solution.py:20
  37.1 0.6 slice_dynamic-update-slice_fusion.3
  37.8 1.6 collective-permute-done.3
  39.5 0.2 copy.183
  39.8 6.1 %collective-permute-start.4 = (bf16[2,64,256]{2,1,0:T(8,128)(2,1)S(1)}, bf16[2,64,256]{2,1,0:T(8,128)(2,1)S(1)}, u32[]{:S(2)}, u32[]{:S(2)}) collective-permute-start(bf16[2,64,256]{2,1,0:T(8,128)(2,1)S(1)} %fusion.79), channel_id=1, source_target_pairs={{0,128},{128,0},{8,136},{136,8},{16,144},{144,16},{24,152},{152,24... | collective-permute-start | bytes 196616 | tf_op jit(solution)/shard_map/ppermute | solution.py:20
  45.9 0.6 fusion.63
  46.5 2.2 %collective-permute-done.4 = bf16[2,64,256]{2,1,0:T(8,128)(2,1)S(1)} collective-permute-done((bf16[2,64,256]{2,1,0:T(8,128)(2,1)S(1)}, bf16[2,64,256]{2,1,0:T(8,128)(2,1)S(1)}, u32[]{:S(2)}, u32[]{:S(2)}) %collective-permute-start.4) | collective-permute-done | bytes 65568 | tf_op jit(solution)/shard_map/ppermute | solution.py:20
  48.8 0.2 copy.186
  49.1 8.5 %collective-permute-start.5 = (bf16[2,64,256]{2,1,0:T(8,128)(2,1)S(1)}, bf16[2,64,256]{2,1,0:T(8,128)(2,1)S(1)}, u32[]{:S(2)}, u32[]{:S(2)}) collective-permute-start(bf16[2,64,256]{2,1,0:T(8,128)(2,1)S(1)} %fusion.51), channel_id=1, source_target_pairs={{0,256},{256,0},{8,264},{264,8},{16,272},{272,16},{24,280},{280,24... | collective-permute-start | bytes 196616 | tf_op jit(solution)/shard_map/ppermute | solution.py:20
  57.6 1.0 broadcast_in_dim.16
  58.7 5.3 %all-to-all-start = ((bf16[8,256,256]{1,2,0:T(8,128)(2,1)}), bf16[8,256,256]{1,2,0:T(8,128)(2,1)S(1)}, u32[]{:S(2)}, u32[]{:S(2)}) async-start(bf16[8,256,256]{1,2,0:T(8,128)(2,1)} %broadcast_in_dim.16), calls=%async_computation | async-start | bytes 2097152 | tf_op jit(solution)/shard_map/all_to_all | solution.py:31
  64.0 0.6 fusion.62
  64.6 0.3 copy.207
  64.9 0.6 fusion.61
  65.5 0.2 fusion.97
  65.8 0.2 fusion.98
  66.1 1.1 convolution_convert_fusion.2
  67.3 1.1 convolution_convert_fusion.3
  68.4 0.4 fusion.75
  68.9 1.0 copy.373
  69.9 20.8 %all-to-all-done = bf16[8,256,256]{1,2,0:T(8,128)(2,1)S(1)} async-done(((bf16[8,256,256]{1,2,0:T(8,128)(2,1)}), bf16[8,256,256]{1,2,0:T(8,128)(2,1)S(1)}, u32[]{:S(2)}, u32[]{:S(2)}) %all-to-all-start) | async-done | bytes 1048608 | tf_op jit(solution)/shard_map/all_to_all | solution.py:31
  90.8 3.6 %all-to-all-start.2 = ((bf16[8,256,256]{1,2,0:T(8,128)(2,1)}), bf16[8,256,256]{1,2,0:T(8,128)(2,1)S(1)}, u32[]{:S(2)}, u32[]{:S(2)}) async-start(bf16[8,256,256]{1,2,0:T(8,128)(2,1)} %bitcast.132), calls=%async_computation.2 | async-start | bytes 2097152 | tf_op jit(solution)/shard_map/all_to_all | solution.py:153
  94.3 0.4 fusion.1
  94.8 0.5 copy-done.1
  95.3 1.1 fusion.5
  96.4 1.1 fusion.8
  97.5 0.2 fusion.53
  97.7 0.2 fusion.52
  98.0 0.2 fusion.68
  98.2 0.2 fusion.71
  98.5 7.8 %collective-permute-start.6 = (bf16[2,64,256]{2,1,0:T(8,128)(2,1)S(1)}, bf16[2,64,256]{2,1,0:T(8,128)(2,1)S(1)}, u32[]{:S(2)}, u32[]{:S(2)}) collective-permute-start(bf16[2,64,256]{2,1,0:T(8,128)(2,1)S(1)} %fusion.20), channel_id=1, source_target_pairs={{0,256},{256,0},{8,264},{264,8},{16,272},{272,16},{24,280},{280,24... | collective-permute-start | bytes 196616 | tf_op jit(solution)/shard_map/ppermute | solution.py:20
  106.3 17.8 %collective-permute-done.6 = bf16[2,64,256]{2,1,0:T(8,128)(2,1)S(1)} collective-permute-done((bf16[2,64,256]{2,1,0:T(8,128)(2,1)S(1)}, bf16[2,64,256]{2,1,0:T(8,128)(2,1)S(1)}, u32[]{:S(2)}, u32[]{:S(2)}) %collective-permute-start.6) | collective-permute-done | bytes 65568 | tf_op jit(solution)/shard_map/ppermute | solution.py:20
  124.4 1.9 %collective-permute-start.7 = (bf16[2,64,256]{2,1,0:T(8,128)(2,1)S(1)}, bf16[2,64,256]{2,1,0:T(8,128)(2,1)S(1)}, u32[]{:S(2)}, u32[]{:S(2)}) collective-permute-start(bf16[2,64,256]{2,1,0:T(8,128)(2,1)S(1)} %fusion.23), channel_id=1, source_target_pairs={{0,128},{128,0},{8,136},{136,8},{16,144},{144,16},{24,152},{152,24... | collective-permute-start | bytes 196616 | tf_op jit(solution)/shard_map/ppermute | solution.py:20
  126.3 0.7 copy.224
  127.1 5.0 %collective-permute-done.7 = bf16[2,64,256]{2,1,0:T(8,128)(2,1)S(1)} collective-permute-done((bf16[2,64,256]{2,1,0:T(8,128)(2,1)S(1)}, bf16[2,64,256]{2,1,0:T(8,128)(2,1)S(1)}, u32[]{:S(2)}, u32[]{:S(2)}) %collective-permute-start.7) | collective-permute-done | bytes 65568 | tf_op jit(solution)/shard_map/ppermute | solution.py:20
  132.3 1.9 %collective-permute-start.8 = (bf16[2,64,256]{2,1,0:T(8,128)(2,1)S(1)}, bf16[2,64,256]{2,1,0:T(8,128)(2,1)S(1)}, u32[]{:S(2)}, u32[]{:S(2)}) collective-permute-start(bf16[2,64,256]{2,1,0:T(8,128)(2,1)S(1)} %fusion.26), channel_id=1, source_target_pairs={{0,64},{64,0},{8,72},{72,8},{16,80},{80,16},{24,88},{88,24},{32,96... | collective-permute-start | bytes 196616 | tf_op jit(solution)/shard_map/ppermute | solution.py:20
  134.3 0.1 convert_reduce_fusion
  134.4 4.1 %collective-permute-done.8 = bf16[2,64,256]{2,1,0:T(8,128)(2,1)S(1)} collective-permute-done((bf16[2,64,256]{2,1,0:T(8,128)(2,1)S(1)}, bf16[2,64,256]{2,1,0:T(8,128)(2,1)S(1)}, u32[]{:S(2)}, u32[]{:S(2)}) %collective-permute-start.8) | collective-permute-done | bytes 65568 | tf_op jit(solution)/shard_map/ppermute | solution.py:20
  138.9 1.9 %collective-permute-start.9 = (bf16[256,256]{0,1:T(8,128)(2,1)S(1)}, bf16[256,256]{0,1:T(8,128)(2,1)S(1)}, u32[]{:S(2)}, u32[]{:S(2)}) collective-permute-start(bf16[256,256]{0,1:T(8,128)(2,1)S(1)} %pad_maximum_fusion.9), channel_id=1, source_target_pairs={{0,32},{32,0},{8,40},{40,8},{16,48},{48,16},{24,56},{56,24},{64,96... | collective-permute-start | bytes 393224 | tf_op jit(solution)/shard_map/ppermute | solution.py:20
  140.9 0.2 convolution_convert_fusion
  141.1 8.8 %collective-permute-done.9 = bf16[256,256]{0,1:T(8,128)(2,1)S(1)} collective-permute-done((bf16[256,256]{0,1:T(8,128)(2,1)S(1)}, bf16[256,256]{0,1:T(8,128)(2,1)S(1)}, u32[]{:S(2)}, u32[]{:S(2)}) %collective-permute-start.9) | collective-permute-done | bytes 131104 | tf_op jit(solution)/shard_map/ppermute | solution.py:20
  150.5 2.0 %collective-permute-start.10 = (bf16[192,256]{0,1:T(8,128)(2,1)S(1)}, bf16[192,256]{0,1:T(8,128)(2,1)S(1)}, u32[]{:S(2)}, u32[]{:S(2)}) collective-permute-start(bf16[192,256]{0,1:T(8,128)(2,1)S(1)} %pad_maximum_fusion.10), channel_id=1, source_target_pairs={{0,16},{16,0},{8,24},{24,8},{32,48},{48,32},{40,56},{56,40},{64,80... | collective-permute-start | bytes 294920 | tf_op jit(solution)/shard_map/ppermute | solution.py:20
  152.5 0.2 convolution_convert_fusion.1
  152.8 6.9 %collective-permute-done.10 = bf16[192,256]{0,1:T(8,128)(2,1)S(1)} collective-permute-done((bf16[192,256]{0,1:T(8,128)(2,1)S(1)}, bf16[192,256]{0,1:T(8,128)(2,1)S(1)}, u32[]{:S(2)}, u32[]{:S(2)}) %collective-permute-start.10) | collective-permute-done | bytes 98336 | tf_op jit(solution)/shard_map/ppermute | solution.py:20
  160.4 2.4 %collective-permute-start.11 = (bf16[160,256]{0,1:T(8,128)(2,1)S(1)}, bf16[160,256]{0,1:T(8,128)(2,1)S(1)}, u32[]{:S(2)}, u32[]{:S(2)}) collective-permute-start(bf16[160,256]{0,1:T(8,128)(2,1)S(1)} %pad_maximum_fusion.11), channel_id=1, source_target_pairs={{0,8},{8,0},{16,24},{24,16},{32,40},{40,32},{48,56},{56,48},{64,72... | collective-permute-start | bytes 245768 | tf_op jit(solution)/shard_map/ppermute | solution.py:20
  162.9 0.7 copy.225
  163.6 3.7 %collective-permute-done.11 = bf16[160,256]{0,1:T(8,128)(2,1)S(1)} collective-permute-done((bf16[160,256]{0,1:T(8,128)(2,1)S(1)}, bf16[160,256]{0,1:T(8,128)(2,1)S(1)}, u32[]{:S(2)}, u32[]{:S(2)}) %collective-permute-start.11) | collective-permute-done | bytes 81952 | tf_op jit(solution)/shard_map/ppermute | solution.py:20
  167.7 0.7 slice_bitcast_fusion
  168.5 0.7 copy.226
  (112 shorter events, 4.1 us)
Async XLA Ops:
  0.6 5.7 %copy-start.5 = (bf16[128,256]{1,0:T(8,128)(2,1)S(1)}, bf16[128,256]{1,0:T(8,128)(2,1)}, u32[]{:S(2)}) copy-start(bf16[128,256]{1,0:T(8,128)(2,1)} %param.7) | copy-start | bytes 196612
  0.6 5.7 %copy-start.4 = (bf16[128,256]{1,0:T(8,128)(2,1)S(1)}, bf16[128,256]{1,0:T(8,128)(2,1)}, u32[]{:S(2)}) copy-start(bf16[128,256]{1,0:T(8,128)(2,1)} %param.6) | copy-start | bytes 196612
  0.7 2.1 %copy-start.8 = (bf16[32,256]{1,0:T(8,128)(2,1)S(1)}, bf16[32,256]{1,0:T(8,128)(2,1)}, u32[]{:S(2)}) copy-start(bf16[32,256]{1,0:T(8,128)(2,1)} %param.9) | copy-start | bytes 49156
  2.8 6.3 %collective-permute-start = (bf16[160,256]{1,0:T(8,128)(2,1)S(1)}, bf16[160,256]{1,0:T(8,128)(2,1)S(1)}, u32[]{:S(2)}, u32[]{:S(2)}) collective-permute-start(bf16[160,256]{1,0:T(8,128)(2,1)S(1)} %pad_maximum_fusion.13), channel_id=1, source_target_pairs={{0,8},{8,0},{16,24},{24,16},{32,40},{40,32},{48,56},{56,48},{64,72... | collective-permute-start | bytes 245768 | tf_op jit(solution)/shard_map/ppermute | solution.py:20
  9.6 7.4 %collective-permute-start.1 = (bf16[192,256]{1,0:T(8,128)(2,1)S(1)}, bf16[192,256]{1,0:T(8,128)(2,1)S(1)}, u32[]{:S(2)}, u32[]{:S(2)}) collective-permute-start(bf16[192,256]{1,0:T(8,128)(2,1)S(1)} %pad_maximum_fusion.12), channel_id=1, source_target_pairs={{0,16},{16,0},{8,24},{24,8},{32,48},{48,32},{40,56},{56,40},{64,80... | collective-permute-start | bytes 294920 | tf_op jit(solution)/shard_map/ppermute | solution.py:20
  17.7 9.1 %copy-start.7 = (bf16[128,256]{1,0:T(8,128)(2,1)S(1)}, bf16[128,256]{1,0:T(8,128)(2,1)}, u32[]{:S(2)}) copy-start(bf16[128,256]{1,0:T(8,128)(2,1)} %param.8) | copy-start | bytes 196612
  18.0 14.4 %collective-permute-start.2 = (bf16[256,256]{1,0:T(8,128)(2,1)S(1)}, bf16[256,256]{1,0:T(8,128)(2,1)S(1)}, u32[]{:S(2)}, u32[]{:S(2)}) collective-permute-start(bf16[256,256]{1,0:T(8,128)(2,1)S(1)} %pad_maximum_fusion.6), channel_id=1, source_target_pairs={{0,32},{32,0},{8,40},{40,8},{16,48},{48,16},{24,56},{56,24},{64,96... | collective-permute-start | bytes 393224 | tf_op jit(solution)/shard_map/ppermute | solution.py:20
  27.6 30.0 %all-to-all-start.1 = ((bf16[8,128,256]{2,1,0:T(8,128)(2,1)}), bf16[8,128,256]{2,1,0:T(8,128)(2,1)S(1)}, u32[]{:S(2)}, u32[]{:S(2)}) async-start(bf16[8,128,256]{2,1,0:T(8,128)(2,1)} %broadcast_in_dim.17), calls=%async_computation.1 | async-start | bytes 1048576 | tf_op jit(solution)/shard_map/all_to_all | solution.py:31
  32.8 6.7 %collective-permute-start.3 = (bf16[2,64,256]{2,1,0:T(8,128)(2,1)S(1)}, bf16[2,64,256]{2,1,0:T(8,128)(2,1)S(1)}, u32[]{:S(2)}, u32[]{:S(2)}) collective-permute-start(bf16[2,64,256]{2,1,0:T(8,128)(2,1)S(1)} %fusion.78), channel_id=1, source_target_pairs={{0,64},{64,0},{8,72},{72,8},{16,80},{80,16},{24,88},{88,24},{32,96... | collective-permute-start | bytes 196616 | tf_op jit(solution)/shard_map/ppermute | solution.py:20
  39.8 8.9 %collective-permute-start.4 = (bf16[2,64,256]{2,1,0:T(8,128)(2,1)S(1)}, bf16[2,64,256]{2,1,0:T(8,128)(2,1)S(1)}, u32[]{:S(2)}, u32[]{:S(2)}) collective-permute-start(bf16[2,64,256]{2,1,0:T(8,128)(2,1)S(1)} %fusion.79), channel_id=1, source_target_pairs={{0,128},{128,0},{8,136},{136,8},{16,144},{144,16},{24,152},{152,24... | collective-permute-start | bytes 196616 | tf_op jit(solution)/shard_map/ppermute | solution.py:20
  49.1 15.7 %collective-permute-start.5 = (bf16[2,64,256]{2,1,0:T(8,128)(2,1)S(1)}, bf16[2,64,256]{2,1,0:T(8,128)(2,1)S(1)}, u32[]{:S(2)}, u32[]{:S(2)}) collective-permute-start(bf16[2,64,256]{2,1,0:T(8,128)(2,1)S(1)} %fusion.51), channel_id=1, source_target_pairs={{0,256},{256,0},{8,264},{264,8},{16,272},{272,16},{24,280},{280,24... | collective-permute-start | bytes 196616 | tf_op jit(solution)/shard_map/ppermute | solution.py:20
  58.7 32.1 %all-to-all-start = ((bf16[8,256,256]{1,2,0:T(8,128)(2,1)}), bf16[8,256,256]{1,2,0:T(8,128)(2,1)S(1)}, u32[]{:S(2)}, u32[]{:S(2)}) async-start(bf16[8,256,256]{1,2,0:T(8,128)(2,1)} %broadcast_in_dim.16), calls=%async_computation | async-start | bytes 2097152 | tf_op jit(solution)/shard_map/all_to_all | solution.py:31
  63.9 1.5 copy-start.6
  65.5 1.8 %copy-start.2 = (bf16[512,256]{1,0:T(8,128)(2,1)}, bf16[512,256]{1,0:T(8,128)(2,1)S(1)}, u32[]{:S(2)}) copy-start(bf16[512,256]{1,0:T(8,128)(2,1)S(1)} %get-tuple-element.70) | copy-start | bytes 786436
  65.7 1.6 copy-start
  90.8 43.5 %all-to-all-start.2 = ((bf16[8,256,256]{1,2,0:T(8,128)(2,1)}), bf16[8,256,256]{1,2,0:T(8,128)(2,1)S(1)}, u32[]{:S(2)}, u32[]{:S(2)}) async-start(bf16[8,256,256]{1,2,0:T(8,128)(2,1)} %bitcast.132), calls=%async_computation.2 | async-start | bytes 2097152 | tf_op jit(solution)/shard_map/all_to_all | solution.py:153
  94.3 1.0 copy-start.1
  98.5 25.6 %collective-permute-start.6 = (bf16[2,64,256]{2,1,0:T(8,128)(2,1)S(1)}, bf16[2,64,256]{2,1,0:T(8,128)(2,1)S(1)}, u32[]{:S(2)}, u32[]{:S(2)}) collective-permute-start(bf16[2,64,256]{2,1,0:T(8,128)(2,1)S(1)} %fusion.20), channel_id=1, source_target_pairs={{0,256},{256,0},{8,264},{264,8},{16,272},{272,16},{24,280},{280,24... | collective-permute-start | bytes 196616 | tf_op jit(solution)/shard_map/ppermute | solution.py:20
  124.4 7.7 %collective-permute-start.7 = (bf16[2,64,256]{2,1,0:T(8,128)(2,1)S(1)}, bf16[2,64,256]{2,1,0:T(8,128)(2,1)S(1)}, u32[]{:S(2)}, u32[]{:S(2)}) collective-permute-start(bf16[2,64,256]{2,1,0:T(8,128)(2,1)S(1)} %fusion.23), channel_id=1, source_target_pairs={{0,128},{128,0},{8,136},{136,8},{16,144},{144,16},{24,152},{152,24... | collective-permute-start | bytes 196616 | tf_op jit(solution)/shard_map/ppermute | solution.py:20
  132.3 6.2 %collective-permute-start.8 = (bf16[2,64,256]{2,1,0:T(8,128)(2,1)S(1)}, bf16[2,64,256]{2,1,0:T(8,128)(2,1)S(1)}, u32[]{:S(2)}, u32[]{:S(2)}) collective-permute-start(bf16[2,64,256]{2,1,0:T(8,128)(2,1)S(1)} %fusion.26), channel_id=1, source_target_pairs={{0,64},{64,0},{8,72},{72,8},{16,80},{80,16},{24,88},{88,24},{32,96... | collective-permute-start | bytes 196616 | tf_op jit(solution)/shard_map/ppermute | solution.py:20
  138.7 2.1 %copy-start.3 = (bf16[512,256]{1,0:T(8,128)(2,1)S(1)}, bf16[512,256]{1,0:T(8,128)(2,1)}, u32[]{:S(2)}) copy-start(bf16[512,256]{1,0:T(8,128)(2,1)} %copy-done.2) | copy-start | bytes 786436
  138.9 10.9 %collective-permute-start.9 = (bf16[256,256]{0,1:T(8,128)(2,1)S(1)}, bf16[256,256]{0,1:T(8,128)(2,1)S(1)}, u32[]{:S(2)}, u32[]{:S(2)}) collective-permute-start(bf16[256,256]{0,1:T(8,128)(2,1)S(1)} %pad_maximum_fusion.9), channel_id=1, source_target_pairs={{0,32},{32,0},{8,40},{40,8},{16,48},{48,16},{24,56},{56,24},{64,96... | collective-permute-start | bytes 393224 | tf_op jit(solution)/shard_map/ppermute | solution.py:20
  150.5 9.2 %collective-permute-start.10 = (bf16[192,256]{0,1:T(8,128)(2,1)S(1)}, bf16[192,256]{0,1:T(8,128)(2,1)S(1)}, u32[]{:S(2)}, u32[]{:S(2)}) collective-permute-start(bf16[192,256]{0,1:T(8,128)(2,1)S(1)} %pad_maximum_fusion.10), channel_id=1, source_target_pairs={{0,16},{16,0},{8,24},{24,8},{32,48},{48,32},{40,56},{56,40},{64,80... | collective-permute-start | bytes 294920 | tf_op jit(solution)/shard_map/ppermute | solution.py:20
  160.4 6.9 %collective-permute-start.11 = (bf16[160,256]{0,1:T(8,128)(2,1)S(1)}, bf16[160,256]{0,1:T(8,128)(2,1)S(1)}, u32[]{:S(2)}, u32[]{:S(2)}) collective-permute-start(bf16[160,256]{0,1:T(8,128)(2,1)S(1)} %pad_maximum_fusion.11), channel_id=1, source_target_pairs={{0,8},{8,0},{16,24},{24,16},{32,40},{40,32},{48,56},{56,48},{64,72... | collective-permute-start | bytes 245768 | tf_op jit(solution)/shard_map/ppermute | solution.py:20

commit v15 on v13

--- a/solution.py
+++ b/solution.py
@@ -36,9 +36,14 @@
 
 
 def own_rows(running, axes):
-    count = lax.axis_size(axes)
-    parts = running.astype(jnp.bfloat16).reshape(count, running.shape[0] // count, running.shape[1])
-    return jnp.sum(lax.all_to_all(parts, axes, 0, 0, tiled=True).astype(jnp.float32), axis=0)
+    major, minor = axes
+    n_major = lax.axis_size(major)
+    n_minor = lax.axis_size(minor)
+    rows = running.shape[0] // (n_major * n_minor)
+    parts = running.astype(jnp.bfloat16).reshape(n_major, n_minor, rows, running.shape[1])
+    parts = jnp.moveaxis(parts, 1, 0)
+    summed = jnp.sum(lax.all_to_all(parts, minor, 0, 0, tiled=True).astype(jnp.float32), axis=0)
+    return jnp.sum(lax.all_to_all(summed.astype(jnp.bfloat16), major, 0, 0, tiled=True).astype(jnp.float32), axis=0)
 
 
 def pair_mean(table):

time: 163 us -> 176 us (1.080)
  the two profiles are of different devices: /device:TPU:6 before, /device:TPU:8 now
where the time goes in v15:
time: 176 us; the launch traced here: 175 us
  waiting for transfers between devices  89.1 us (51%)
  starting transfers between devices  64.6 us (37%)
  local copies, waits for them, and re-layouts  12.4 us (7%)
  other arithmetic  4.15 us (2%)
  matrix products  3.41 us (2%)
    ppermute x12, waiting for transfers between devices, from_partner(): return lax.ppermute(block, axis, route)  81 us
    ppermute x12, starting transfers between devices, from_partner(): return lax.ppermute(block, axis, route)  43.6 us
    all_to_all x2, starting transfers between devices, from_everyone(): return lax.all_to_all(copies, axis, split_axis=0, concat_axis=0, tiled=True)  11.9 us
    all_to_all x1, waiting for transfers between devices, own_rows(): lax.all_to_all(summed.astype(jnp.bfloat16), major, 0, 0, tiled=True)  8.06 us
    all_to_all x1, starting transfers between devices, own_rows(): lax.all_to_all(parts, minor, 0, 0, tiled=True).astype(jnp.float32)  5.78 us
    unnamed x26, local copies, waits for them, and re-layouts  4.28 us
  transfers between devices with their start and end apart: 16, of which 11 were waited for; matrix products, arithmetic and copies ran while one was open for 6% of the time, Pallas kernels for 0%

profile of v15, /device:TPU:8, one launch (start us, length us, event | category | flops | bytes accessed | tf_op | source)
XLA Modules:
  0.0 175.1 jit_solution(5314121698310285201)
XLA Ops:
  0.6 0.9 reshape.226
  1.7 0.7 copy-done.4
  2.6 0.7 copy-done.8
  3.3 7.9 %collective-permute-start = (bf16[160,256]{1,0:T(8,128)(2,1)S(1)}, bf16[160,256]{1,0:T(8,128)(2,1)S(1)}, u32[]{:S(2)}, u32[]{:S(2)}) collective-permute-start(bf16[160,256]{1,0:T(8,128)(2,1)S(1)} %pad_maximum_fusion.10), channel_id=1, source_target_pairs={{0,8},{8,0},{16,24},{24,16},{32,40},{40,32},{48,56},{56,48},{64,72... | collective-permute-start | bytes 245768 | tf_op jit(solution)/shard_map/ppermute | solution.py:20
  11.2 2.9 %collective-permute-done = bf16[160,256]{1,0:T(8,128)(2,1)S(1)} collective-permute-done((bf16[160,256]{1,0:T(8,128)(2,1)S(1)}, bf16[160,256]{1,0:T(8,128)(2,1)S(1)}, u32[]{:S(2)}, u32[]{:S(2)}) %collective-permute-start) | collective-permute-done | bytes 81952 | tf_op jit(solution)/shard_map/ppermute | solution.py:20
  14.2 0.2 copy.219
  14.5 1.9 %collective-permute-start.1 = (bf16[192,256]{1,0:T(8,128)(2,1)S(1)}, bf16[192,256]{1,0:T(8,128)(2,1)S(1)}, u32[]{:S(2)}, u32[]{:S(2)}) collective-permute-start(bf16[192,256]{1,0:T(8,128)(2,1)S(1)} %pad_maximum_fusion.9), channel_id=1, source_target_pairs={{0,16},{16,0},{8,24},{24,8},{32,48},{48,32},{40,56},{56,40},{64,80... | collective-permute-start | bytes 294920 | tf_op jit(solution)/shard_map/ppermute | solution.py:20
  16.5 5.5 %collective-permute-done.1 = bf16[192,256]{1,0:T(8,128)(2,1)S(1)} collective-permute-done((bf16[192,256]{1,0:T(8,128)(2,1)S(1)}, bf16[192,256]{1,0:T(8,128)(2,1)S(1)}, u32[]{:S(2)}, u32[]{:S(2)}) %collective-permute-start.1) | collective-permute-done | bytes 98336 | tf_op jit(solution)/shard_map/ppermute | solution.py:20
  22.0 0.2 copy.222
  22.4 2.6 %collective-permute-start.2 = (bf16[256,256]{1,0:T(8,128)(2,1)S(1)}, bf16[256,256]{1,0:T(8,128)(2,1)S(1)}, u32[]{:S(2)}, u32[]{:S(2)}) collective-permute-start(bf16[256,256]{1,0:T(8,128)(2,1)S(1)} %pad_maximum_fusion.6), channel_id=1, source_target_pairs={{0,32},{32,0},{8,40},{40,8},{16,48},{48,16},{24,56},{56,24},{64,96... | collective-permute-start | bytes 393224 | tf_op jit(solution)/shard_map/ppermute | solution.py:20
  25.0 0.8 broadcast_in_dim.17
  25.8 4.3 %all-to-all-start.1 = ((bf16[8,128,256]{2,1,0:T(8,128)(2,1)}), bf16[8,128,256]{2,1,0:T(8,128)(2,1)S(1)}, u32[]{:S(2)}, u32[]{:S(2)}) async-start(bf16[8,128,256]{2,1,0:T(8,128)(2,1)} %broadcast_in_dim.17), calls=%async_computation.1 | async-start | bytes 1048576 | tf_op jit(solution)/shard_map/all_to_all | solution.py:31
  30.1 3.9 %collective-permute-done.2 = bf16[256,256]{1,0:T(8,128)(2,1)S(1)} collective-permute-done((bf16[256,256]{1,0:T(8,128)(2,1)S(1)}, bf16[256,256]{1,0:T(8,128)(2,1)S(1)}, u32[]{:S(2)}, u32[]{:S(2)}) %collective-permute-start.2) | collective-permute-done | bytes 131104 | tf_op jit(solution)/shard_map/ppermute | solution.py:20
  34.1 0.2 copy.225
  34.4 1.9 %collective-permute-start.3 = (bf16[2,64,256]{2,1,0:T(8,128)(2,1)S(1)}, bf16[2,64,256]{2,1,0:T(8,128)(2,1)S(1)}, u32[]{:S(2)}, u32[]{:S(2)}) collective-permute-start(bf16[2,64,256]{2,1,0:T(8,128)(2,1)S(1)} %fusion.77), channel_id=1, source_target_pairs={{0,64},{64,0},{8,72},{72,8},{16,80},{80,16},{24,88},{88,24},{32,96... | collective-permute-start | bytes 196616 | tf_op jit(solution)/shard_map/ppermute | solution.py:20
  36.4 4.1 %collective-permute-done.3 = bf16[2,64,256]{2,1,0:T(8,128)(2,1)S(1)} collective-permute-done((bf16[2,64,256]{2,1,0:T(8,128)(2,1)S(1)}, bf16[2,64,256]{2,1,0:T(8,128)(2,1)S(1)}, u32[]{:S(2)}, u32[]{:S(2)}) %collective-permute-start.3) | collective-permute-done | bytes 65568 | tf_op jit(solution)/shard_map/ppermute | solution.py:20
  40.6 0.2 copy.228
  40.9 3.1 %collective-permute-start.4 = (bf16[2,64,256]{2,1,0:T(8,128)(2,1)S(1)}, bf16[2,64,256]{2,1,0:T(8,128)(2,1)S(1)}, u32[]{:S(2)}, u32[]{:S(2)}) collective-permute-start(bf16[2,64,256]{2,1,0:T(8,128)(2,1)S(1)} %fusion.78), channel_id=1, source_target_pairs={{0,128},{128,0},{8,136},{136,8},{16,144},{144,16},{24,152},{152,24... | collective-permute-start | bytes 196616 | tf_op jit(solution)/shard_map/ppermute | solution.py:20
  44.0 4.1 %collective-permute-done.4 = bf16[2,64,256]{2,1,0:T(8,128)(2,1)S(1)} collective-permute-done((bf16[2,64,256]{2,1,0:T(8,128)(2,1)S(1)}, bf16[2,64,256]{2,1,0:T(8,128)(2,1)S(1)}, u32[]{:S(2)}, u32[]{:S(2)}) %collective-permute-start.4) | collective-permute-done | bytes 65568 | tf_op jit(solution)/shard_map/ppermute | solution.py:20
  48.1 0.2 copy.231
  48.4 1.0 broadcast_in_dim.16
  49.4 7.6 %all-to-all-start = ((bf16[8,256,256]{1,2,0:T(8,128)(2,1)}), bf16[8,256,256]{1,2,0:T(8,128)(2,1)S(1)}, u32[]{:S(2)}, u32[]{:S(2)}) async-start(bf16[8,256,256]{1,2,0:T(8,128)(2,1)} %broadcast_in_dim.16), calls=%async_computation | async-start | bytes 2097152 | tf_op jit(solution)/shard_map/all_to_all | solution.py:31
  57.1 7.8 %collective-permute-start.5 = (bf16[2,64,256]{2,1,0:T(8,128)(2,1)S(1)}, bf16[2,64,256]{2,1,0:T(8,128)(2,1)S(1)}, u32[]{:S(2)}, u32[]{:S(2)}) collective-permute-start(bf16[2,64,256]{2,1,0:T(8,128)(2,1)S(1)} %fusion.51), channel_id=1, source_target_pairs={{0,256},{256,0},{8,264},{264,8},{16,272},{272,16},{24,280},{280,24... | collective-permute-start | bytes 196616 | tf_op jit(solution)/shard_map/ppermute | solution.py:20
  64.9 0.3 copy.260
  65.2 22.8 %collective-permute-done.5 = bf16[2,64,256]{2,1,0:T(8,128)(2,1)S(1)} collective-permute-done((bf16[2,64,256]{2,1,0:T(8,128)(2,1)S(1)}, bf16[2,64,256]{2,1,0:T(8,128)(2,1)S(1)}, u32[]{:S(2)}, u32[]{:S(2)}) %collective-permute-start.5) | collective-permute-done | bytes 65568 | tf_op jit(solution)/shard_map/ppermute | solution.py:20
  88.1 0.8 copy-done.6
  88.9 0.2 fusion.96
  89.2 0.2 fusion.97
  89.5 0.2 convolution_convert_fusion.2
  89.8 0.4 fusion.1
  90.2 0.2 fusion.5
  90.4 0.2 fusion.53
  90.6 0.2 fusion.8
  90.9 0.2 fusion.52
  91.2 0.2 fusion.68
  91.3 0.5 copy-done
  91.9 0.2 fusion.71
  92.2 1.9 %collective-permute-start.6 = (bf16[2,64,256]{2,1,0:T(8,128)(2,1)S(1)}, bf16[2,64,256]{2,1,0:T(8,128)(2,1)S(1)}, u32[]{:S(2)}, u32[]{:S(2)}) collective-permute-start(bf16[2,64,256]{2,1,0:T(8,128)(2,1)S(1)} %fusion.20), channel_id=1, source_target_pairs={{0,256},{256,0},{8,264},{264,8},{16,272},{272,16},{24,280},{280,24... | collective-permute-start | bytes 196616 | tf_op jit(solution)/shard_map/ppermute | solution.py:20
  94.1 0.2 convolution_convert_fusion.3
  94.3 8.8 %collective-permute-done.6 = bf16[2,64,256]{2,1,0:T(8,128)(2,1)S(1)} collective-permute-done((bf16[2,64,256]{2,1,0:T(8,128)(2,1)S(1)}, bf16[2,64,256]{2,1,0:T(8,128)(2,1)S(1)}, u32[]{:S(2)}, u32[]{:S(2)}) %collective-permute-start.6) | collective-permute-done | bytes 65568 | tf_op jit(solution)/shard_map/ppermute | solution.py:20
  103.4 1.9 %collective-permute-start.7 = (bf16[2,64,256]{2,1,0:T(8,128)(2,1)S(1)}, bf16[2,64,256]{2,1,0:T(8,128)(2,1)S(1)}, u32[]{:S(2)}, u32[]{:S(2)}) collective-permute-start(bf16[2,64,256]{2,1,0:T(8,128)(2,1)S(1)} %fusion.23), channel_id=1, source_target_pairs={{0,128},{128,0},{8,136},{136,8},{16,144},{144,16},{24,152},{152,24... | collective-permute-start | bytes 196616 | tf_op jit(solution)/shard_map/ppermute | solution.py:20
  105.4 0.4 convolution_bitcast_fusion
  105.8 4.7 %collective-permute-done.7 = bf16[2,64,256]{2,1,0:T(8,128)(2,1)S(1)} collective-permute-done((bf16[2,64,256]{2,1,0:T(8,128)(2,1)S(1)}, bf16[2,64,256]{2,1,0:T(8,128)(2,1)S(1)}, u32[]{:S(2)}, u32[]{:S(2)}) %collective-permute-start.7) | collective-permute-done | bytes 65568 | tf_op jit(solution)/shard_map/ppermute | solution.py:20
  110.7 0.7 fusion.26
  111.4 1.9 %collective-permute-start.8 = (bf16[2,64,256]{2,1,0:T(8,128)(2,1)}, bf16[2,64,256]{2,1,0:T(8,128)(2,1)}, u32[]{:S(2)}, u32[]{:S(2)}) collective-permute-start(bf16[2,64,256]{2,1,0:T(8,128)(2,1)} %fusion.26), channel_id=1, source_target_pairs={{0,64},{64,0},{8,72},{72,8},{16,80},{80,16},{24,88},{88,24},{32,96... | collective-permute-start | bytes 196616 | tf_op jit(solution)/shard_map/ppermute | solution.py:20
  113.3 0.7 copy.263
  114.1 0.5 copy.261
  114.6 1.1 copy.262
  115.7 5.8 %all-to-all-start.2 = ((bf16[8,8,32,256]{3,2,1,0:T(8,128)(2,1)}), bf16[8,8,32,256]{3,2,1,0:T(8,128)(2,1)S(1)}, u32[]{:S(2)}, u32[]{:S(2)}) async-start(bf16[8,8,32,256]{3,2,1,0:T(8,128)(2,1)} %copy.262), calls=%async_computation.2 | async-start | bytes 2097152 | tf_op jit(solution)/shard_map/all_to_all | solution.py:45
  121.4 0.9 add_multiply_fusion.3
  122.6 6.5 %collective-permute-start.9 = (bf16[2,64,256]{2,1,0:T(8,128)(2,1)S(1)}, bf16[2,64,256]{2,1,0:T(8,128)(2,1)S(1)}, u32[]{:S(2)}, u32[]{:S(2)}) collective-permute-start(bf16[2,64,256]{2,1,0:T(8,128)(2,1)S(1)} %fusion.29), channel_id=1, source_target_pairs={{0,32},{32,0},{8,40},{40,8},{16,48},{48,16},{24,56},{56,24},{64,96... | collective-permute-start | bytes 196616 | tf_op jit(solution)/shard_map/ppermute | solution.py:20
  129.2 0.2 convolution_convert_fusion
  129.4 19.3 %collective-permute-done.9 = bf16[2,64,256]{2,1,0:T(8,128)(2,1)S(1)} collective-permute-done((bf16[2,64,256]{2,1,0:T(8,128)(2,1)S(1)}, bf16[2,64,256]{2,1,0:T(8,128)(2,1)S(1)}, u32[]{:S(2)}, u32[]{:S(2)}) %collective-permute-start.9) | collective-permute-done | bytes 65568 | tf_op jit(solution)/shard_map/ppermute | solution.py:20
  148.8 0.1 copy.252
  149.0 2.3 %collective-permute-start.10 = (bf16[2,64,256]{2,1,0:T(8,128)(2,1)S(1)}, bf16[2,64,256]{2,1,0:T(8,128)(2,1)S(1)}, u32[]{:S(2)}, u32[]{:S(2)}) collective-permute-start(bf16[2,64,256]{2,1,0:T(8,128)(2,1)S(1)} %fusion.18), channel_id=1, source_target_pairs={{0,16},{16,0},{8,24},{24,8},{32,48},{48,32},{40,56},{56,40},{64,80... | collective-permute-start | bytes 196616 | tf_op jit(solution)/shard_map/ppermute | solution.py:20
  151.4 0.2 convolution_convert_fusion.1
  151.6 4.9 %collective-permute-done.10 = bf16[2,64,256]{2,1,0:T(8,128)(2,1)S(1)} collective-permute-done((bf16[2,64,256]{2,1,0:T(8,128)(2,1)S(1)}, bf16[2,64,256]{2,1,0:T(8,128)(2,1)S(1)}, u32[]{:S(2)}, u32[]{:S(2)}) %collective-permute-start.10) | collective-permute-done | bytes 65568 | tf_op jit(solution)/shard_map/ppermute | solution.py:20
  156.8 3.7 %collective-permute-start.11 = (bf16[2,64,256]{2,1,0:T(8,128)(2,1)S(1)}, bf16[2,64,256]{2,1,0:T(8,128)(2,1)S(1)}, u32[]{:S(2)}, u32[]{:S(2)}) collective-permute-start(bf16[2,64,256]{2,1,0:T(8,128)(2,1)S(1)} %fusion.31), channel_id=1, source_target_pairs={{0,8},{8,0},{16,24},{24,16},{32,40},{40,32},{48,56},{56,48},{64,72... | collective-permute-start | bytes 196616 | tf_op jit(solution)/shard_map/ppermute | solution.py:20
  160.5 0.7 copy.264
  161.3 0.8 reduce_sum.61
  162.1 3.4 %all-to-all-start.3 = ((bf16[8,32,256]{2,1,0:T(8,128)(2,1)}), bf16[8,32,256]{2,1,0:T(8,128)(2,1)S(1)}, u32[]{:S(2)}, u32[]{:S(2)}) async-start(bf16[8,32,256]{2,1,0:T(8,128)(2,1)} %reduce_sum.61), calls=%async_computation.3 | async-start | bytes 262144 | tf_op jit(solution)/shard_map/all_to_all | solution.py:46
  165.8 0.7 slice_bitcast_fusion
  166.4 8.1 %all-to-all-done.3 = bf16[8,32,256]{2,1,0:T(8,128)(2,1)S(1)} async-done(((bf16[8,32,256]{2,1,0:T(8,128)(2,1)}), bf16[8,32,256]{2,1,0:T(8,128)(2,1)S(1)}, u32[]{:S(2)}, u32[]{:S(2)}) %all-to-all-start.3) | async-done | bytes 131104 | tf_op jit(solution)/shard_map/all_to_all | solution.py:46
  174.5 0.6 convert_reduce_fusion
  (97 shorter events, 2.9 us)
Async XLA Ops:
  1.5 0.8 copy-start.4
  2.6 0.7 copy-start.8
  3.3 7.9 %copy-start.5 = (bf16[128,256]{1,0:T(8,128)(2,1)S(1)}, bf16[128,256]{1,0:T(8,128)(2,1)}, u32[]{:S(2)}) copy-start(bf16[128,256]{1,0:T(8,128)(2,1)} %param.7) | copy-start | bytes 196612
  3.3 10.8 %collective-permute-start = (bf16[160,256]{1,0:T(8,128)(2,1)S(1)}, bf16[160,256]{1,0:T(8,128)(2,1)S(1)}, u32[]{:S(2)}, u32[]{:S(2)}) collective-permute-start(bf16[160,256]{1,0:T(8,128)(2,1)S(1)} %pad_maximum_fusion.10), channel_id=1, source_target_pairs={{0,8},{8,0},{16,24},{24,16},{32,40},{40,32},{48,56},{56,48},{64,72... | collective-permute-start | bytes 245768 | tf_op jit(solution)/shard_map/ppermute | solution.py:20
  14.5 7.4 %collective-permute-start.1 = (bf16[192,256]{1,0:T(8,128)(2,1)S(1)}, bf16[192,256]{1,0:T(8,128)(2,1)S(1)}, u32[]{:S(2)}, u32[]{:S(2)}) collective-permute-start(bf16[192,256]{1,0:T(8,128)(2,1)S(1)} %pad_maximum_fusion.9), channel_id=1, source_target_pairs={{0,16},{16,0},{8,24},{24,8},{32,48},{48,32},{40,56},{56,40},{64,80... | collective-permute-start | bytes 294920 | tf_op jit(solution)/shard_map/ppermute | solution.py:20
  22.3 2.6 %copy-start.7 = (bf16[128,256]{1,0:T(8,128)(2,1)S(1)}, bf16[128,256]{1,0:T(8,128)(2,1)}, u32[]{:S(2)}) copy-start(bf16[128,256]{1,0:T(8,128)(2,1)} %param.8) | copy-start | bytes 196612
  22.4 11.6 %collective-permute-start.2 = (bf16[256,256]{1,0:T(8,128)(2,1)S(1)}, bf16[256,256]{1,0:T(8,128)(2,1)S(1)}, u32[]{:S(2)}, u32[]{:S(2)}) collective-permute-start(bf16[256,256]{1,0:T(8,128)(2,1)S(1)} %pad_maximum_fusion.6), channel_id=1, source_target_pairs={{0,32},{32,0},{8,40},{40,8},{16,48},{48,16},{24,56},{56,24},{64,96... | collective-permute-start | bytes 393224 | tf_op jit(solution)/shard_map/ppermute | solution.py:20
  25.8 22.5 %all-to-all-start.1 = ((bf16[8,128,256]{2,1,0:T(8,128)(2,1)}), bf16[8,128,256]{2,1,0:T(8,128)(2,1)S(1)}, u32[]{:S(2)}, u32[]{:S(2)}) async-start(bf16[8,128,256]{2,1,0:T(8,128)(2,1)} %broadcast_in_dim.17), calls=%async_computation.1 | async-start | bytes 1048576 | tf_op jit(solution)/shard_map/all_to_all | solution.py:31
  34.4 6.2 %collective-permute-start.3 = (bf16[2,64,256]{2,1,0:T(8,128)(2,1)S(1)}, bf16[2,64,256]{2,1,0:T(8,128)(2,1)S(1)}, u32[]{:S(2)}, u32[]{:S(2)}) collective-permute-start(bf16[2,64,256]{2,1,0:T(8,128)(2,1)S(1)} %fusion.77), channel_id=1, source_target_pairs={{0,64},{64,0},{8,72},{72,8},{16,80},{80,16},{24,88},{88,24},{32,96... | collective-permute-start | bytes 196616 | tf_op jit(solution)/shard_map/ppermute | solution.py:20
  40.9 7.2 %collective-permute-start.4 = (bf16[2,64,256]{2,1,0:T(8,128)(2,1)S(1)}, bf16[2,64,256]{2,1,0:T(8,128)(2,1)S(1)}, u32[]{:S(2)}, u32[]{:S(2)}) collective-permute-start(bf16[2,64,256]{2,1,0:T(8,128)(2,1)S(1)} %fusion.78), channel_id=1, source_target_pairs={{0,128},{128,0},{8,136},{136,8},{16,144},{144,16},{24,152},{152,24... | collective-permute-start | bytes 196616 | tf_op jit(solution)/shard_map/ppermute | solution.py:20
  49.4 40.4 %all-to-all-start = ((bf16[8,256,256]{1,2,0:T(8,128)(2,1)}), bf16[8,256,256]{1,2,0:T(8,128)(2,1)S(1)}, u32[]{:S(2)}, u32[]{:S(2)}) async-start(bf16[8,256,256]{1,2,0:T(8,128)(2,1)} %broadcast_in_dim.16), calls=%async_computation | async-start | bytes 2097152 | tf_op jit(solution)/shard_map/all_to_all | solution.py:31
  57.1 31.0 %collective-permute-start.5 = (bf16[2,64,256]{2,1,0:T(8,128)(2,1)S(1)}, bf16[2,64,256]{2,1,0:T(8,128)(2,1)S(1)}, u32[]{:S(2)}, u32[]{:S(2)}) collective-permute-start(bf16[2,64,256]{2,1,0:T(8,128)(2,1)S(1)} %fusion.51), channel_id=1, source_target_pairs={{0,256},{256,0},{8,264},{264,8},{16,272},{272,16},{24,280},{280,24... | collective-permute-start | bytes 196616 | tf_op jit(solution)/shard_map/ppermute | solution.py:20
  88.0 0.8 copy-start.6
  88.0 1.2 copy-start.2
  91.1 0.7 copy-start
  92.2 11.0 %collective-permute-start.6 = (bf16[2,64,256]{2,1,0:T(8,128)(2,1)S(1)}, bf16[2,64,256]{2,1,0:T(8,128)(2,1)S(1)}, u32[]{:S(2)}, u32[]{:S(2)}) collective-permute-start(bf16[2,64,256]{2,1,0:T(8,128)(2,1)S(1)} %fusion.20), channel_id=1, source_target_pairs={{0,256},{256,0},{8,264},{264,8},{16,272},{272,16},{24,280},{280,24... | collective-permute-start | bytes 196616 | tf_op jit(solution)/shard_map/ppermute | solution.py:20
  103.4 7.1 %collective-permute-start.7 = (bf16[2,64,256]{2,1,0:T(8,128)(2,1)S(1)}, bf16[2,64,256]{2,1,0:T(8,128)(2,1)S(1)}, u32[]{:S(2)}, u32[]{:S(2)}) collective-permute-start(bf16[2,64,256]{2,1,0:T(8,128)(2,1)S(1)} %fusion.23), channel_id=1, source_target_pairs={{0,128},{128,0},{8,136},{136,8},{16,144},{144,16},{24,152},{152,24... | collective-permute-start | bytes 196616 | tf_op jit(solution)/shard_map/ppermute | solution.py:20
  111.4 10.0 %collective-permute-start.8 = (bf16[2,64,256]{2,1,0:T(8,128)(2,1)}, bf16[2,64,256]{2,1,0:T(8,128)(2,1)}, u32[]{:S(2)}, u32[]{:S(2)}) collective-permute-start(bf16[2,64,256]{2,1,0:T(8,128)(2,1)} %fusion.26), channel_id=1, source_target_pairs={{0,64},{64,0},{8,72},{72,8},{16,80},{80,16},{24,88},{88,24},{32,96... | collective-permute-start | bytes 196616 | tf_op jit(solution)/shard_map/ppermute | solution.py:20
  115.7 45.6 %all-to-all-start.2 = ((bf16[8,8,32,256]{3,2,1,0:T(8,128)(2,1)}), bf16[8,8,32,256]{3,2,1,0:T(8,128)(2,1)S(1)}, u32[]{:S(2)}, u32[]{:S(2)}) async-start(bf16[8,8,32,256]{3,2,1,0:T(8,128)(2,1)} %copy.262), calls=%async_computation.2 | async-start | bytes 2097152 | tf_op jit(solution)/shard_map/all_to_all | solution.py:45
  122.5 6.6 %copy-start.1 = (bf16[128,512]{0,1:T(8,128)(2,1)S(1)}, bf16[128,512]{0,1:T(8,128)(2,1)}, u32[]{:S(2)}) copy-start(bf16[128,512]{0,1:T(8,128)(2,1)} %copy-done) | copy-start | bytes 393220
  122.5 6.6 %copy-start.3 = (bf16[512,256]{1,0:T(8,128)(2,1)S(1)}, bf16[512,256]{1,0:T(8,128)(2,1)}, u32[]{:S(2)}) copy-start(bf16[512,256]{1,0:T(8,128)(2,1)} %copy-done.2) | copy-start | bytes 786436
  122.6 26.1 %collective-permute-start.9 = (bf16[2,64,256]{2,1,0:T(8,128)(2,1)S(1)}, bf16[2,64,256]{2,1,0:T(8,128)(2,1)S(1)}, u32[]{:S(2)}, u32[]{:S(2)}) collective-permute-start(bf16[2,64,256]{2,1,0:T(8,128)(2,1)S(1)} %fusion.29), channel_id=1, source_target_pairs={{0,32},{32,0},{8,40},{40,8},{16,48},{48,16},{24,56},{56,24},{64,96... | collective-permute-start | bytes 196616 | tf_op jit(solution)/shard_map/ppermute | solution.py:20
  149.0 7.5 %collective-permute-start.10 = (bf16[2,64,256]{2,1,0:T(8,128)(2,1)S(1)}, bf16[2,64,256]{2,1,0:T(8,128)(2,1)S(1)}, u32[]{:S(2)}, u32[]{:S(2)}) collective-permute-start(bf16[2,64,256]{2,1,0:T(8,128)(2,1)S(1)} %fusion.18), channel_id=1, source_target_pairs={{0,16},{16,0},{8,24},{24,8},{32,48},{48,32},{40,56},{56,40},{64,80... | collective-permute-start | bytes 196616 | tf_op jit(solution)/shard_map/ppermute | solution.py:20
  156.8 8.7 %collective-permute-start.11 = (bf16[2,64,256]{2,1,0:T(8,128)(2,1)S(1)}, bf16[2,64,256]{2,1,0:T(8,128)(2,1)S(1)}, u32[]{:S(2)}, u32[]{:S(2)}) collective-permute-start(bf16[2,64,256]{2,1,0:T(8,128)(2,1)S(1)} %fusion.31), channel_id=1, source_target_pairs={{0,8},{8,0},{16,24},{24,16},{32,40},{40,32},{48,56},{56,48},{64,72... | collective-permute-start | bytes 196616 | tf_op jit(solution)/shard_map/ppermute | solution.py:20
  162.1 12.4 %all-to-all-start.3 = ((bf16[8,32,256]{2,1,0:T(8,128)(2,1)}), bf16[8,32,256]{2,1,0:T(8,128)(2,1)S(1)}, u32[]{:S(2)}, u32[]{:S(2)}) async-start(bf16[8,32,256]{2,1,0:T(8,128)(2,1)} %reduce_sum.61), calls=%async_computation.3 | async-start | bytes 262144 | tf_op jit(solution)/shard_map/all_to_all | solution.py:46
